TPU v7x, 32 devices: a whole 2x2x4 slice. The times are simulated.
32 devices in a mesh: row: 8 (over y, x, core), col: 4 (over z).
Axes of the slice: x: 2, y: 2, z: 4, core: 2. Of those that a mesh axis runs over, the one named last changes fastest.
Arguments:
- features: bfloat16 [6144, 256], P(('col', 'row')), may hold values from -6 to 6
- edge_tiles: bfloat16 [8, 4, 12, 256, 256], P('row', 'col'), may hold values from 0.006225586 to 0.0625
- tile_rows: int32 [8, 4, 12], P('row', 'col'), may hold values from 0 to 2, as said below
- tile_cols: int32 [8, 4, 12], P('row', 'col'), may hold values from 0 to 5
- tile_count: int32 [8, 4], P('row', 'col'), may hold values from 3 to 12, as said below
- weight: bfloat16 [256, 256], replicated, may hold values from -0.375 to 0.375
- cotangent: bfloat16 [6144, 256], P(('row', 'col')), may hold values from -6 to 6
Outputs:
- activated: bfloat16 [6144, 256], P(('row', 'col'))
- feature_grad: bfloat16 [6144, 256], P(('col', 'row'))
Inputs may be any that keep to these rules, and one draw needn't show every extreme that they name: Within one device the pairs (tile_rows, tile_cols) of all 12 slots are distinct. Slots at or past tile_count hold no edges of the graph.
All inputs are finite; a program needn't handle non-finite values.
Results may differ from a plain program's by a relative error of at most 0.006.
Values may be sent and summed in bfloat16 or wider, within the bound.
No kernel may reach another device: no remote copies, remote signals or barrier semaphores. Data moves between devices by JAX's collectives and lax.ppermute only.
A program may use at most 64 MiB of HBM per device.

v0:
```python
import jax
import jax.numpy as jnp
from jax import lax
from jax.sharding import PartitionSpec as P


def silu_slope(mixed):
    sigma = jax.nn.sigmoid(mixed)
    return sigma * (1.0 + mixed * (1.0 - sigma))


def dense_layer(summed, grad_rows, weight):
    aggregated = summed.astype(jnp.bfloat16)
    mixed = jnp.dot(aggregated, weight, preferred_element_type=jnp.float32)
    activated = jax.nn.silu(mixed).astype(jnp.bfloat16)
    scaled = (grad_rows.astype(jnp.float32) * silu_slope(mixed)).astype(jnp.bfloat16)
    pulled = jnp.dot(scaled, weight.T, preferred_element_type=jnp.float32).astype(jnp.bfloat16)
    return (activated, pulled)


def place(results, targets, occupied, count):
    masked = results * occupied[:, None, None]
    return jax.ops.segment_sum(masked, targets, num_segments=count)


def on_device(features, edge_tiles, tile_rows, tile_cols, tile_count, weight, cotangent):
    blocks = edge_tiles[0, 0]
    row_slots = tile_rows[0, 0]
    col_slots = tile_cols[0, 0]
    filled = tile_count[0, 0]
    slot_total = blocks.shape[0]
    tile_size = blocks.shape[1]
    feat_width = features.shape[1]
    own_rows = features.shape[0]
    row_tiles = own_rows * lax.axis_size("col") // tile_size
    col_tiles = own_rows * lax.axis_size("row") // tile_size
    occupied = (jnp.arange(slot_total, dtype=jnp.int32) < filled).astype(jnp.float32)
    gathered = lax.all_gather(features, "row", axis=0, tiled=True)
    picked = gathered.reshape(col_tiles, tile_size, feat_width)[col_slots]
    products = jnp.einsum("kij,kjf->kif", blocks, picked, preferred_element_type=jnp.float32)
    partial_value = place(products, row_slots, occupied, row_tiles).reshape(
        row_tiles * tile_size, feat_width
    )
    own_sums = lax.psum_scatter(partial_value, "col", scatter_dimension=0, tiled=True)
    activated, pulled_own = dense_layer(own_sums, cotangent, weight)
    pulled_block = lax.all_gather(pulled_own, "col", axis=0, tiled=True)
    chosen = pulled_block.reshape(row_tiles, tile_size, feat_width)[row_slots]
    flipped = jnp.einsum("kij,kif->kjf", blocks, chosen, preferred_element_type=jnp.float32)
    partial_grad = place(flipped, col_slots, occupied, col_tiles).reshape(
        col_tiles * tile_size, feat_width
    )
    feature_grad = lax.psum_scatter(partial_grad, "row", scatter_dimension=0, tiled=True).astype(
        jnp.bfloat16
    )
    return (activated, feature_grad)


def solution(mesh):
    return jax.shard_map(
        on_device,
        mesh=mesh,
        in_specs=(
            P(("col", "row"), None),
            P("row", "col", None, None, None),
            P("row", "col", None),
            P("row", "col", None),
            P("row", "col"),
            P(),
            P(("row", "col"), None),
        ),
        out_specs=(P(("row", "col"), None), P(("col", "row"), None)),
        check_vma=False,
    )
```

profile of v0, /device:TPU:0, one launch (start us, length us, event | category | flops | bytes accessed | tf_op | source)
XLA Modules:
  0.0 138.2 jit_solution(2664074008607419204)
XLA Ops:
  7.2 0.0 copy-start
  7.2 0.0 reduce-scatter.3.cloned.1.call-start
  8.0 12.2 %all_gather.6 = bf16[1536,256]{1,0:T(8,128)(2,1)S(1)} all-gather(bf16[192,256]{1,0:T(8,128)(2,1)} %param.7), channel_id=1, replica_groups=mesh['row'=8,'col'=4] {'row'}, dimensions={0}, use_global_device_ids=true | all-gather | bytes 884736 | tf_op jit(solution)/shard_map/all_gather | solution.py:38
  20.2 0.7 fusion.4
  20.9 1.8 %gather_fusion = bf16[12,256,256]{2,1,0:T(8,128)(2,1)} fusion(bf16[6,256,256]{2,1,0:T(8,128)(2,1)S(1)} %bitcast.32, s32[1024]{0:T(1024)S(1)} %pad_clamp_fusion.1), kind=kCustom, calls=%fused_computation | custom fusion | bytes 3145776 | tf_op jit(solution)/shard_map/gather | solution.py:39
  22.7 0.0 copy-done
  22.7 3.8 %multiply_bitcast_fusion.1 = f32[12,256,256]{1,2,0:T(8,128)} fusion(bf16[12,256,256]{2,1,0:T(8,128)(2,1)} %gather_fusion, bf16[1,1,12,256,256]{4,3,2,1,0:T(8,128)(2,1)S(1)} %copy-done, f32[12]{0:T(128)S(1)} %compare_convert_fusion), kind=kOutput, calls=%fused_computation.5 | convolution fusion | flops 403439616 | bytes 6291504 | tf_op jit(solution)/shard_map/kij,kjf->kif/dot_general | solution.py:40
  26.6 3.6 %copy.12 = f32[12,256,256]{2,1,0:T(8,128)} copy(f32[12,256,256]{1,2,0:T(8,128)} %multiply_bitcast_fusion.1) | data formatting | bytes 6291456 | tf_op jit(solution)/shard_map/mul | solution.py:22
  30.1 0.1 broadcast_in_dim.4
  30.2 0.0 copy-done.3
  30.2 0.0 copy-start.5
  30.2 5.7 %scatter_fusion = f32[3,256,256]{2,1,0:T(8,128)S(1)} fusion(f32[3,256,256]{2,1,0:T(8,128)S(1)} %broadcast_in_dim.4, s32[12]{0:T(128)S(1)} %bitcast.33, f32[12,256,256]{2,1,0:T(8,128)} %copy.12), kind=kCustom, calls=%fused_computation.2 | custom fusion | flops 786432 | bytes 9437232 | tf_op jit(solution)/shard_map/scatter-add | solution.py:23
  35.9 0.0 copy-start.1
  36.0 0.0 copy-start.6
  36.0 0.9 copy-done.1
  36.8 0.0 reduce-scatter.3.cloned.1.call-update
  36.9 0.0 reduce-scatter.5.cloned.1.call-start
  36.9 23.5 %reduce-scatter.3.cloned.1.call-done = f32[192,256]{1,0:T(8,128)} async-done(((f32[768,256]{1,0:T(8,128)}), f32[192,256]{1,0:T(8,128)}) %reduce-scatter.3.cloned.1.call-update) | async-done | bytes 196624 | tf_op jit(solution)/shard_map/reduce_scatter | solution.py:44
  60.4 0.0 copy-done.5
  60.4 1.8 %multiply_convert_fusion.1 = (bf16[192,256]{1,0:T(8,128)(2,1)}, f32[192,256]{1,0:T(8,128)S(1)}) fusion(bf16[256,256]{1,0:T(8,128)(2,1)S(1)} %copy-done.5, f32[192,256]{1,0:T(8,128)} %reduce-scatter.3.cloned.1.call-done), kind=kOutput, calls=%fused_computation.10 | convolution fusion | flops 25460736 | bytes 622592 | tf_op jit(solution)/shard_map/dot_general | solution.py:14
  62.2 0.2 convolution_convert_fusion
  62.5 15.3 %all_gather.7 = bf16[768,256]{1,0:T(8,128)(2,1)S(1)} all-gather(bf16[192,256]{1,0:T(8,128)(2,1)S(1)} %convolution_convert_fusion), channel_id=1, replica_groups=mesh['row'=8,'col'=4] {'col'}, dimensions={0}, use_global_device_ids=true | all-gather | bytes 491520 | tf_op jit(solution)/shard_map/all_gather | solution.py:46
  77.7 0.6 gather_fusion.1
  78.4 2.4 %multiply_bitcast_fusion = f32[12,256,256]{1,2,0:T(8,128)} fusion(bf16[12,256,256]{2,1,0:T(8,128)(2,1)S(1)} %gather_fusion.1, bf16[1,1,12,256,256]{4,3,2,1,0:T(8,128)(2,1)S(1)} %copy-done, f32[12]{0:T(128)S(1)} %compare_convert_fusion), kind=kOutput, calls=%fused_computation.4 | convolution fusion | flops 403439616 | bytes 6291504 | tf_op jit(solution)/shard_map/kij,kif->kjf/dot_general | solution.py:48
  80.8 3.6 %copy.14 = f32[12,256,256]{2,1,0:T(8,128)} copy(f32[12,256,256]{1,2,0:T(8,128)} %multiply_bitcast_fusion) | data formatting | bytes 6291456 | tf_op jit(solution)/shard_map/mul | solution.py:22
  84.4 0.1 broadcast_in_dim.5
  84.5 0.5 copy-done.4
  85.0 5.7 %scatter_fusion.1 = f32[6,256,256]{2,1,0:T(8,128)S(1)} fusion(f32[6,256,256]{2,1,0:T(8,128)S(1)} %broadcast_in_dim.5, s32[12]{0:T(128)S(1)} %bitcast.34, f32[12,256,256]{2,1,0:T(8,128)} %copy.14), kind=kCustom, calls=%fused_computation.3 | custom fusion | flops 786432 | bytes 9437232 | tf_op jit(solution)/shard_map/scatter-add | solution.py:23
  90.8 1.2 copy-done.2
  91.9 0.0 reduce-scatter.5.cloned.1.call-update
  91.9 37.8 %reduce-scatter.5.cloned.1.call-done = f32[192,256]{1,0:T(8,128)} async-done(((f32[1536,256]{1,0:T(8,128)}), f32[192,256]{1,0:T(8,128)}) %reduce-scatter.5.cloned.1.call-update) | async-done | bytes 196624 | tf_op jit(solution)/shard_map/reduce_scatter | solution.py:52
  129.8 1.6 %convert_element_type.31 = bf16[192,256]{1,0:T(8,128)(2,1)} convert(f32[192,256]{1,0:T(8,128)} %reduce-scatter.5.cloned.1.call-done) | non-fusion elementwise | flops 49152 | bytes 294912 | tf_op jit(solution)/shard_map/convert_element_type | solution.py:52
  (8 shorter events, 0.0 us)
Async XLA Ops:
  7.2 15.6 %copy-start = (bf16[1,1,12,256,256]{4,3,2,1,0:T(8,128)(2,1)S(1)}, bf16[1,1,12,256,256]{4,3,2,1,0:T(8,128)(2,1)}, u32[]{:S(2)}) copy-start(bf16[1,1,12,256,256]{4,3,2,1,0:T(8,128)(2,1)} %param.8) | copy-start | bytes 4718596
  7.2 53.2 %reduce-scatter.3.cloned.1.call-start = ((), (), s32[]{:S(2)}) async-start(), calls=%async_computation.2 | async-start | bytes 983040 | tf_op jit(solution)/shard_map/reduce_scatter | solution.py:44
  26.6 3.6 %copy-start.3 = (s32[1,1,12]{2,1,0:T(1,128)S(1)}, s32[1,1,12]{2,1,0:T(1,128)}, u32[]{:S(2)}) copy-start(s32[1,1,12]{2,1,0:T(1,128)} %param.9) | copy-start | bytes 148
  30.2 30.2 %copy-start.5 = (bf16[256,256]{1,0:T(8,128)(2,1)S(1)}, bf16[256,256]{1,0:T(8,128)(2,1)}, u32[]{:S(2)}) copy-start(bf16[256,256]{1,0:T(8,128)(2,1)} %param.12) | copy-start | bytes 393220
  35.9 0.9 copy-start.1
  36.0 26.3 %copy-start.6 = (bf16[192,256]{1,0:T(8,128)(2,1)S(1)}, bf16[192,256]{1,0:T(8,128)(2,1)}, u32[]{:S(2)}) copy-start(bf16[192,256]{1,0:T(8,128)(2,1)} %param.13) | copy-start | bytes 294916
  36.9 92.9 %reduce-scatter.5.cloned.1.call-start = ((), (), s32[]{:S(2)}) async-start(), calls=%async_computation.3 | async-start | bytes 1769472 | tf_op jit(solution)/shard_map/reduce_scatter | solution.py:52
  84.3 0.7 copy-start.4
  90.8 1.2 copy-start.2
Sparse Core Ops, SparseCore 0:
  37.0 23.3 reduce-scatter.2
  92.1 37.6 reduce-scatter.4
where the time goes:
time: 139 us; the launch traced here: 138 us
  waiting for transfers between devices  61.4 us (44%)
  blocking collectives  27.5 us (20%)
  between operations  14.9 us (11%)
  other arithmetic  13.7 us (10%)
  local copies, waits for them, and re-layouts  12.4 us (9%)
  matrix products  8.23 us (6%)
    reduce_scatter x1, waiting for transfers between devices, on_device(): lax.psum_scatter(partial_grad, 'row', scatter_dimension=0, tiled=True)  37.8 us
    reduce_scatter x1, waiting for transfers between devices, on_device(): lax.psum_scatter(partial_value, 'col', scatter_dimension=0, tiled=True)  23.5 us
    all_gather x1, blocking collectives, on_device(): pulled_block = lax.all_gather(pulled_own, 'col', axis=0, tiled=True)  15.3 us
    all_gather x1, blocking collectives, on_device(): gathered = lax.all_gather(features, 'row', axis=0, tiled=True)  12.2 us
    scatter-add x2, other arithmetic, place(): return jax.ops.segment_sum(masked, targets, num_segments=count)  11.5 us
    mul x2, local copies, waits for them, and re-layouts, place(): masked = results * occupied[:, None, None]  7.13 us
    dot_general x1, matrix products, on_device(): jnp.einsum('kij,kjf->kif', blocks, picked, preferred_element_type=jnp.flo...  3.81 us
  transfers between devices with their start and end apart: 2, of which 2 were waited for; matrix products, arithmetic and copies ran while one was open for 0% of the time, Pallas kernels for 0%

commit v1 on v0

v1 whole, which is shorter than its diff:
```python
import jax
import jax.numpy as jnp
from jax import lax
from jax.sharding import PartitionSpec as P


def silu_slope(mixed):
    sigma = jax.nn.sigmoid(mixed)
    return sigma * (1.0 + mixed * (1.0 - sigma))


def dense_layer(summed, grad_rows, weight):
    aggregated = summed.astype(jnp.bfloat16)
    mixed = jnp.dot(aggregated, weight, preferred_element_type=jnp.float32)
    activated = jax.nn.silu(mixed).astype(jnp.bfloat16)
    scaled = (grad_rows.astype(jnp.float32) * silu_slope(mixed)).astype(jnp.bfloat16)
    pulled = jnp.dot(scaled, weight.T, preferred_element_type=jnp.float32).astype(jnp.bfloat16)
    return (activated, pulled)


def scatter_sum(partial, axis):
    n = lax.axis_size(axis)
    me = lax.axis_index(axis)
    chunks = partial.reshape(n, partial.shape[0] // n, partial.shape[1])
    sent = chunks.astype(jnp.bfloat16)
    total = lax.dynamic_index_in_dim(chunks, me, 0, keepdims=False)
    for shift in range(1, n):
        piece = lax.dynamic_index_in_dim(sent, (me + shift) % n, 0, keepdims=False)
        got = lax.ppermute(piece, axis, [(i, (i + shift) % n) for i in range(n)])
        total = total + got.astype(jnp.float32)
    return total


def gather_rows(rows, axis):
    n = lax.axis_size(axis)
    me = lax.axis_index(axis)
    out = jnp.zeros((n,) + rows.shape, rows.dtype)
    out = lax.dynamic_update_index_in_dim(out, rows, me, 0)
    for shift in range(1, n):
        got = lax.ppermute(rows, axis, [(i, (i + shift) % n) for i in range(n)])
        out = lax.dynamic_update_index_in_dim(out, got, (me - shift) % n, 0)
    return out.reshape(n * rows.shape[0], rows.shape[1])


def on_device(features, edge_tiles, tile_rows, tile_cols, tile_count, weight, cotangent):
    blocks = edge_tiles[0, 0]
    row_slots = tile_rows[0, 0]
    col_slots = tile_cols[0, 0]
    filled = tile_count[0, 0]
    slot_total = blocks.shape[0]
    tile_size = blocks.shape[1]
    feat_width = features.shape[1]
    own_rows = features.shape[0]
    row_tiles = own_rows * lax.axis_size("col") // tile_size
    col_tiles = own_rows * lax.axis_size("row") // tile_size
    occupied = (jnp.arange(slot_total, dtype=jnp.int32) < filled).astype(jnp.bfloat16)
    row_hot = (row_slots[None, :] == jnp.arange(row_tiles, dtype=jnp.int32)[:, None]).astype(jnp.bfloat16)
    col_hot = (col_slots[None, :] == jnp.arange(col_tiles, dtype=jnp.int32)[:, None]).astype(jnp.bfloat16)
    select = row_hot[:, None, :] * col_hot[None, :, :] * occupied[None, None, :]
    dense = jnp.einsum("tck,kij->ticj", select, blocks, preferred_element_type=jnp.float32)
    dense = dense.astype(jnp.bfloat16).reshape(row_tiles * tile_size, col_tiles * tile_size)

    gathered = lax.all_gather(features, "row", axis=0, tiled=True)
    partial_value = jnp.dot(dense, gathered, preferred_element_type=jnp.float32)
    own_sums = scatter_sum(partial_value, "col")
    activated, pulled_own = dense_layer(own_sums, cotangent, weight)
    pulled_block = gather_rows(pulled_own, "col")
    partial_grad = lax.dot_general(
        dense, pulled_block, (((0,), (0,)), ((), ())), preferred_element_type=jnp.float32
    )
    feature_grad = scatter_sum(partial_grad, "row").astype(jnp.bfloat16)
    return (activated, feature_grad)


def solution(mesh):
    return jax.shard_map(
        on_device,
        mesh=mesh,
        in_specs=(
            P(("col", "row"), None),
            P("row", "col", None, None, None),
            P("row", "col", None),
            P("row", "col", None),
            P("row", "col"),
            P(),
            P(("row", "col"), None),
        ),
        out_specs=(P(("row", "col"), None), P(("col", "row"), None)),
        check_vma=False,
    )
```

time: 139 us -> 77.1 us (0.55)
  waiting for transfers between devices: 61.4 us -> 19 us
  blocking collectives: 27.5 us -> 11.9 us
  starting transfers between devices: 0.08 us -> 15.5 us
  between operations: 14.9 us -> 1.47 us
  other arithmetic: 13.7 us -> 2.99 us
  matrix products: 8.23 us -> 12.7 us
    reduce_scatter x2 -> x0, waiting for transfers between devices: 61.3 us -> none  [the longest x1 37.8 us: on_device(): lax.psum_scatter(partial_grad, 'row', scatter_dimension=0, tiled=True)]
    ppermute x0 -> x13, waiting for transfers between devices: none -> 19 us  [the longest x10 16.1 us: scatter_sum(): got = lax.ppermute(piece, axis, [(i, (i + shift) % n) for i in range(n)])]
    ppermute x0 -> x13, starting transfers between devices: none -> 15.5 us  [the longest x10 10.6 us: scatter_sum(): got = lax.ppermute(piece, axis, [(i, (i + shift) % n) for i in range(n)])]
    all_gather x1 -> x0, blocking collectives: 15.3 us -> none  [on_device(): pulled_block = lax.all_gather(pulled_own, 'col', axis=0, tiled=True)]
    scatter-add x2 -> x0, other arithmetic: 11.5 us -> none  [place(): return jax.ops.segment_sum(masked, targets, num_segments=count)]
    mul x2 -> x0, local copies, waits for them, and re-layouts: 7.13 us -> none  [place(): masked = results * occupied[:, None, None]]
    dot_general x0 -> x2, local copies, waits for them, and re-layouts: none -> 6.45 us  [the longest x1 3.62 us: on_device(): partial_value = jnp.dot(dense, gathered, preferred_element_type=jnp.float32)]
    dot_general x2 -> x3, matrix products: 6.22 us -> 9.05 us  [the longest x1 3.48 us: on_device(): partial_value = jnp.dot(dense, gathered, preferred_element_type=jnp.float32)]
  transfers between devices with their start and end apart: 2 -> 13, of which waited for: 2 -> 7; matrix products, arithmetic and copies ran while one was open for 0% -> 8% of each run, Pallas kernels for 0% -> 0%
where the time goes in v1:
time: 77.1 us; the launch traced here: 76.7 us
  waiting for transfers between devices  19 us (25%)
  starting transfers between devices  15.5 us (20%)
  local copies, waits for them, and re-layouts  13.1 us (17%)
  matrix products  12.7 us (16%)
  blocking collectives  11.9 us (15%)
  other arithmetic  2.99 us (4%)
  between operations  1.47 us (2%)
    ppermute x10, waiting for transfers between devices, scatter_sum(): got = lax.ppermute(piece, axis, [(i, (i + shift) % n) for i in range(n)])  16.1 us
    all_gather x1, blocking collectives, on_device(): gathered = lax.all_gather(features, 'row', axis=0, tiled=True)  11.9 us
    ppermute x10, starting transfers between devices, scatter_sum(): got = lax.ppermute(piece, axis, [(i, (i + shift) % n) for i in range(n)])  10.6 us
    ppermute x3, starting transfers between devices, gather_rows(): got = lax.ppermute(rows, axis, [(i, (i + shift) % n) for i in range(n)])  4.89 us
    dot_general x1, local copies, waits for them, and re-layouts, on_device(): partial_value = jnp.dot(dense, gathered, preferred_element_type=jnp.float32)  3.62 us
    dot_general x1, matrix products, on_device(): partial_value = jnp.dot(dense, gathered, preferred_element_type=jnp.float32)  3.48 us
    dot_general x1, matrix products, on_device(): lax.dot_general(dense, pulled_block, (((0,), (0,)), ((), ())), preferred_...  2.95 us
    ppermute x3, waiting for transfers between devices, gather_rows(): got = lax.ppermute(rows, axis, [(i, (i + shift) % n) for i in range(n)])  2.94 us
  transfers between devices with their start and end apart: 13, of which 7 were waited for; matrix products, arithmetic and copies ran while one was open for 8% of the time, Pallas kernels for 0%

profile of v1, /device:TPU:0, one launch (start us, length us, event | category | flops | bytes accessed | tf_op | source)
XLA Modules:
  0.0 76.7 jit_solution(16350948291646581301)
XLA Ops:
  1.4 0.7 fusion.20
  2.0 0.7 fusion.24
  2.7 2.6 %convolution_convert_fusion = bf16[3,6,256,256]{3,1,2,0:T(8,128)(2,1)S(1)} fusion(bf16[12,256,256]{2,1,0:T(8,128)(2,1)} %bitcast.92, bf16[12]{0:T(256)(128)(2,1)S(1)} %compare_convert_fusion, bf16[6,12]{1,0:T(8,128)(2,1)S(1)} %fusion.20, bf16[3,12]{1,0:T(4,128)(2,1)S(1)} %fusion.24), kind=kOutput, calls=%fused_computation | convolution fusion | flops 29492496 | bytes 3932400 | tf_op jit(solution)/shard_map/tck,kij->ticj/dot_general | solution.py:60
  5.3 3.6 %dot_general.22 = bf16[4,192,1536]{2,1,0:T(8,128)(2,1)} reshape(bf16[3,256,6,256]{3,2,1,0:T(8,128)(2,1)S(1)} %bitcast.88) | data formatting | bytes 4718592 | tf_op jit(solution)/shard_map/dot_general | solution.py:64
  9.0 11.9 %all_gather.3 = bf16[1536,256]{1,0:T(8,128)(2,1)S(1)} all-gather(bf16[192,256]{1,0:T(8,128)(2,1)S(1)} %copy-done.1), channel_id=1, replica_groups=mesh['row'=8,'col'=4] {'row'}, dimensions={0}, use_global_device_ids=true | all-gather | bytes 884736 | tf_op jit(solution)/shard_map/all_gather | solution.py:63
  20.8 3.5 %fusion.26 = (bf16[4,192,256]{2,1,0:T(8,128)(2,1)}, f32[4,192,256]{2,1,0:T(8,128)}) fusion(bf16[4,192,1536]{2,1,0:T(8,128)(2,1)} %dot_general.22, bf16[1536,256]{1,0:T(8,128)(2,1)S(1)} %all_gather.3), kind=kOutput, calls=%fused_computation.49 | convolution fusion | flops 604176384 | bytes 4325376 | tf_op jit(solution)/shard_map/dot_general | solution.py:64
  24.3 1.6 %dynamic-slice_bitcast_fusion.9 = (bf16[192,256]{1,0:T(8,128)(2,1)S(1)}, bf16[192,256]{1,0:T(8,128)(2,1)}, bf16[192,256]{1,0:T(8,128)(2,1)S(1)}) fusion(bf16[4,192,256]{2,1,0:T(8,128)(2,1)} %get-tuple-element.12, s32[]{:T(128)S(6)} %select_n.108, s32[]{:T(128)S(6)} %select_n.112, s32[]{:T(128)S(6)} %select_n.110), kind=kLoop, calls=%fused_computation.35 | loop fusion | bytes 589836 | tf_op jit(solution)/shard_map/jit(dynamic_index_in_dim)/squeeze | solution.py:28
  25.9 3.6 %collective-permute-start.2 = (bf16[192,256]{1,0:T(8,128)(2,1)}, bf16[192,256]{1,0:T(8,128)(2,1)}, u32[]{:S(2)}, u32[]{:S(2)}) collective-permute-start(bf16[192,256]{1,0:T(8,128)(2,1)} %get-tuple-element.10), channel_id=1, source_target_pairs={{0,3},{1,0},{2,1},{3,2},{4,7},{5,4},{6,5},{7,6},{8,11},{9,8},{10,9... | collective-permute-start | bytes 294920 | tf_op jit(solution)/shard_map/ppermute | solution.py:29
  29.6 1.0 %collective-permute-start = (bf16[192,256]{1,0:T(8,128)(2,1)S(1)}, bf16[192,256]{1,0:T(8,128)(2,1)}, u32[]{:S(2)}, u32[]{:S(2)}) collective-permute-start(bf16[192,256]{1,0:T(8,128)(2,1)S(1)} %get-tuple-element.9), channel_id=1, source_target_pairs={{0,1},{1,2},{2,3},{3,0},{4,5},{5,6},{6,7},{7,4},{8,9},{9,10},{10,1... | collective-permute-start | bytes 294920 | tf_op jit(solution)/shard_map/ppermute | solution.py:29
  30.6 2.5 %collective-permute-done.2 = bf16[192,256]{1,0:T(8,128)(2,1)} collective-permute-done((bf16[192,256]{1,0:T(8,128)(2,1)}, bf16[192,256]{1,0:T(8,128)(2,1)}, u32[]{:S(2)}, u32[]{:S(2)}) %collective-permute-start.2) | collective-permute-done | bytes 98336 | tf_op jit(solution)/shard_map/ppermute | solution.py:29
  33.1 6.2 %collective-permute-done.1 = bf16[192,256]{1,0:T(8,128)(2,1)} collective-permute-done((bf16[192,256]{1,0:T(8,128)(2,1)S(1)}, bf16[192,256]{1,0:T(8,128)(2,1)}, u32[]{:S(2)}, u32[]{:S(2)}) %collective-permute-start.1) | collective-permute-done | bytes 98336 | tf_op jit(solution)/shard_map/ppermute | solution.py:29
  39.3 1.9 %multiply_convert_fusion.1 = (bf16[192,256]{1,0:T(8,128)(2,1)}, f32[192,256]{1,0:T(8,128)S(1)}) fusion(bf16[256,256]{1,0:T(8,128)(2,1)S(1)} %copy-done, bf16[192,256]{1,0:T(8,128)(2,1)} %collective-permute-done.2, bf16[192,256]{1,0:T(8,128)(2,1)} %collective-permute-done.1, bf16[192,256]{1,0:T(8,128)(2,1)} %collective-permute-done, ...), kind=kOutput, calls=%fused_computation.19 | convolution fusion | flops 25755648 | bytes 917508 | tf_op jit(solution)/shard_map/dot_general | solution.py:14
  41.2 0.8 %broadcast_in_dim.21 = bf16[4,192,256]{2,1,0:T(8,128)(2,1)} broadcast(bf16[]{:T(256)} %constant.130.clone.1), dimensions={} | broadcast | bytes 393218 | tf_op jit(solution)/shard_map/broadcast_in_dim | solution.py:37
  42.0 1.8 %bitcast_dynamic-update-slice_fusion.3 = (bf16[4,192,256]{2,1,0:T(8,128)(2,1)}, bf16[192,256]{1,0:T(8,128)(2,1)S(1)}) fusion(bf16[4,192,256]{2,1,0:T(8,128)(2,1)} %broadcast_in_dim.21, s32[]{:T(128)S(6)} %select_n.106, bf16[256,256]{1,0:T(8,128)(2,1)S(1)} %copy-done, f32[192,256]{1,0:T(8,128)S(1)} %get-tuple-element.15, bf16[192,256]{1,0:T(8,128)(2,1)} %param.13), kind=kOutput, calls=%fused_computation.25 | convolution fusion | flops 25706496 | bytes 622596 | tf_op jit(solution)/shard_map/dot_general | solution.py:17
  43.8 2.2 %copy.16 = bf16[96,8,6,256]{3,1,2,0:T(8,128)(2,1)} copy(bf16[96,8,6,256]{3,2,1,0:T(8,128)(2,1)S(1)} %bitcast.89) | data formatting | bytes 4718592
  46.0 2.8 %copy.14 = bf16[1536,768]{1,0:T(8,128)(2,1)S(1)} copy(bf16[1536,768]{0,1:T(8,128)(2,1)} %bitcast.91) | data formatting | bytes 4718592 | tf_op jit(solution)/shard_map/dot_general | solution.py:68
  48.9 2.2 %collective-permute-start.4 = (bf16[192,256]{1,0:T(8,128)(2,1)S(1)}, bf16[192,256]{1,0:T(8,128)(2,1)S(1)}, u32[]{:S(2)}, u32[]{:S(2)}) collective-permute-start(bf16[192,256]{1,0:T(8,128)(2,1)S(1)} %get-tuple-element.17), channel_id=1, source_target_pairs={{0,2},{1,3},{2,0},{3,1},{4,6},{5,7},{6,4},{7,5},{8,10},{9,11},{10,... | collective-permute-start | bytes 294920 | tf_op jit(solution)/shard_map/ppermute | solution.py:40
  51.1 2.7 %collective-permute-start.5 = (bf16[192,256]{1,0:T(8,128)(2,1)S(1)}, bf16[192,256]{1,0:T(8,128)(2,1)S(1)}, u32[]{:S(2)}, u32[]{:S(2)}) collective-permute-start(bf16[192,256]{1,0:T(8,128)(2,1)S(1)} %get-tuple-element.17), channel_id=1, source_target_pairs={{0,3},{1,0},{2,1},{3,2},{4,7},{5,4},{6,5},{7,6},{8,11},{9,8},{10,9... | collective-permute-start | bytes 294920 | tf_op jit(solution)/shard_map/ppermute | solution.py:40
  53.8 0.6 bitcast_dynamic-update-slice_fusion.2
  54.4 2.9 %collective-permute-done.4 = bf16[192,256]{1,0:T(8,128)(2,1)S(1)} collective-permute-done((bf16[192,256]{1,0:T(8,128)(2,1)S(1)}, bf16[192,256]{1,0:T(8,128)(2,1)S(1)}, u32[]{:S(2)}, u32[]{:S(2)}) %collective-permute-start.4) | collective-permute-done | bytes 98336 | tf_op jit(solution)/shard_map/ppermute | solution.py:40
  57.4 0.6 bitcast_dynamic-update-slice_fusion.1
  58.0 0.6 bitcast_dynamic-update-slice_fusion
  58.7 2.9 %fusion.27 = (bf16[8,192,256]{2,1,0:T(8,128)(2,1)S(1)}, f32[8,192,256]{2,1,0:T(8,128)}) fusion(bf16[8,192,768]{2,1,0:T(8,128)(2,1)S(1)} %bitcast.90, bf16[768,256,1]{1,0,2:T(8,128)(2,1)} %bitcast.20), kind=kOutput, calls=%fused_computation.50 | convolution fusion | flops 604372992 | bytes 5111808 | tf_op jit(solution)/shard_map/dot_general | solution.py:68
  61.7 1.5 %collective-permute-start.11 = (bf16[192,256]{1,0:T(8,128)(2,1)S(1)}, bf16[192,256]{1,0:T(8,128)(2,1)S(1)}, u32[]{:S(2)}, u32[]{:S(2)}) collective-permute-start(bf16[192,256]{1,0:T(8,128)(2,1)S(1)} %get-tuple-element.4), channel_id=1, source_target_pairs={{0,24},{4,28},{8,0},{12,4},{16,8},{20,12},{24,16},{28,20},{1,25},{... | collective-permute-start | bytes 294920 | tf_op jit(solution)/shard_map/ppermute | solution.py:29
  63.3 1.2 %collective-permute-start.10 = (bf16[192,256]{1,0:T(8,128)(2,1)S(1)}, bf16[192,256]{1,0:T(8,128)(2,1)S(1)}, u32[]{:S(2)}, u32[]{:S(2)}) collective-permute-start(bf16[192,256]{1,0:T(8,128)(2,1)S(1)} %get-tuple-element.5), channel_id=1, source_target_pairs={{0,20},{4,24},{8,28},{12,0},{16,4},{20,8},{24,12},{28,16},{1,21},{... | collective-permute-start | bytes 294920 | tf_op jit(solution)/shard_map/ppermute | solution.py:29
  64.5 0.5 collective-permute-start.9
  65.1 1.1 %collective-permute-start.8 = (bf16[192,256]{1,0:T(8,128)(2,1)S(1)}, bf16[192,256]{1,0:T(8,128)(2,1)S(1)}, u32[]{:S(2)}, u32[]{:S(2)}) collective-permute-start(bf16[192,256]{1,0:T(8,128)(2,1)S(1)} %get-tuple-element.7), channel_id=1, source_target_pairs={{0,12},{4,16},{8,20},{12,24},{16,28},{20,0},{24,4},{28,8},{1,13},{... | collective-permute-start | bytes 294920 | tf_op jit(solution)/shard_map/ppermute | solution.py:29
  66.2 1.5 %collective-permute-start.7 = (bf16[192,256]{1,0:T(8,128)(2,1)S(1)}, bf16[192,256]{1,0:T(8,128)(2,1)S(1)}, u32[]{:S(2)}, u32[]{:S(2)}) collective-permute-start(bf16[192,256]{1,0:T(8,128)(2,1)S(1)} %get-tuple-element.8), channel_id=1, source_target_pairs={{0,8},{4,12},{8,16},{12,20},{16,24},{20,28},{24,0},{28,4},{1,9},{5... | collective-permute-start | bytes 294920 | tf_op jit(solution)/shard_map/ppermute | solution.py:29
  67.7 1.2 %collective-permute-done.11 = bf16[192,256]{1,0:T(8,128)(2,1)S(1)} collective-permute-done((bf16[192,256]{1,0:T(8,128)(2,1)S(1)}, bf16[192,256]{1,0:T(8,128)(2,1)S(1)}, u32[]{:S(2)}, u32[]{:S(2)}) %collective-permute-start.11) | collective-permute-done | bytes 98336 | tf_op jit(solution)/shard_map/ppermute | solution.py:29
  69.0 5.4 %collective-permute-done.9 = bf16[192,256]{1,0:T(8,128)(2,1)S(1)} collective-permute-done((bf16[192,256]{1,0:T(8,128)(2,1)S(1)}, bf16[192,256]{1,0:T(8,128)(2,1)S(1)}, u32[]{:S(2)}, u32[]{:S(2)}) %collective-permute-start.9) | collective-permute-done | bytes 98336 | tf_op jit(solution)/shard_map/ppermute | solution.py:29
  74.4 0.6 collective-permute-done.8
  75.0 1.7 %fusion.10 = bf16[192,256]{1,0:T(8,128)(2,1)} fusion(bf16[192,256]{1,0:T(8,128)(2,1)S(1)} %collective-permute-done.12, bf16[192,256]{1,0:T(8,128)(2,1)S(1)} %collective-permute-done.11, bf16[192,256]{1,0:T(8,128)(2,1)S(1)} %collective-permute-done.10, bf16[192,256]{1,0:T(8,128)(2,1)S(1)} %collective-permute-done.9, ...), kind=kLoop, calls=%fused_computation.13 | loop fusion | flops 737280 | bytes 983044 | tf_op jit(solution)/shard_map/convert_element_type | solution.py:71
  (17 shorter events, 0.2 us)
Async XLA Ops:
  0.6 38.7 %copy-start = (bf16[256,256]{1,0:T(8,128)(2,1)S(1)}, bf16[256,256]{1,0:T(8,128)(2,1)}, u32[]{:S(2)}) copy-start(bf16[256,256]{1,0:T(8,128)(2,1)} %param.12) | copy-start | bytes 393220
  5.3 3.6 %copy-start.1 = (bf16[192,256]{1,0:T(8,128)(2,1)S(1)}, bf16[192,256]{1,0:T(8,128)(2,1)}, u32[]{:S(2)}) copy-start(bf16[192,256]{1,0:T(8,128)(2,1)} %param.7) | copy-start | bytes 294916
  25.9 7.2 %collective-permute-start.2 = (bf16[192,256]{1,0:T(8,128)(2,1)}, bf16[192,256]{1,0:T(8,128)(2,1)}, u32[]{:S(2)}, u32[]{:S(2)}) collective-permute-start(bf16[192,256]{1,0:T(8,128)(2,1)} %get-tuple-element.10), channel_id=1, source_target_pairs={{0,3},{1,0},{2,1},{3,2},{4,7},{5,4},{6,5},{7,6},{8,11},{9,8},{10,9... | collective-permute-start | bytes 294920 | tf_op jit(solution)/shard_map/ppermute | solution.py:29
  29.5 9.7 %collective-permute-start.1 = (bf16[192,256]{1,0:T(8,128)(2,1)S(1)}, bf16[192,256]{1,0:T(8,128)(2,1)}, u32[]{:S(2)}, u32[]{:S(2)}) collective-permute-start(bf16[192,256]{1,0:T(8,128)(2,1)S(1)} %get-tuple-element.11), channel_id=1, source_target_pairs={{0,2},{1,3},{2,0},{3,1},{4,6},{5,7},{6,4},{7,5},{8,10},{9,11},{10,... | collective-permute-start | bytes 294920 | tf_op jit(solution)/shard_map/ppermute | solution.py:29
  29.6 9.7 %collective-permute-start = (bf16[192,256]{1,0:T(8,128)(2,1)S(1)}, bf16[192,256]{1,0:T(8,128)(2,1)}, u32[]{:S(2)}, u32[]{:S(2)}) collective-permute-start(bf16[192,256]{1,0:T(8,128)(2,1)S(1)} %get-tuple-element.9), channel_id=1, source_target_pairs={{0,1},{1,2},{2,3},{3,0},{4,5},{5,6},{6,7},{7,4},{8,9},{9,10},{10,1... | collective-permute-start | bytes 294920 | tf_op jit(solution)/shard_map/ppermute | solution.py:29
  43.8 10.0 %collective-permute-start.3 = (bf16[192,256]{1,0:T(8,128)(2,1)S(1)}, bf16[192,256]{1,0:T(8,128)(2,1)S(1)}, u32[]{:S(2)}, u32[]{:S(2)}) collective-permute-start(bf16[192,256]{1,0:T(8,128)(2,1)S(1)} %get-tuple-element.17), channel_id=1, source_target_pairs={{0,1},{1,2},{2,3},{3,0},{4,5},{5,6},{6,7},{7,4},{8,9},{9,10},{10,1... | collective-permute-start | bytes 294920 | tf_op jit(solution)/shard_map/ppermute | solution.py:40
  48.9 8.5 %collective-permute-start.4 = (bf16[192,256]{1,0:T(8,128)(2,1)S(1)}, bf16[192,256]{1,0:T(8,128)(2,1)S(1)}, u32[]{:S(2)}, u32[]{:S(2)}) collective-permute-start(bf16[192,256]{1,0:T(8,128)(2,1)S(1)} %get-tuple-element.17), channel_id=1, source_target_pairs={{0,2},{1,3},{2,0},{3,1},{4,6},{5,7},{6,4},{7,5},{8,10},{9,11},{10,... | collective-permute-start | bytes 294920 | tf_op jit(solution)/shard_map/ppermute | solution.py:40
  51.1 6.9 %collective-permute-start.5 = (bf16[192,256]{1,0:T(8,128)(2,1)S(1)}, bf16[192,256]{1,0:T(8,128)(2,1)S(1)}, u32[]{:S(2)}, u32[]{:S(2)}) collective-permute-start(bf16[192,256]{1,0:T(8,128)(2,1)S(1)} %get-tuple-element.17), channel_id=1, source_target_pairs={{0,3},{1,0},{2,1},{3,2},{4,7},{5,4},{6,5},{7,6},{8,11},{9,8},{10,9... | collective-permute-start | bytes 294920 | tf_op jit(solution)/shard_map/ppermute | solution.py:40
  61.7 4.5 %collective-permute-start.12 = (bf16[192,256]{1,0:T(8,128)(2,1)S(1)}, bf16[192,256]{1,0:T(8,128)(2,1)S(1)}, u32[]{:S(2)}, u32[]{:S(2)}) collective-permute-start(bf16[192,256]{1,0:T(8,128)(2,1)S(1)} %get-tuple-element.3), channel_id=1, source_target_pairs={{0,28},{4,0},{8,4},{12,8},{16,12},{20,16},{24,20},{28,24},{1,29},{... | collective-permute-start | bytes 294920 | tf_op jit(solution)/shard_map/ppermute | solution.py:29
  61.7 7.2 %collective-permute-start.11 = (bf16[192,256]{1,0:T(8,128)(2,1)S(1)}, bf16[192,256]{1,0:T(8,128)(2,1)S(1)}, u32[]{:S(2)}, u32[]{:S(2)}) collective-permute-start(bf16[192,256]{1,0:T(8,128)(2,1)S(1)} %get-tuple-element.4), channel_id=1, source_target_pairs={{0,24},{4,28},{8,0},{12,4},{16,8},{20,12},{24,16},{28,20},{1,25},{... | collective-permute-start | bytes 294920 | tf_op jit(solution)/shard_map/ppermute | solution.py:29
  63.3 5.7 %collective-permute-start.10 = (bf16[192,256]{1,0:T(8,128)(2,1)S(1)}, bf16[192,256]{1,0:T(8,128)(2,1)S(1)}, u32[]{:S(2)}, u32[]{:S(2)}) collective-permute-start(bf16[192,256]{1,0:T(8,128)(2,1)S(1)} %get-tuple-element.5), channel_id=1, source_target_pairs={{0,20},{4,24},{8,28},{12,0},{16,4},{20,8},{24,12},{28,16},{1,21},{... | collective-permute-start | bytes 294920 | tf_op jit(solution)/shard_map/ppermute | solution.py:29
  64.5 9.9 %collective-permute-start.9 = (bf16[192,256]{1,0:T(8,128)(2,1)S(1)}, bf16[192,256]{1,0:T(8,128)(2,1)S(1)}, u32[]{:S(2)}, u32[]{:S(2)}) collective-permute-start(bf16[192,256]{1,0:T(8,128)(2,1)S(1)} %get-tuple-element.6), channel_id=1, source_target_pairs={{0,16},{4,20},{8,24},{12,28},{16,0},{20,4},{24,8},{28,12},{1,17},{... | collective-permute-start | bytes 294920 | tf_op jit(solution)/shard_map/ppermute | solution.py:29
  65.1 10.0 %collective-permute-start.8 = (bf16[192,256]{1,0:T(8,128)(2,1)S(1)}, bf16[192,256]{1,0:T(8,128)(2,1)S(1)}, u32[]{:S(2)}, u32[]{:S(2)}) collective-permute-start(bf16[192,256]{1,0:T(8,128)(2,1)S(1)} %get-tuple-element.7), channel_id=1, source_target_pairs={{0,12},{4,16},{8,20},{12,24},{16,28},{20,0},{24,4},{28,8},{1,13},{... | collective-permute-start | bytes 294920 | tf_op jit(solution)/shard_map/ppermute | solution.py:29
  66.2 8.8 %collective-permute-start.7 = (bf16[192,256]{1,0:T(8,128)(2,1)S(1)}, bf16[192,256]{1,0:T(8,128)(2,1)S(1)}, u32[]{:S(2)}, u32[]{:S(2)}) collective-permute-start(bf16[192,256]{1,0:T(8,128)(2,1)S(1)} %get-tuple-element.8), channel_id=1, source_target_pairs={{0,8},{4,12},{8,16},{12,20},{16,24},{20,28},{24,0},{28,4},{1,9},{5... | collective-permute-start | bytes 294920 | tf_op jit(solution)/shard_map/ppermute | solution.py:29
  68.9 6.1 %collective-permute-start.6 = (bf16[192,256]{1,0:T(8,128)(2,1)S(1)}, bf16[192,256]{1,0:T(8,128)(2,1)S(1)}, u32[]{:S(2)}, u32[]{:S(2)}) collective-permute-start(bf16[192,256]{1,0:T(8,128)(2,1)S(1)} %get-tuple-element.2), channel_id=1, source_target_pairs={{0,4},{4,8},{8,12},{12,16},{16,20},{20,24},{24,28},{28,0},{1,5},{5... | collective-permute-start | bytes 294920 | tf_op jit(solution)/shard_map/ppermute | solution.py:29

commit v2 on v0

v2 whole, which is shorter than its diff:
```python
import jax
import jax.numpy as jnp
from jax import lax
from jax.experimental import pallas as pl
from jax.experimental.pallas import tpu as pltpu
from jax.sharding import PartitionSpec as P


def silu_slope(mixed):
    sigma = jax.nn.sigmoid(mixed)
    return sigma * (1.0 + mixed * (1.0 - sigma))


def dense_layer(summed, grad_rows, weight):
    aggregated = summed.astype(jnp.bfloat16)
    mixed = jnp.dot(aggregated, weight, preferred_element_type=jnp.float32)
    activated = jax.nn.silu(mixed).astype(jnp.bfloat16)
    scaled = (grad_rows.astype(jnp.float32) * silu_slope(mixed)).astype(jnp.bfloat16)
    pulled = jnp.dot(scaled, weight.T, preferred_element_type=jnp.float32).astype(jnp.bfloat16)
    return (activated, pulled)


def split_out(acc_ref, own_ref, send_ref, me):
    chunk = own_ref.shape[0]
    n = send_ref.shape[0] + 1
    own_ref[...] = acc_ref[pl.ds(pl.multiple_of(me * chunk, 8), chunk), :]
    for shift in range(1, n):
        start = pl.multiple_of(((me + shift) % n) * chunk, 8)
        send_ref[shift - 1] = acc_ref[pl.ds(start, chunk), :].astype(send_ref.dtype)


def forward_kernel(rows_ref, cols_ref, info_ref, a_ref, f_ref, own_ref, send_ref, acc_ref):
    tile = a_ref.shape[1]
    acc_ref[...] = jnp.zeros_like(acc_ref)

    def step(k, carry):
        f = f_ref[pl.ds(pl.multiple_of(cols_ref[k] * tile, tile), tile), :]
        rows = pl.ds(pl.multiple_of(rows_ref[k] * tile, tile), tile)
        acc_ref[rows, :] += jnp.dot(a_ref[k], f, preferred_element_type=jnp.float32)
        return carry

    lax.fori_loop(0, jnp.minimum(info_ref[0], a_ref.shape[0]), step, 0)
    split_out(acc_ref, own_ref, send_ref, info_ref[1])


def backward_kernel(rows_ref, cols_ref, info_ref, a_ref, mine_ref, *rest):
    got_refs = rest[:-4]
    own_ref, send_ref, block_ref, acc_ref = rest[-4:]
    tile = a_ref.shape[1]
    chunk = mine_ref.shape[0]
    n = len(got_refs) + 1
    me = info_ref[1]
    block_ref[pl.ds(pl.multiple_of(me * chunk, 16), chunk), :] = mine_ref[...]
    for shift in range(1, n):
        start = pl.multiple_of(((me - shift + n) % n) * chunk, 16)
        block_ref[pl.ds(start, chunk), :] = got_refs[shift - 1][...]
    acc_ref[...] = jnp.zeros_like(acc_ref)

    def step(k, carry):
        p = block_ref[pl.ds(pl.multiple_of(rows_ref[k] * tile, tile), tile), :]
        cols = pl.ds(pl.multiple_of(cols_ref[k] * tile, tile), tile)
        acc_ref[cols, :] += lax.dot_general(
            a_ref[k], p, (((0,), (0,)), ((), ())), preferred_element_type=jnp.float32
        )
        return carry

    lax.fori_loop(0, jnp.minimum(info_ref[0], a_ref.shape[0]), step, 0)
    split_out(acc_ref, own_ref, send_ref, info_ref[2])


SMEM = pl.BlockSpec(memory_space=pltpu.SMEM)
VMEM = pl.BlockSpec(memory_space=pltpu.VMEM)


def tile_products(rows, cols, info, blocks, features, parts):
    out_rows = parts[0] * parts[1]
    chunk = parts[1]
    return pl.pallas_call(
        forward_kernel,
        out_shape=(
            jax.ShapeDtypeStruct((chunk, features.shape[1]), jnp.float32),
            jax.ShapeDtypeStruct((parts[0] - 1, chunk, features.shape[1]), jnp.bfloat16),
        ),
        in_specs=[SMEM, SMEM, SMEM, VMEM, VMEM],
        out_specs=(VMEM, VMEM),
        scratch_shapes=[pltpu.VMEM((out_rows, features.shape[1]), jnp.float32)],
    )(rows, cols, info, blocks, features)


def tile_products_t(rows, cols, info, blocks, mine, got, n_out, out_rows):
    chunk = out_rows // n_out
    width = mine.shape[1]
    return pl.pallas_call(
        backward_kernel,
        out_shape=(
            jax.ShapeDtypeStruct((chunk, width), jnp.float32),
            jax.ShapeDtypeStruct((n_out - 1, chunk, width), jnp.bfloat16),
        ),
        in_specs=[SMEM, SMEM, SMEM, VMEM, VMEM] + [VMEM] * len(got),
        out_specs=(VMEM, VMEM),
        scratch_shapes=[
            pltpu.VMEM(((len(got) + 1) * mine.shape[0], width), jnp.bfloat16),
            pltpu.VMEM((out_rows, width), jnp.float32),
        ],
    )(rows, cols, info, blocks, mine, *got)


def shifts(axis):
    n = lax.axis_size(axis)
    return [[(i, (i + shift) % n) for i in range(n)] for shift in range(1, n)]


def on_device(features, edge_tiles, tile_rows, tile_cols, tile_count, weight, cotangent):
    blocks = edge_tiles[0, 0]
    row_slots = tile_rows[0, 0]
    col_slots = tile_cols[0, 0]
    filled = tile_count[0, 0]
    n_row = lax.axis_size("row")
    n_col = lax.axis_size("col")
    me_row = lax.axis_index("row")
    me_col = lax.axis_index("col")
    own_rows = features.shape[0]

    gathered = lax.all_gather(features, "row", axis=0, tiled=True)
    info = jnp.stack([filled, me_col, me_row]).astype(jnp.int32)
    own, send = tile_products(row_slots, col_slots, info, blocks, gathered, (n_col, own_rows))
    total = own
    for shift, perm in enumerate(shifts("col")):
        total = total + lax.ppermute(send[shift], "col", perm).astype(jnp.float32)
    activated, pulled_own = dense_layer(total, cotangent, weight)
    got = [lax.ppermute(pulled_own, "col", perm) for perm in shifts("col")]
    own_g, send_g = tile_products_t(
        row_slots, col_slots, info, blocks, pulled_own, got, n_row, n_row * own_rows
    )
    total_g = own_g
    for shift, perm in enumerate(shifts("row")):
        total_g = total_g + lax.ppermute(send_g[shift], "row", perm).astype(jnp.float32)
    return (activated, total_g.astype(jnp.bfloat16))


def solution(mesh):
    return jax.shard_map(
        on_device,
        mesh=mesh,
        in_specs=(
            P(("col", "row"), None),
            P("row", "col", None, None, None),
            P("row", "col", None),
            P("row", "col", None),
            P("row", "col"),
            P(),
            P(("row", "col"), None),
        ),
        out_specs=(P(("row", "col"), None), P(("col", "row"), None)),
        check_vma=False,
    )
```

time: 139 us -> 70 us (0.50)
  waiting for transfers between devices: 61.4 us -> 22.5 us
  blocking collectives: 27.5 us -> 13.8 us
  between operations: 14.9 us -> 1.38 us
  starting transfers between devices: 0.08 us -> 13.5 us
  other arithmetic: 13.7 us -> 2.28 us
  Pallas kernels: 0 us -> 10.3 us
  local copies, waits for them, and re-layouts: 12.4 us -> 3.5 us
  matrix products: 8.23 us -> 2.02 us
    reduce_scatter x2 -> x0, waiting for transfers between devices: 61.3 us -> none  [the longest x1 37.8 us: on_device(): lax.psum_scatter(partial_grad, 'row', scatter_dimension=0, tiled=True)]
    ppermute x0 -> x13, waiting for transfers between devices: none -> 22.5 us  [the longest x3 8.69 us: on_device(): total = total + lax.ppermute(send[shift], 'col', perm).astype(jnp.float32)]
    all_gather x1 -> x0, blocking collectives: 15.3 us -> none  [on_device(): pulled_block = lax.all_gather(pulled_own, 'col', axis=0, tiled=True)]
    ppermute x0 -> x13, starting transfers between devices: none -> 13.5 us  [the longest x7 7.58 us: on_device(): lax.ppermute(send_g[shift], 'row', perm).astype(jnp.float32)]
    scatter-add x2 -> x0, other arithmetic: 11.5 us -> none  [place(): return jax.ops.segment_sum(masked, targets, num_segments=count)]
    pallas_call x0 -> x2, Pallas kernels: none -> 10.3 us  [the longest x1 5.42 us: tile_products_t(): pl.pallas_call(backward_kernel, out_shape=(jax.ShapeDtypeStruct((chunk, w...]
    mul x2 -> x0, local copies, waits for them, and re-layouts: 7.13 us -> none  [place(): masked = results * occupied[:, None, None]]
    dot_general x2 -> x0, matrix products: 6.22 us -> none  [the longest x1 3.81 us: on_device(): jnp.einsum('kij,kjf->kif', blocks, picked, preferred_element_type=jnp.flo...]
  transfers between devices with their start and end apart: 2 -> 13, of which waited for: 2 -> 8; matrix products, arithmetic and copies ran while one was open for 0% -> 0% of each run, Pallas kernels for 0% -> 0%
where the time goes in v2:
time: 70 us; the launch traced here: 69.3 us
  waiting for transfers between devices  22.5 us (32%)
  blocking collectives  13.8 us (20%)
  starting transfers between devices  13.5 us (19%)
  Pallas kernels  10.3 us (15%)
  local copies, waits for them, and re-layouts  3.5 us (5%)
  other arithmetic  2.28 us (3%)
  matrix products  2.02 us (3%)
  between operations  1.38 us (2%)
    all_gather x1, blocking collectives, on_device(): gathered = lax.all_gather(features, 'row', axis=0, tiled=True)  13.8 us
    ppermute x3, waiting for transfers between devices, on_device(): total = total + lax.ppermute(send[shift], 'col', perm).astype(jnp.float32)  8.69 us
    ppermute x3, waiting for transfers between devices, on_device(): got = [lax.ppermute(pulled_own, 'col', perm) for perm in shifts('col')]  7.81 us
    ppermute x7, starting transfers between devices, on_device(): lax.ppermute(send_g[shift], 'row', perm).astype(jnp.float32)  7.58 us
    ppermute x7, waiting for transfers between devices, on_device(): lax.ppermute(send_g[shift], 'row', perm).astype(jnp.float32)  5.96 us
    pallas_call x1, Pallas kernels, tile_products_t(): pl.pallas_call(backward_kernel, out_shape=(jax.ShapeDtypeStruct((chunk, w...  5.42 us
    pallas_call x1, Pallas kernels, tile_products(): pl.pallas_call(forward_kernel, out_shape=(jax.ShapeDtypeStruct((chunk, fe...  4.86 us
    ppermute x3, starting transfers between devices, on_device(): total = total + lax.ppermute(send[shift], 'col', perm).astype(jnp.float32)  3.88 us
  transfers between devices with their start and end apart: 13, of which 8 were waited for; matrix products, arithmetic and copies ran while one was open for 0% of the time, Pallas kernels for 0%

profile of v2, /device:TPU:0, one launch (start us, length us, event | category | flops | bytes accessed | tf_op | source)
XLA Modules:
  0.0 69.3 jit_solution(5315988851360405714)
XLA Ops:
  0.6 0.0 copy-start
  1.3 13.8 %all_gather.3.f_ref = bf16[1536,256]{1,0:T(8,128)(2,1)} all-gather(bf16[192,256]{1,0:T(8,128)(2,1)} %param.7), channel_id=1, replica_groups=mesh['row'=8,'col'=4] {'row'}, dimensions={0}, use_global_device_ids=true | all-gather | bytes 884736 | tf_op jit(solution)/shard_map/all_gather | solution.py:124
  15.2 0.6 pad_add_fusion.info_ref
  15.8 4.9 %shard_map.86 = (f32[192,256]{1,0:T(8,128)}, bf16[3,192,256]{2,1,0:T(8,128)(2,1)}) custom-call(s32[12]{0:T(128)} %bitcast.31, s32[12]{0:T(128)} %bitcast.33, s32[3]{0:T(128)} %pad_add_fusion.info_ref, bf16[12,256,256]{2,1,0:T(8,128)(2,1)} %bitcast.29, bf16[1536,256]{1,0:T(8,128)(2,1)} %all_gather.3.f_ref), custom_call_target="tpu_custom_call" | custom-call | tf_op jit(solution)/shard_map/pallas_call | solution.py:78
  20.6 1.0 %slice_bitcast_fusion.9 = (bf16[192,256]{1,0:T(8,128)(2,1)S(1)}, bf16[192,256]{1,0:T(8,128)(2,1)S(1)}, bf16[192,256]{1,0:T(8,128)(2,1)S(1)}) fusion(bf16[3,192,256]{2,1,0:T(8,128)(2,1)} %get-tuple-element.7), kind=kLoop, calls=%fused_computation.16 | loop fusion | bytes 589824 | tf_op jit(solution)/shard_map/squeeze | solution.py:129
  21.6 0.5 collective-permute-start
  22.1 3.4 %collective-permute-start.2 = (bf16[192,256]{1,0:T(8,128)(2,1)S(1)}, bf16[192,256]{1,0:T(8,128)(2,1)S(1)}, u32[]{:S(2)}, u32[]{:S(2)}) collective-permute-start(bf16[192,256]{1,0:T(8,128)(2,1)S(1)} %get-tuple-element.18), channel_id=1, source_target_pairs={{0,3},{1,0},{2,1},{3,2},{4,7},{5,4},{6,5},{7,6},{8,11},{9,8},{10,9... | collective-permute-start | bytes 294920 | tf_op jit(solution)/shard_map/ppermute | solution.py:129
  25.5 3.7 %collective-permute-done = bf16[192,256]{1,0:T(8,128)(2,1)S(1)} collective-permute-done((bf16[192,256]{1,0:T(8,128)(2,1)S(1)}, bf16[192,256]{1,0:T(8,128)(2,1)S(1)}, u32[]{:S(2)}, u32[]{:S(2)}) %collective-permute-start) | collective-permute-done | bytes 98336 | tf_op jit(solution)/shard_map/ppermute | solution.py:129
  29.2 0.5 collective-permute-done.2
  29.8 4.5 %collective-permute-done.1 = bf16[192,256]{1,0:T(8,128)(2,1)S(1)} collective-permute-done((bf16[192,256]{1,0:T(8,128)(2,1)S(1)}, bf16[192,256]{1,0:T(8,128)(2,1)S(1)}, u32[]{:S(2)}, u32[]{:S(2)}) %collective-permute-start.1) | collective-permute-done | bytes 98336 | tf_op jit(solution)/shard_map/ppermute | solution.py:129
  34.2 1.8 %multiply_convert_fusion.1 = (bf16[192,256]{1,0:T(8,128)(2,1)}, f32[192,256]{1,0:T(8,128)S(1)}) fusion(bf16[256,256]{1,0:T(8,128)(2,1)S(1)} %copy-done, bf16[192,256]{1,0:T(8,128)(2,1)S(1)} %collective-permute-done.2, bf16[192,256]{1,0:T(8,128)(2,1)S(1)} %collective-permute-done.1, f32[192,256]{1,0:T(8,128)} %get-tuple-element.6, ...), kind=kOutput, calls=%fused_computation.3 | convolution fusion | flops 25755648 | bytes 917504 | tf_op jit(solution)/shard_map/dot_general | solution.py:16
  36.0 0.2 convolution_convert_fusion.mine_ref
  36.3 0.0 copy-start.1
  36.3 1.2 %collective-permute-start.5 = (bf16[192,256]{1,0:T(8,128)(2,1)S(1)}, bf16[192,256]{1,0:T(8,128)(2,1)S(1)}, u32[]{:S(2)}, u32[]{:S(2)}) collective-permute-start(bf16[192,256]{1,0:T(8,128)(2,1)S(1)} %convolution_convert_fusion.mine_ref), channel_id=1, source_target_pairs={{0,3},{1,0},{2,1},{3,2},{4,7},{5,4},{6,5},{7,6},{8,11},{9,8},{10,9... | collective-permute-start | bytes 294920 | tf_op jit(solution)/shard_map/ppermute | solution.py:131
  37.5 0.8 %collective-permute-start.3 = (bf16[192,256]{1,0:T(8,128)(2,1)S(1)}, bf16[192,256]{1,0:T(8,128)(2,1)S(1)}, u32[]{:S(2)}, u32[]{:S(2)}) collective-permute-start(bf16[192,256]{1,0:T(8,128)(2,1)S(1)} %convolution_convert_fusion.mine_ref), channel_id=1, source_target_pairs={{0,1},{1,2},{2,3},{3,0},{4,5},{5,6},{6,7},{7,4},{8,9},{9,10},{10,1... | collective-permute-start | bytes 294920 | tf_op jit(solution)/shard_map/ppermute | solution.py:131
  38.3 3.4 %collective-permute-done.5.rest_2_ = bf16[192,256]{1,0:T(8,128)(2,1)S(1)} collective-permute-done((bf16[192,256]{1,0:T(8,128)(2,1)S(1)}, bf16[192,256]{1,0:T(8,128)(2,1)S(1)}, u32[]{:S(2)}, u32[]{:S(2)}) %collective-permute-start.5) | collective-permute-done | bytes 98336 | tf_op jit(solution)/shard_map/ppermute | solution.py:131
  41.8 4.4 %collective-permute-done.4.rest_1_ = bf16[192,256]{1,0:T(8,128)(2,1)S(1)} collective-permute-done((bf16[192,256]{1,0:T(8,128)(2,1)S(1)}, bf16[192,256]{1,0:T(8,128)(2,1)S(1)}, u32[]{:S(2)}, u32[]{:S(2)}) %collective-permute-start.4) | collective-permute-done | bytes 98336 | tf_op jit(solution)/shard_map/ppermute | solution.py:131
  46.2 0.6 copy-done.3
  46.8 0.6 copy-done.4
  47.4 5.4 %shard_map.87 = (f32[192,256]{1,0:T(8,128)}, bf16[7,192,256]{2,1,0:T(8,128)(2,1)}) custom-call(s32[12]{0:T(128)} %bitcast.32, s32[12]{0:T(128)} %bitcast.34, s32[3]{0:T(128)} %pad_add_fusion.info_ref, bf16[12,256,256]{2,1,0:T(8,128)(2,1)} %bitcast.30, bf16[192,256]{1,0:T(8,128)(2,1)} %copy-done.1, bf16[192,256]{1,0:T(8,128)(2,1)} %copy-done.4, ...), custom_call_target="tpu_custom_call" | custom-call | tf_op jit(solution)/shard_map/pallas_call | solution.py:93
  52.8 1.2 %slice_bitcast_fusion.6 = (bf16[192,256]{1,0:T(8,128)(2,1)S(1)}, bf16[192,256]{1,0:T(8,128)(2,1)S(1)}, bf16[192,256]{1,0:T(8,128)(2,1)S(1)}, bf16[192,256]{1,0:T...) fusion(bf16[7,192,256]{2,1,0:T(8,128)(2,1)} %get-tuple-element.9), kind=kLoop, calls=%fused_computation.13 | loop fusion | bytes 1376256 | tf_op jit(solution)/shard_map/squeeze | solution.py:137
  54.1 0.1 collective-permute-start.6
  54.1 2.6 %collective-permute-start.12 = (bf16[192,256]{1,0:T(8,128)(2,1)S(1)}, bf16[192,256]{1,0:T(8,128)(2,1)S(1)}, u32[]{:S(2)}, u32[]{:S(2)}) collective-permute-start(bf16[192,256]{1,0:T(8,128)(2,1)S(1)} %get-tuple-element.11), channel_id=1, source_target_pairs={{0,28},{4,0},{8,4},{12,8},{16,12},{20,16},{24,20},{28,24},{1,29},{... | collective-permute-start | bytes 294920 | tf_op jit(solution)/shard_map/ppermute | solution.py:137
  56.8 0.5 collective-permute-start.11
  57.3 0.4 collective-permute-start.10
  57.7 0.8 %collective-permute-start.9 = (bf16[192,256]{1,0:T(8,128)(2,1)S(1)}, bf16[192,256]{1,0:T(8,128)(2,1)S(1)}, u32[]{:S(2)}, u32[]{:S(2)}) collective-permute-start(bf16[192,256]{1,0:T(8,128)(2,1)S(1)} %get-tuple-element.14), channel_id=1, source_target_pairs={{0,16},{4,20},{8,24},{12,28},{16,0},{20,4},{24,8},{28,12},{1,17},{... | collective-permute-start | bytes 294920 | tf_op jit(solution)/shard_map/ppermute | solution.py:137
  58.5 0.8 %collective-permute-done.6 = bf16[192,256]{1,0:T(8,128)(2,1)S(1)} collective-permute-done((bf16[192,256]{1,0:T(8,128)(2,1)S(1)}, bf16[192,256]{1,0:T(8,128)(2,1)S(1)}, u32[]{:S(2)}, u32[]{:S(2)}) %collective-permute-start.6) | collective-permute-done | bytes 98336 | tf_op jit(solution)/shard_map/ppermute | solution.py:137
  59.3 0.2 collective-permute-start.8
  59.5 2.9 %collective-permute-start.7 = (bf16[192,256]{1,0:T(8,128)(2,1)S(1)}, bf16[192,256]{1,0:T(8,128)(2,1)S(1)}, u32[]{:S(2)}, u32[]{:S(2)}) collective-permute-start(bf16[192,256]{1,0:T(8,128)(2,1)S(1)} %get-tuple-element.16), channel_id=1, source_target_pairs={{0,8},{4,12},{8,16},{12,20},{16,24},{20,28},{24,0},{28,4},{1,9},{5... | collective-permute-start | bytes 294920 | tf_op jit(solution)/shard_map/ppermute | solution.py:137
  62.4 0.1 collective-permute-done.9
  62.5 5.1 %collective-permute-done.8 = bf16[192,256]{1,0:T(8,128)(2,1)S(1)} collective-permute-done((bf16[192,256]{1,0:T(8,128)(2,1)S(1)}, bf16[192,256]{1,0:T(8,128)(2,1)S(1)}, u32[]{:S(2)}, u32[]{:S(2)}) %collective-permute-start.8) | collective-permute-done | bytes 98336 | tf_op jit(solution)/shard_map/ppermute | solution.py:137
  67.6 1.7 %add_convert_fusion = bf16[192,256]{1,0:T(8,128)(2,1)} fusion(bf16[192,256]{1,0:T(8,128)(2,1)S(1)} %collective-permute-done.12, bf16[192,256]{1,0:T(8,128)(2,1)S(1)} %collective-permute-done.11, bf16[192,256]{1,0:T(8,128)(2,1)S(1)} %collective-permute-done.10, bf16[192,256]{1,0:T(8,128)(2,1)S(1)} %collective-permute-done.9, ...), kind=kLoop, calls=%fused_computation.1 | loop fusion | flops 737280 | bytes 983040 | tf_op jit(solution)/shard_map/convert_element_type | solution.py:138
  (15 shorter events, 0.0 us)
Async XLA Ops:
  0.6 33.6 %copy-start = (bf16[256,256]{1,0:T(8,128)(2,1)S(1)}, bf16[256,256]{1,0:T(8,128)(2,1)}, u32[]{:S(2)}) copy-start(bf16[256,256]{1,0:T(8,128)(2,1)} %param.12) | copy-start | bytes 393220
  15.8 20.2 %copy-start.5 = (bf16[192,256]{1,0:T(8,128)(2,1)S(1)}, bf16[192,256]{1,0:T(8,128)(2,1)}, u32[]{:S(2)}) copy-start(bf16[192,256]{1,0:T(8,128)(2,1)} %param.13) | copy-start | bytes 294916
  21.6 7.6 %collective-permute-start = (bf16[192,256]{1,0:T(8,128)(2,1)S(1)}, bf16[192,256]{1,0:T(8,128)(2,1)S(1)}, u32[]{:S(2)}, u32[]{:S(2)}) collective-permute-start(bf16[192,256]{1,0:T(8,128)(2,1)S(1)} %get-tuple-element.17), channel_id=1, source_target_pairs={{0,1},{1,2},{2,3},{3,0},{4,5},{5,6},{6,7},{7,4},{8,9},{9,10},{10,1... | collective-permute-start | bytes 294920 | tf_op jit(solution)/shard_map/ppermute | solution.py:129
  22.1 7.6 %collective-permute-start.2 = (bf16[192,256]{1,0:T(8,128)(2,1)S(1)}, bf16[192,256]{1,0:T(8,128)(2,1)S(1)}, u32[]{:S(2)}, u32[]{:S(2)}) collective-permute-start(bf16[192,256]{1,0:T(8,128)(2,1)S(1)} %get-tuple-element.18), channel_id=1, source_target_pairs={{0,3},{1,0},{2,1},{3,2},{4,7},{5,4},{6,5},{7,6},{8,11},{9,8},{10,9... | collective-permute-start | bytes 294920 | tf_op jit(solution)/shard_map/ppermute | solution.py:129
  25.5 8.7 %collective-permute-start.1 = (bf16[192,256]{1,0:T(8,128)(2,1)S(1)}, bf16[192,256]{1,0:T(8,128)(2,1)S(1)}, u32[]{:S(2)}, u32[]{:S(2)}) collective-permute-start(bf16[192,256]{1,0:T(8,128)(2,1)S(1)} %get-tuple-element.19), channel_id=1, source_target_pairs={{0,2},{1,3},{2,0},{3,1},{4,6},{5,7},{6,4},{7,5},{8,10},{9,11},{10,... | collective-permute-start | bytes 294920 | tf_op jit(solution)/shard_map/ppermute | solution.py:129
  36.3 9.9 %copy-start.1 = (bf16[192,256]{1,0:T(8,128)(2,1)}, bf16[192,256]{1,0:T(8,128)(2,1)S(1)}, u32[]{:S(2)}) copy-start(bf16[192,256]{1,0:T(8,128)(2,1)S(1)} %convolution_convert_fusion.mine_ref) | copy-start | bytes 294916
  36.3 5.5 %collective-permute-start.5 = (bf16[192,256]{1,0:T(8,128)(2,1)S(1)}, bf16[192,256]{1,0:T(8,128)(2,1)S(1)}, u32[]{:S(2)}, u32[]{:S(2)}) collective-permute-start(bf16[192,256]{1,0:T(8,128)(2,1)S(1)} %convolution_convert_fusion.mine_ref), channel_id=1, source_target_pairs={{0,3},{1,0},{2,1},{3,2},{4,7},{5,4},{6,5},{7,6},{8,11},{9,8},{10,9... | collective-permute-start | bytes 294920 | tf_op jit(solution)/shard_map/ppermute | solution.py:131
  37.5 8.6 %collective-permute-start.4 = (bf16[192,256]{1,0:T(8,128)(2,1)S(1)}, bf16[192,256]{1,0:T(8,128)(2,1)S(1)}, u32[]{:S(2)}, u32[]{:S(2)}) collective-permute-start(bf16[192,256]{1,0:T(8,128)(2,1)S(1)} %convolution_convert_fusion.mine_ref), channel_id=1, source_target_pairs={{0,2},{1,3},{2,0},{3,1},{4,6},{5,7},{6,4},{7,5},{8,10},{9,11},{10,... | collective-permute-start | bytes 294920 | tf_op jit(solution)/shard_map/ppermute | solution.py:131
  37.5 8.7 %collective-permute-start.3 = (bf16[192,256]{1,0:T(8,128)(2,1)S(1)}, bf16[192,256]{1,0:T(8,128)(2,1)S(1)}, u32[]{:S(2)}, u32[]{:S(2)}) collective-permute-start(bf16[192,256]{1,0:T(8,128)(2,1)S(1)} %convolution_convert_fusion.mine_ref), channel_id=1, source_target_pairs={{0,1},{1,2},{2,3},{3,0},{4,5},{5,6},{6,7},{7,4},{8,9},{9,10},{10,1... | collective-permute-start | bytes 294920 | tf_op jit(solution)/shard_map/ppermute | solution.py:131
  41.8 4.4 %copy-start.2 = (bf16[192,256]{1,0:T(8,128)(2,1)}, bf16[192,256]{1,0:T(8,128)(2,1)S(1)}, u32[]{:S(2)}) copy-start(bf16[192,256]{1,0:T(8,128)(2,1)S(1)} %collective-permute-done.5.rest_2_) | copy-start | bytes 294916
  46.2 0.6 copy-start.3
  46.8 0.6 copy-start.4
  54.1 5.2 %collective-permute-start.6 = (bf16[192,256]{1,0:T(8,128)(2,1)S(1)}, bf16[192,256]{1,0:T(8,128)(2,1)S(1)}, u32[]{:S(2)}, u32[]{:S(2)}) collective-permute-start(bf16[192,256]{1,0:T(8,128)(2,1)S(1)} %get-tuple-element.10), channel_id=1, source_target_pairs={{0,4},{4,8},{8,12},{12,16},{16,20},{20,24},{24,28},{28,0},{1,5},{5... | collective-permute-start | bytes 294920 | tf_op jit(solution)/shard_map/ppermute | solution.py:137
  54.1 5.4 %collective-permute-start.12 = (bf16[192,256]{1,0:T(8,128)(2,1)S(1)}, bf16[192,256]{1,0:T(8,128)(2,1)S(1)}, u32[]{:S(2)}, u32[]{:S(2)}) collective-permute-start(bf16[192,256]{1,0:T(8,128)(2,1)S(1)} %get-tuple-element.11), channel_id=1, source_target_pairs={{0,28},{4,0},{8,4},{12,8},{16,12},{20,16},{24,20},{28,24},{1,29},{... | collective-permute-start | bytes 294920 | tf_op jit(solution)/shard_map/ppermute | solution.py:137
  56.8 5.7 %collective-permute-start.11 = (bf16[192,256]{1,0:T(8,128)(2,1)S(1)}, bf16[192,256]{1,0:T(8,128)(2,1)S(1)}, u32[]{:S(2)}, u32[]{:S(2)}) collective-permute-start(bf16[192,256]{1,0:T(8,128)(2,1)S(1)} %get-tuple-element.12), channel_id=1, source_target_pairs={{0,24},{4,28},{8,0},{12,4},{16,8},{20,12},{24,16},{28,20},{1,25},{... | collective-permute-start | bytes 294920 | tf_op jit(solution)/shard_map/ppermute | solution.py:137
  57.3 5.1 %collective-permute-start.10 = (bf16[192,256]{1,0:T(8,128)(2,1)S(1)}, bf16[192,256]{1,0:T(8,128)(2,1)S(1)}, u32[]{:S(2)}, u32[]{:S(2)}) collective-permute-start(bf16[192,256]{1,0:T(8,128)(2,1)S(1)} %get-tuple-element.13), channel_id=1, source_target_pairs={{0,20},{4,24},{8,28},{12,0},{16,4},{20,8},{24,12},{28,16},{1,21},{... | collective-permute-start | bytes 294920 | tf_op jit(solution)/shard_map/ppermute | solution.py:137
  57.7 4.8 %collective-permute-start.9 = (bf16[192,256]{1,0:T(8,128)(2,1)S(1)}, bf16[192,256]{1,0:T(8,128)(2,1)S(1)}, u32[]{:S(2)}, u32[]{:S(2)}) collective-permute-start(bf16[192,256]{1,0:T(8,128)(2,1)S(1)} %get-tuple-element.14), channel_id=1, source_target_pairs={{0,16},{4,20},{8,24},{12,28},{16,0},{20,4},{24,8},{28,12},{1,17},{... | collective-permute-start | bytes 294920 | tf_op jit(solution)/shard_map/ppermute | solution.py:137
  59.3 8.4 %collective-permute-start.8 = (bf16[192,256]{1,0:T(8,128)(2,1)S(1)}, bf16[192,256]{1,0:T(8,128)(2,1)S(1)}, u32[]{:S(2)}, u32[]{:S(2)}) collective-permute-start(bf16[192,256]{1,0:T(8,128)(2,1)S(1)} %get-tuple-element.15), channel_id=1, source_target_pairs={{0,12},{4,16},{8,20},{12,24},{16,28},{20,0},{24,4},{28,8},{1,13},{... | collective-permute-start | bytes 294920 | tf_op jit(solution)/shard_map/ppermute | solution.py:137
  59.5 8.1 %collective-permute-start.7 = (bf16[192,256]{1,0:T(8,128)(2,1)S(1)}, bf16[192,256]{1,0:T(8,128)(2,1)S(1)}, u32[]{:S(2)}, u32[]{:S(2)}) collective-permute-start(bf16[192,256]{1,0:T(8,128)(2,1)S(1)} %get-tuple-element.16), channel_id=1, source_target_pairs={{0,8},{4,12},{8,16},{12,20},{16,24},{20,28},{24,0},{28,4},{1,9},{5... | collective-permute-start | bytes 294920 | tf_op jit(solution)/shard_map/ppermute | solution.py:137

commit v3 on v2

--- a/solution.py
+++ b/solution.py
@@ -1,3 +1,5 @@
+import functools
+
 import jax
 import jax.numpy as jnp
 from jax import lax
@@ -20,16 +22,17 @@
     return (activated, pulled)
 
 
-def split_out(acc_ref, own_ref, send_ref, me):
+def split_out(acc_ref, own_ref, send_refs, me):
     chunk = own_ref.shape[0]
-    n = send_ref.shape[0] + 1
+    n = len(send_refs) + 1
     own_ref[...] = acc_ref[pl.ds(pl.multiple_of(me * chunk, 8), chunk), :]
     for shift in range(1, n):
         start = pl.multiple_of(((me + shift) % n) * chunk, 8)
-        send_ref[shift - 1] = acc_ref[pl.ds(start, chunk), :].astype(send_ref.dtype)
+        send_refs[shift - 1][...] = acc_ref[pl.ds(start, chunk), :].astype(send_refs[shift - 1].dtype)
 
 
-def forward_kernel(rows_ref, cols_ref, info_ref, a_ref, f_ref, own_ref, send_ref, acc_ref):
+def forward_kernel(rows_ref, cols_ref, info_ref, a_ref, f_ref, own_ref, *rest):
+    send_refs, acc_ref = rest[:-1], rest[-1]
     tile = a_ref.shape[1]
     acc_ref[...] = jnp.zeros_like(acc_ref)
 
@@ -40,16 +43,17 @@
         return carry
 
     lax.fori_loop(0, jnp.minimum(info_ref[0], a_ref.shape[0]), step, 0)
-    split_out(acc_ref, own_ref, send_ref, info_ref[1])
+    split_out(acc_ref, own_ref, send_refs, lax.axis_index("col"))
 
 
-def backward_kernel(rows_ref, cols_ref, info_ref, a_ref, mine_ref, *rest):
-    got_refs = rest[:-4]
-    own_ref, send_ref, block_ref, acc_ref = rest[-4:]
+def backward_kernel(n, rows_ref, cols_ref, info_ref, a_ref, mine_ref, *rest):
+    got_refs = rest[: n - 1]
+    own_ref = rest[n - 1]
+    send_refs = rest[n:-2]
+    block_ref, acc_ref = rest[-2:]
     tile = a_ref.shape[1]
     chunk = mine_ref.shape[0]
-    n = len(got_refs) + 1
-    me = info_ref[1]
+    me = lax.axis_index("col")
     block_ref[pl.ds(pl.multiple_of(me * chunk, 16), chunk), :] = mine_ref[...]
     for shift in range(1, n):
         start = pl.multiple_of(((me - shift + n) % n) * chunk, 16)
@@ -65,7 +69,7 @@
         return carry
 
     lax.fori_loop(0, jnp.minimum(info_ref[0], a_ref.shape[0]), step, 0)
-    split_out(acc_ref, own_ref, send_ref, info_ref[2])
+    split_out(acc_ref, own_ref, send_refs, lax.axis_index("row"))
 
 
 SMEM = pl.BlockSpec(memory_space=pltpu.SMEM)
@@ -77,12 +81,10 @@
     chunk = parts[1]
     return pl.pallas_call(
         forward_kernel,
-        out_shape=(
-            jax.ShapeDtypeStruct((chunk, features.shape[1]), jnp.float32),
-            jax.ShapeDtypeStruct((parts[0] - 1, chunk, features.shape[1]), jnp.bfloat16),
-        ),
+        out_shape=(jax.ShapeDtypeStruct((chunk, features.shape[1]), jnp.float32),)
+        + (jax.ShapeDtypeStruct((chunk, features.shape[1]), jnp.bfloat16),) * (parts[0] - 1),
         in_specs=[SMEM, SMEM, SMEM, VMEM, VMEM],
-        out_specs=(VMEM, VMEM),
+        out_specs=(VMEM,) * parts[0],
         scratch_shapes=[pltpu.VMEM((out_rows, features.shape[1]), jnp.float32)],
     )(rows, cols, info, blocks, features)
 
@@ -91,13 +93,11 @@
     chunk = out_rows // n_out
     width = mine.shape[1]
     return pl.pallas_call(
-        backward_kernel,
-        out_shape=(
-            jax.ShapeDtypeStruct((chunk, width), jnp.float32),
-            jax.ShapeDtypeStruct((n_out - 1, chunk, width), jnp.bfloat16),
-        ),
+        functools.partial(backward_kernel, len(got) + 1),
+        out_shape=(jax.ShapeDtypeStruct((chunk, width), jnp.float32),)
+        + (jax.ShapeDtypeStruct((chunk, width), jnp.bfloat16),) * (n_out - 1),
         in_specs=[SMEM, SMEM, SMEM, VMEM, VMEM] + [VMEM] * len(got),
-        out_specs=(VMEM, VMEM),
+        out_specs=(VMEM,) * n_out,
         scratch_shapes=[
             pltpu.VMEM(((len(got) + 1) * mine.shape[0], width), jnp.bfloat16),
             pltpu.VMEM((out_rows, width), jnp.float32),
@@ -114,22 +114,19 @@
     blocks = edge_tiles[0, 0]
     row_slots = tile_rows[0, 0]
     col_slots = tile_cols[0, 0]
-    filled = tile_count[0, 0]
     n_row = lax.axis_size("row")
     n_col = lax.axis_size("col")
-    me_row = lax.axis_index("row")
-    me_col = lax.axis_index("col")
     own_rows = features.shape[0]
 
     gathered = lax.all_gather(features, "row", axis=0, tiled=True)
-    info = jnp.stack([filled, me_col, me_row]).astype(jnp.int32)
-    own, send = tile_products(row_slots, col_slots, info, blocks, gathered, (n_col, own_rows))
+    info = tile_count.reshape(1)
+    own, *send = tile_products(row_slots, col_slots, info, blocks, gathered, (n_col, own_rows))
     total = own
     for shift, perm in enumerate(shifts("col")):
         total = total + lax.ppermute(send[shift], "col", perm).astype(jnp.float32)
     activated, pulled_own = dense_layer(total, cotangent, weight)
     got = [lax.ppermute(pulled_own, "col", perm) for perm in shifts("col")]
-    own_g, send_g = tile_products_t(
+    own_g, *send_g = tile_products_t(
         row_slots, col_slots, info, blocks, pulled_own, got, n_row, n_row * own_rows
     )
     total_g = own_g

time: 70 us -> 64 us (0.914)
  Pallas kernels: 10.3 us -> 7.34 us
  starting transfers between devices: 13.5 us -> 16.4 us
  local copies, waits for them, and re-layouts: 3.5 us -> 0.67 us
  waiting for transfers between devices: 22.5 us -> 19.9 us
    ppermute x3, waiting for transfers between devices: 8.69 us -> 4.94 us  [on_device(): total = total + lax.ppermute(send[shift], 'col', perm).astype(jnp.float32)]
    ppermute x3, starting transfers between devices: 3.88 us -> 6.87 us  [on_device(): total = total + lax.ppermute(send[shift], 'col', perm).astype(jnp.float32)]
    ppermute x7, starting transfers between devices: 7.58 us -> 4.61 us  [on_device(): lax.ppermute(send_g[shift], 'row', perm).astype(jnp.float32)]
    ppermute x3, starting transfers between devices: 2.08 us -> 4.87 us  [on_device(): got = [lax.ppermute(pulled_own, 'col', perm) for perm in shifts('col')]]
    squeeze x2 -> x0, local copies, waits for them, and re-layouts: 2.23 us -> none  [the longest x1 1.23 us: on_device(): send_g[shift]]
    pallas_call x1, Pallas kernels: 5.42 us -> 3.86 us  [tile_products_t(): pl.pallas_call(functools.partial(backward_kernel, len(got) + 1), out_shap...]
    pallas_call x1, Pallas kernels: 4.86 us -> 3.48 us  [tile_products(): pl.pallas_call(forward_kernel, out_shape=(jax.ShapeDtypeStruct((chunk, fe...]
  transfers between devices with their start and end apart: 13 -> 13, of which waited for: 8 -> 9; matrix products, arithmetic and copies ran while one was open for 0% -> 0% of each run, Pallas kernels for 0% -> 0%
where the time goes in v3:
time: 64 us; the launch traced here: 63.2 us
  waiting for transfers between devices  19.9 us (31%)
  starting transfers between devices  16.4 us (26%)
  blocking collectives  13.9 us (22%)
  Pallas kernels  7.34 us (11%)
  matrix products  2.02 us (3%)
  other arithmetic  1.67 us (3%)
  between operations  1.37 us (2%)
  local copies, waits for them, and re-layouts  0.67 us (1%)
    all_gather x1, blocking collectives, on_device(): gathered = lax.all_gather(features, 'row', axis=0, tiled=True)  13.9 us
    ppermute x3, waiting for transfers between devices, on_device(): got = [lax.ppermute(pulled_own, 'col', perm) for perm in shifts('col')]  8.42 us
    ppermute x3, starting transfers between devices, on_device(): total = total + lax.ppermute(send[shift], 'col', perm).astype(jnp.float32)  6.87 us
    ppermute x7, waiting for transfers between devices, on_device(): lax.ppermute(send_g[shift], 'row', perm).astype(jnp.float32)  6.5 us
    ppermute x3, waiting for transfers between devices, on_device(): total = total + lax.ppermute(send[shift], 'col', perm).astype(jnp.float32)  4.94 us
    ppermute x3, starting transfers between devices, on_device(): got = [lax.ppermute(pulled_own, 'col', perm) for perm in shifts('col')]  4.87 us
    ppermute x7, starting transfers between devices, on_device(): lax.ppermute(send_g[shift], 'row', perm).astype(jnp.float32)  4.61 us
    pallas_call x1, Pallas kernels, tile_products_t(): pl.pallas_call(functools.partial(backward_kernel, len(got) + 1), out_shap...  3.86 us
  transfers between devices with their start and end apart: 13, of which 9 were waited for; matrix products, arithmetic and copies ran while one was open for 0% of the time, Pallas kernels for 0%

profile of v3, /device:TPU:0, one launch (start us, length us, event | category | flops | bytes accessed | tf_op | source)
XLA Modules:
  0.0 63.2 jit_solution(7710802808351314718)
XLA Ops:
  0.6 0.0 copy-start
  1.3 13.9 %all_gather.3.f_ref = bf16[1536,256]{1,0:T(8,128)(2,1)} all-gather(bf16[192,256]{1,0:T(8,128)(2,1)} %param.7), channel_id=1, replica_groups=mesh['row'=8,'col'=4] {'row'}, dimensions={0}, use_global_device_ids=true | all-gather | bytes 884736 | tf_op jit(solution)/shard_map/all_gather | solution.py:121
  15.2 3.5 %shard_map.86 = (f32[192,256]{1,0:T(8,128)}, bf16[192,256]{1,0:T(8,128)(2,1)}, bf16[192,256]{1,0:T(8,128)(2,1)}, bf16[192,256]{1,0:T(8,128)(2,1)}) custom-call(s32[12]{0:T(128)} %bitcast.10, s32[12]{0:T(128)} %bitcast.12, s32[1]{0:T(128)} %bitcast.6.info_ref, bf16[12,256,256]{2,1,0:T(8,128)(2,1)} %bitcast.8, bf16[1536,256]{1,0:T(8,128)(2,1)} %all_gather.3.f_ref), custom_call_target="tpu_custom_call" | custom-call | tf_op jit(solution)/shard_map/pallas_call | solution.py:82
  18.7 1.2 %collective-permute-start = (bf16[192,256]{1,0:T(8,128)(2,1)}, bf16[192,256]{1,0:T(8,128)(2,1)S(1)}, u32[]{:S(2)}, u32[]{:S(2)}) collective-permute-start(bf16[192,256]{1,0:T(8,128)(2,1)} %get-tuple-element.15), channel_id=1, source_target_pairs={{0,1},{1,2},{2,3},{3,0},{4,5},{5,6},{6,7},{7,4},{8,9},{9,10},{10,1... | collective-permute-start | bytes 294920 | tf_op jit(solution)/shard_map/ppermute | solution.py:126
  19.9 2.8 %collective-permute-start.1 = (bf16[192,256]{1,0:T(8,128)(2,1)}, bf16[192,256]{1,0:T(8,128)(2,1)S(1)}, u32[]{:S(2)}, u32[]{:S(2)}) collective-permute-start(bf16[192,256]{1,0:T(8,128)(2,1)} %get-tuple-element.16), channel_id=1, source_target_pairs={{0,2},{1,3},{2,0},{3,1},{4,6},{5,7},{6,4},{7,5},{8,10},{9,11},{10,... | collective-permute-start | bytes 294920 | tf_op jit(solution)/shard_map/ppermute | solution.py:126
  22.7 2.9 %collective-permute-start.2 = (bf16[192,256]{1,0:T(8,128)(2,1)}, bf16[192,256]{1,0:T(8,128)(2,1)S(1)}, u32[]{:S(2)}, u32[]{:S(2)}) collective-permute-start(bf16[192,256]{1,0:T(8,128)(2,1)} %get-tuple-element.17), channel_id=1, source_target_pairs={{0,3},{1,0},{2,1},{3,2},{4,7},{5,4},{6,5},{7,6},{8,11},{9,8},{10,9... | collective-permute-start | bytes 294920 | tf_op jit(solution)/shard_map/ppermute | solution.py:126
  25.5 0.1 collective-permute-done
  25.6 4.8 %collective-permute-done.1 = bf16[192,256]{1,0:T(8,128)(2,1)S(1)} collective-permute-done((bf16[192,256]{1,0:T(8,128)(2,1)}, bf16[192,256]{1,0:T(8,128)(2,1)S(1)}, u32[]{:S(2)}, u32[]{:S(2)}) %collective-permute-start.1) | collective-permute-done | bytes 98336 | tf_op jit(solution)/shard_map/ppermute | solution.py:126
  30.5 0.0 collective-permute-done.2
  30.5 1.8 %multiply_convert_fusion.1 = (bf16[192,256]{1,0:T(8,128)(2,1)}, f32[192,256]{1,0:T(8,128)S(1)}) fusion(bf16[256,256]{1,0:T(8,128)(2,1)S(1)} %copy-done, bf16[192,256]{1,0:T(8,128)(2,1)S(1)} %collective-permute-done.2, bf16[192,256]{1,0:T(8,128)(2,1)S(1)} %collective-permute-done.1, f32[192,256]{1,0:T(8,128)} %get-tuple-element.14, ...), kind=kOutput, calls=%fused_computation.3 | convolution fusion | flops 25755648 | bytes 917504 | tf_op jit(solution)/shard_map/dot_general | solution.py:18
  32.3 0.2 convolution_convert_fusion.mine_ref
  32.5 0.0 copy-start.1
  32.5 4.2 %collective-permute-start.5 = (bf16[192,256]{1,0:T(8,128)(2,1)S(1)}, bf16[192,256]{1,0:T(8,128)(2,1)S(1)}, u32[]{:S(2)}, u32[]{:S(2)}) collective-permute-start(bf16[192,256]{1,0:T(8,128)(2,1)S(1)} %convolution_convert_fusion.mine_ref), channel_id=1, source_target_pairs={{0,3},{1,0},{2,1},{3,2},{4,7},{5,4},{6,5},{7,6},{8,11},{9,8},{10,9... | collective-permute-start | bytes 294920 | tf_op jit(solution)/shard_map/ppermute | solution.py:128
  36.8 0.0 collective-permute-start.4
  36.8 0.6 %collective-permute-start.3 = (bf16[192,256]{1,0:T(8,128)(2,1)S(1)}, bf16[192,256]{1,0:T(8,128)(2,1)S(1)}, u32[]{:S(2)}, u32[]{:S(2)}) collective-permute-start(bf16[192,256]{1,0:T(8,128)(2,1)S(1)} %convolution_convert_fusion.mine_ref), channel_id=1, source_target_pairs={{0,1},{1,2},{2,3},{3,0},{4,5},{5,6},{6,7},{7,4},{8,9},{9,10},{10,1... | collective-permute-start | bytes 294920 | tf_op jit(solution)/shard_map/ppermute | solution.py:128
  37.4 2.5 %collective-permute-done.5.rest_2_ = bf16[192,256]{1,0:T(8,128)(2,1)S(1)} collective-permute-done((bf16[192,256]{1,0:T(8,128)(2,1)S(1)}, bf16[192,256]{1,0:T(8,128)(2,1)S(1)}, u32[]{:S(2)}, u32[]{:S(2)}) %collective-permute-start.5) | collective-permute-done | bytes 98336 | tf_op jit(solution)/shard_map/ppermute | solution.py:128
  40.0 5.9 %collective-permute-done.4.rest_1_ = bf16[192,256]{1,0:T(8,128)(2,1)S(1)} collective-permute-done((bf16[192,256]{1,0:T(8,128)(2,1)S(1)}, bf16[192,256]{1,0:T(8,128)(2,1)S(1)}, u32[]{:S(2)}, u32[]{:S(2)}) %collective-permute-start.4) | collective-permute-done | bytes 98336 | tf_op jit(solution)/shard_map/ppermute | solution.py:128
  45.8 0.6 copy-done.3
  46.5 0.0 copy-done.4
  46.5 3.9 %shard_map.87 = (f32[192,256]{1,0:T(8,128)}, bf16[192,256]{1,0:T(8,128)(2,1)}, bf16[192,256]{1,0:T(8,128)(2,1)}, bf16[192,256]{1,0:T(8,128)(2,1)}, bf16[192,256]...) custom-call(s32[12]{0:T(128)} %bitcast.11, s32[12]{0:T(128)} %bitcast.13, ...), custom_call_target="tpu_custom_call" | custom-call | tf_op jit(solution)/shard_map/pallas_call | solution.py:95
  50.4 0.1 collective-permute-start.7
  50.4 2.1 %collective-permute-start.8 = (bf16[192,256]{1,0:T(8,128)(2,1)}, bf16[192,256]{1,0:T(8,128)(2,1)S(1)}, u32[]{:S(2)}, u32[]{:S(2)}) collective-permute-start(bf16[192,256]{1,0:T(8,128)(2,1)} %get-tuple-element.21), channel_id=1, source_target_pairs={{0,12},{4,16},{8,20},{12,24},{16,28},{20,0},{24,4},{28,8},{1,13},{... | collective-permute-start | bytes 294920 | tf_op jit(solution)/shard_map/ppermute | solution.py:134
  52.5 1.1 %collective-permute-start.9 = (bf16[192,256]{1,0:T(8,128)(2,1)}, bf16[192,256]{1,0:T(8,128)(2,1)S(1)}, u32[]{:S(2)}, u32[]{:S(2)}) collective-permute-start(bf16[192,256]{1,0:T(8,128)(2,1)} %get-tuple-element.22), channel_id=1, source_target_pairs={{0,16},{4,20},{8,24},{12,28},{16,0},{20,4},{24,8},{28,12},{1,17},{... | collective-permute-start | bytes 294920 | tf_op jit(solution)/shard_map/ppermute | solution.py:134
  53.6 0.4 collective-permute-start.10
  54.0 2.1 %collective-permute-done.6 = bf16[192,256]{1,0:T(8,128)(2,1)S(1)} collective-permute-done((bf16[192,256]{1,0:T(8,128)(2,1)}, bf16[192,256]{1,0:T(8,128)(2,1)S(1)}, u32[]{:S(2)}, u32[]{:S(2)}) %collective-permute-start.6) | collective-permute-done | bytes 98336 | tf_op jit(solution)/shard_map/ppermute | solution.py:134
  56.0 0.2 collective-permute-start.11
  56.2 1.1 %collective-permute-done.7 = bf16[192,256]{1,0:T(8,128)(2,1)S(1)} collective-permute-done((bf16[192,256]{1,0:T(8,128)(2,1)}, bf16[192,256]{1,0:T(8,128)(2,1)S(1)}, u32[]{:S(2)}, u32[]{:S(2)}) %collective-permute-start.7) | collective-permute-done | bytes 98336 | tf_op jit(solution)/shard_map/ppermute | solution.py:134
  57.3 0.8 %collective-permute-start.12 = (bf16[192,256]{1,0:T(8,128)(2,1)}, bf16[192,256]{1,0:T(8,128)(2,1)S(1)}, u32[]{:S(2)}, u32[]{:S(2)}) collective-permute-start(bf16[192,256]{1,0:T(8,128)(2,1)} %get-tuple-element.25), channel_id=1, source_target_pairs={{0,28},{4,0},{8,4},{12,8},{16,12},{20,16},{24,20},{28,24},{1,29},{... | collective-permute-start | bytes 294920 | tf_op jit(solution)/shard_map/ppermute | solution.py:134
  58.1 2.6 %collective-permute-done.8 = bf16[192,256]{1,0:T(8,128)(2,1)S(1)} collective-permute-done((bf16[192,256]{1,0:T(8,128)(2,1)}, bf16[192,256]{1,0:T(8,128)(2,1)S(1)}, u32[]{:S(2)}, u32[]{:S(2)}) %collective-permute-start.8) | collective-permute-done | bytes 98336 | tf_op jit(solution)/shard_map/ppermute | solution.py:134
  60.7 0.2 collective-permute-done.9
  60.9 0.6 collective-permute-done.10
  61.5 1.7 %add_convert_fusion = bf16[192,256]{1,0:T(8,128)(2,1)} fusion(bf16[192,256]{1,0:T(8,128)(2,1)S(1)} %collective-permute-done.12, bf16[192,256]{1,0:T(8,128)(2,1)S(1)} %collective-permute-done.11, bf16[192,256]{1,0:T(8,128)(2,1)S(1)} %collective-permute-done.10, bf16[192,256]{1,0:T(8,128)(2,1)S(1)} %collective-permute-done.9, ...), kind=kLoop, calls=%fused_computation.1 | loop fusion | flops 737280 | bytes 983040 | tf_op jit(solution)/shard_map/convert_element_type | solution.py:135
  (12 shorter events, 0.0 us)
Async XLA Ops:
  0.6 29.9 %copy-start = (bf16[256,256]{1,0:T(8,128)(2,1)S(1)}, bf16[256,256]{1,0:T(8,128)(2,1)}, u32[]{:S(2)}) copy-start(bf16[256,256]{1,0:T(8,128)(2,1)} %param.12) | copy-start | bytes 393220
  15.2 17.1 %copy-start.5 = (bf16[192,256]{1,0:T(8,128)(2,1)S(1)}, bf16[192,256]{1,0:T(8,128)(2,1)}, u32[]{:S(2)}) copy-start(bf16[192,256]{1,0:T(8,128)(2,1)} %param.13) | copy-start | bytes 294916
  18.7 7.0 %collective-permute-start = (bf16[192,256]{1,0:T(8,128)(2,1)}, bf16[192,256]{1,0:T(8,128)(2,1)S(1)}, u32[]{:S(2)}, u32[]{:S(2)}) collective-permute-start(bf16[192,256]{1,0:T(8,128)(2,1)} %get-tuple-element.15), channel_id=1, source_target_pairs={{0,1},{1,2},{2,3},{3,0},{4,5},{5,6},{6,7},{7,4},{8,9},{9,10},{10,1... | collective-permute-start | bytes 294920 | tf_op jit(solution)/shard_map/ppermute | solution.py:126
  19.9 10.6 %collective-permute-start.1 = (bf16[192,256]{1,0:T(8,128)(2,1)}, bf16[192,256]{1,0:T(8,128)(2,1)S(1)}, u32[]{:S(2)}, u32[]{:S(2)}) collective-permute-start(bf16[192,256]{1,0:T(8,128)(2,1)} %get-tuple-element.16), channel_id=1, source_target_pairs={{0,2},{1,3},{2,0},{3,1},{4,6},{5,7},{6,4},{7,5},{8,10},{9,11},{10,... | collective-permute-start | bytes 294920 | tf_op jit(solution)/shard_map/ppermute | solution.py:126
  22.7 7.8 %collective-permute-start.2 = (bf16[192,256]{1,0:T(8,128)(2,1)}, bf16[192,256]{1,0:T(8,128)(2,1)S(1)}, u32[]{:S(2)}, u32[]{:S(2)}) collective-permute-start(bf16[192,256]{1,0:T(8,128)(2,1)} %get-tuple-element.17), channel_id=1, source_target_pairs={{0,3},{1,0},{2,1},{3,2},{4,7},{5,4},{6,5},{7,6},{8,11},{9,8},{10,9... | collective-permute-start | bytes 294920 | tf_op jit(solution)/shard_map/ppermute | solution.py:126
  32.5 13.3 %copy-start.1 = (bf16[192,256]{1,0:T(8,128)(2,1)}, bf16[192,256]{1,0:T(8,128)(2,1)S(1)}, u32[]{:S(2)}) copy-start(bf16[192,256]{1,0:T(8,128)(2,1)S(1)} %convolution_convert_fusion.mine_ref) | copy-start | bytes 294916
  32.5 7.4 %collective-permute-start.5 = (bf16[192,256]{1,0:T(8,128)(2,1)S(1)}, bf16[192,256]{1,0:T(8,128)(2,1)S(1)}, u32[]{:S(2)}, u32[]{:S(2)}) collective-permute-start(bf16[192,256]{1,0:T(8,128)(2,1)S(1)} %convolution_convert_fusion.mine_ref), channel_id=1, source_target_pairs={{0,3},{1,0},{2,1},{3,2},{4,7},{5,4},{6,5},{7,6},{8,11},{9,8},{10,9... | collective-permute-start | bytes 294920 | tf_op jit(solution)/shard_map/ppermute | solution.py:128
  36.8 9.1 %collective-permute-start.4 = (bf16[192,256]{1,0:T(8,128)(2,1)S(1)}, bf16[192,256]{1,0:T(8,128)(2,1)S(1)}, u32[]{:S(2)}, u32[]{:S(2)}) collective-permute-start(bf16[192,256]{1,0:T(8,128)(2,1)S(1)} %convolution_convert_fusion.mine_ref), channel_id=1, source_target_pairs={{0,2},{1,3},{2,0},{3,1},{4,6},{5,7},{6,4},{7,5},{8,10},{9,11},{10,... | collective-permute-start | bytes 294920 | tf_op jit(solution)/shard_map/ppermute | solution.py:128
  36.8 9.1 %collective-permute-start.3 = (bf16[192,256]{1,0:T(8,128)(2,1)S(1)}, bf16[192,256]{1,0:T(8,128)(2,1)S(1)}, u32[]{:S(2)}, u32[]{:S(2)}) collective-permute-start(bf16[192,256]{1,0:T(8,128)(2,1)S(1)} %convolution_convert_fusion.mine_ref), channel_id=1, source_target_pairs={{0,1},{1,2},{2,3},{3,0},{4,5},{5,6},{6,7},{7,4},{8,9},{9,10},{10,1... | collective-permute-start | bytes 294920 | tf_op jit(solution)/shard_map/ppermute | solution.py:128
  40.0 5.9 %copy-start.2 = (bf16[192,256]{1,0:T(8,128)(2,1)}, bf16[192,256]{1,0:T(8,128)(2,1)S(1)}, u32[]{:S(2)}) copy-start(bf16[192,256]{1,0:T(8,128)(2,1)S(1)} %collective-permute-done.5.rest_2_) | copy-start | bytes 294916
  45.8 0.6 %copy-start.3 = (bf16[192,256]{1,0:T(8,128)(2,1)}, bf16[192,256]{1,0:T(8,128)(2,1)S(1)}, u32[]{:S(2)}) copy-start(bf16[192,256]{1,0:T(8,128)(2,1)S(1)} %collective-permute-done.4.rest_1_) | copy-start | bytes 294916
  45.8 0.7 %copy-start.4 = (bf16[192,256]{1,0:T(8,128)(2,1)}, bf16[192,256]{1,0:T(8,128)(2,1)S(1)}, u32[]{:S(2)}) copy-start(bf16[192,256]{1,0:T(8,128)(2,1)S(1)} %collective-permute-done.3.rest_0_) | copy-start | bytes 294916
  50.4 5.7 %collective-permute-start.6 = (bf16[192,256]{1,0:T(8,128)(2,1)}, bf16[192,256]{1,0:T(8,128)(2,1)S(1)}, u32[]{:S(2)}, u32[]{:S(2)}) collective-permute-start(bf16[192,256]{1,0:T(8,128)(2,1)} %get-tuple-element.19), channel_id=1, source_target_pairs={{0,4},{4,8},{8,12},{12,16},{16,20},{20,24},{24,28},{28,0},{1,5},{5... | collective-permute-start | bytes 294920 | tf_op jit(solution)/shard_map/ppermute | solution.py:134
  50.4 6.9 %collective-permute-start.7 = (bf16[192,256]{1,0:T(8,128)(2,1)}, bf16[192,256]{1,0:T(8,128)(2,1)S(1)}, u32[]{:S(2)}, u32[]{:S(2)}) collective-permute-start(bf16[192,256]{1,0:T(8,128)(2,1)} %get-tuple-element.20), channel_id=1, source_target_pairs={{0,8},{4,12},{8,16},{12,20},{16,24},{20,28},{24,0},{28,4},{1,9},{5... | collective-permute-start | bytes 294920 | tf_op jit(solution)/shard_map/ppermute | solution.py:134
  50.4 10.3 %collective-permute-start.8 = (bf16[192,256]{1,0:T(8,128)(2,1)}, bf16[192,256]{1,0:T(8,128)(2,1)S(1)}, u32[]{:S(2)}, u32[]{:S(2)}) collective-permute-start(bf16[192,256]{1,0:T(8,128)(2,1)} %get-tuple-element.21), channel_id=1, source_target_pairs={{0,12},{4,16},{8,20},{12,24},{16,28},{20,0},{24,4},{28,8},{1,13},{... | collective-permute-start | bytes 294920 | tf_op jit(solution)/shard_map/ppermute | solution.py:134
  52.5 8.4 %collective-permute-start.9 = (bf16[192,256]{1,0:T(8,128)(2,1)}, bf16[192,256]{1,0:T(8,128)(2,1)S(1)}, u32[]{:S(2)}, u32[]{:S(2)}) collective-permute-start(bf16[192,256]{1,0:T(8,128)(2,1)} %get-tuple-element.22), channel_id=1, source_target_pairs={{0,16},{4,20},{8,24},{12,28},{16,0},{20,4},{24,8},{28,12},{1,17},{... | collective-permute-start | bytes 294920 | tf_op jit(solution)/shard_map/ppermute | solution.py:134
  53.6 7.9 %collective-permute-start.10 = (bf16[192,256]{1,0:T(8,128)(2,1)}, bf16[192,256]{1,0:T(8,128)(2,1)S(1)}, u32[]{:S(2)}, u32[]{:S(2)}) collective-permute-start(bf16[192,256]{1,0:T(8,128)(2,1)} %get-tuple-element.23), channel_id=1, source_target_pairs={{0,20},{4,24},{8,28},{12,0},{16,4},{20,8},{24,12},{28,16},{1,21},{... | collective-permute-start | bytes 294920 | tf_op jit(solution)/shard_map/ppermute | solution.py:134
  56.0 5.4 %collective-permute-start.11 = (bf16[192,256]{1,0:T(8,128)(2,1)}, bf16[192,256]{1,0:T(8,128)(2,1)S(1)}, u32[]{:S(2)}, u32[]{:S(2)}) collective-permute-start(bf16[192,256]{1,0:T(8,128)(2,1)} %get-tuple-element.24), channel_id=1, source_target_pairs={{0,24},{4,28},{8,0},{12,4},{16,8},{20,12},{24,16},{28,20},{1,25},{... | collective-permute-start | bytes 294920 | tf_op jit(solution)/shard_map/ppermute | solution.py:134
  57.3 4.2 %collective-permute-start.12 = (bf16[192,256]{1,0:T(8,128)(2,1)}, bf16[192,256]{1,0:T(8,128)(2,1)S(1)}, u32[]{:S(2)}, u32[]{:S(2)}) collective-permute-start(bf16[192,256]{1,0:T(8,128)(2,1)} %get-tuple-element.25), channel_id=1, source_target_pairs={{0,28},{4,0},{8,4},{12,8},{16,12},{20,16},{24,20},{28,24},{1,29},{... | collective-permute-start | bytes 294920 | tf_op jit(solution)/shard_map/ppermute | solution.py:134

commit v4 on v3

--- a/solution.py
+++ b/solution.py
@@ -6,6 +6,9 @@
 from jax.experimental import pallas as pl
 from jax.experimental.pallas import tpu as pltpu
 from jax.sharding import PartitionSpec as P
+
+SMEM = pl.BlockSpec(memory_space=pltpu.SMEM)
+VMEM = pl.BlockSpec(memory_space=pltpu.VMEM)
 
 
 def silu_slope(mixed):
@@ -20,6 +23,33 @@
     scaled = (grad_rows.astype(jnp.float32) * silu_slope(mixed)).astype(jnp.bfloat16)
     pulled = jnp.dot(scaled, weight.T, preferred_element_type=jnp.float32).astype(jnp.bfloat16)
     return (activated, pulled)
+
+
+def dense_kernel(n, own_ref, *rest):
+    got_refs = rest[: n - 1]
+    grad_ref, weight_ref, act_ref, pulled_ref = rest[n - 1:]
+    total = own_ref[...]
+    for got in got_refs:
+        total = total + got[...].astype(jnp.float32)
+    weight = weight_ref[...]
+    mixed = jnp.dot(total.astype(jnp.bfloat16), weight, preferred_element_type=jnp.float32)
+    sigma = jax.nn.sigmoid(mixed)
+    act_ref[...] = (mixed * sigma).astype(act_ref.dtype)
+    slope = sigma * (1.0 + mixed * (1.0 - sigma))
+    scaled = (grad_ref[...].astype(jnp.float32) * slope).astype(jnp.bfloat16)
+    pulled_ref[...] = lax.dot_general(
+        scaled, weight, (((1,), (1,)), ((), ())), preferred_element_type=jnp.float32
+    ).astype(pulled_ref.dtype)
+
+
+def dense_layer_kernel(own, got, grad_rows, weight):
+    shape = jax.ShapeDtypeStruct(own.shape, jnp.bfloat16)
+    return pl.pallas_call(
+        functools.partial(dense_kernel, len(got) + 1),
+        out_shape=(shape, shape),
+        in_specs=[VMEM] * (len(got) + 3),
+        out_specs=(VMEM, VMEM),
+    )(own, *got, grad_rows, weight)
 
 
 def split_out(acc_ref, own_ref, send_refs, me):
@@ -72,10 +102,6 @@
     split_out(acc_ref, own_ref, send_refs, lax.axis_index("row"))
 
 
-SMEM = pl.BlockSpec(memory_space=pltpu.SMEM)
-VMEM = pl.BlockSpec(memory_space=pltpu.VMEM)
-
-
 def tile_products(rows, cols, info, blocks, features, parts):
     out_rows = parts[0] * parts[1]
     chunk = parts[1]
@@ -121,10 +147,8 @@
     gathered = lax.all_gather(features, "row", axis=0, tiled=True)
     info = tile_count.reshape(1)
     own, *send = tile_products(row_slots, col_slots, info, blocks, gathered, (n_col, own_rows))
-    total = own
-    for shift, perm in enumerate(shifts("col")):
-        total = total + lax.ppermute(send[shift], "col", perm).astype(jnp.float32)
-    activated, pulled_own = dense_layer(total, cotangent, weight)
+    got_f = [lax.ppermute(send[shift], "col", perm) for shift, perm in enumerate(shifts("col"))]
+    activated, pulled_own = dense_layer_kernel(own, got_f, cotangent, weight)
     got = [lax.ppermute(pulled_own, "col", perm) for perm in shifts("col")]
     own_g, *send_g = tile_products_t(
         row_slots, col_slots, info, blocks, pulled_own, got, n_row, n_row * own_rows

time: 64 us -> 64.3 us (level)
  matrix products: 2.02 us -> 0 us
  Pallas kernels: 7.34 us -> 8.63 us
  waiting for transfers between devices: 19.9 us -> 20.8 us
  starting transfers between devices: 16.4 us -> 15.5 us
  local copies, waits for them, and re-layouts: 0.67 us -> 1.32 us
    pallas_call x0 -> x1, Pallas kernels: none -> 2.17 us  [dense_layer_kernel(): pl.pallas_call(functools.partial(dense_kernel, len(got) + 1), out_shape=(...]
    dot_general x2 -> x0, matrix products: 2.02 us -> none  [the longest x1 1.79 us: dense_layer(): mixed = jnp.dot(aggregated, weight, preferred_element_type=jnp.float32)]
    ppermute x3, waiting for transfers between devices: 4.94 us -> 6.23 us  [on_device(): lax.ppermute(send[shift], 'col', perm)]
    ppermute x3, starting transfers between devices: 6.87 us -> 5.72 us  [on_device(): lax.ppermute(send[shift], 'col', perm)]
    ppermute x7, starting transfers between devices: 4.61 us -> 5.75 us  [on_device(): lax.ppermute(send_g[shift], 'row', perm).astype(jnp.float32)]
    ppermute x7, waiting for transfers between devices: 6.5 us -> 5.4 us  [on_device(): lax.ppermute(send_g[shift], 'row', perm).astype(jnp.float32)]
    ppermute x3, starting transfers between devices: 4.87 us -> 4.01 us  [on_device(): got = [lax.ppermute(pulled_own, 'col', perm) for perm in shifts('col')]]
    ppermute x3, waiting for transfers between devices: 8.42 us -> 9.22 us  [on_device(): got = [lax.ppermute(pulled_own, 'col', perm) for perm in shifts('col')]]
where the time goes in v4:
time: 64.3 us; the launch traced here: 63.1 us
  waiting for transfers between devices  20.8 us (32%)
  starting transfers between devices  15.5 us (24%)
  blocking collectives  13.9 us (22%)
  Pallas kernels  8.63 us (13%)
  other arithmetic  1.67 us (3%)
  local copies, waits for them, and re-layouts  1.32 us (2%)
  between operations  1.3 us (2%)
    all_gather x1, blocking collectives, on_device(): gathered = lax.all_gather(features, 'row', axis=0, tiled=True)  13.9 us
    ppermute x3, waiting for transfers between devices, on_device(): got = [lax.ppermute(pulled_own, 'col', perm) for perm in shifts('col')]  9.22 us
    ppermute x3, waiting for transfers between devices, on_device(): lax.ppermute(send[shift], 'col', perm)  6.23 us
    ppermute x7, starting transfers between devices, on_device(): lax.ppermute(send_g[shift], 'row', perm).astype(jnp.float32)  5.75 us
    ppermute x3, starting transfers between devices, on_device(): lax.ppermute(send[shift], 'col', perm)  5.72 us
    ppermute x7, waiting for transfers between devices, on_device(): lax.ppermute(send_g[shift], 'row', perm).astype(jnp.float32)  5.4 us
    ppermute x3, starting transfers between devices, on_device(): got = [lax.ppermute(pulled_own, 'col', perm) for perm in shifts('col')]  4.01 us
    pallas_call x1, Pallas kernels, tile_products_t(): pl.pallas_call(functools.partial(backward_kernel, len(got) + 1), out_shap...  3.4 us
  transfers between devices with their start and end apart: 13, of which 9 were waited for; matrix products, arithmetic and copies ran while one was open for 0% of the time, Pallas kernels for 0%

profile of v4, /device:TPU:0, one launch (start us, length us, event | category | flops | bytes accessed | tf_op | source)
XLA Modules:
  0.0 63.1 jit_solution(7862547679639685276)
XLA Ops:
  1.3 13.9 %all_gather.3.f_ref = bf16[1536,256]{1,0:T(8,128)(2,1)} all-gather(bf16[192,256]{1,0:T(8,128)(2,1)} %param.7), channel_id=1, replica_groups=mesh['row'=8,'col'=4] {'row'}, dimensions={0}, use_global_device_ids=true | all-gather | bytes 884736 | tf_op jit(solution)/shard_map/all_gather | solution.py:147
  15.1 3.1 %shard_map.86 = (f32[192,256]{1,0:T(8,128)}, bf16[192,256]{1,0:T(8,128)(2,1)}, bf16[192,256]{1,0:T(8,128)(2,1)}, bf16[192,256]{1,0:T(8,128)(2,1)}) custom-call(s32[12]{0:T(128)} %bitcast.8, s32[12]{0:T(128)} %bitcast.10, s32[1]{0:T(128)} %bitcast.4.info_ref, bf16[12,256,256]{2,1,0:T(8,128)(2,1)} %bitcast.6, bf16[1536,256]{1,0:T(8,128)(2,1)} %all_gather.3.f_ref), custom_call_target="tpu_custom_call" | custom-call | tf_op jit(solution)/shard_map/pallas_call | solution.py:108
  18.2 3.3 %collective-permute-start = (bf16[192,256]{1,0:T(8,128)(2,1)}, bf16[192,256]{1,0:T(8,128)(2,1)S(1)}, u32[]{:S(2)}, u32[]{:S(2)}) collective-permute-start(bf16[192,256]{1,0:T(8,128)(2,1)} %get-tuple-element.17), channel_id=1, source_target_pairs={{0,1},{1,2},{2,3},{3,0},{4,5},{5,6},{6,7},{7,4},{8,9},{9,10},{10,1... | collective-permute-start | bytes 294920 | tf_op jit(solution)/shard_map/ppermute | solution.py:150
  21.5 1.0 %collective-permute-start.1 = (bf16[192,256]{1,0:T(8,128)(2,1)}, bf16[192,256]{1,0:T(8,128)(2,1)S(1)}, u32[]{:S(2)}, u32[]{:S(2)}) collective-permute-start(bf16[192,256]{1,0:T(8,128)(2,1)} %get-tuple-element.18), channel_id=1, source_target_pairs={{0,2},{1,3},{2,0},{3,1},{4,6},{5,7},{6,4},{7,5},{8,10},{9,11},{10,... | collective-permute-start | bytes 294920 | tf_op jit(solution)/shard_map/ppermute | solution.py:150
  22.6 1.4 %collective-permute-start.2 = (bf16[192,256]{1,0:T(8,128)(2,1)}, bf16[192,256]{1,0:T(8,128)(2,1)S(1)}, u32[]{:S(2)}, u32[]{:S(2)}) collective-permute-start(bf16[192,256]{1,0:T(8,128)(2,1)} %get-tuple-element.19), channel_id=1, source_target_pairs={{0,3},{1,0},{2,1},{3,2},{4,7},{5,4},{6,5},{7,6},{8,11},{9,8},{10,9... | collective-permute-start | bytes 294920 | tf_op jit(solution)/shard_map/ppermute | solution.py:150
  23.9 2.1 %collective-permute-done.rest_0_ = bf16[192,256]{1,0:T(8,128)(2,1)S(1)} collective-permute-done((bf16[192,256]{1,0:T(8,128)(2,1)}, bf16[192,256]{1,0:T(8,128)(2,1)S(1)}, u32[]{:S(2)}, u32[]{:S(2)}) %collective-permute-start) | collective-permute-done | bytes 98336 | tf_op jit(solution)/shard_map/ppermute | solution.py:150
  26.0 4.1 %collective-permute-done.1.rest_1_ = bf16[192,256]{1,0:T(8,128)(2,1)S(1)} collective-permute-done((bf16[192,256]{1,0:T(8,128)(2,1)}, bf16[192,256]{1,0:T(8,128)(2,1)S(1)}, u32[]{:S(2)}, u32[]{:S(2)}) %collective-permute-start.1) | collective-permute-done | bytes 98336 | tf_op jit(solution)/shard_map/ppermute | solution.py:150
  30.2 0.6 copy-done.4
  30.8 0.0 copy-done.5
  30.8 2.2 %shard_map.87 = (bf16[192,256]{1,0:T(8,128)(2,1)}, bf16[192,256]{1,0:T(8,128)(2,1)}) custom-call(f32[192,256]{1,0:T(8,128)} %get-tuple-element.16.own_ref, bf16[192,256]{1,0:T(8,128)(2,1)} %copy-done.3, bf16[192,256]{1,0:T(8,128)(2,1)} %copy-done.4, bf16[192,256]{1,0:T(8,128)(2,1)} %copy-done.5, bf16[192,256]{1,0:T(8,128)(2,1)} %rest_3_.1, ...), custom_call_target="tpu_custom_call" | custom-call | tf_op jit(solution)/shard_map/pallas_call | solution.py:47
  33.0 3.1 %collective-permute-start.5 = (bf16[192,256]{1,0:T(8,128)(2,1)}, bf16[192,256]{1,0:T(8,128)(2,1)S(1)}, u32[]{:S(2)}, u32[]{:S(2)}) collective-permute-start(bf16[192,256]{1,0:T(8,128)(2,1)} %get-tuple-element.21.mine_ref), channel_id=1, source_target_pairs={{0,3},{1,0},{2,1},{3,2},{4,7},{5,4},{6,5},{7,6},{8,11},{9,8},{10,9... | collective-permute-start | bytes 294920 | tf_op jit(solution)/shard_map/ppermute | solution.py:152
  36.1 0.9 %collective-permute-start.4 = (bf16[192,256]{1,0:T(8,128)(2,1)}, bf16[192,256]{1,0:T(8,128)(2,1)S(1)}, u32[]{:S(2)}, u32[]{:S(2)}) collective-permute-start(bf16[192,256]{1,0:T(8,128)(2,1)} %get-tuple-element.21.mine_ref), channel_id=1, source_target_pairs={{0,2},{1,3},{2,0},{3,1},{4,6},{5,7},{6,4},{7,5},{8,10},{9,11},{10,... | collective-permute-start | bytes 294920 | tf_op jit(solution)/shard_map/ppermute | solution.py:152
  37.0 0.0 collective-permute-start.3
  37.0 2.6 %collective-permute-done.5.rest_2_ = bf16[192,256]{1,0:T(8,128)(2,1)S(1)} collective-permute-done((bf16[192,256]{1,0:T(8,128)(2,1)}, bf16[192,256]{1,0:T(8,128)(2,1)S(1)}, u32[]{:S(2)}, u32[]{:S(2)}) %collective-permute-start.5) | collective-permute-done | bytes 98336 | tf_op jit(solution)/shard_map/ppermute | solution.py:152
  39.6 6.6 %collective-permute-done.4.rest_1_ = bf16[192,256]{1,0:T(8,128)(2,1)S(1)} collective-permute-done((bf16[192,256]{1,0:T(8,128)(2,1)}, bf16[192,256]{1,0:T(8,128)(2,1)S(1)}, u32[]{:S(2)}, u32[]{:S(2)}) %collective-permute-start.4) | collective-permute-done | bytes 98336 | tf_op jit(solution)/shard_map/ppermute | solution.py:152
  46.2 0.0 collective-permute-done.3.rest_0_
  46.2 0.6 copy-done.1
  46.9 0.0 copy-done.2
  46.9 3.4 %shard_map.88 = (f32[192,256]{1,0:T(8,128)}, bf16[192,256]{1,0:T(8,128)(2,1)}, bf16[192,256]{1,0:T(8,128)(2,1)}, bf16[192,256]{1,0:T(8,128)(2,1)}, bf16[192,256]...) custom-call(s32[12]{0:T(128)} %bitcast.9, s32[12]{0:T(128)} %bitcast.11, ...), custom_call_target="tpu_custom_call" | custom-call | tf_op jit(solution)/shard_map/pallas_call | solution.py:121
  50.3 2.6 %collective-permute-start.7 = (bf16[192,256]{1,0:T(8,128)(2,1)}, bf16[192,256]{1,0:T(8,128)(2,1)S(1)}, u32[]{:S(2)}, u32[]{:S(2)}) collective-permute-start(bf16[192,256]{1,0:T(8,128)(2,1)} %get-tuple-element.24), channel_id=1, source_target_pairs={{0,8},{4,12},{8,16},{12,20},{16,24},{20,28},{24,0},{28,4},{1,9},{5... | collective-permute-start | bytes 294920 | tf_op jit(solution)/shard_map/ppermute | solution.py:158
  52.9 0.3 collective-permute-start.8
  53.2 0.8 %collective-permute-start.9 = (bf16[192,256]{1,0:T(8,128)(2,1)}, bf16[192,256]{1,0:T(8,128)(2,1)S(1)}, u32[]{:S(2)}, u32[]{:S(2)}) collective-permute-start(bf16[192,256]{1,0:T(8,128)(2,1)} %get-tuple-element.26), channel_id=1, source_target_pairs={{0,16},{4,20},{8,24},{12,28},{16,0},{20,4},{24,8},{28,12},{1,17},{... | collective-permute-start | bytes 294920 | tf_op jit(solution)/shard_map/ppermute | solution.py:158
  54.0 0.6 collective-permute-start.10
  54.6 1.2 %collective-permute-done.6 = bf16[192,256]{1,0:T(8,128)(2,1)S(1)} collective-permute-done((bf16[192,256]{1,0:T(8,128)(2,1)}, bf16[192,256]{1,0:T(8,128)(2,1)S(1)}, u32[]{:S(2)}, u32[]{:S(2)}) %collective-permute-start.6) | collective-permute-done | bytes 98336 | tf_op jit(solution)/shard_map/ppermute | solution.py:158
  55.9 0.5 collective-permute-start.11
  56.4 0.8 %collective-permute-done.7 = bf16[192,256]{1,0:T(8,128)(2,1)S(1)} collective-permute-done((bf16[192,256]{1,0:T(8,128)(2,1)}, bf16[192,256]{1,0:T(8,128)(2,1)S(1)}, u32[]{:S(2)}, u32[]{:S(2)}) %collective-permute-start.7) | collective-permute-done | bytes 98336 | tf_op jit(solution)/shard_map/ppermute | solution.py:158
  57.2 0.9 %collective-permute-start.12 = (bf16[192,256]{1,0:T(8,128)(2,1)}, bf16[192,256]{1,0:T(8,128)(2,1)S(1)}, u32[]{:S(2)}, u32[]{:S(2)}) collective-permute-start(bf16[192,256]{1,0:T(8,128)(2,1)} %get-tuple-element.29), channel_id=1, source_target_pairs={{0,28},{4,0},{8,4},{12,8},{16,12},{20,16},{24,20},{28,24},{1,29},{... | collective-permute-start | bytes 294920 | tf_op jit(solution)/shard_map/ppermute | solution.py:158
  58.1 2.5 %collective-permute-done.8 = bf16[192,256]{1,0:T(8,128)(2,1)S(1)} collective-permute-done((bf16[192,256]{1,0:T(8,128)(2,1)}, bf16[192,256]{1,0:T(8,128)(2,1)S(1)}, u32[]{:S(2)}, u32[]{:S(2)}) %collective-permute-start.8) | collective-permute-done | bytes 98336 | tf_op jit(solution)/shard_map/ppermute | solution.py:158
  60.6 0.2 collective-permute-done.9
  60.8 0.7 %collective-permute-done.10 = bf16[192,256]{1,0:T(8,128)(2,1)S(1)} collective-permute-done((bf16[192,256]{1,0:T(8,128)(2,1)}, bf16[192,256]{1,0:T(8,128)(2,1)S(1)}, u32[]{:S(2)}, u32[]{:S(2)}) %collective-permute-start.10) | collective-permute-done | bytes 98336 | tf_op jit(solution)/shard_map/ppermute | solution.py:158
  61.4 0.0 collective-permute-done.11
  61.5 1.7 %add_convert_fusion = bf16[192,256]{1,0:T(8,128)(2,1)} fusion(bf16[192,256]{1,0:T(8,128)(2,1)S(1)} %collective-permute-done.12, bf16[192,256]{1,0:T(8,128)(2,1)S(1)} %collective-permute-done.11, bf16[192,256]{1,0:T(8,128)(2,1)S(1)} %collective-permute-done.10, bf16[192,256]{1,0:T(8,128)(2,1)S(1)} %collective-permute-done.9, ...), kind=kLoop, calls=%fused_computation | loop fusion | flops 737280 | bytes 983040 | tf_op jit(solution)/shard_map/convert_element_type | solution.py:159
  (11 shorter events, 0.0 us)
Async XLA Ops:
  18.2 7.8 %collective-permute-start = (bf16[192,256]{1,0:T(8,128)(2,1)}, bf16[192,256]{1,0:T(8,128)(2,1)S(1)}, u32[]{:S(2)}, u32[]{:S(2)}) collective-permute-start(bf16[192,256]{1,0:T(8,128)(2,1)} %get-tuple-element.17), channel_id=1, source_target_pairs={{0,1},{1,2},{2,3},{3,0},{4,5},{5,6},{6,7},{7,4},{8,9},{9,10},{10,1... | collective-permute-start | bytes 294920 | tf_op jit(solution)/shard_map/ppermute | solution.py:150
  21.5 8.6 %collective-permute-start.1 = (bf16[192,256]{1,0:T(8,128)(2,1)}, bf16[192,256]{1,0:T(8,128)(2,1)S(1)}, u32[]{:S(2)}, u32[]{:S(2)}) collective-permute-start(bf16[192,256]{1,0:T(8,128)(2,1)} %get-tuple-element.18), channel_id=1, source_target_pairs={{0,2},{1,3},{2,0},{3,1},{4,6},{5,7},{6,4},{7,5},{8,10},{9,11},{10,... | collective-permute-start | bytes 294920 | tf_op jit(solution)/shard_map/ppermute | solution.py:150
  22.6 7.6 %collective-permute-start.2 = (bf16[192,256]{1,0:T(8,128)(2,1)}, bf16[192,256]{1,0:T(8,128)(2,1)S(1)}, u32[]{:S(2)}, u32[]{:S(2)}) collective-permute-start(bf16[192,256]{1,0:T(8,128)(2,1)} %get-tuple-element.19), channel_id=1, source_target_pairs={{0,3},{1,0},{2,1},{3,2},{4,7},{5,4},{6,5},{7,6},{8,11},{9,8},{10,9... | collective-permute-start | bytes 294920 | tf_op jit(solution)/shard_map/ppermute | solution.py:150
  26.0 4.2 %copy-start.3 = (bf16[192,256]{1,0:T(8,128)(2,1)}, bf16[192,256]{1,0:T(8,128)(2,1)S(1)}, u32[]{:S(2)}) copy-start(bf16[192,256]{1,0:T(8,128)(2,1)S(1)} %collective-permute-done.rest_0_) | copy-start | bytes 294916
  30.2 0.6 %copy-start.4 = (bf16[192,256]{1,0:T(8,128)(2,1)}, bf16[192,256]{1,0:T(8,128)(2,1)S(1)}, u32[]{:S(2)}) copy-start(bf16[192,256]{1,0:T(8,128)(2,1)S(1)} %collective-permute-done.1.rest_1_) | copy-start | bytes 294916
  30.2 0.7 %copy-start.5 = (bf16[192,256]{1,0:T(8,128)(2,1)}, bf16[192,256]{1,0:T(8,128)(2,1)S(1)}, u32[]{:S(2)}) copy-start(bf16[192,256]{1,0:T(8,128)(2,1)S(1)} %collective-permute-done.2.rest_2_) | copy-start | bytes 294916
  33.0 6.6 %collective-permute-start.5 = (bf16[192,256]{1,0:T(8,128)(2,1)}, bf16[192,256]{1,0:T(8,128)(2,1)S(1)}, u32[]{:S(2)}, u32[]{:S(2)}) collective-permute-start(bf16[192,256]{1,0:T(8,128)(2,1)} %get-tuple-element.21.mine_ref), channel_id=1, source_target_pairs={{0,3},{1,0},{2,1},{3,2},{4,7},{5,4},{6,5},{7,6},{8,11},{9,8},{10,9... | collective-permute-start | bytes 294920 | tf_op jit(solution)/shard_map/ppermute | solution.py:152
  36.1 10.1 %collective-permute-start.4 = (bf16[192,256]{1,0:T(8,128)(2,1)}, bf16[192,256]{1,0:T(8,128)(2,1)S(1)}, u32[]{:S(2)}, u32[]{:S(2)}) collective-permute-start(bf16[192,256]{1,0:T(8,128)(2,1)} %get-tuple-element.21.mine_ref), channel_id=1, source_target_pairs={{0,2},{1,3},{2,0},{3,1},{4,6},{5,7},{6,4},{7,5},{8,10},{9,11},{10,... | collective-permute-start | bytes 294920 | tf_op jit(solution)/shard_map/ppermute | solution.py:152
  37.0 9.2 %collective-permute-start.3 = (bf16[192,256]{1,0:T(8,128)(2,1)}, bf16[192,256]{1,0:T(8,128)(2,1)S(1)}, u32[]{:S(2)}, u32[]{:S(2)}) collective-permute-start(bf16[192,256]{1,0:T(8,128)(2,1)} %get-tuple-element.21.mine_ref), channel_id=1, source_target_pairs={{0,1},{1,2},{2,3},{3,0},{4,5},{5,6},{6,7},{7,4},{8,9},{9,10},{10,1... | collective-permute-start | bytes 294920 | tf_op jit(solution)/shard_map/ppermute | solution.py:152
  39.6 6.6 %copy-start = (bf16[192,256]{1,0:T(8,128)(2,1)}, bf16[192,256]{1,0:T(8,128)(2,1)S(1)}, u32[]{:S(2)}) copy-start(bf16[192,256]{1,0:T(8,128)(2,1)S(1)} %collective-permute-done.5.rest_2_) | copy-start | bytes 294916
  46.2 0.6 %copy-start.1 = (bf16[192,256]{1,0:T(8,128)(2,1)}, bf16[192,256]{1,0:T(8,128)(2,1)S(1)}, u32[]{:S(2)}) copy-start(bf16[192,256]{1,0:T(8,128)(2,1)S(1)} %collective-permute-done.4.rest_1_) | copy-start | bytes 294916
  46.2 0.7 %copy-start.2 = (bf16[192,256]{1,0:T(8,128)(2,1)}, bf16[192,256]{1,0:T(8,128)(2,1)S(1)}, u32[]{:S(2)}) copy-start(bf16[192,256]{1,0:T(8,128)(2,1)S(1)} %collective-permute-done.3.rest_0_) | copy-start | bytes 294916
  50.3 5.6 %collective-permute-start.6 = (bf16[192,256]{1,0:T(8,128)(2,1)}, bf16[192,256]{1,0:T(8,128)(2,1)S(1)}, u32[]{:S(2)}, u32[]{:S(2)}) collective-permute-start(bf16[192,256]{1,0:T(8,128)(2,1)} %get-tuple-element.23), channel_id=1, source_target_pairs={{0,4},{4,8},{8,12},{12,16},{16,20},{20,24},{24,28},{28,0},{1,5},{5... | collective-permute-start | bytes 294920 | tf_op jit(solution)/shard_map/ppermute | solution.py:158
  50.3 6.9 %collective-permute-start.7 = (bf16[192,256]{1,0:T(8,128)(2,1)}, bf16[192,256]{1,0:T(8,128)(2,1)S(1)}, u32[]{:S(2)}, u32[]{:S(2)}) collective-permute-start(bf16[192,256]{1,0:T(8,128)(2,1)} %get-tuple-element.24), channel_id=1, source_target_pairs={{0,8},{4,12},{8,16},{12,20},{16,24},{20,28},{24,0},{28,4},{1,9},{5... | collective-permute-start | bytes 294920 | tf_op jit(solution)/shard_map/ppermute | solution.py:158
  52.9 7.7 %collective-permute-start.8 = (bf16[192,256]{1,0:T(8,128)(2,1)}, bf16[192,256]{1,0:T(8,128)(2,1)S(1)}, u32[]{:S(2)}, u32[]{:S(2)}) collective-permute-start(bf16[192,256]{1,0:T(8,128)(2,1)} %get-tuple-element.25), channel_id=1, source_target_pairs={{0,12},{4,16},{8,20},{12,24},{16,28},{20,0},{24,4},{28,8},{1,13},{... | collective-permute-start | bytes 294920 | tf_op jit(solution)/shard_map/ppermute | solution.py:158
  53.2 7.6 %collective-permute-start.9 = (bf16[192,256]{1,0:T(8,128)(2,1)}, bf16[192,256]{1,0:T(8,128)(2,1)S(1)}, u32[]{:S(2)}, u32[]{:S(2)}) collective-permute-start(bf16[192,256]{1,0:T(8,128)(2,1)} %get-tuple-element.26), channel_id=1, source_target_pairs={{0,16},{4,20},{8,24},{12,28},{16,0},{20,4},{24,8},{28,12},{1,17},{... | collective-permute-start | bytes 294920 | tf_op jit(solution)/shard_map/ppermute | solution.py:158
  54.0 7.4 %collective-permute-start.10 = (bf16[192,256]{1,0:T(8,128)(2,1)}, bf16[192,256]{1,0:T(8,128)(2,1)S(1)}, u32[]{:S(2)}, u32[]{:S(2)}) collective-permute-start(bf16[192,256]{1,0:T(8,128)(2,1)} %get-tuple-element.27), channel_id=1, source_target_pairs={{0,20},{4,24},{8,28},{12,0},{16,4},{20,8},{24,12},{28,16},{1,21},{... | collective-permute-start | bytes 294920 | tf_op jit(solution)/shard_map/ppermute | solution.py:158
  55.9 5.6 %collective-permute-start.11 = (bf16[192,256]{1,0:T(8,128)(2,1)}, bf16[192,256]{1,0:T(8,128)(2,1)S(1)}, u32[]{:S(2)}, u32[]{:S(2)}) collective-permute-start(bf16[192,256]{1,0:T(8,128)(2,1)} %get-tuple-element.28), channel_id=1, source_target_pairs={{0,24},{4,28},{8,0},{12,4},{16,8},{20,12},{24,16},{28,20},{1,25},{... | collective-permute-start | bytes 294920 | tf_op jit(solution)/shard_map/ppermute | solution.py:158
  57.2 4.2 %collective-permute-start.12 = (bf16[192,256]{1,0:T(8,128)(2,1)}, bf16[192,256]{1,0:T(8,128)(2,1)S(1)}, u32[]{:S(2)}, u32[]{:S(2)}) collective-permute-start(bf16[192,256]{1,0:T(8,128)(2,1)} %get-tuple-element.29), channel_id=1, source_target_pairs={{0,28},{4,0},{8,4},{12,8},{16,12},{20,16},{24,20},{28,24},{1,29},{... | collective-permute-start | bytes 294920 | tf_op jit(solution)/shard_map/ppermute | solution.py:158

commit v5 on v3

--- a/solution.py
+++ b/solution.py
@@ -31,9 +31,18 @@
         send_refs[shift - 1][...] = acc_ref[pl.ds(start, chunk), :].astype(send_refs[shift - 1].dtype)
 
 
-def forward_kernel(rows_ref, cols_ref, info_ref, a_ref, f_ref, own_ref, *rest):
-    send_refs, acc_ref = rest[:-1], rest[-1]
+def forward_kernel(rows_ref, cols_ref, info_ref, a_ref, near_ref, far_ref, own_ref, *rest):
+    send_refs, f_ref, acc_ref = rest[:-2], rest[-2], rest[-1]
     tile = a_ref.shape[1]
+    chips, piece = near_ref.shape[0], near_ref.shape[1]
+    me = lax.axis_index("row")
+    core, chip = me % 2, me // 2
+    for shift in range(chips):
+        owner = (chip - shift + chips) % chips
+        near = pl.multiple_of((owner * 2 + core) * piece, 16)
+        far = pl.multiple_of((owner * 2 + 1 - core) * piece, 16)
+        f_ref[pl.ds(near, piece), :] = near_ref[shift]
+        f_ref[pl.ds(far, piece), :] = far_ref[shift]
     acc_ref[...] = jnp.zeros_like(acc_ref)
 
     def step(k, carry):
@@ -48,9 +57,7 @@
 
 def backward_kernel(n, rows_ref, cols_ref, info_ref, a_ref, mine_ref, *rest):
     got_refs = rest[: n - 1]
-    own_ref = rest[n - 1]
-    send_refs = rest[n:-2]
-    block_ref, acc_ref = rest[-2:]
+    near_ref, far_ref, block_ref, acc_ref = rest[n - 1:]
     tile = a_ref.shape[1]
     chunk = mine_ref.shape[0]
     me = lax.axis_index("col")
@@ -69,35 +76,46 @@
         return carry
 
     lax.fori_loop(0, jnp.minimum(info_ref[0], a_ref.shape[0]), step, 0)
-    split_out(acc_ref, own_ref, send_refs, lax.axis_index("row"))
+    chips = near_ref.shape[0]
+    piece = near_ref.shape[1]
+    me_row = lax.axis_index("row")
+    core, chip = me_row % 2, me_row // 2
+    for shift in range(chips):
+        owner = (chip + shift) % chips
+        near_ref[shift] = acc_ref[pl.ds(pl.multiple_of((owner * 2 + core) * piece, 8), piece), :]
+        far_ref[shift] = acc_ref[pl.ds(pl.multiple_of((owner * 2 + 1 - core) * piece, 8), piece), :]
 
 
 SMEM = pl.BlockSpec(memory_space=pltpu.SMEM)
 VMEM = pl.BlockSpec(memory_space=pltpu.VMEM)
 
 
-def tile_products(rows, cols, info, blocks, features, parts):
+def tile_products(rows, cols, info, blocks, near, far, parts):
     out_rows = parts[0] * parts[1]
     chunk = parts[1]
+    width = near.shape[2]
     return pl.pallas_call(
         forward_kernel,
-        out_shape=(jax.ShapeDtypeStruct((chunk, features.shape[1]), jnp.float32),)
-        + (jax.ShapeDtypeStruct((chunk, features.shape[1]), jnp.bfloat16),) * (parts[0] - 1),
-        in_specs=[SMEM, SMEM, SMEM, VMEM, VMEM],
+        out_shape=(jax.ShapeDtypeStruct((chunk, width), jnp.float32),)
+        + (jax.ShapeDtypeStruct((chunk, width), jnp.bfloat16),) * (parts[0] - 1),
+        in_specs=[SMEM, SMEM, SMEM, VMEM, VMEM, VMEM],
         out_specs=(VMEM,) * parts[0],
-        scratch_shapes=[pltpu.VMEM((out_rows, features.shape[1]), jnp.float32)],
-    )(rows, cols, info, blocks, features)
+        scratch_shapes=[
+            pltpu.VMEM((2 * near.shape[0] * near.shape[1], width), jnp.bfloat16),
+            pltpu.VMEM((out_rows, width), jnp.float32),
+        ],
+    )(rows, cols, info, blocks, near, far)
 
 
 def tile_products_t(rows, cols, info, blocks, mine, got, n_out, out_rows):
     chunk = out_rows // n_out
     width = mine.shape[1]
+    stack = jax.ShapeDtypeStruct((n_out // 2, chunk, width), jnp.float32)
     return pl.pallas_call(
         functools.partial(backward_kernel, len(got) + 1),
-        out_shape=(jax.ShapeDtypeStruct((chunk, width), jnp.float32),)
-        + (jax.ShapeDtypeStruct((chunk, width), jnp.bfloat16),) * (n_out - 1),
+        out_shape=(stack, stack),
         in_specs=[SMEM, SMEM, SMEM, VMEM, VMEM] + [VMEM] * len(got),
-        out_specs=(VMEM,) * n_out,
+        out_specs=(VMEM, VMEM),
         scratch_shapes=[
             pltpu.VMEM(((len(got) + 1) * mine.shape[0], width), jnp.bfloat16),
             pltpu.VMEM((out_rows, width), jnp.float32),
@@ -110,6 +128,15 @@
     return [[(i, (i + shift) % n) for i in range(n)] for shift in range(1, n)]
 
 
+def chip_shifts(n):
+    chips = n // 2
+    return [[(i, ((i // 2 + shift) % chips) * 2 + i % 2) for i in range(n)] for shift in range(1, chips)]
+
+
+def partner(n):
+    return [(i, i ^ 1) for i in range(n)]
+
+
 def on_device(features, edge_tiles, tile_rows, tile_cols, tile_count, weight, cotangent):
     blocks = edge_tiles[0, 0]
     row_slots = tile_rows[0, 0]
@@ -118,20 +145,23 @@
     n_col = lax.axis_size("col")
     own_rows = features.shape[0]
 
-    gathered = lax.all_gather(features, "row", axis=0, tiled=True)
+    near = jnp.stack([features] + [lax.ppermute(features, "row", perm) for perm in chip_shifts(n_row)])
+    far = lax.ppermute(near, "row", partner(n_row))
     info = tile_count.reshape(1)
-    own, *send = tile_products(row_slots, col_slots, info, blocks, gathered, (n_col, own_rows))
+    own, *send = tile_products(row_slots, col_slots, info, blocks, near, far, (n_col, own_rows))
     total = own
     for shift, perm in enumerate(shifts("col")):
         total = total + lax.ppermute(send[shift], "col", perm).astype(jnp.float32)
     activated, pulled_own = dense_layer(total, cotangent, weight)
     got = [lax.ppermute(pulled_own, "col", perm) for perm in shifts("col")]
-    own_g, *send_g = tile_products_t(
+    near_g, far_g = tile_products_t(
         row_slots, col_slots, info, blocks, pulled_own, got, n_row, n_row * own_rows
     )
-    total_g = own_g
-    for shift, perm in enumerate(shifts("row")):
-        total_g = total_g + lax.ppermute(send_g[shift], "row", perm).astype(jnp.float32)
+    chip_sums = near_g + lax.ppermute(far_g, "row", partner(n_row))
+    total_g = chip_sums[0]
+    for shift, perm in enumerate(chip_shifts(n_row)):
+        piece = chip_sums[shift + 1].astype(jnp.bfloat16)
+        total_g = total_g + lax.ppermute(piece, "row", perm).astype(jnp.float32)
     return (activated, total_g.astype(jnp.bfloat16))
 
 

time: 64 us -> 61.5 us (0.961); the launches traced: 63.2 us -> 61.4 us
  blocking collectives: 13.9 us -> 0 us
  starting transfers between devices: 16.4 us -> 21.6 us
  waiting for transfers between devices: 19.9 us -> 24.5 us
  other arithmetic: 1.67 us -> 2.89 us
  local copies, waits for them, and re-layouts: 0.67 us -> 1.45 us
    all_gather x1 -> x0, blocking collectives: 13.9 us -> none  [on_device(): gathered = lax.all_gather(features, 'row', axis=0, tiled=True)]
    ppermute x7 -> x8, starting transfers between devices: 4.61 us -> 11.2 us  [the longest x3 5.97 us: on_device(): lax.ppermute(features, 'row', perm)]
    ppermute x7 -> x8, waiting for transfers between devices: 6.5 us -> 10.7 us  [the longest x3 3.86 us: on_device(): total_g = total_g + lax.ppermute(piece, 'row', perm).astype(jnp.float32)]
    another operation x0 -> x2, other arithmetic: none -> 2.2 us
    ppermute x3, starting transfers between devices: 6.87 us -> 5.63 us  [on_device(): total = total + lax.ppermute(send[shift], 'col', perm).astype(jnp.float32)]
    convert_element_type x1, other arithmetic: 1.67 us -> 0.69 us  [on_device(): return (activated, total_g.astype(jnp.bfloat16))]
    unnamed x12 -> x16, local copies, waits for them, and re-layouts: 0.67 us -> 1.43 us
  transfers between devices with their start and end apart: 13 -> 14, of which waited for: 9 -> 11; matrix products, arithmetic and copies ran while one was open for 0% -> 0% of each run, Pallas kernels for 0% -> 0%
where the time goes in v5:
time: 61.5 us; the launch traced here: 61.4 us
  waiting for transfers between devices  24.5 us (40%)
  starting transfers between devices  21.6 us (35%)
  Pallas kernels  7.61 us (12%)
  other arithmetic  2.89 us (5%)
  matrix products  2.01 us (3%)
  local copies, waits for them, and re-layouts  1.45 us (2%)
  between operations  1.39 us (2%)
    ppermute x3, waiting for transfers between devices, on_device(): got = [lax.ppermute(pulled_own, 'col', perm) for perm in shifts('col')]  8.39 us
    ppermute x3, starting transfers between devices, on_device(): lax.ppermute(features, 'row', perm)  5.97 us
    ppermute x3, starting transfers between devices, on_device(): total = total + lax.ppermute(send[shift], 'col', perm).astype(jnp.float32)  5.63 us
    ppermute x3, waiting for transfers between devices, on_device(): total = total + lax.ppermute(send[shift], 'col', perm).astype(jnp.float32)  5.33 us
    ppermute x3, starting transfers between devices, on_device(): total_g = total_g + lax.ppermute(piece, 'row', perm).astype(jnp.float32)  5.2 us
    ppermute x3, starting transfers between devices, on_device(): got = [lax.ppermute(pulled_own, 'col', perm) for perm in shifts('col')]  4.71 us
    pallas_call x1, Pallas kernels, tile_products_t(): pl.pallas_call(functools.partial(backward_kernel, len(got) + 1), out_shap...  4.1 us
    ppermute x3, waiting for transfers between devices, on_device(): total_g = total_g + lax.ppermute(piece, 'row', perm).astype(jnp.float32)  3.86 us
  transfers between devices with their start and end apart: 14, of which 11 were waited for; matrix products, arithmetic and copies ran while one was open for 0% of the time, Pallas kernels for 0%

profile of v5, /device:TPU:0, one launch (start us, length us, event | category | flops | bytes accessed | tf_op | source)
XLA Modules:
  0.0 61.4 jit_solution(10716788714103718313)
XLA Ops:
  0.6 3.0 %collective-permute-start = (bf16[192,256]{1,0:T(8,128)(2,1)}, bf16[192,256]{1,0:T(8,128)(2,1)S(1)}, u32[]{:S(2)}, u32[]{:S(2)}) collective-permute-start(bf16[192,256]{1,0:T(8,128)(2,1)} %param.7), channel_id=1, source_target_pairs={{0,8},{4,12},{8,16},{12,20},{16,24},{20,28},{24,0},{28,4},{1,9},{5... | collective-permute-start | bytes 294920 | tf_op jit(solution)/shard_map/ppermute | solution.py:148
  3.7 1.0 %collective-permute-start.2 = (bf16[192,256]{1,0:T(8,128)(2,1)}, bf16[192,256]{1,0:T(8,128)(2,1)S(1)}, u32[]{:S(2)}, u32[]{:S(2)}) collective-permute-start(bf16[192,256]{1,0:T(8,128)(2,1)} %param.7), channel_id=1, source_target_pairs={{0,24},{4,28},{8,0},{12,4},{16,8},{20,12},{24,16},{28,20},{1,25},{... | collective-permute-start | bytes 294920 | tf_op jit(solution)/shard_map/ppermute | solution.py:148
  4.7 1.9 %collective-permute-start.1 = (bf16[192,256]{1,0:T(8,128)(2,1)}, bf16[192,256]{1,0:T(8,128)(2,1)S(1)}, u32[]{:S(2)}, u32[]{:S(2)}) collective-permute-start(bf16[192,256]{1,0:T(8,128)(2,1)} %param.7), channel_id=1, source_target_pairs={{0,16},{4,20},{8,24},{12,28},{16,0},{20,4},{24,8},{28,12},{1,17},{... | collective-permute-start | bytes 294920 | tf_op jit(solution)/shard_map/ppermute | solution.py:148
  6.6 1.6 %collective-permute-done = bf16[192,256]{1,0:T(8,128)(2,1)S(1)} collective-permute-done((bf16[192,256]{1,0:T(8,128)(2,1)}, bf16[192,256]{1,0:T(8,128)(2,1)S(1)}, u32[]{:S(2)}, u32[]{:S(2)}) %collective-permute-start) | collective-permute-done | bytes 98336 | tf_op jit(solution)/shard_map/ppermute | solution.py:148
  8.3 1.7 %collective-permute-done.2 = bf16[192,256]{1,0:T(8,128)(2,1)S(1)} collective-permute-done((bf16[192,256]{1,0:T(8,128)(2,1)}, bf16[192,256]{1,0:T(8,128)(2,1)S(1)}, u32[]{:S(2)}, u32[]{:S(2)}) %collective-permute-start.2) | collective-permute-done | bytes 98336 | tf_op jit(solution)/shard_map/ppermute | solution.py:148
  10.0 0.9 %pad_maximum_fusion.near_ref = bf16[4,192,256]{2,1,0:T(8,128)(2,1)S(1)} fusion(bf16[1,192,256]{2,1,0:T(8,128)(2,1)S(1)} %bitcast.32, bf16[1,192,256]{2,1,0:T(8,128)(2,1)S(1)} %bitcast.33, bf16[1,192,256]{2,1,0:T(8,128)(2,1)S(1)} %bitcast.31, bf16[1,192,256]{2,1,0:T(8,128)(2,1)} %bitcast.30), kind=kLoop, calls=%fused_computation.1 | loop fusion | flops 589824 | bytes 786432 | tf_op jit(solution)/shard_map/stack | solution.py:148
  10.9 0.1 collective-permute-start.3
  11.7 1.0 %collective-permute-done.3.far_ref = bf16[4,192,256]{2,1,0:T(8,128)(2,1)S(1)} collective-permute-done((bf16[4,192,256]{2,1,0:T(8,128)(2,1)S(1)}, bf16[4,192,256]{2,1,0:T(8,128)(2,1)S(1)}, u32[]{:S(2)}, u32[]{:S(2)}) %collective-permute-start.3) | collective-permute-done | bytes 393248 | tf_op jit(solution)/shard_map/ppermute | solution.py:149
  12.7 0.7 %copy-done.2 = bf16[4,192,256]{2,1,0:T(8,128)(2,1)} copy-done((bf16[4,192,256]{2,1,0:T(8,128)(2,1)}, bf16[4,192,256]{2,1,0:T(8,128)(2,1)S(1)}, u32[]{:S(2)}) %copy-start.2) | copy-done | bytes 393240
  13.5 3.5 %shard_map.86 = (f32[192,256]{1,0:T(8,128)}, bf16[192,256]{1,0:T(8,128)(2,1)}, bf16[192,256]{1,0:T(8,128)(2,1)}, bf16[192,256]{1,0:T(8,128)(2,1)}) custom-call(s32[12]{0:T(128)} %bitcast.34, s32[12]{0:T(128)} %bitcast.36, s32[1]{0:T(128)} %bitcast.26.info_ref, bf16[12,256,256]{2,1,0:T(8,128)(2,1)} %bitcast.28, bf16[4,192,256]{2,1,0:T(8,128)(2,1)} %copy-done.1, ...), custom_call_target="tpu_custom_call" | custom-call | tf_op jit(solution)/shard_map/pallas_call | solution.py:97
  17.0 1.9 %collective-permute-start.4 = (bf16[192,256]{1,0:T(8,128)(2,1)}, bf16[192,256]{1,0:T(8,128)(2,1)S(1)}, u32[]{:S(2)}, u32[]{:S(2)}) collective-permute-start(bf16[192,256]{1,0:T(8,128)(2,1)} %get-tuple-element.9), channel_id=1, source_target_pairs={{0,1},{1,2},{2,3},{3,0},{4,5},{5,6},{6,7},{7,4},{8,9},{9,10},{10,1... | collective-permute-start | bytes 294920 | tf_op jit(solution)/shard_map/ppermute | solution.py:154
  18.9 2.2 %collective-permute-start.5 = (bf16[192,256]{1,0:T(8,128)(2,1)}, bf16[192,256]{1,0:T(8,128)(2,1)S(1)}, u32[]{:S(2)}, u32[]{:S(2)}) collective-permute-start(bf16[192,256]{1,0:T(8,128)(2,1)} %get-tuple-element.10), channel_id=1, source_target_pairs={{0,2},{1,3},{2,0},{3,1},{4,6},{5,7},{6,4},{7,5},{8,10},{9,11},{10,... | collective-permute-start | bytes 294920 | tf_op jit(solution)/shard_map/ppermute | solution.py:154
  21.1 1.5 %collective-permute-start.6 = (bf16[192,256]{1,0:T(8,128)(2,1)}, bf16[192,256]{1,0:T(8,128)(2,1)S(1)}, u32[]{:S(2)}, u32[]{:S(2)}) collective-permute-start(bf16[192,256]{1,0:T(8,128)(2,1)} %get-tuple-element.11), channel_id=1, source_target_pairs={{0,3},{1,0},{2,1},{3,2},{4,7},{5,4},{6,5},{7,6},{8,11},{9,8},{10,9... | collective-permute-start | bytes 294920 | tf_op jit(solution)/shard_map/ppermute | solution.py:154
  22.6 1.5 %collective-permute-done.4 = bf16[192,256]{1,0:T(8,128)(2,1)S(1)} collective-permute-done((bf16[192,256]{1,0:T(8,128)(2,1)}, bf16[192,256]{1,0:T(8,128)(2,1)S(1)}, u32[]{:S(2)}, u32[]{:S(2)}) %collective-permute-start.4) | collective-permute-done | bytes 98336 | tf_op jit(solution)/shard_map/ppermute | solution.py:154
  24.1 3.9 %collective-permute-done.5 = bf16[192,256]{1,0:T(8,128)(2,1)S(1)} collective-permute-done((bf16[192,256]{1,0:T(8,128)(2,1)}, bf16[192,256]{1,0:T(8,128)(2,1)S(1)}, u32[]{:S(2)}, u32[]{:S(2)}) %collective-permute-start.5) | collective-permute-done | bytes 98336 | tf_op jit(solution)/shard_map/ppermute | solution.py:154
  28.0 1.8 %multiply_convert_fusion.1 = (bf16[192,256]{1,0:T(8,128)(2,1)}, f32[192,256]{1,0:T(8,128)S(1)}) fusion(bf16[256,256]{1,0:T(8,128)(2,1)S(1)} %copy-done, bf16[192,256]{1,0:T(8,128)(2,1)S(1)} %collective-permute-done.6, bf16[192,256]{1,0:T(8,128)(2,1)S(1)} %collective-permute-done.5, f32[192,256]{1,0:T(8,128)} %get-tuple-element.8, ...), kind=kOutput, calls=%fused_computation.8 | convolution fusion | flops 25755648 | bytes 917504 | tf_op jit(solution)/shard_map/dot_general | solution.py:18
  29.7 0.2 convolution_convert_fusion.mine_ref
  30.0 4.1 %collective-permute-start.9 = (bf16[192,256]{1,0:T(8,128)(2,1)S(1)}, bf16[192,256]{1,0:T(8,128)(2,1)S(1)}, u32[]{:S(2)}, u32[]{:S(2)}) collective-permute-start(bf16[192,256]{1,0:T(8,128)(2,1)S(1)} %convolution_convert_fusion.mine_ref), channel_id=1, source_target_pairs={{0,3},{1,0},{2,1},{3,2},{4,7},{5,4},{6,5},{7,6},{8,11},{9,8},{10,9... | collective-permute-start | bytes 294920 | tf_op jit(solution)/shard_map/ppermute | solution.py:156
  34.1 0.6 %collective-permute-start.7 = (bf16[192,256]{1,0:T(8,128)(2,1)S(1)}, bf16[192,256]{1,0:T(8,128)(2,1)S(1)}, u32[]{:S(2)}, u32[]{:S(2)}) collective-permute-start(bf16[192,256]{1,0:T(8,128)(2,1)S(1)} %convolution_convert_fusion.mine_ref), channel_id=1, source_target_pairs={{0,1},{1,2},{2,3},{3,0},{4,5},{5,6},{6,7},{7,4},{8,9},{9,10},{10,1... | collective-permute-start | bytes 294920 | tf_op jit(solution)/shard_map/ppermute | solution.py:156
  34.7 2.5 %collective-permute-done.9.rest_2_ = bf16[192,256]{1,0:T(8,128)(2,1)S(1)} collective-permute-done((bf16[192,256]{1,0:T(8,128)(2,1)S(1)}, bf16[192,256]{1,0:T(8,128)(2,1)S(1)}, u32[]{:S(2)}, u32[]{:S(2)}) %collective-permute-start.9) | collective-permute-done | bytes 98336 | tf_op jit(solution)/shard_map/ppermute | solution.py:156
  37.2 5.8 %collective-permute-done.8.rest_1_ = bf16[192,256]{1,0:T(8,128)(2,1)S(1)} collective-permute-done((bf16[192,256]{1,0:T(8,128)(2,1)S(1)}, bf16[192,256]{1,0:T(8,128)(2,1)S(1)}, u32[]{:S(2)}, u32[]{:S(2)}) %collective-permute-start.8) | collective-permute-done | bytes 98336 | tf_op jit(solution)/shard_map/ppermute | solution.py:156
  43.1 0.6 %copy-done.5 = bf16[192,256]{1,0:T(8,128)(2,1)} copy-done((bf16[192,256]{1,0:T(8,128)(2,1)}, bf16[192,256]{1,0:T(8,128)(2,1)S(1)}, u32[]{:S(2)}) %copy-start.5) | copy-done | bytes 98328
  43.8 4.1 %shard_map.87 = (f32[4,192,256]{2,1,0:T(8,128)}, f32[4,192,256]{2,1,0:T(8,128)}) custom-call(s32[12]{0:T(128)} %bitcast.35, s32[12]{0:T(128)} %bitcast.37, s32[1]{0:T(128)} %bitcast.27.info_ref, bf16[12,256,256]{2,1,0:T(8,128)(2,1)} %bitcast.29, bf16[192,256]{1,0:T(8,128)(2,1)} %copy-done.3, bf16[192,256]{1,0:T(8,128)(2,1)} %copy-done.6, ...), custom_call_target="tpu_custom_call" | custom-call | tf_op jit(solution)/shard_map/pallas_call | solution.py:114
  47.9 2.5 %collective-permute-done.10 = f32[4,192,256]{2,1,0:T(8,128)S(1)} collective-permute-done((f32[4,192,256]{2,1,0:T(8,128)}, f32[4,192,256]{2,1,0:T(8,128)S(1)}, u32[]{:S(2)}, u32[]{:S(2)}) %collective-permute-start.10) | collective-permute-done | bytes 786464 | tf_op jit(solution)/shard_map/ppermute | solution.py:160
  50.4 1.3 %fusion.6 = (bf16[4,192,256]{2,1,0:T(8,128)(2,1)S(1)}, f32[4,192,256]{2,1,0:T(8,128)S(1)}) fusion(f32[4,192,256]{2,1,0:T(8,128)} %get-tuple-element.12, f32[4,192,256]{2,1,0:T(8,128)S(1)} %collective-permute-done.10), kind=kLoop, calls=%fused_computation.16 | loop fusion | flops 393216 | bytes 2752512 | tf_op jit(solution)/shard_map/convert.2
  51.7 2.4 %collective-permute-start.11 = (bf16[192,256]{1,0:T(8,128)(2,1)S(1)}, bf16[192,256]{1,0:T(8,128)(2,1)S(1)}, u32[]{:S(2)}, u32[]{:S(2)}) collective-permute-start(bf16[192,256]{1,0:T(8,128)(2,1)S(1)} %get-tuple-element.16), channel_id=1, source_target_pairs={{0,8},{4,12},{8,16},{12,20},{16,24},{20,28},{24,0},{28,4},{1,9},{5... | collective-permute-start | bytes 294920 | tf_op jit(solution)/shard_map/ppermute | solution.py:164
  54.1 1.5 %collective-permute-start.13 = (bf16[192,256]{1,0:T(8,128)(2,1)S(1)}, bf16[192,256]{1,0:T(8,128)(2,1)S(1)}, u32[]{:S(2)}, u32[]{:S(2)}) collective-permute-start(bf16[192,256]{1,0:T(8,128)(2,1)S(1)} %get-tuple-element.17), channel_id=1, source_target_pairs={{0,24},{4,28},{8,0},{12,4},{16,8},{20,12},{24,16},{28,20},{1,25},{... | collective-permute-start | bytes 294920 | tf_op jit(solution)/shard_map/ppermute | solution.py:164
  55.6 1.3 %collective-permute-start.12 = (bf16[192,256]{1,0:T(8,128)(2,1)S(1)}, bf16[192,256]{1,0:T(8,128)(2,1)S(1)}, u32[]{:S(2)}, u32[]{:S(2)}) collective-permute-start(bf16[192,256]{1,0:T(8,128)(2,1)S(1)} %get-tuple-element.18), channel_id=1, source_target_pairs={{0,16},{4,20},{8,24},{12,28},{16,0},{20,4},{24,8},{28,12},{1,17},{... | collective-permute-start | bytes 294920 | tf_op jit(solution)/shard_map/ppermute | solution.py:164
  56.9 2.3 %collective-permute-done.11 = bf16[192,256]{1,0:T(8,128)(2,1)S(1)} collective-permute-done((bf16[192,256]{1,0:T(8,128)(2,1)S(1)}, bf16[192,256]{1,0:T(8,128)(2,1)S(1)}, u32[]{:S(2)}, u32[]{:S(2)}) %collective-permute-start.11) | collective-permute-done | bytes 98336 | tf_op jit(solution)/shard_map/ppermute | solution.py:164
  59.2 1.2 %collective-permute-done.13 = bf16[192,256]{1,0:T(8,128)(2,1)S(1)} collective-permute-done((bf16[192,256]{1,0:T(8,128)(2,1)S(1)}, bf16[192,256]{1,0:T(8,128)(2,1)S(1)}, u32[]{:S(2)}, u32[]{:S(2)}) %collective-permute-start.13) | collective-permute-done | bytes 98336 | tf_op jit(solution)/shard_map/ppermute | solution.py:164
  60.3 0.4 collective-permute-done.12
  60.7 0.7 %fusion.3 = bf16[192,256]{1,0:T(8,128)(2,1)} fusion(f32[4,192,256]{2,1,0:T(8,128)S(1)} %get-tuple-element.15, bf16[192,256]{1,0:T(8,128)(2,1)S(1)} %collective-permute-done.13, bf16[192,256]{1,0:T(8,128)(2,1)S(1)} %collective-permute-done.12, bf16[192,256]{1,0:T(8,128)(2,1)S(1)} %collective-permute-done.11), kind=kLoop, calls=%fused_computation.6 | loop fusion | flops 344064 | bytes 589824 | tf_op jit(solution)/shard_map/convert_element_type | solution.py:165
  (20 shorter events, 0.1 us)
Async XLA Ops:
  0.6 27.3 %copy-start = (bf16[256,256]{1,0:T(8,128)(2,1)S(1)}, bf16[256,256]{1,0:T(8,128)(2,1)}, u32[]{:S(2)}) copy-start(bf16[256,256]{1,0:T(8,128)(2,1)} %param.12) | copy-start | bytes 393220
  0.6 7.6 %collective-permute-start = (bf16[192,256]{1,0:T(8,128)(2,1)}, bf16[192,256]{1,0:T(8,128)(2,1)S(1)}, u32[]{:S(2)}, u32[]{:S(2)}) collective-permute-start(bf16[192,256]{1,0:T(8,128)(2,1)} %param.7), channel_id=1, source_target_pairs={{0,8},{4,12},{8,16},{12,20},{16,24},{20,28},{24,0},{28,4},{1,9},{5... | collective-permute-start | bytes 294920 | tf_op jit(solution)/shard_map/ppermute | solution.py:148
  3.7 6.3 %collective-permute-start.2 = (bf16[192,256]{1,0:T(8,128)(2,1)}, bf16[192,256]{1,0:T(8,128)(2,1)S(1)}, u32[]{:S(2)}, u32[]{:S(2)}) collective-permute-start(bf16[192,256]{1,0:T(8,128)(2,1)} %param.7), channel_id=1, source_target_pairs={{0,24},{4,28},{8,0},{12,4},{16,8},{20,12},{24,16},{28,20},{1,25},{... | collective-permute-start | bytes 294920 | tf_op jit(solution)/shard_map/ppermute | solution.py:148
  4.7 5.3 %collective-permute-start.1 = (bf16[192,256]{1,0:T(8,128)(2,1)}, bf16[192,256]{1,0:T(8,128)(2,1)S(1)}, u32[]{:S(2)}, u32[]{:S(2)}) collective-permute-start(bf16[192,256]{1,0:T(8,128)(2,1)} %param.7), channel_id=1, source_target_pairs={{0,16},{4,20},{8,24},{12,28},{16,0},{20,4},{24,8},{28,12},{1,17},{... | collective-permute-start | bytes 294920 | tf_op jit(solution)/shard_map/ppermute | solution.py:148
  10.9 1.8 %copy-start.1 = (bf16[4,192,256]{2,1,0:T(8,128)(2,1)}, bf16[4,192,256]{2,1,0:T(8,128)(2,1)S(1)}, u32[]{:S(2)}) copy-start(bf16[4,192,256]{2,1,0:T(8,128)(2,1)S(1)} %pad_maximum_fusion.near_ref) | copy-start | bytes 1179652
  10.9 1.8 %collective-permute-start.3 = (bf16[4,192,256]{2,1,0:T(8,128)(2,1)S(1)}, bf16[4,192,256]{2,1,0:T(8,128)(2,1)S(1)}, u32[]{:S(2)}, u32[]{:S(2)}) collective-permute-start(bf16[4,192,256]{2,1,0:T(8,128)(2,1)S(1)} %pad_maximum_fusion.near_ref), channel_id=1, source_target_pairs={{0,4},{4,0},{8,12},{12,8},{16,20},{20,16},{24,28},{28,24},{1,5},{5... | collective-permute-start | bytes 1179656 | tf_op jit(solution)/shard_map/ppermute | solution.py:149
  12.7 0.7 %copy-start.2 = (bf16[4,192,256]{2,1,0:T(8,128)(2,1)}, bf16[4,192,256]{2,1,0:T(8,128)(2,1)S(1)}, u32[]{:S(2)}) copy-start(bf16[4,192,256]{2,1,0:T(8,128)(2,1)S(1)} %collective-permute-done.3.far_ref) | copy-start | bytes 1179652
  13.5 16.3 %copy-start.7 = (bf16[192,256]{1,0:T(8,128)(2,1)S(1)}, bf16[192,256]{1,0:T(8,128)(2,1)}, u32[]{:S(2)}) copy-start(bf16[192,256]{1,0:T(8,128)(2,1)} %param.13) | copy-start | bytes 294916
  17.0 7.1 %collective-permute-start.4 = (bf16[192,256]{1,0:T(8,128)(2,1)}, bf16[192,256]{1,0:T(8,128)(2,1)S(1)}, u32[]{:S(2)}, u32[]{:S(2)}) collective-permute-start(bf16[192,256]{1,0:T(8,128)(2,1)} %get-tuple-element.9), channel_id=1, source_target_pairs={{0,1},{1,2},{2,3},{3,0},{4,5},{5,6},{6,7},{7,4},{8,9},{9,10},{10,1... | collective-permute-start | bytes 294920 | tf_op jit(solution)/shard_map/ppermute | solution.py:154
  18.9 9.1 %collective-permute-start.5 = (bf16[192,256]{1,0:T(8,128)(2,1)}, bf16[192,256]{1,0:T(8,128)(2,1)S(1)}, u32[]{:S(2)}, u32[]{:S(2)}) collective-permute-start(bf16[192,256]{1,0:T(8,128)(2,1)} %get-tuple-element.10), channel_id=1, source_target_pairs={{0,2},{1,3},{2,0},{3,1},{4,6},{5,7},{6,4},{7,5},{8,10},{9,11},{10,... | collective-permute-start | bytes 294920 | tf_op jit(solution)/shard_map/ppermute | solution.py:154
  21.1 6.9 %collective-permute-start.6 = (bf16[192,256]{1,0:T(8,128)(2,1)}, bf16[192,256]{1,0:T(8,128)(2,1)S(1)}, u32[]{:S(2)}, u32[]{:S(2)}) collective-permute-start(bf16[192,256]{1,0:T(8,128)(2,1)} %get-tuple-element.11), channel_id=1, source_target_pairs={{0,3},{1,0},{2,1},{3,2},{4,7},{5,4},{6,5},{7,6},{8,11},{9,8},{10,9... | collective-permute-start | bytes 294920 | tf_op jit(solution)/shard_map/ppermute | solution.py:154
  30.0 13.1 %copy-start.3 = (bf16[192,256]{1,0:T(8,128)(2,1)}, bf16[192,256]{1,0:T(8,128)(2,1)S(1)}, u32[]{:S(2)}) copy-start(bf16[192,256]{1,0:T(8,128)(2,1)S(1)} %convolution_convert_fusion.mine_ref) | copy-start | bytes 294916
  30.0 7.3 %collective-permute-start.9 = (bf16[192,256]{1,0:T(8,128)(2,1)S(1)}, bf16[192,256]{1,0:T(8,128)(2,1)S(1)}, u32[]{:S(2)}, u32[]{:S(2)}) collective-permute-start(bf16[192,256]{1,0:T(8,128)(2,1)S(1)} %convolution_convert_fusion.mine_ref), channel_id=1, source_target_pairs={{0,3},{1,0},{2,1},{3,2},{4,7},{5,4},{6,5},{7,6},{8,11},{9,8},{10,9... | collective-permute-start | bytes 294920 | tf_op jit(solution)/shard_map/ppermute | solution.py:156
  34.0 9.0 %collective-permute-start.8 = (bf16[192,256]{1,0:T(8,128)(2,1)S(1)}, bf16[192,256]{1,0:T(8,128)(2,1)S(1)}, u32[]{:S(2)}, u32[]{:S(2)}) collective-permute-start(bf16[192,256]{1,0:T(8,128)(2,1)S(1)} %convolution_convert_fusion.mine_ref), channel_id=1, source_target_pairs={{0,2},{1,3},{2,0},{3,1},{4,6},{5,7},{6,4},{7,5},{8,10},{9,11},{10,... | collective-permute-start | bytes 294920 | tf_op jit(solution)/shard_map/ppermute | solution.py:156
  34.1 9.0 %collective-permute-start.7 = (bf16[192,256]{1,0:T(8,128)(2,1)S(1)}, bf16[192,256]{1,0:T(8,128)(2,1)S(1)}, u32[]{:S(2)}, u32[]{:S(2)}) collective-permute-start(bf16[192,256]{1,0:T(8,128)(2,1)S(1)} %convolution_convert_fusion.mine_ref), channel_id=1, source_target_pairs={{0,1},{1,2},{2,3},{3,0},{4,5},{5,6},{6,7},{7,4},{8,9},{9,10},{10,1... | collective-permute-start | bytes 294920 | tf_op jit(solution)/shard_map/ppermute | solution.py:156
  37.2 5.9 %copy-start.4 = (bf16[192,256]{1,0:T(8,128)(2,1)}, bf16[192,256]{1,0:T(8,128)(2,1)S(1)}, u32[]{:S(2)}) copy-start(bf16[192,256]{1,0:T(8,128)(2,1)S(1)} %collective-permute-done.9.rest_2_) | copy-start | bytes 294916
  43.1 0.6 %copy-start.5 = (bf16[192,256]{1,0:T(8,128)(2,1)}, bf16[192,256]{1,0:T(8,128)(2,1)S(1)}, u32[]{:S(2)}) copy-start(bf16[192,256]{1,0:T(8,128)(2,1)S(1)} %collective-permute-done.8.rest_1_) | copy-start | bytes 294916
  43.1 0.7 %copy-start.6 = (bf16[192,256]{1,0:T(8,128)(2,1)}, bf16[192,256]{1,0:T(8,128)(2,1)S(1)}, u32[]{:S(2)}) copy-start(bf16[192,256]{1,0:T(8,128)(2,1)S(1)} %collective-permute-done.7.rest_0_) | copy-start | bytes 294916
  47.9 2.5 %collective-permute-start.10 = (f32[4,192,256]{2,1,0:T(8,128)}, f32[4,192,256]{2,1,0:T(8,128)S(1)}, u32[]{:S(2)}, u32[]{:S(2)}) collective-permute-start(f32[4,192,256]{2,1,0:T(8,128)} %get-tuple-element.13), channel_id=1, source_target_pairs={{0,4},{4,0},{8,12},{12,8},{16,20},{20,16},{24,28},{28,24},{1,5},{5... | collective-permute-start | bytes 2359304 | tf_op jit(solution)/shard_map/ppermute | solution.py:160
  51.7 7.5 %collective-permute-start.11 = (bf16[192,256]{1,0:T(8,128)(2,1)S(1)}, bf16[192,256]{1,0:T(8,128)(2,1)S(1)}, u32[]{:S(2)}, u32[]{:S(2)}) collective-permute-start(bf16[192,256]{1,0:T(8,128)(2,1)S(1)} %get-tuple-element.16), channel_id=1, source_target_pairs={{0,8},{4,12},{8,16},{12,20},{16,24},{20,28},{24,0},{28,4},{1,9},{5... | collective-permute-start | bytes 294920 | tf_op jit(solution)/shard_map/ppermute | solution.py:164
  54.1 6.3 %collective-permute-start.13 = (bf16[192,256]{1,0:T(8,128)(2,1)S(1)}, bf16[192,256]{1,0:T(8,128)(2,1)S(1)}, u32[]{:S(2)}, u32[]{:S(2)}) collective-permute-start(bf16[192,256]{1,0:T(8,128)(2,1)S(1)} %get-tuple-element.17), channel_id=1, source_target_pairs={{0,24},{4,28},{8,0},{12,4},{16,8},{20,12},{24,16},{28,20},{1,25},{... | collective-permute-start | bytes 294920 | tf_op jit(solution)/shard_map/ppermute | solution.py:164
  55.6 5.1 %collective-permute-start.12 = (bf16[192,256]{1,0:T(8,128)(2,1)S(1)}, bf16[192,256]{1,0:T(8,128)(2,1)S(1)}, u32[]{:S(2)}, u32[]{:S(2)}) collective-permute-start(bf16[192,256]{1,0:T(8,128)(2,1)S(1)} %get-tuple-element.18), channel_id=1, source_target_pairs={{0,16},{4,20},{8,24},{12,28},{16,0},{20,4},{24,8},{28,12},{1,17},{... | collective-permute-start | bytes 294920 | tf_op jit(solution)/shard_map/ppermute | solution.py:164

commit v6 on v5

--- a/solution.py
+++ b/solution.py
@@ -6,6 +6,10 @@
 from jax.experimental import pallas as pl
 from jax.experimental.pallas import tpu as pltpu
 from jax.sharding import PartitionSpec as P
+
+SMEM = pl.BlockSpec(memory_space=pltpu.SMEM)
+VMEM = pl.BlockSpec(memory_space=pltpu.VMEM)
+ANY = pl.BlockSpec(memory_space=pl.ANY)
 
 
 def silu_slope(mixed):
@@ -31,51 +35,78 @@
         send_refs[shift - 1][...] = acc_ref[pl.ds(start, chunk), :].astype(send_refs[shift - 1].dtype)
 
 
-def forward_kernel(rows_ref, cols_ref, info_ref, a_ref, near_ref, far_ref, own_ref, *rest):
-    send_refs, f_ref, acc_ref = rest[:-2], rest[-2], rest[-1]
-    tile = a_ref.shape[1]
-    chips, piece = near_ref.shape[0], near_ref.shape[1]
+def start_tiles(a_hbm, a_vmem, sems, count):
+    def begin(k, carry):
+        pltpu.make_async_copy(a_hbm.at[k], a_vmem.at[k], sems.at[k]).start()
+        return carry
+
+    lax.fori_loop(0, count, begin, 0)
+
+
+def wait_tile(a_hbm, a_vmem, sems, k):
+    pltpu.make_async_copy(a_hbm.at[k], a_vmem.at[k], sems.at[k]).wait()
+
+
+def forward_kernel(rows_ref, cols_ref, info_ref, a_hbm, near_hbm, far_hbm, own_ref, *rest):
+    send_refs = rest[:-5]
+    a_vmem, f_ref, acc_ref, tile_sems, piece_sems = rest[-5:]
+    slots, tile = a_hbm.shape[0], a_hbm.shape[1]
+    chips, piece = near_hbm.shape[0], near_hbm.shape[1]
     me = lax.axis_index("row")
     core, chip = me % 2, me // 2
+    pieces = []
     for shift in range(chips):
         owner = (chip - shift + chips) % chips
-        near = pl.multiple_of((owner * 2 + core) * piece, 16)
-        far = pl.multiple_of((owner * 2 + 1 - core) * piece, 16)
-        f_ref[pl.ds(near, piece), :] = near_ref[shift]
-        f_ref[pl.ds(far, piece), :] = far_ref[shift]
+        for side, src in ((core, near_hbm), (1 - core, far_hbm)):
+            dst = f_ref.at[pl.ds(pl.multiple_of((owner * 2 + side) * piece, 16), piece)]
+            copy = pltpu.make_async_copy(src.at[shift], dst, piece_sems.at[len(pieces)])
+            copy.start()
+            pieces.append(copy)
+    count = jnp.minimum(info_ref[0], slots)
+    start_tiles(a_hbm, a_vmem, tile_sems, count)
     acc_ref[...] = jnp.zeros_like(acc_ref)
+    for copy in pieces:
+        copy.wait()
 
     def step(k, carry):
+        wait_tile(a_hbm, a_vmem, tile_sems, k)
         f = f_ref[pl.ds(pl.multiple_of(cols_ref[k] * tile, tile), tile), :]
         rows = pl.ds(pl.multiple_of(rows_ref[k] * tile, tile), tile)
-        acc_ref[rows, :] += jnp.dot(a_ref[k], f, preferred_element_type=jnp.float32)
+        acc_ref[rows, :] += jnp.dot(a_vmem[k], f, preferred_element_type=jnp.float32)
         return carry
 
-    lax.fori_loop(0, jnp.minimum(info_ref[0], a_ref.shape[0]), step, 0)
+    lax.fori_loop(0, count, step, 0)
     split_out(acc_ref, own_ref, send_refs, lax.axis_index("col"))
 
 
-def backward_kernel(n, rows_ref, cols_ref, info_ref, a_ref, mine_ref, *rest):
-    got_refs = rest[: n - 1]
-    near_ref, far_ref, block_ref, acc_ref = rest[n - 1:]
-    tile = a_ref.shape[1]
-    chunk = mine_ref.shape[0]
+def backward_kernel(n, rows_ref, cols_ref, info_ref, a_hbm, mine_hbm, *rest):
+    got_hbm = rest[: n - 1]
+    near_ref, far_ref, a_vmem, block_ref, acc_ref, tile_sems, piece_sems = rest[n - 1:]
+    slots, tile = a_hbm.shape[0], a_hbm.shape[1]
+    chunk = mine_hbm.shape[0]
     me = lax.axis_index("col")
-    block_ref[pl.ds(pl.multiple_of(me * chunk, 16), chunk), :] = mine_ref[...]
-    for shift in range(1, n):
-        start = pl.multiple_of(((me - shift + n) % n) * chunk, 16)
-        block_ref[pl.ds(start, chunk), :] = got_refs[shift - 1][...]
+    pieces = []
+    for shift, src in enumerate((mine_hbm,) + tuple(got_hbm)):
+        dst = block_ref.at[pl.ds(pl.multiple_of(((me - shift + n) % n) * chunk, 16), chunk)]
+        copy = pltpu.make_async_copy(src, dst, piece_sems.at[shift])
+        copy.start()
+        pieces.append(copy)
+    count = jnp.minimum(info_ref[0], slots)
+    start_tiles(a_hbm, a_vmem, tile_sems, count)
     acc_ref[...] = jnp.zeros_like(acc_ref)
+    for copy in pieces:
+        copy.wait()
 
     def step(k, carry):
+        wait_tile(a_hbm, a_vmem, tile_sems, k)
         p = block_ref[pl.ds(pl.multiple_of(rows_ref[k] * tile, tile), tile), :]
         cols = pl.ds(pl.multiple_of(cols_ref[k] * tile, tile), tile)
         acc_ref[cols, :] += lax.dot_general(
-            a_ref[k], p, (((0,), (0,)), ((), ())), preferred_element_type=jnp.float32
+            a_vmem[k], p, (((0,), (0,)), ((), ())), preferred_element_type=jnp.float32
         )
         return carry
 
-    lax.fori_loop(0, jnp.minimum(info_ref[0], a_ref.shape[0]), step, 0)
+    lax.fori_loop(0, count, step, 0)
     chips = near_ref.shape[0]
     piece = near_ref.shape[1]
     me_row = lax.axis_index("row")
@@ -86,10 +117,6 @@
         far_ref[shift] = acc_ref[pl.ds(pl.multiple_of((owner * 2 + 1 - core) * piece, 8), piece), :]
 
 
-SMEM = pl.BlockSpec(memory_space=pltpu.SMEM)
-VMEM = pl.BlockSpec(memory_space=pltpu.VMEM)
-
-
 def tile_products(rows, cols, info, blocks, near, far, parts):
     out_rows = parts[0] * parts[1]
     chunk = parts[1]
@@ -98,11 +125,14 @@
         forward_kernel,
         out_shape=(jax.ShapeDtypeStruct((chunk, width), jnp.float32),)
         + (jax.ShapeDtypeStruct((chunk, width), jnp.bfloat16),) * (parts[0] - 1),
-        in_specs=[SMEM, SMEM, SMEM, VMEM, VMEM, VMEM],
+        in_specs=[SMEM, SMEM, SMEM, ANY, ANY, ANY],
         out_specs=(VMEM,) * parts[0],
         scratch_shapes=[
+            pltpu.VMEM(blocks.shape, blocks.dtype),
             pltpu.VMEM((2 * near.shape[0] * near.shape[1], width), jnp.bfloat16),
             pltpu.VMEM((out_rows, width), jnp.float32),
+            pltpu.SemaphoreType.DMA((blocks.shape[0],)),
+            pltpu.SemaphoreType.DMA((2 * near.shape[0],)),
         ],
     )(rows, cols, info, blocks, near, far)
 
@@ -114,11 +144,14 @@
     return pl.pallas_call(
         functools.partial(backward_kernel, len(got) + 1),
         out_shape=(stack, stack),
-        in_specs=[SMEM, SMEM, SMEM, VMEM, VMEM] + [VMEM] * len(got),
+        in_specs=[SMEM, SMEM, SMEM, ANY, ANY] + [ANY] * len(got),
         out_specs=(VMEM, VMEM),
         scratch_shapes=[
+            pltpu.VMEM(blocks.shape, blocks.dtype),
             pltpu.VMEM(((len(got) + 1) * mine.shape[0], width), jnp.bfloat16),
             pltpu.VMEM((out_rows, width), jnp.float32),
+            pltpu.SemaphoreType.DMA((blocks.shape[0],)),
+            pltpu.SemaphoreType.DMA((len(got) + 1,)),
         ],
     )(rows, cols, info, blocks, mine, *got)
 

time: 61.5 us -> 62.7 us (1.020)
  Pallas kernels: 7.61 us -> 8.81 us
    pallas_call x1, Pallas kernels: 3.51 us -> 4.23 us  [tile_products(): pl.pallas_call(forward_kernel, out_shape=(jax.ShapeDtypeStruct((chunk, wi...]
  transfers between devices with their start and end apart: 14 -> 14, of which waited for: 11 -> 10; matrix products, arithmetic and copies ran while one was open for 0% -> 0% of each run, Pallas kernels for 0% -> 0%
where the time goes in v6:
time: 62.7 us; the launch traced here: 62.9 us
  waiting for transfers between devices  25.1 us (40%)
  starting transfers between devices  21.2 us (34%)
  Pallas kernels  8.81 us (14%)
  other arithmetic  2.89 us (5%)
  matrix products  2.01 us (3%)
  local copies, waits for them, and re-layouts  1.45 us (2%)
  between operations  1.41 us (2%)
    ppermute x3, waiting for transfers between devices, on_device(): got = [lax.ppermute(pulled_own, 'col', perm) for perm in shifts('col')]  8.76 us
    ppermute x3, starting transfers between devices, on_device(): lax.ppermute(features, 'row', perm)  5.97 us
    ppermute x3, waiting for transfers between devices, on_device(): total = total + lax.ppermute(send[shift], 'col', perm).astype(jnp.float32)  5.78 us
    ppermute x3, starting transfers between devices, on_device(): total_g = total_g + lax.ppermute(piece, 'row', perm).astype(jnp.float32)  5.27 us
    ppermute x3, starting transfers between devices, on_device(): total = total + lax.ppermute(send[shift], 'col', perm).astype(jnp.float32)  5.11 us
    ppermute x3, starting transfers between devices, on_device(): got = [lax.ppermute(pulled_own, 'col', perm) for perm in shifts('col')]  4.67 us
    pallas_call x1, Pallas kernels, tile_products_t(): pl.pallas_call(functools.partial(backward_kernel, len(got) + 1), out_shap...  4.58 us
    pallas_call x1, Pallas kernels, tile_products(): pl.pallas_call(forward_kernel, out_shape=(jax.ShapeDtypeStruct((chunk, wi...  4.23 us
  transfers between devices with their start and end apart: 14, of which 10 were waited for; matrix products, arithmetic and copies ran while one was open for 0% of the time, Pallas kernels for 0%

profile of v6, /device:TPU:0, one launch (start us, length us, event | category | flops | bytes accessed | tf_op | source)
XLA Modules:
  0.0 62.9 jit_solution(5022966302565601463)
XLA Ops:
  0.6 3.0 %collective-permute-start = (bf16[192,256]{1,0:T(8,128)(2,1)}, bf16[192,256]{1,0:T(8,128)(2,1)S(1)}, u32[]{:S(2)}, u32[]{:S(2)}) collective-permute-start(bf16[192,256]{1,0:T(8,128)(2,1)} %param.7), channel_id=1, source_target_pairs={{0,8},{4,12},{8,16},{12,20},{16,24},{20,28},{24,0},{28,4},{1,9},{5... | collective-permute-start | bytes 294920 | tf_op jit(solution)/shard_map/ppermute | solution.py:181
  3.7 1.0 %collective-permute-start.2 = (bf16[192,256]{1,0:T(8,128)(2,1)}, bf16[192,256]{1,0:T(8,128)(2,1)S(1)}, u32[]{:S(2)}, u32[]{:S(2)}) collective-permute-start(bf16[192,256]{1,0:T(8,128)(2,1)} %param.7), channel_id=1, source_target_pairs={{0,24},{4,28},{8,0},{12,4},{16,8},{20,12},{24,16},{28,20},{1,25},{... | collective-permute-start | bytes 294920 | tf_op jit(solution)/shard_map/ppermute | solution.py:181
  4.7 1.9 %collective-permute-start.1 = (bf16[192,256]{1,0:T(8,128)(2,1)}, bf16[192,256]{1,0:T(8,128)(2,1)S(1)}, u32[]{:S(2)}, u32[]{:S(2)}) collective-permute-start(bf16[192,256]{1,0:T(8,128)(2,1)} %param.7), channel_id=1, source_target_pairs={{0,16},{4,20},{8,24},{12,28},{16,0},{20,4},{24,8},{28,12},{1,17},{... | collective-permute-start | bytes 294920 | tf_op jit(solution)/shard_map/ppermute | solution.py:181
  6.6 1.6 %collective-permute-done = bf16[192,256]{1,0:T(8,128)(2,1)S(1)} collective-permute-done((bf16[192,256]{1,0:T(8,128)(2,1)}, bf16[192,256]{1,0:T(8,128)(2,1)S(1)}, u32[]{:S(2)}, u32[]{:S(2)}) %collective-permute-start) | collective-permute-done | bytes 98336 | tf_op jit(solution)/shard_map/ppermute | solution.py:181
  8.3 1.7 %collective-permute-done.2 = bf16[192,256]{1,0:T(8,128)(2,1)S(1)} collective-permute-done((bf16[192,256]{1,0:T(8,128)(2,1)}, bf16[192,256]{1,0:T(8,128)(2,1)S(1)}, u32[]{:S(2)}, u32[]{:S(2)}) %collective-permute-start.2) | collective-permute-done | bytes 98336 | tf_op jit(solution)/shard_map/ppermute | solution.py:181
  10.0 0.9 %pad_maximum_fusion.near_hbm = bf16[4,192,256]{2,1,0:T(8,128)(2,1)S(1)} fusion(bf16[1,192,256]{2,1,0:T(8,128)(2,1)S(1)} %bitcast.32, bf16[1,192,256]{2,1,0:T(8,128)(2,1)S(1)} %bitcast.33, bf16[1,192,256]{2,1,0:T(8,128)(2,1)S(1)} %bitcast.31, bf16[1,192,256]{2,1,0:T(8,128)(2,1)} %bitcast.30), kind=kLoop, calls=%fused_computation.1 | loop fusion | flops 589824 | bytes 786432 | tf_op jit(solution)/shard_map/stack | solution.py:181
  10.9 0.1 collective-permute-start.3
  11.7 1.0 %collective-permute-done.3.far_hbm = bf16[4,192,256]{2,1,0:T(8,128)(2,1)S(1)} collective-permute-done((bf16[4,192,256]{2,1,0:T(8,128)(2,1)S(1)}, bf16[4,192,256]{2,1,0:T(8,128)(2,1)S(1)}, u32[]{:S(2)}, u32[]{:S(2)}) %collective-permute-start.3) | collective-permute-done | bytes 393248 | tf_op jit(solution)/shard_map/ppermute | solution.py:182
  12.7 0.7 %copy-done.2 = bf16[4,192,256]{2,1,0:T(8,128)(2,1)} copy-done((bf16[4,192,256]{2,1,0:T(8,128)(2,1)}, bf16[4,192,256]{2,1,0:T(8,128)(2,1)S(1)}, u32[]{:S(2)}) %copy-start.2) | copy-done | bytes 393240
  13.5 4.2 %shard_map.86 = (f32[192,256]{1,0:T(8,128)}, bf16[192,256]{1,0:T(8,128)(2,1)}, bf16[192,256]{1,0:T(8,128)(2,1)}, bf16[192,256]{1,0:T(8,128)(2,1)}) custom-call(s32[12]{0:T(128)} %bitcast.34, s32[12]{0:T(128)} %bitcast.36, s32[1]{0:T(128)} %bitcast.26.info_ref, bf16[12,256,256]{2,1,0:T(8,128)(2,1)} %bitcast.28, bf16[4,192,256]{2,1,0:T(8,128)(2,1)} %copy-done.1, ...), custom_call_target="tpu_custom_call" | custom-call | tf_op jit(solution)/shard_map/pallas_call | solution.py:124
  17.7 1.2 %collective-permute-start.4 = (bf16[192,256]{1,0:T(8,128)(2,1)}, bf16[192,256]{1,0:T(8,128)(2,1)S(1)}, u32[]{:S(2)}, u32[]{:S(2)}) collective-permute-start(bf16[192,256]{1,0:T(8,128)(2,1)} %get-tuple-element.9), channel_id=1, source_target_pairs={{0,1},{1,2},{2,3},{3,0},{4,5},{5,6},{6,7},{7,4},{8,9},{9,10},{10,1... | collective-permute-start | bytes 294920 | tf_op jit(solution)/shard_map/ppermute | solution.py:187
  18.9 2.8 %collective-permute-start.5 = (bf16[192,256]{1,0:T(8,128)(2,1)}, bf16[192,256]{1,0:T(8,128)(2,1)S(1)}, u32[]{:S(2)}, u32[]{:S(2)}) collective-permute-start(bf16[192,256]{1,0:T(8,128)(2,1)} %get-tuple-element.10), channel_id=1, source_target_pairs={{0,2},{1,3},{2,0},{3,1},{4,6},{5,7},{6,4},{7,5},{8,10},{9,11},{10,... | collective-permute-start | bytes 294920 | tf_op jit(solution)/shard_map/ppermute | solution.py:187
  21.7 1.2 %collective-permute-start.6 = (bf16[192,256]{1,0:T(8,128)(2,1)}, bf16[192,256]{1,0:T(8,128)(2,1)S(1)}, u32[]{:S(2)}, u32[]{:S(2)}) collective-permute-start(bf16[192,256]{1,0:T(8,128)(2,1)} %get-tuple-element.11), channel_id=1, source_target_pairs={{0,3},{1,0},{2,1},{3,2},{4,7},{5,4},{6,5},{7,6},{8,11},{9,8},{10,9... | collective-permute-start | bytes 294920 | tf_op jit(solution)/shard_map/ppermute | solution.py:187
  22.8 1.6 %collective-permute-done.4 = bf16[192,256]{1,0:T(8,128)(2,1)S(1)} collective-permute-done((bf16[192,256]{1,0:T(8,128)(2,1)}, bf16[192,256]{1,0:T(8,128)(2,1)S(1)}, u32[]{:S(2)}, u32[]{:S(2)}) %collective-permute-start.4) | collective-permute-done | bytes 98336 | tf_op jit(solution)/shard_map/ppermute | solution.py:187
  24.4 4.2 %collective-permute-done.5 = bf16[192,256]{1,0:T(8,128)(2,1)S(1)} collective-permute-done((bf16[192,256]{1,0:T(8,128)(2,1)}, bf16[192,256]{1,0:T(8,128)(2,1)S(1)}, u32[]{:S(2)}, u32[]{:S(2)}) %collective-permute-start.5) | collective-permute-done | bytes 98336 | tf_op jit(solution)/shard_map/ppermute | solution.py:187
  28.6 1.8 %multiply_convert_fusion.1 = (bf16[192,256]{1,0:T(8,128)(2,1)}, f32[192,256]{1,0:T(8,128)S(1)}) fusion(bf16[256,256]{1,0:T(8,128)(2,1)S(1)} %copy-done, bf16[192,256]{1,0:T(8,128)(2,1)S(1)} %collective-permute-done.6, bf16[192,256]{1,0:T(8,128)(2,1)S(1)} %collective-permute-done.5, f32[192,256]{1,0:T(8,128)} %get-tuple-element.8, ...), kind=kOutput, calls=%fused_computation.8 | convolution fusion | flops 25755648 | bytes 917504 | tf_op jit(solution)/shard_map/dot_general | solution.py:22
  30.4 0.2 convolution_convert_fusion.mine_hbm
  30.6 4.0 %collective-permute-start.9 = (bf16[192,256]{1,0:T(8,128)(2,1)S(1)}, bf16[192,256]{1,0:T(8,128)(2,1)S(1)}, u32[]{:S(2)}, u32[]{:S(2)}) collective-permute-start(bf16[192,256]{1,0:T(8,128)(2,1)S(1)} %convolution_convert_fusion.mine_hbm), channel_id=1, source_target_pairs={{0,3},{1,0},{2,1},{3,2},{4,7},{5,4},{6,5},{7,6},{8,11},{9,8},{10,9... | collective-permute-start | bytes 294920 | tf_op jit(solution)/shard_map/ppermute | solution.py:189
  34.7 0.6 %collective-permute-start.7 = (bf16[192,256]{1,0:T(8,128)(2,1)S(1)}, bf16[192,256]{1,0:T(8,128)(2,1)S(1)}, u32[]{:S(2)}, u32[]{:S(2)}) collective-permute-start(bf16[192,256]{1,0:T(8,128)(2,1)S(1)} %convolution_convert_fusion.mine_hbm), channel_id=1, source_target_pairs={{0,1},{1,2},{2,3},{3,0},{4,5},{5,6},{6,7},{7,4},{8,9},{9,10},{10,1... | collective-permute-start | bytes 294920 | tf_op jit(solution)/shard_map/ppermute | solution.py:189
  35.3 2.6 %collective-permute-done.9.rest_2_ = bf16[192,256]{1,0:T(8,128)(2,1)S(1)} collective-permute-done((bf16[192,256]{1,0:T(8,128)(2,1)S(1)}, bf16[192,256]{1,0:T(8,128)(2,1)S(1)}, u32[]{:S(2)}, u32[]{:S(2)}) %collective-permute-start.9) | collective-permute-done | bytes 98336 | tf_op jit(solution)/shard_map/ppermute | solution.py:189
  37.9 6.2 %collective-permute-done.8.rest_1_ = bf16[192,256]{1,0:T(8,128)(2,1)S(1)} collective-permute-done((bf16[192,256]{1,0:T(8,128)(2,1)S(1)}, bf16[192,256]{1,0:T(8,128)(2,1)S(1)}, u32[]{:S(2)}, u32[]{:S(2)}) %collective-permute-start.8) | collective-permute-done | bytes 98336 | tf_op jit(solution)/shard_map/ppermute | solution.py:189
  44.1 0.6 copy-done.5
  44.7 0.0 copy-done.6
  44.8 4.6 %shard_map.87 = (f32[4,192,256]{2,1,0:T(8,128)}, f32[4,192,256]{2,1,0:T(8,128)}) custom-call(s32[12]{0:T(128)} %bitcast.35, s32[12]{0:T(128)} %bitcast.37, s32[1]{0:T(128)} %bitcast.27.info_ref, bf16[12,256,256]{2,1,0:T(8,128)(2,1)} %bitcast.29, bf16[192,256]{1,0:T(8,128)(2,1)} %copy-done.3, bf16[192,256]{1,0:T(8,128)(2,1)} %copy-done.6, ...), custom_call_target="tpu_custom_call" | custom-call | tf_op jit(solution)/shard_map/pallas_call | solution.py:144
  49.4 0.1 collective-permute-start.10
  49.4 2.5 %collective-permute-done.10 = f32[4,192,256]{2,1,0:T(8,128)S(1)} collective-permute-done((f32[4,192,256]{2,1,0:T(8,128)}, f32[4,192,256]{2,1,0:T(8,128)S(1)}, u32[]{:S(2)}, u32[]{:S(2)}) %collective-permute-start.10) | collective-permute-done | bytes 786464 | tf_op jit(solution)/shard_map/ppermute | solution.py:193
  51.9 1.3 %fusion.6 = (bf16[4,192,256]{2,1,0:T(8,128)(2,1)S(1)}, f32[4,192,256]{2,1,0:T(8,128)S(1)}) fusion(f32[4,192,256]{2,1,0:T(8,128)} %get-tuple-element.12, f32[4,192,256]{2,1,0:T(8,128)S(1)} %collective-permute-done.10), kind=kLoop, calls=%fused_computation.16 | loop fusion | flops 393216 | bytes 2752512 | tf_op jit(solution)/shard_map/convert.2
  53.2 3.7 %collective-permute-start.11 = (bf16[192,256]{1,0:T(8,128)(2,1)S(1)}, bf16[192,256]{1,0:T(8,128)(2,1)S(1)}, u32[]{:S(2)}, u32[]{:S(2)}) collective-permute-start(bf16[192,256]{1,0:T(8,128)(2,1)S(1)} %get-tuple-element.16), channel_id=1, source_target_pairs={{0,8},{4,12},{8,16},{12,20},{16,24},{20,28},{24,0},{28,4},{1,9},{5... | collective-permute-start | bytes 294920 | tf_op jit(solution)/shard_map/ppermute | solution.py:197
  57.0 1.5 %collective-permute-start.12 = (bf16[192,256]{1,0:T(8,128)(2,1)S(1)}, bf16[192,256]{1,0:T(8,128)(2,1)S(1)}, u32[]{:S(2)}, u32[]{:S(2)}) collective-permute-start(bf16[192,256]{1,0:T(8,128)(2,1)S(1)} %get-tuple-element.18), channel_id=1, source_target_pairs={{0,16},{4,20},{8,24},{12,28},{16,0},{20,4},{24,8},{28,12},{1,17},{... | collective-permute-start | bytes 294920 | tf_op jit(solution)/shard_map/ppermute | solution.py:197
  58.5 1.7 %collective-permute-done.11 = bf16[192,256]{1,0:T(8,128)(2,1)S(1)} collective-permute-done((bf16[192,256]{1,0:T(8,128)(2,1)S(1)}, bf16[192,256]{1,0:T(8,128)(2,1)S(1)}, u32[]{:S(2)}, u32[]{:S(2)}) %collective-permute-start.11) | collective-permute-done | bytes 98336 | tf_op jit(solution)/shard_map/ppermute | solution.py:197
  60.1 2.0 %collective-permute-done.13 = bf16[192,256]{1,0:T(8,128)(2,1)S(1)} collective-permute-done((bf16[192,256]{1,0:T(8,128)(2,1)S(1)}, bf16[192,256]{1,0:T(8,128)(2,1)S(1)}, u32[]{:S(2)}, u32[]{:S(2)}) %collective-permute-start.13) | collective-permute-done | bytes 98336 | tf_op jit(solution)/shard_map/ppermute | solution.py:197
  62.2 0.7 %fusion.3 = bf16[192,256]{1,0:T(8,128)(2,1)} fusion(f32[4,192,256]{2,1,0:T(8,128)S(1)} %get-tuple-element.15, bf16[192,256]{1,0:T(8,128)(2,1)S(1)} %collective-permute-done.13, bf16[192,256]{1,0:T(8,128)(2,1)S(1)} %collective-permute-done.12, bf16[192,256]{1,0:T(8,128)(2,1)S(1)} %collective-permute-done.11), kind=kLoop, calls=%fused_computation.6 | loop fusion | flops 344064 | bytes 589824 | tf_op jit(solution)/shard_map/convert_element_type | solution.py:198
  (20 shorter events, 0.1 us)
Async XLA Ops:
  0.6 28.0 %copy-start = (bf16[256,256]{1,0:T(8,128)(2,1)S(1)}, bf16[256,256]{1,0:T(8,128)(2,1)}, u32[]{:S(2)}) copy-start(bf16[256,256]{1,0:T(8,128)(2,1)} %param.12) | copy-start | bytes 393220
  0.6 7.6 %collective-permute-start = (bf16[192,256]{1,0:T(8,128)(2,1)}, bf16[192,256]{1,0:T(8,128)(2,1)S(1)}, u32[]{:S(2)}, u32[]{:S(2)}) collective-permute-start(bf16[192,256]{1,0:T(8,128)(2,1)} %param.7), channel_id=1, source_target_pairs={{0,8},{4,12},{8,16},{12,20},{16,24},{20,28},{24,0},{28,4},{1,9},{5... | collective-permute-start | bytes 294920 | tf_op jit(solution)/shard_map/ppermute | solution.py:181
  3.7 6.3 %collective-permute-start.2 = (bf16[192,256]{1,0:T(8,128)(2,1)}, bf16[192,256]{1,0:T(8,128)(2,1)S(1)}, u32[]{:S(2)}, u32[]{:S(2)}) collective-permute-start(bf16[192,256]{1,0:T(8,128)(2,1)} %param.7), channel_id=1, source_target_pairs={{0,24},{4,28},{8,0},{12,4},{16,8},{20,12},{24,16},{28,20},{1,25},{... | collective-permute-start | bytes 294920 | tf_op jit(solution)/shard_map/ppermute | solution.py:181
  4.7 5.3 %collective-permute-start.1 = (bf16[192,256]{1,0:T(8,128)(2,1)}, bf16[192,256]{1,0:T(8,128)(2,1)S(1)}, u32[]{:S(2)}, u32[]{:S(2)}) collective-permute-start(bf16[192,256]{1,0:T(8,128)(2,1)} %param.7), channel_id=1, source_target_pairs={{0,16},{4,20},{8,24},{12,28},{16,0},{20,4},{24,8},{28,12},{1,17},{... | collective-permute-start | bytes 294920 | tf_op jit(solution)/shard_map/ppermute | solution.py:181
  10.9 1.8 %copy-start.1 = (bf16[4,192,256]{2,1,0:T(8,128)(2,1)}, bf16[4,192,256]{2,1,0:T(8,128)(2,1)S(1)}, u32[]{:S(2)}) copy-start(bf16[4,192,256]{2,1,0:T(8,128)(2,1)S(1)} %pad_maximum_fusion.near_hbm) | copy-start | bytes 1179652
  10.9 1.8 %collective-permute-start.3 = (bf16[4,192,256]{2,1,0:T(8,128)(2,1)S(1)}, bf16[4,192,256]{2,1,0:T(8,128)(2,1)S(1)}, u32[]{:S(2)}, u32[]{:S(2)}) collective-permute-start(bf16[4,192,256]{2,1,0:T(8,128)(2,1)S(1)} %pad_maximum_fusion.near_hbm), channel_id=1, source_target_pairs={{0,4},{4,0},{8,12},{12,8},{16,20},{20,16},{24,28},{28,24},{1,5},{5... | collective-permute-start | bytes 1179656 | tf_op jit(solution)/shard_map/ppermute | solution.py:182
  12.7 0.7 %copy-start.2 = (bf16[4,192,256]{2,1,0:T(8,128)(2,1)}, bf16[4,192,256]{2,1,0:T(8,128)(2,1)S(1)}, u32[]{:S(2)}) copy-start(bf16[4,192,256]{2,1,0:T(8,128)(2,1)S(1)} %collective-permute-done.3.far_hbm) | copy-start | bytes 1179652
  13.5 16.9 %copy-start.7 = (bf16[192,256]{1,0:T(8,128)(2,1)S(1)}, bf16[192,256]{1,0:T(8,128)(2,1)}, u32[]{:S(2)}) copy-start(bf16[192,256]{1,0:T(8,128)(2,1)} %param.13) | copy-start | bytes 294916
  17.7 6.7 %collective-permute-start.4 = (bf16[192,256]{1,0:T(8,128)(2,1)}, bf16[192,256]{1,0:T(8,128)(2,1)S(1)}, u32[]{:S(2)}, u32[]{:S(2)}) collective-permute-start(bf16[192,256]{1,0:T(8,128)(2,1)} %get-tuple-element.9), channel_id=1, source_target_pairs={{0,1},{1,2},{2,3},{3,0},{4,5},{5,6},{6,7},{7,4},{8,9},{9,10},{10,1... | collective-permute-start | bytes 294920 | tf_op jit(solution)/shard_map/ppermute | solution.py:187
  18.9 9.7 %collective-permute-start.5 = (bf16[192,256]{1,0:T(8,128)(2,1)}, bf16[192,256]{1,0:T(8,128)(2,1)S(1)}, u32[]{:S(2)}, u32[]{:S(2)}) collective-permute-start(bf16[192,256]{1,0:T(8,128)(2,1)} %get-tuple-element.10), channel_id=1, source_target_pairs={{0,2},{1,3},{2,0},{3,1},{4,6},{5,7},{6,4},{7,5},{8,10},{9,11},{10,... | collective-permute-start | bytes 294920 | tf_op jit(solution)/shard_map/ppermute | solution.py:187
  21.7 6.9 %collective-permute-start.6 = (bf16[192,256]{1,0:T(8,128)(2,1)}, bf16[192,256]{1,0:T(8,128)(2,1)S(1)}, u32[]{:S(2)}, u32[]{:S(2)}) collective-permute-start(bf16[192,256]{1,0:T(8,128)(2,1)} %get-tuple-element.11), channel_id=1, source_target_pairs={{0,3},{1,0},{2,1},{3,2},{4,7},{5,4},{6,5},{7,6},{8,11},{9,8},{10,9... | collective-permute-start | bytes 294920 | tf_op jit(solution)/shard_map/ppermute | solution.py:187
  30.6 13.5 %copy-start.3 = (bf16[192,256]{1,0:T(8,128)(2,1)}, bf16[192,256]{1,0:T(8,128)(2,1)S(1)}, u32[]{:S(2)}) copy-start(bf16[192,256]{1,0:T(8,128)(2,1)S(1)} %convolution_convert_fusion.mine_hbm) | copy-start | bytes 294916
  30.6 7.3 %collective-permute-start.9 = (bf16[192,256]{1,0:T(8,128)(2,1)S(1)}, bf16[192,256]{1,0:T(8,128)(2,1)S(1)}, u32[]{:S(2)}, u32[]{:S(2)}) collective-permute-start(bf16[192,256]{1,0:T(8,128)(2,1)S(1)} %convolution_convert_fusion.mine_hbm), channel_id=1, source_target_pairs={{0,3},{1,0},{2,1},{3,2},{4,7},{5,4},{6,5},{7,6},{8,11},{9,8},{10,9... | collective-permute-start | bytes 294920 | tf_op jit(solution)/shard_map/ppermute | solution.py:189
  34.7 9.4 %collective-permute-start.8 = (bf16[192,256]{1,0:T(8,128)(2,1)S(1)}, bf16[192,256]{1,0:T(8,128)(2,1)S(1)}, u32[]{:S(2)}, u32[]{:S(2)}) collective-permute-start(bf16[192,256]{1,0:T(8,128)(2,1)S(1)} %convolution_convert_fusion.mine_hbm), channel_id=1, source_target_pairs={{0,2},{1,3},{2,0},{3,1},{4,6},{5,7},{6,4},{7,5},{8,10},{9,11},{10,... | collective-permute-start | bytes 294920 | tf_op jit(solution)/shard_map/ppermute | solution.py:189
  34.7 9.4 %collective-permute-start.7 = (bf16[192,256]{1,0:T(8,128)(2,1)S(1)}, bf16[192,256]{1,0:T(8,128)(2,1)S(1)}, u32[]{:S(2)}, u32[]{:S(2)}) collective-permute-start(bf16[192,256]{1,0:T(8,128)(2,1)S(1)} %convolution_convert_fusion.mine_hbm), channel_id=1, source_target_pairs={{0,1},{1,2},{2,3},{3,0},{4,5},{5,6},{6,7},{7,4},{8,9},{9,10},{10,1... | collective-permute-start | bytes 294920 | tf_op jit(solution)/shard_map/ppermute | solution.py:189
  37.9 6.2 %copy-start.4 = (bf16[192,256]{1,0:T(8,128)(2,1)}, bf16[192,256]{1,0:T(8,128)(2,1)S(1)}, u32[]{:S(2)}) copy-start(bf16[192,256]{1,0:T(8,128)(2,1)S(1)} %collective-permute-done.9.rest_2_) | copy-start | bytes 294916
  44.1 0.6 %copy-start.5 = (bf16[192,256]{1,0:T(8,128)(2,1)}, bf16[192,256]{1,0:T(8,128)(2,1)S(1)}, u32[]{:S(2)}) copy-start(bf16[192,256]{1,0:T(8,128)(2,1)S(1)} %collective-permute-done.8.rest_1_) | copy-start | bytes 294916
  44.1 0.7 %copy-start.6 = (bf16[192,256]{1,0:T(8,128)(2,1)}, bf16[192,256]{1,0:T(8,128)(2,1)S(1)}, u32[]{:S(2)}) copy-start(bf16[192,256]{1,0:T(8,128)(2,1)S(1)} %collective-permute-done.7.rest_0_) | copy-start | bytes 294916
  49.4 2.6 %collective-permute-start.10 = (f32[4,192,256]{2,1,0:T(8,128)}, f32[4,192,256]{2,1,0:T(8,128)S(1)}, u32[]{:S(2)}, u32[]{:S(2)}) collective-permute-start(f32[4,192,256]{2,1,0:T(8,128)} %get-tuple-element.13), channel_id=1, source_target_pairs={{0,4},{4,0},{8,12},{12,8},{16,20},{20,16},{24,28},{28,24},{1,5},{5... | collective-permute-start | bytes 2359304 | tf_op jit(solution)/shard_map/ppermute | solution.py:193
  53.2 6.9 %collective-permute-start.11 = (bf16[192,256]{1,0:T(8,128)(2,1)S(1)}, bf16[192,256]{1,0:T(8,128)(2,1)S(1)}, u32[]{:S(2)}, u32[]{:S(2)}) collective-permute-start(bf16[192,256]{1,0:T(8,128)(2,1)S(1)} %get-tuple-element.16), channel_id=1, source_target_pairs={{0,8},{4,12},{8,16},{12,20},{16,24},{20,28},{24,0},{28,4},{1,9},{5... | collective-permute-start | bytes 294920 | tf_op jit(solution)/shard_map/ppermute | solution.py:197
  57.0 5.2 %collective-permute-start.13 = (bf16[192,256]{1,0:T(8,128)(2,1)S(1)}, bf16[192,256]{1,0:T(8,128)(2,1)S(1)}, u32[]{:S(2)}, u32[]{:S(2)}) collective-permute-start(bf16[192,256]{1,0:T(8,128)(2,1)S(1)} %get-tuple-element.17), channel_id=1, source_target_pairs={{0,24},{4,28},{8,0},{12,4},{16,8},{20,12},{24,16},{28,20},{1,25},{... | collective-permute-start | bytes 294920 | tf_op jit(solution)/shard_map/ppermute | solution.py:197
  57.0 5.2 %collective-permute-start.12 = (bf16[192,256]{1,0:T(8,128)(2,1)S(1)}, bf16[192,256]{1,0:T(8,128)(2,1)S(1)}, u32[]{:S(2)}, u32[]{:S(2)}) collective-permute-start(bf16[192,256]{1,0:T(8,128)(2,1)S(1)} %get-tuple-element.18), channel_id=1, source_target_pairs={{0,16},{4,20},{8,24},{12,28},{16,0},{20,4},{24,8},{28,12},{1,17},{... | collective-permute-start | bytes 294920 | tf_op jit(solution)/shard_map/ppermute | solution.py:197

commit v7 on v5

--- a/solution.py
+++ b/solution.py
@@ -20,6 +20,25 @@
     scaled = (grad_rows.astype(jnp.float32) * silu_slope(mixed)).astype(jnp.bfloat16)
     pulled = jnp.dot(scaled, weight.T, preferred_element_type=jnp.float32).astype(jnp.bfloat16)
     return (activated, pulled)
+
+
+UNROLL = 4
+
+
+def run_slots(count, product, place):
+    def group(g, carry):
+        base = g * UNROLL
+        values = [product(base + j) for j in range(UNROLL)]
+        for j, value in enumerate(values):
+            place(base + j, value)
+        return carry
+
+    def single(k, carry):
+        place(k, product(k))
+        return carry
+
+    lax.fori_loop(0, count // UNROLL, group, 0)
+    lax.fori_loop((count // UNROLL) * UNROLL, count, single, 0)
 
 
 def split_out(acc_ref, own_ref, send_refs, me):
@@ -45,13 +64,15 @@
         f_ref[pl.ds(far, piece), :] = far_ref[shift]
     acc_ref[...] = jnp.zeros_like(acc_ref)
 
-    def step(k, carry):
+    def product(k):
         f = f_ref[pl.ds(pl.multiple_of(cols_ref[k] * tile, tile), tile), :]
+        return jnp.dot(a_ref[k], f, preferred_element_type=jnp.float32)
+
+    def place(k, value):
         rows = pl.ds(pl.multiple_of(rows_ref[k] * tile, tile), tile)
-        acc_ref[rows, :] += jnp.dot(a_ref[k], f, preferred_element_type=jnp.float32)
-        return carry
-
-    lax.fori_loop(0, jnp.minimum(info_ref[0], a_ref.shape[0]), step, 0)
+        acc_ref[rows, :] += value
+
+    run_slots(jnp.minimum(info_ref[0], a_ref.shape[0]), product, place)
     split_out(acc_ref, own_ref, send_refs, lax.axis_index("col"))
 
 
@@ -67,15 +88,17 @@
         block_ref[pl.ds(start, chunk), :] = got_refs[shift - 1][...]
     acc_ref[...] = jnp.zeros_like(acc_ref)
 
-    def step(k, carry):
+    def product(k):
         p = block_ref[pl.ds(pl.multiple_of(rows_ref[k] * tile, tile), tile), :]
-        cols = pl.ds(pl.multiple_of(cols_ref[k] * tile, tile), tile)
-        acc_ref[cols, :] += lax.dot_general(
+        return lax.dot_general(
             a_ref[k], p, (((0,), (0,)), ((), ())), preferred_element_type=jnp.float32
         )
-        return carry
-
-    lax.fori_loop(0, jnp.minimum(info_ref[0], a_ref.shape[0]), step, 0)
+
+    def place(k, value):
+        cols = pl.ds(pl.multiple_of(cols_ref[k] * tile, tile), tile)
+        acc_ref[cols, :] += value
+
+    run_slots(jnp.minimum(info_ref[0], a_ref.shape[0]), product, place)
     chips = near_ref.shape[0]
     piece = near_ref.shape[1]
     me_row = lax.axis_index("row")

time: 61.5 us -> 60.8 us (0.989)
  starting transfers between devices: 21.6 us -> 20.3 us
  waiting for transfers between devices: 24.5 us -> 25.8 us
  Pallas kernels: 7.61 us -> 6.78 us
    ppermute x3, waiting for transfers between devices: 5.33 us -> 5.98 us  [on_device(): total = total + lax.ppermute(send[shift], 'col', perm).astype(jnp.float32)]
    ppermute x3, starting transfers between devices: 5.2 us -> 4.56 us  [on_device(): total_g = total_g + lax.ppermute(piece, 'row', perm).astype(jnp.float32)]
where the time goes in v7:
time: 60.8 us; the launch traced here: 60.6 us
  waiting for transfers between devices  25.8 us (42%)
  starting transfers between devices  20.3 us (33%)
  Pallas kernels  6.78 us (11%)
  other arithmetic  2.89 us (5%)
  matrix products  2.01 us (3%)
  local copies, waits for them, and re-layouts  1.45 us (2%)
  between operations  1.39 us (2%)
    ppermute x3, waiting for transfers between devices, on_device(): got = [lax.ppermute(pulled_own, 'col', perm) for perm in shifts('col')]  9.01 us
    ppermute x3, waiting for transfers between devices, on_device(): total = total + lax.ppermute(send[shift], 'col', perm).astype(jnp.float32)  5.98 us
    ppermute x3, starting transfers between devices, on_device(): lax.ppermute(features, 'row', perm)  5.97 us
    ppermute x3, starting transfers between devices, on_device(): total = total + lax.ppermute(send[shift], 'col', perm).astype(jnp.float32)  5.57 us
    ppermute x3, starting transfers between devices, on_device(): total_g = total_g + lax.ppermute(piece, 'row', perm).astype(jnp.float32)  4.56 us
    ppermute x3, starting transfers between devices, on_device(): got = [lax.ppermute(pulled_own, 'col', perm) for perm in shifts('col')]  4.09 us
    ppermute x3, waiting for transfers between devices, on_device(): total_g = total_g + lax.ppermute(piece, 'row', perm).astype(jnp.float32)  3.96 us
    pallas_call x1, Pallas kernels, tile_products_t(): pl.pallas_call(functools.partial(backward_kernel, len(got) + 1), out_shap...  3.65 us
  transfers between devices with their start and end apart: 14, of which 11 were waited for; matrix products, arithmetic and copies ran while one was open for 0% of the time, Pallas kernels for 0%

profile of v7, /device:TPU:0, one launch (start us, length us, event | category | flops | bytes accessed | tf_op | source)
XLA Modules:
  0.0 60.6 jit_solution(11769262374104094252)
XLA Ops:
  0.6 3.0 %collective-permute-start = (bf16[192,256]{1,0:T(8,128)(2,1)}, bf16[192,256]{1,0:T(8,128)(2,1)S(1)}, u32[]{:S(2)}, u32[]{:S(2)}) collective-permute-start(bf16[192,256]{1,0:T(8,128)(2,1)} %param.7), channel_id=1, source_target_pairs={{0,8},{4,12},{8,16},{12,20},{16,24},{20,28},{24,0},{28,4},{1,9},{5... | collective-permute-start | bytes 294920 | tf_op jit(solution)/shard_map/ppermute | solution.py:171
  3.7 1.0 %collective-permute-start.2 = (bf16[192,256]{1,0:T(8,128)(2,1)}, bf16[192,256]{1,0:T(8,128)(2,1)S(1)}, u32[]{:S(2)}, u32[]{:S(2)}) collective-permute-start(bf16[192,256]{1,0:T(8,128)(2,1)} %param.7), channel_id=1, source_target_pairs={{0,24},{4,28},{8,0},{12,4},{16,8},{20,12},{24,16},{28,20},{1,25},{... | collective-permute-start | bytes 294920 | tf_op jit(solution)/shard_map/ppermute | solution.py:171
  4.7 1.9 %collective-permute-start.1 = (bf16[192,256]{1,0:T(8,128)(2,1)}, bf16[192,256]{1,0:T(8,128)(2,1)S(1)}, u32[]{:S(2)}, u32[]{:S(2)}) collective-permute-start(bf16[192,256]{1,0:T(8,128)(2,1)} %param.7), channel_id=1, source_target_pairs={{0,16},{4,20},{8,24},{12,28},{16,0},{20,4},{24,8},{28,12},{1,17},{... | collective-permute-start | bytes 294920 | tf_op jit(solution)/shard_map/ppermute | solution.py:171
  6.6 1.6 %collective-permute-done = bf16[192,256]{1,0:T(8,128)(2,1)S(1)} collective-permute-done((bf16[192,256]{1,0:T(8,128)(2,1)}, bf16[192,256]{1,0:T(8,128)(2,1)S(1)}, u32[]{:S(2)}, u32[]{:S(2)}) %collective-permute-start) | collective-permute-done | bytes 98336 | tf_op jit(solution)/shard_map/ppermute | solution.py:171
  8.3 1.7 %collective-permute-done.2 = bf16[192,256]{1,0:T(8,128)(2,1)S(1)} collective-permute-done((bf16[192,256]{1,0:T(8,128)(2,1)}, bf16[192,256]{1,0:T(8,128)(2,1)S(1)}, u32[]{:S(2)}, u32[]{:S(2)}) %collective-permute-start.2) | collective-permute-done | bytes 98336 | tf_op jit(solution)/shard_map/ppermute | solution.py:171
  10.0 0.9 %pad_maximum_fusion.near_ref = bf16[4,192,256]{2,1,0:T(8,128)(2,1)S(1)} fusion(bf16[1,192,256]{2,1,0:T(8,128)(2,1)S(1)} %bitcast.32, bf16[1,192,256]{2,1,0:T(8,128)(2,1)S(1)} %bitcast.33, bf16[1,192,256]{2,1,0:T(8,128)(2,1)S(1)} %bitcast.31, bf16[1,192,256]{2,1,0:T(8,128)(2,1)} %bitcast.30), kind=kLoop, calls=%fused_computation.1 | loop fusion | flops 589824 | bytes 786432 | tf_op jit(solution)/shard_map/stack | solution.py:171
  10.9 0.1 collective-permute-start.3
  11.7 1.0 %collective-permute-done.3.far_ref = bf16[4,192,256]{2,1,0:T(8,128)(2,1)S(1)} collective-permute-done((bf16[4,192,256]{2,1,0:T(8,128)(2,1)S(1)}, bf16[4,192,256]{2,1,0:T(8,128)(2,1)S(1)}, u32[]{:S(2)}, u32[]{:S(2)}) %collective-permute-start.3) | collective-permute-done | bytes 393248 | tf_op jit(solution)/shard_map/ppermute | solution.py:172
  12.7 0.7 %copy-done.2 = bf16[4,192,256]{2,1,0:T(8,128)(2,1)} copy-done((bf16[4,192,256]{2,1,0:T(8,128)(2,1)}, bf16[4,192,256]{2,1,0:T(8,128)(2,1)S(1)}, u32[]{:S(2)}) %copy-start.2) | copy-done | bytes 393240
  13.5 3.1 %shard_map.86 = (f32[192,256]{1,0:T(8,128)}, bf16[192,256]{1,0:T(8,128)(2,1)}, bf16[192,256]{1,0:T(8,128)(2,1)}, bf16[192,256]{1,0:T(8,128)(2,1)}) custom-call(s32[12]{0:T(128)} %bitcast.34, s32[12]{0:T(128)} %bitcast.36, s32[1]{0:T(128)} %bitcast.26.info_ref, bf16[12,256,256]{2,1,0:T(8,128)(2,1)} %bitcast.28, bf16[4,192,256]{2,1,0:T(8,128)(2,1)} %copy-done.1, ...), custom_call_target="tpu_custom_call" | custom-call | tf_op jit(solution)/shard_map/pallas_call | solution.py:120
  16.6 1.7 %collective-permute-start.4 = (bf16[192,256]{1,0:T(8,128)(2,1)}, bf16[192,256]{1,0:T(8,128)(2,1)S(1)}, u32[]{:S(2)}, u32[]{:S(2)}) collective-permute-start(bf16[192,256]{1,0:T(8,128)(2,1)} %get-tuple-element.9), channel_id=1, source_target_pairs={{0,1},{1,2},{2,3},{3,0},{4,5},{5,6},{6,7},{7,4},{8,9},{9,10},{10,1... | collective-permute-start | bytes 294920 | tf_op jit(solution)/shard_map/ppermute | solution.py:177
  18.3 2.6 %collective-permute-start.5 = (bf16[192,256]{1,0:T(8,128)(2,1)}, bf16[192,256]{1,0:T(8,128)(2,1)S(1)}, u32[]{:S(2)}, u32[]{:S(2)}) collective-permute-start(bf16[192,256]{1,0:T(8,128)(2,1)} %get-tuple-element.10), channel_id=1, source_target_pairs={{0,2},{1,3},{2,0},{3,1},{4,6},{5,7},{6,4},{7,5},{8,10},{9,11},{10,... | collective-permute-start | bytes 294920 | tf_op jit(solution)/shard_map/ppermute | solution.py:177
  20.9 1.3 %collective-permute-start.6 = (bf16[192,256]{1,0:T(8,128)(2,1)}, bf16[192,256]{1,0:T(8,128)(2,1)S(1)}, u32[]{:S(2)}, u32[]{:S(2)}) collective-permute-start(bf16[192,256]{1,0:T(8,128)(2,1)} %get-tuple-element.11), channel_id=1, source_target_pairs={{0,3},{1,0},{2,1},{3,2},{4,7},{5,4},{6,5},{7,6},{8,11},{9,8},{10,9... | collective-permute-start | bytes 294920 | tf_op jit(solution)/shard_map/ppermute | solution.py:177
  22.2 2.2 %collective-permute-done.4 = bf16[192,256]{1,0:T(8,128)(2,1)S(1)} collective-permute-done((bf16[192,256]{1,0:T(8,128)(2,1)}, bf16[192,256]{1,0:T(8,128)(2,1)S(1)}, u32[]{:S(2)}, u32[]{:S(2)}) %collective-permute-start.4) | collective-permute-done | bytes 98336 | tf_op jit(solution)/shard_map/ppermute | solution.py:177
  24.4 3.8 %collective-permute-done.5 = bf16[192,256]{1,0:T(8,128)(2,1)S(1)} collective-permute-done((bf16[192,256]{1,0:T(8,128)(2,1)}, bf16[192,256]{1,0:T(8,128)(2,1)S(1)}, u32[]{:S(2)}, u32[]{:S(2)}) %collective-permute-start.5) | collective-permute-done | bytes 98336 | tf_op jit(solution)/shard_map/ppermute | solution.py:177
  28.2 1.8 %multiply_convert_fusion.1 = (bf16[192,256]{1,0:T(8,128)(2,1)}, f32[192,256]{1,0:T(8,128)S(1)}) fusion(bf16[256,256]{1,0:T(8,128)(2,1)S(1)} %copy-done, bf16[192,256]{1,0:T(8,128)(2,1)S(1)} %collective-permute-done.6, bf16[192,256]{1,0:T(8,128)(2,1)S(1)} %collective-permute-done.5, f32[192,256]{1,0:T(8,128)} %get-tuple-element.8, ...), kind=kOutput, calls=%fused_computation.8 | convolution fusion | flops 25755648 | bytes 917504 | tf_op jit(solution)/shard_map/dot_general | solution.py:18
  29.9 0.2 convolution_convert_fusion.mine_ref
  30.2 3.2 %collective-permute-start.9 = (bf16[192,256]{1,0:T(8,128)(2,1)S(1)}, bf16[192,256]{1,0:T(8,128)(2,1)S(1)}, u32[]{:S(2)}, u32[]{:S(2)}) collective-permute-start(bf16[192,256]{1,0:T(8,128)(2,1)S(1)} %convolution_convert_fusion.mine_ref), channel_id=1, source_target_pairs={{0,3},{1,0},{2,1},{3,2},{4,7},{5,4},{6,5},{7,6},{8,11},{9,8},{10,9... | collective-permute-start | bytes 294920 | tf_op jit(solution)/shard_map/ppermute | solution.py:179
  33.4 0.9 %collective-permute-start.8 = (bf16[192,256]{1,0:T(8,128)(2,1)S(1)}, bf16[192,256]{1,0:T(8,128)(2,1)S(1)}, u32[]{:S(2)}, u32[]{:S(2)}) collective-permute-start(bf16[192,256]{1,0:T(8,128)(2,1)S(1)} %convolution_convert_fusion.mine_ref), channel_id=1, source_target_pairs={{0,2},{1,3},{2,0},{3,1},{4,6},{5,7},{6,4},{7,5},{8,10},{9,11},{10,... | collective-permute-start | bytes 294920 | tf_op jit(solution)/shard_map/ppermute | solution.py:179
  34.3 2.3 %collective-permute-done.9.rest_2_ = bf16[192,256]{1,0:T(8,128)(2,1)S(1)} collective-permute-done((bf16[192,256]{1,0:T(8,128)(2,1)S(1)}, bf16[192,256]{1,0:T(8,128)(2,1)S(1)}, u32[]{:S(2)}, u32[]{:S(2)}) %collective-permute-start.9) | collective-permute-done | bytes 98336 | tf_op jit(solution)/shard_map/ppermute | solution.py:179
  36.6 6.7 %collective-permute-done.8.rest_1_ = bf16[192,256]{1,0:T(8,128)(2,1)S(1)} collective-permute-done((bf16[192,256]{1,0:T(8,128)(2,1)S(1)}, bf16[192,256]{1,0:T(8,128)(2,1)S(1)}, u32[]{:S(2)}, u32[]{:S(2)}) %collective-permute-start.8) | collective-permute-done | bytes 98336 | tf_op jit(solution)/shard_map/ppermute | solution.py:179
  43.3 0.6 %copy-done.5 = bf16[192,256]{1,0:T(8,128)(2,1)} copy-done((bf16[192,256]{1,0:T(8,128)(2,1)}, bf16[192,256]{1,0:T(8,128)(2,1)S(1)}, u32[]{:S(2)}) %copy-start.5) | copy-done | bytes 98328
  44.0 3.6 %shard_map.87 = (f32[4,192,256]{2,1,0:T(8,128)}, f32[4,192,256]{2,1,0:T(8,128)}) custom-call(s32[12]{0:T(128)} %bitcast.35, s32[12]{0:T(128)} %bitcast.37, s32[1]{0:T(128)} %bitcast.27.info_ref, bf16[12,256,256]{2,1,0:T(8,128)(2,1)} %bitcast.29, bf16[192,256]{1,0:T(8,128)(2,1)} %copy-done.3, bf16[192,256]{1,0:T(8,128)(2,1)} %copy-done.6, ...), custom_call_target="tpu_custom_call" | custom-call | tf_op jit(solution)/shard_map/pallas_call | solution.py:137
  47.6 2.5 %collective-permute-done.10 = f32[4,192,256]{2,1,0:T(8,128)S(1)} collective-permute-done((f32[4,192,256]{2,1,0:T(8,128)}, f32[4,192,256]{2,1,0:T(8,128)S(1)}, u32[]{:S(2)}, u32[]{:S(2)}) %collective-permute-start.10) | collective-permute-done | bytes 786464 | tf_op jit(solution)/shard_map/ppermute | solution.py:183
  50.1 1.3 %fusion.6 = (bf16[4,192,256]{2,1,0:T(8,128)(2,1)S(1)}, f32[4,192,256]{2,1,0:T(8,128)S(1)}) fusion(f32[4,192,256]{2,1,0:T(8,128)} %get-tuple-element.12, f32[4,192,256]{2,1,0:T(8,128)S(1)} %collective-permute-done.10), kind=kLoop, calls=%fused_computation.16 | loop fusion | flops 393216 | bytes 2752512 | tf_op jit(solution)/shard_map/convert.2
  51.4 1.9 %collective-permute-start.11 = (bf16[192,256]{1,0:T(8,128)(2,1)S(1)}, bf16[192,256]{1,0:T(8,128)(2,1)S(1)}, u32[]{:S(2)}, u32[]{:S(2)}) collective-permute-start(bf16[192,256]{1,0:T(8,128)(2,1)S(1)} %get-tuple-element.16), channel_id=1, source_target_pairs={{0,8},{4,12},{8,16},{12,20},{16,24},{20,28},{24,0},{28,4},{1,9},{5... | collective-permute-start | bytes 294920 | tf_op jit(solution)/shard_map/ppermute | solution.py:187
  53.3 1.5 %collective-permute-start.13 = (bf16[192,256]{1,0:T(8,128)(2,1)S(1)}, bf16[192,256]{1,0:T(8,128)(2,1)S(1)}, u32[]{:S(2)}, u32[]{:S(2)}) collective-permute-start(bf16[192,256]{1,0:T(8,128)(2,1)S(1)} %get-tuple-element.17), channel_id=1, source_target_pairs={{0,24},{4,28},{8,0},{12,4},{16,8},{20,12},{24,16},{28,20},{1,25},{... | collective-permute-start | bytes 294920 | tf_op jit(solution)/shard_map/ppermute | solution.py:187
  54.8 1.2 %collective-permute-start.12 = (bf16[192,256]{1,0:T(8,128)(2,1)S(1)}, bf16[192,256]{1,0:T(8,128)(2,1)S(1)}, u32[]{:S(2)}, u32[]{:S(2)}) collective-permute-start(bf16[192,256]{1,0:T(8,128)(2,1)S(1)} %get-tuple-element.18), channel_id=1, source_target_pairs={{0,16},{4,20},{8,24},{12,28},{16,0},{20,4},{24,8},{28,12},{1,17},{... | collective-permute-start | bytes 294920 | tf_op jit(solution)/shard_map/ppermute | solution.py:187
  56.0 2.4 %collective-permute-done.11 = bf16[192,256]{1,0:T(8,128)(2,1)S(1)} collective-permute-done((bf16[192,256]{1,0:T(8,128)(2,1)S(1)}, bf16[192,256]{1,0:T(8,128)(2,1)S(1)}, u32[]{:S(2)}, u32[]{:S(2)}) %collective-permute-start.11) | collective-permute-done | bytes 98336 | tf_op jit(solution)/shard_map/ppermute | solution.py:187
  58.4 1.0 %collective-permute-done.13 = bf16[192,256]{1,0:T(8,128)(2,1)S(1)} collective-permute-done((bf16[192,256]{1,0:T(8,128)(2,1)S(1)}, bf16[192,256]{1,0:T(8,128)(2,1)S(1)}, u32[]{:S(2)}, u32[]{:S(2)}) %collective-permute-start.13) | collective-permute-done | bytes 98336 | tf_op jit(solution)/shard_map/ppermute | solution.py:187
  59.4 0.5 collective-permute-done.12
  59.9 0.7 %fusion.3 = bf16[192,256]{1,0:T(8,128)(2,1)} fusion(f32[4,192,256]{2,1,0:T(8,128)S(1)} %get-tuple-element.15, bf16[192,256]{1,0:T(8,128)(2,1)S(1)} %collective-permute-done.13, bf16[192,256]{1,0:T(8,128)(2,1)S(1)} %collective-permute-done.12, bf16[192,256]{1,0:T(8,128)(2,1)S(1)} %collective-permute-done.11), kind=kLoop, calls=%fused_computation.6 | loop fusion | flops 344064 | bytes 589824 | tf_op jit(solution)/shard_map/convert_element_type | solution.py:188
  (20 shorter events, 0.1 us)
Async XLA Ops:
  0.6 27.5 %copy-start = (bf16[256,256]{1,0:T(8,128)(2,1)S(1)}, bf16[256,256]{1,0:T(8,128)(2,1)}, u32[]{:S(2)}) copy-start(bf16[256,256]{1,0:T(8,128)(2,1)} %param.12) | copy-start | bytes 393220
  0.6 7.6 %collective-permute-start = (bf16[192,256]{1,0:T(8,128)(2,1)}, bf16[192,256]{1,0:T(8,128)(2,1)S(1)}, u32[]{:S(2)}, u32[]{:S(2)}) collective-permute-start(bf16[192,256]{1,0:T(8,128)(2,1)} %param.7), channel_id=1, source_target_pairs={{0,8},{4,12},{8,16},{12,20},{16,24},{20,28},{24,0},{28,4},{1,9},{5... | collective-permute-start | bytes 294920 | tf_op jit(solution)/shard_map/ppermute | solution.py:171
  3.7 6.3 %collective-permute-start.2 = (bf16[192,256]{1,0:T(8,128)(2,1)}, bf16[192,256]{1,0:T(8,128)(2,1)S(1)}, u32[]{:S(2)}, u32[]{:S(2)}) collective-permute-start(bf16[192,256]{1,0:T(8,128)(2,1)} %param.7), channel_id=1, source_target_pairs={{0,24},{4,28},{8,0},{12,4},{16,8},{20,12},{24,16},{28,20},{1,25},{... | collective-permute-start | bytes 294920 | tf_op jit(solution)/shard_map/ppermute | solution.py:171
  4.7 5.3 %collective-permute-start.1 = (bf16[192,256]{1,0:T(8,128)(2,1)}, bf16[192,256]{1,0:T(8,128)(2,1)S(1)}, u32[]{:S(2)}, u32[]{:S(2)}) collective-permute-start(bf16[192,256]{1,0:T(8,128)(2,1)} %param.7), channel_id=1, source_target_pairs={{0,16},{4,20},{8,24},{12,28},{16,0},{20,4},{24,8},{28,12},{1,17},{... | collective-permute-start | bytes 294920 | tf_op jit(solution)/shard_map/ppermute | solution.py:171
  10.9 1.8 %copy-start.1 = (bf16[4,192,256]{2,1,0:T(8,128)(2,1)}, bf16[4,192,256]{2,1,0:T(8,128)(2,1)S(1)}, u32[]{:S(2)}) copy-start(bf16[4,192,256]{2,1,0:T(8,128)(2,1)S(1)} %pad_maximum_fusion.near_ref) | copy-start | bytes 1179652
  10.9 1.8 %collective-permute-start.3 = (bf16[4,192,256]{2,1,0:T(8,128)(2,1)S(1)}, bf16[4,192,256]{2,1,0:T(8,128)(2,1)S(1)}, u32[]{:S(2)}, u32[]{:S(2)}) collective-permute-start(bf16[4,192,256]{2,1,0:T(8,128)(2,1)S(1)} %pad_maximum_fusion.near_ref), channel_id=1, source_target_pairs={{0,4},{4,0},{8,12},{12,8},{16,20},{20,16},{24,28},{28,24},{1,5},{5... | collective-permute-start | bytes 1179656 | tf_op jit(solution)/shard_map/ppermute | solution.py:172
  12.7 0.7 %copy-start.2 = (bf16[4,192,256]{2,1,0:T(8,128)(2,1)}, bf16[4,192,256]{2,1,0:T(8,128)(2,1)S(1)}, u32[]{:S(2)}) copy-start(bf16[4,192,256]{2,1,0:T(8,128)(2,1)S(1)} %collective-permute-done.3.far_ref) | copy-start | bytes 1179652
  13.5 16.5 %copy-start.7 = (bf16[192,256]{1,0:T(8,128)(2,1)S(1)}, bf16[192,256]{1,0:T(8,128)(2,1)}, u32[]{:S(2)}) copy-start(bf16[192,256]{1,0:T(8,128)(2,1)} %param.13) | copy-start | bytes 294916
  16.6 7.8 %collective-permute-start.4 = (bf16[192,256]{1,0:T(8,128)(2,1)}, bf16[192,256]{1,0:T(8,128)(2,1)S(1)}, u32[]{:S(2)}, u32[]{:S(2)}) collective-permute-start(bf16[192,256]{1,0:T(8,128)(2,1)} %get-tuple-element.9), channel_id=1, source_target_pairs={{0,1},{1,2},{2,3},{3,0},{4,5},{5,6},{6,7},{7,4},{8,9},{9,10},{10,1... | collective-permute-start | bytes 294920 | tf_op jit(solution)/shard_map/ppermute | solution.py:177
  18.3 9.9 %collective-permute-start.5 = (bf16[192,256]{1,0:T(8,128)(2,1)}, bf16[192,256]{1,0:T(8,128)(2,1)S(1)}, u32[]{:S(2)}, u32[]{:S(2)}) collective-permute-start(bf16[192,256]{1,0:T(8,128)(2,1)} %get-tuple-element.10), channel_id=1, source_target_pairs={{0,2},{1,3},{2,0},{3,1},{4,6},{5,7},{6,4},{7,5},{8,10},{9,11},{10,... | collective-permute-start | bytes 294920 | tf_op jit(solution)/shard_map/ppermute | solution.py:177
  20.9 7.3 %collective-permute-start.6 = (bf16[192,256]{1,0:T(8,128)(2,1)}, bf16[192,256]{1,0:T(8,128)(2,1)S(1)}, u32[]{:S(2)}, u32[]{:S(2)}) collective-permute-start(bf16[192,256]{1,0:T(8,128)(2,1)} %get-tuple-element.11), channel_id=1, source_target_pairs={{0,3},{1,0},{2,1},{3,2},{4,7},{5,4},{6,5},{7,6},{8,11},{9,8},{10,9... | collective-permute-start | bytes 294920 | tf_op jit(solution)/shard_map/ppermute | solution.py:177
  30.2 13.1 %copy-start.3 = (bf16[192,256]{1,0:T(8,128)(2,1)}, bf16[192,256]{1,0:T(8,128)(2,1)S(1)}, u32[]{:S(2)}) copy-start(bf16[192,256]{1,0:T(8,128)(2,1)S(1)} %convolution_convert_fusion.mine_ref) | copy-start | bytes 294916
  30.2 6.4 %collective-permute-start.9 = (bf16[192,256]{1,0:T(8,128)(2,1)S(1)}, bf16[192,256]{1,0:T(8,128)(2,1)S(1)}, u32[]{:S(2)}, u32[]{:S(2)}) collective-permute-start(bf16[192,256]{1,0:T(8,128)(2,1)S(1)} %convolution_convert_fusion.mine_ref), channel_id=1, source_target_pairs={{0,3},{1,0},{2,1},{3,2},{4,7},{5,4},{6,5},{7,6},{8,11},{9,8},{10,9... | collective-permute-start | bytes 294920 | tf_op jit(solution)/shard_map/ppermute | solution.py:179
  33.4 9.9 %collective-permute-start.8 = (bf16[192,256]{1,0:T(8,128)(2,1)S(1)}, bf16[192,256]{1,0:T(8,128)(2,1)S(1)}, u32[]{:S(2)}, u32[]{:S(2)}) collective-permute-start(bf16[192,256]{1,0:T(8,128)(2,1)S(1)} %convolution_convert_fusion.mine_ref), channel_id=1, source_target_pairs={{0,2},{1,3},{2,0},{3,1},{4,6},{5,7},{6,4},{7,5},{8,10},{9,11},{10,... | collective-permute-start | bytes 294920 | tf_op jit(solution)/shard_map/ppermute | solution.py:179
  34.3 9.0 %collective-permute-start.7 = (bf16[192,256]{1,0:T(8,128)(2,1)S(1)}, bf16[192,256]{1,0:T(8,128)(2,1)S(1)}, u32[]{:S(2)}, u32[]{:S(2)}) collective-permute-start(bf16[192,256]{1,0:T(8,128)(2,1)S(1)} %convolution_convert_fusion.mine_ref), channel_id=1, source_target_pairs={{0,1},{1,2},{2,3},{3,0},{4,5},{5,6},{6,7},{7,4},{8,9},{9,10},{10,1... | collective-permute-start | bytes 294920 | tf_op jit(solution)/shard_map/ppermute | solution.py:179
  36.6 6.7 %copy-start.4 = (bf16[192,256]{1,0:T(8,128)(2,1)}, bf16[192,256]{1,0:T(8,128)(2,1)S(1)}, u32[]{:S(2)}) copy-start(bf16[192,256]{1,0:T(8,128)(2,1)S(1)} %collective-permute-done.9.rest_2_) | copy-start | bytes 294916
  43.3 0.6 %copy-start.5 = (bf16[192,256]{1,0:T(8,128)(2,1)}, bf16[192,256]{1,0:T(8,128)(2,1)S(1)}, u32[]{:S(2)}) copy-start(bf16[192,256]{1,0:T(8,128)(2,1)S(1)} %collective-permute-done.8.rest_1_) | copy-start | bytes 294916
  43.3 0.7 %copy-start.6 = (bf16[192,256]{1,0:T(8,128)(2,1)}, bf16[192,256]{1,0:T(8,128)(2,1)S(1)}, u32[]{:S(2)}) copy-start(bf16[192,256]{1,0:T(8,128)(2,1)S(1)} %collective-permute-done.7.rest_0_) | copy-start | bytes 294916
  47.6 2.5 %collective-permute-start.10 = (f32[4,192,256]{2,1,0:T(8,128)}, f32[4,192,256]{2,1,0:T(8,128)S(1)}, u32[]{:S(2)}, u32[]{:S(2)}) collective-permute-start(f32[4,192,256]{2,1,0:T(8,128)} %get-tuple-element.13), channel_id=1, source_target_pairs={{0,4},{4,0},{8,12},{12,8},{16,20},{20,16},{24,28},{28,24},{1,5},{5... | collective-permute-start | bytes 2359304 | tf_op jit(solution)/shard_map/ppermute | solution.py:183
  51.4 7.0 %collective-permute-start.11 = (bf16[192,256]{1,0:T(8,128)(2,1)S(1)}, bf16[192,256]{1,0:T(8,128)(2,1)S(1)}, u32[]{:S(2)}, u32[]{:S(2)}) collective-permute-start(bf16[192,256]{1,0:T(8,128)(2,1)S(1)} %get-tuple-element.16), channel_id=1, source_target_pairs={{0,8},{4,12},{8,16},{12,20},{16,24},{20,28},{24,0},{28,4},{1,9},{5... | collective-permute-start | bytes 294920 | tf_op jit(solution)/shard_map/ppermute | solution.py:187
  53.3 6.1 %collective-permute-start.13 = (bf16[192,256]{1,0:T(8,128)(2,1)S(1)}, bf16[192,256]{1,0:T(8,128)(2,1)S(1)}, u32[]{:S(2)}, u32[]{:S(2)}) collective-permute-start(bf16[192,256]{1,0:T(8,128)(2,1)S(1)} %get-tuple-element.17), channel_id=1, source_target_pairs={{0,24},{4,28},{8,0},{12,4},{16,8},{20,12},{24,16},{28,20},{1,25},{... | collective-permute-start | bytes 294920 | tf_op jit(solution)/shard_map/ppermute | solution.py:187
  54.8 5.1 %collective-permute-start.12 = (bf16[192,256]{1,0:T(8,128)(2,1)S(1)}, bf16[192,256]{1,0:T(8,128)(2,1)S(1)}, u32[]{:S(2)}, u32[]{:S(2)}) collective-permute-start(bf16[192,256]{1,0:T(8,128)(2,1)S(1)} %get-tuple-element.18), channel_id=1, source_target_pairs={{0,16},{4,20},{8,24},{12,28},{16,0},{20,4},{24,8},{28,12},{1,17},{... | collective-permute-start | bytes 294920 | tf_op jit(solution)/shard_map/ppermute | solution.py:187

commit v8 on v7

--- a/solution.py
+++ b/solution.py
@@ -50,18 +50,20 @@
         send_refs[shift - 1][...] = acc_ref[pl.ds(start, chunk), :].astype(send_refs[shift - 1].dtype)
 
 
-def forward_kernel(rows_ref, cols_ref, info_ref, a_ref, near_ref, far_ref, own_ref, *rest):
-    send_refs, f_ref, acc_ref = rest[:-2], rest[-2], rest[-1]
+def forward_kernel(chips, rows_ref, cols_ref, info_ref, a_ref, *rest):
+    near_refs, far_refs = rest[:chips], rest[chips : 2 * chips]
+    own_ref = rest[2 * chips]
+    send_refs, f_ref, acc_ref = rest[2 * chips + 1 : -2], rest[-2], rest[-1]
     tile = a_ref.shape[1]
-    chips, piece = near_ref.shape[0], near_ref.shape[1]
+    piece = near_refs[0].shape[0]
     me = lax.axis_index("row")
     core, chip = me % 2, me // 2
     for shift in range(chips):
         owner = (chip - shift + chips) % chips
         near = pl.multiple_of((owner * 2 + core) * piece, 16)
         far = pl.multiple_of((owner * 2 + 1 - core) * piece, 16)
-        f_ref[pl.ds(near, piece), :] = near_ref[shift]
-        f_ref[pl.ds(far, piece), :] = far_ref[shift]
+        f_ref[pl.ds(near, piece), :] = near_refs[shift][...]
+        f_ref[pl.ds(far, piece), :] = far_refs[shift][...]
     acc_ref[...] = jnp.zeros_like(acc_ref)
 
     def product(k):
@@ -116,18 +118,18 @@
 def tile_products(rows, cols, info, blocks, near, far, parts):
     out_rows = parts[0] * parts[1]
     chunk = parts[1]
-    width = near.shape[2]
+    width = near[0].shape[1]
     return pl.pallas_call(
-        forward_kernel,
+        functools.partial(forward_kernel, len(near)),
         out_shape=(jax.ShapeDtypeStruct((chunk, width), jnp.float32),)
         + (jax.ShapeDtypeStruct((chunk, width), jnp.bfloat16),) * (parts[0] - 1),
-        in_specs=[SMEM, SMEM, SMEM, VMEM, VMEM, VMEM],
+        in_specs=[SMEM, SMEM, SMEM, VMEM] + [VMEM] * (2 * len(near)),
         out_specs=(VMEM,) * parts[0],
         scratch_shapes=[
-            pltpu.VMEM((2 * near.shape[0] * near.shape[1], width), jnp.bfloat16),
+            pltpu.VMEM((2 * len(near) * near[0].shape[0], width), jnp.bfloat16),
             pltpu.VMEM((out_rows, width), jnp.float32),
         ],
-    )(rows, cols, info, blocks, near, far)
+    )(rows, cols, info, blocks, *near, *far)
 
 
 def tile_products_t(rows, cols, info, blocks, mine, got, n_out, out_rows):
@@ -168,8 +170,8 @@
     n_col = lax.axis_size("col")
     own_rows = features.shape[0]
 
-    near = jnp.stack([features] + [lax.ppermute(features, "row", perm) for perm in chip_shifts(n_row)])
-    far = lax.ppermute(near, "row", partner(n_row))
+    near = [features] + [lax.ppermute(features, "row", perm) for perm in chip_shifts(n_row)]
+    far = [lax.ppermute(piece, "row", partner(n_row)) for piece in near]
     info = tile_count.reshape(1)
     own, *send = tile_products(row_slots, col_slots, info, blocks, near, far, (n_col, own_rows))
     total = own

time: 60.8 us -> 60.3 us (level)
  waiting for transfers between devices: 25.8 us -> 28 us
  starting transfers between devices: 20.3 us -> 18.7 us
  other arithmetic: 2.89 us -> 1.95 us
    ppermute x3, waiting for transfers between devices: 3.36 us -> 5.54 us  [on_device(): lax.ppermute(features, 'row', perm)]
    another operation x2 -> x1, other arithmetic: 2.2 us -> 1.25 us
    ppermute x3, starting transfers between devices: 5.97 us -> 5.07 us  [on_device(): lax.ppermute(features, 'row', perm)]
    ppermute x3, starting transfers between devices: 4.56 us -> 3.77 us  [on_device(): total_g = total_g + lax.ppermute(piece, 'row', perm).astype(jnp.float32)]
    ppermute x1 -> x4, waiting for transfers between devices: 1.03 us -> 0.25 us  [on_device(): far = [lax.ppermute(piece, 'row', partner(n_row)) for piece in near]]
    unnamed x16 -> x26, local copies, waits for them, and re-layouts: 1.43 us -> 1.35 us
  transfers between devices with their start and end apart: 14 -> 17, of which waited for: 11 -> 12; matrix products, arithmetic and copies ran while one was open for 0% -> 0% of each run, Pallas kernels for 0% -> 0%
where the time goes in v8:
time: 60.3 us; the launch traced here: 60.1 us
  waiting for transfers between devices  28 us (46%)
  starting transfers between devices  18.7 us (31%)
  Pallas kernels  6.69 us (11%)
  matrix products  2.01 us (3%)
  other arithmetic  1.95 us (3%)
  between operations  1.41 us (2%)
  local copies, waits for them, and re-layouts  1.37 us (2%)
    ppermute x3, waiting for transfers between devices, on_device(): got = [lax.ppermute(pulled_own, 'col', perm) for perm in shifts('col')]  8.94 us
    ppermute x3, waiting for transfers between devices, on_device(): total = total + lax.ppermute(send[shift], 'col', perm).astype(jnp.float32)  6.52 us
    ppermute x3, waiting for transfers between devices, on_device(): lax.ppermute(features, 'row', perm)  5.54 us
    ppermute x3, starting transfers between devices, on_device(): total = total + lax.ppermute(send[shift], 'col', perm).astype(jnp.float32)  5.33 us
    ppermute x3, starting transfers between devices, on_device(): lax.ppermute(features, 'row', perm)  5.07 us
    ppermute x3, waiting for transfers between devices, on_device(): total_g = total_g + lax.ppermute(piece, 'row', perm).astype(jnp.float32)  4.21 us
    ppermute x3, starting transfers between devices, on_device(): got = [lax.ppermute(pulled_own, 'col', perm) for perm in shifts('col')]  4.02 us
    ppermute x3, starting transfers between devices, on_device(): total_g = total_g + lax.ppermute(piece, 'row', perm).astype(jnp.float32)  3.77 us
  transfers between devices with their start and end apart: 17, of which 12 were waited for; matrix products, arithmetic and copies ran while one was open for 0% of the time, Pallas kernels for 0%

profile of v8, /device:TPU:0, one launch (start us, length us, event | category | flops | bytes accessed | tf_op | source)
XLA Modules:
  0.0 60.1 jit_solution(10545727054556368500)
XLA Ops:
  0.6 4.0 %collective-permute-start.2 = (bf16[192,256]{1,0:T(8,128)(2,1)}, bf16[192,256]{1,0:T(8,128)(2,1)S(1)}, u32[]{:S(2)}, u32[]{:S(2)}) collective-permute-start(bf16[192,256]{1,0:T(8,128)(2,1)} %rest_0_.1), channel_id=1, source_target_pairs={{0,24},{4,28},{8,0},{12,4},{16,8},{20,12},{24,16},{28,20},{1,25},{... | collective-permute-start | bytes 294920 | tf_op jit(solution)/shard_map/ppermute | solution.py:173
  4.6 0.5 collective-permute-start.1
  5.1 0.6 collective-permute-start
  5.7 2.4 %collective-permute-done.2.rest_3_ = bf16[192,256]{1,0:T(8,128)(2,1)S(1)} collective-permute-done((bf16[192,256]{1,0:T(8,128)(2,1)}, bf16[192,256]{1,0:T(8,128)(2,1)S(1)}, u32[]{:S(2)}, u32[]{:S(2)}) %collective-permute-start.2) | collective-permute-done | bytes 98336 | tf_op jit(solution)/shard_map/ppermute | solution.py:173
  8.1 3.2 %collective-permute-done.1.rest_2_ = bf16[192,256]{1,0:T(8,128)(2,1)S(1)} collective-permute-done((bf16[192,256]{1,0:T(8,128)(2,1)}, bf16[192,256]{1,0:T(8,128)(2,1)S(1)}, u32[]{:S(2)}, u32[]{:S(2)}) %collective-permute-start.1) | collective-permute-done | bytes 98336 | tf_op jit(solution)/shard_map/ppermute | solution.py:173
  11.3 0.5 collective-permute-start.4
  12.5 0.1 collective-permute-done.5.rest_6_
  12.6 0.2 collective-permute-done.4.rest_5_
  12.7 0.3 copy-done.4
  13.2 0.2 copy-done.8
  13.4 3.2 %shard_map.86 = (f32[192,256]{1,0:T(8,128)}, bf16[192,256]{1,0:T(8,128)(2,1)}, bf16[192,256]{1,0:T(8,128)(2,1)}, bf16[192,256]{1,0:T(8,128)(2,1)}) custom-call(s32[12]{0:T(128)} %bitcast.26, s32[12]{0:T(128)} %bitcast.28, s32[1]{0:T(128)} %bitcast.22.info_ref, bf16[12,256,256]{2,1,0:T(8,128)(2,1)} %bitcast.24, bf16[192,256]{1,0:T(8,128)(2,1)} %rest_0_.1, ...), custom_call_target="tpu_custom_call" | custom-call | tf_op jit(solution)/shard_map/pallas_call | solution.py:122
  16.5 1.8 %collective-permute-start.7 = (bf16[192,256]{1,0:T(8,128)(2,1)}, bf16[192,256]{1,0:T(8,128)(2,1)S(1)}, u32[]{:S(2)}, u32[]{:S(2)}) collective-permute-start(bf16[192,256]{1,0:T(8,128)(2,1)} %get-tuple-element.9), channel_id=1, source_target_pairs={{0,1},{1,2},{2,3},{3,0},{4,5},{5,6},{6,7},{7,4},{8,9},{9,10},{10,1... | collective-permute-start | bytes 294920 | tf_op jit(solution)/shard_map/ppermute | solution.py:179
  18.3 2.2 %collective-permute-start.8 = (bf16[192,256]{1,0:T(8,128)(2,1)}, bf16[192,256]{1,0:T(8,128)(2,1)S(1)}, u32[]{:S(2)}, u32[]{:S(2)}) collective-permute-start(bf16[192,256]{1,0:T(8,128)(2,1)} %get-tuple-element.10), channel_id=1, source_target_pairs={{0,2},{1,3},{2,0},{3,1},{4,6},{5,7},{6,4},{7,5},{8,10},{9,11},{10,... | collective-permute-start | bytes 294920 | tf_op jit(solution)/shard_map/ppermute | solution.py:179
  20.5 1.3 %collective-permute-start.9 = (bf16[192,256]{1,0:T(8,128)(2,1)}, bf16[192,256]{1,0:T(8,128)(2,1)S(1)}, u32[]{:S(2)}, u32[]{:S(2)}) collective-permute-start(bf16[192,256]{1,0:T(8,128)(2,1)} %get-tuple-element.11), channel_id=1, source_target_pairs={{0,3},{1,0},{2,1},{3,2},{4,7},{5,4},{6,5},{7,6},{8,11},{9,8},{10,9... | collective-permute-start | bytes 294920 | tf_op jit(solution)/shard_map/ppermute | solution.py:179
  21.9 2.5 %collective-permute-done.7 = bf16[192,256]{1,0:T(8,128)(2,1)S(1)} collective-permute-done((bf16[192,256]{1,0:T(8,128)(2,1)}, bf16[192,256]{1,0:T(8,128)(2,1)S(1)}, u32[]{:S(2)}, u32[]{:S(2)}) %collective-permute-start.7) | collective-permute-done | bytes 98336 | tf_op jit(solution)/shard_map/ppermute | solution.py:179
  24.3 4.1 %collective-permute-done.8 = bf16[192,256]{1,0:T(8,128)(2,1)S(1)} collective-permute-done((bf16[192,256]{1,0:T(8,128)(2,1)}, bf16[192,256]{1,0:T(8,128)(2,1)S(1)}, u32[]{:S(2)}, u32[]{:S(2)}) %collective-permute-start.8) | collective-permute-done | bytes 98336 | tf_op jit(solution)/shard_map/ppermute | solution.py:179
  28.4 1.8 %multiply_convert_fusion.1 = (bf16[192,256]{1,0:T(8,128)(2,1)}, f32[192,256]{1,0:T(8,128)S(1)}) fusion(bf16[256,256]{1,0:T(8,128)(2,1)S(1)} %copy-done, bf16[192,256]{1,0:T(8,128)(2,1)S(1)} %collective-permute-done.9, bf16[192,256]{1,0:T(8,128)(2,1)S(1)} %collective-permute-done.8, f32[192,256]{1,0:T(8,128)} %get-tuple-element.8, ...), kind=kOutput, calls=%fused_computation.7 | convolution fusion | flops 25755648 | bytes 917504 | tf_op jit(solution)/shard_map/dot_general | solution.py:18
  30.2 0.2 convolution_convert_fusion.mine_ref
  30.4 3.3 %collective-permute-start.12 = (bf16[192,256]{1,0:T(8,128)(2,1)S(1)}, bf16[192,256]{1,0:T(8,128)(2,1)S(1)}, u32[]{:S(2)}, u32[]{:S(2)}) collective-permute-start(bf16[192,256]{1,0:T(8,128)(2,1)S(1)} %convolution_convert_fusion.mine_ref), channel_id=1, source_target_pairs={{0,3},{1,0},{2,1},{3,2},{4,7},{5,4},{6,5},{7,6},{8,11},{9,8},{10,9... | collective-permute-start | bytes 294920 | tf_op jit(solution)/shard_map/ppermute | solution.py:181
  33.7 0.7 %collective-permute-start.11 = (bf16[192,256]{1,0:T(8,128)(2,1)S(1)}, bf16[192,256]{1,0:T(8,128)(2,1)S(1)}, u32[]{:S(2)}, u32[]{:S(2)}) collective-permute-start(bf16[192,256]{1,0:T(8,128)(2,1)S(1)} %convolution_convert_fusion.mine_ref), channel_id=1, source_target_pairs={{0,2},{1,3},{2,0},{3,1},{4,6},{5,7},{6,4},{7,5},{8,10},{9,11},{10,... | collective-permute-start | bytes 294920 | tf_op jit(solution)/shard_map/ppermute | solution.py:181
  34.4 2.4 %collective-permute-done.12.rest_2_ = bf16[192,256]{1,0:T(8,128)(2,1)S(1)} collective-permute-done((bf16[192,256]{1,0:T(8,128)(2,1)S(1)}, bf16[192,256]{1,0:T(8,128)(2,1)S(1)}, u32[]{:S(2)}, u32[]{:S(2)}) %collective-permute-start.12) | collective-permute-done | bytes 98336 | tf_op jit(solution)/shard_map/ppermute | solution.py:181
  36.9 6.5 %collective-permute-done.11.rest_1_ = bf16[192,256]{1,0:T(8,128)(2,1)S(1)} collective-permute-done((bf16[192,256]{1,0:T(8,128)(2,1)S(1)}, bf16[192,256]{1,0:T(8,128)(2,1)S(1)}, u32[]{:S(2)}, u32[]{:S(2)}) %collective-permute-start.11) | collective-permute-done | bytes 98336 | tf_op jit(solution)/shard_map/ppermute | solution.py:181
  43.4 0.6 %copy-done.10 = bf16[192,256]{1,0:T(8,128)(2,1)} copy-done((bf16[192,256]{1,0:T(8,128)(2,1)}, bf16[192,256]{1,0:T(8,128)(2,1)S(1)}, u32[]{:S(2)}) %copy-start.10) | copy-done | bytes 98328
  44.1 3.5 %shard_map.87 = (f32[4,192,256]{2,1,0:T(8,128)}, f32[4,192,256]{2,1,0:T(8,128)}) custom-call(s32[12]{0:T(128)} %bitcast.27, s32[12]{0:T(128)} %bitcast.29, s32[1]{0:T(128)} %bitcast.23.info_ref, bf16[12,256,256]{2,1,0:T(8,128)(2,1)} %bitcast.25, bf16[192,256]{1,0:T(8,128)(2,1)} %copy-done.7, bf16[192,256]{1,0:T(8,128)(2,1)} %copy-done.11, ...), custom_call_target="tpu_custom_call" | custom-call | tf_op jit(solution)/shard_map/pallas_call | solution.py:139
  47.6 2.5 %collective-permute-done.13 = f32[4,192,256]{2,1,0:T(8,128)S(1)} collective-permute-done((f32[4,192,256]{2,1,0:T(8,128)}, f32[4,192,256]{2,1,0:T(8,128)S(1)}, u32[]{:S(2)}, u32[]{:S(2)}) %collective-permute-start.13) | collective-permute-done | bytes 786464 | tf_op jit(solution)/shard_map/ppermute | solution.py:185
  50.1 1.3 %fusion.6 = (bf16[4,192,256]{2,1,0:T(8,128)(2,1)S(1)}, f32[4,192,256]{2,1,0:T(8,128)S(1)}) fusion(f32[4,192,256]{2,1,0:T(8,128)} %get-tuple-element.12, f32[4,192,256]{2,1,0:T(8,128)S(1)} %collective-permute-done.13), kind=kLoop, calls=%fused_computation.15 | loop fusion | flops 393216 | bytes 2752512 | tf_op jit(solution)/shard_map/convert.2
  51.5 2.9 %collective-permute-start.16 = (bf16[192,256]{1,0:T(8,128)(2,1)S(1)}, bf16[192,256]{1,0:T(8,128)(2,1)S(1)}, u32[]{:S(2)}, u32[]{:S(2)}) collective-permute-start(bf16[192,256]{1,0:T(8,128)(2,1)S(1)} %get-tuple-element.17), channel_id=1, source_target_pairs={{0,24},{4,28},{8,0},{12,4},{16,8},{20,12},{24,16},{28,20},{1,25},{... | collective-permute-start | bytes 294920 | tf_op jit(solution)/shard_map/ppermute | solution.py:189
  54.4 0.8 %collective-permute-start.15 = (bf16[192,256]{1,0:T(8,128)(2,1)S(1)}, bf16[192,256]{1,0:T(8,128)(2,1)S(1)}, u32[]{:S(2)}, u32[]{:S(2)}) collective-permute-start(bf16[192,256]{1,0:T(8,128)(2,1)S(1)} %get-tuple-element.18), channel_id=1, source_target_pairs={{0,16},{4,20},{8,24},{12,28},{16,0},{20,4},{24,8},{28,12},{1,17},{... | collective-permute-start | bytes 294920 | tf_op jit(solution)/shard_map/ppermute | solution.py:189
  55.2 2.8 %collective-permute-done.14 = bf16[192,256]{1,0:T(8,128)(2,1)S(1)} collective-permute-done((bf16[192,256]{1,0:T(8,128)(2,1)S(1)}, bf16[192,256]{1,0:T(8,128)(2,1)S(1)}, u32[]{:S(2)}, u32[]{:S(2)}) %collective-permute-start.14) | collective-permute-done | bytes 98336 | tf_op jit(solution)/shard_map/ppermute | solution.py:189
  58.0 0.6 %collective-permute-done.16 = bf16[192,256]{1,0:T(8,128)(2,1)S(1)} collective-permute-done((bf16[192,256]{1,0:T(8,128)(2,1)S(1)}, bf16[192,256]{1,0:T(8,128)(2,1)S(1)}, u32[]{:S(2)}, u32[]{:S(2)}) %collective-permute-start.16) | collective-permute-done | bytes 98336 | tf_op jit(solution)/shard_map/ppermute | solution.py:189
  58.6 0.8 %collective-permute-done.15 = bf16[192,256]{1,0:T(8,128)(2,1)S(1)} collective-permute-done((bf16[192,256]{1,0:T(8,128)(2,1)S(1)}, bf16[192,256]{1,0:T(8,128)(2,1)S(1)}, u32[]{:S(2)}, u32[]{:S(2)}) %collective-permute-start.15) | collective-permute-done | bytes 98336 | tf_op jit(solution)/shard_map/ppermute | solution.py:189
  59.4 0.7 %fusion.3 = bf16[192,256]{1,0:T(8,128)(2,1)} fusion(f32[4,192,256]{2,1,0:T(8,128)S(1)} %get-tuple-element.15, bf16[192,256]{1,0:T(8,128)(2,1)S(1)} %collective-permute-done.16, bf16[192,256]{1,0:T(8,128)(2,1)S(1)} %collective-permute-done.15, bf16[192,256]{1,0:T(8,128)(2,1)S(1)} %collective-permute-done.14), kind=kLoop, calls=%fused_computation.5 | loop fusion | flops 344064 | bytes 589824 | tf_op jit(solution)/shard_map/convert_element_type | solution.py:190
  (35 shorter events, 0.3 us)
Async XLA Ops:
  0.6 27.8 %copy-start = (bf16[256,256]{1,0:T(8,128)(2,1)S(1)}, bf16[256,256]{1,0:T(8,128)(2,1)}, u32[]{:S(2)}) copy-start(bf16[256,256]{1,0:T(8,128)(2,1)} %param.12) | copy-start | bytes 393220
  0.6 7.4 %collective-permute-start.2 = (bf16[192,256]{1,0:T(8,128)(2,1)}, bf16[192,256]{1,0:T(8,128)(2,1)S(1)}, u32[]{:S(2)}, u32[]{:S(2)}) collective-permute-start(bf16[192,256]{1,0:T(8,128)(2,1)} %rest_0_.1), channel_id=1, source_target_pairs={{0,24},{4,28},{8,0},{12,4},{16,8},{20,12},{24,16},{28,20},{1,25},{... | collective-permute-start | bytes 294920 | tf_op jit(solution)/shard_map/ppermute | solution.py:173
  4.6 6.6 %collective-permute-start.1 = (bf16[192,256]{1,0:T(8,128)(2,1)}, bf16[192,256]{1,0:T(8,128)(2,1)S(1)}, u32[]{:S(2)}, u32[]{:S(2)}) collective-permute-start(bf16[192,256]{1,0:T(8,128)(2,1)} %rest_0_.1), channel_id=1, source_target_pairs={{0,16},{4,20},{8,24},{12,28},{16,0},{20,4},{24,8},{28,12},{1,17},{... | collective-permute-start | bytes 294920 | tf_op jit(solution)/shard_map/ppermute | solution.py:173
  5.1 6.1 %collective-permute-start = (bf16[192,256]{1,0:T(8,128)(2,1)}, bf16[192,256]{1,0:T(8,128)(2,1)S(1)}, u32[]{:S(2)}, u32[]{:S(2)}) collective-permute-start(bf16[192,256]{1,0:T(8,128)(2,1)} %rest_0_.1), channel_id=1, source_target_pairs={{0,8},{4,12},{8,16},{12,20},{16,24},{20,28},{24,0},{28,4},{1,9},{5... | collective-permute-start | bytes 294920 | tf_op jit(solution)/shard_map/ppermute | solution.py:173
  5.7 6.7 %collective-permute-start.3 = (bf16[192,256]{1,0:T(8,128)(2,1)}, bf16[192,256]{1,0:T(8,128)(2,1)S(1)}, u32[]{:S(2)}, u32[]{:S(2)}) collective-permute-start(bf16[192,256]{1,0:T(8,128)(2,1)} %rest_0_.1), channel_id=1, source_target_pairs={{0,4},{4,0},{8,12},{12,8},{16,20},{20,16},{24,28},{28,24},{1,5},{5... | collective-permute-start | bytes 294920 | tf_op jit(solution)/shard_map/ppermute | solution.py:174
  8.1 4.6 %copy-start.1 = (bf16[192,256]{1,0:T(8,128)(2,1)}, bf16[192,256]{1,0:T(8,128)(2,1)S(1)}, u32[]{:S(2)}) copy-start(bf16[192,256]{1,0:T(8,128)(2,1)S(1)} %collective-permute-done.2.rest_3_) | copy-start | bytes 294916
  8.1 4.4 %collective-permute-start.6 = (bf16[192,256]{1,0:T(8,128)(2,1)S(1)}, bf16[192,256]{1,0:T(8,128)(2,1)S(1)}, u32[]{:S(2)}, u32[]{:S(2)}) collective-permute-start(bf16[192,256]{1,0:T(8,128)(2,1)S(1)} %collective-permute-done.2.rest_3_), channel_id=1, source_target_pairs={{0,4},{4,0},{8,12},{12,8},{16,20},{20,16},{24,28},{28,24},{1,5},{5... | collective-permute-start | bytes 294920 | tf_op jit(solution)/shard_map/ppermute | solution.py:174
  11.3 1.5 %copy-start.2 = (bf16[192,256]{1,0:T(8,128)(2,1)}, bf16[192,256]{1,0:T(8,128)(2,1)S(1)}, u32[]{:S(2)}) copy-start(bf16[192,256]{1,0:T(8,128)(2,1)S(1)} %collective-permute-done.1.rest_2_) | copy-start | bytes 294916
  11.3 1.3 %collective-permute-start.5 = (bf16[192,256]{1,0:T(8,128)(2,1)S(1)}, bf16[192,256]{1,0:T(8,128)(2,1)S(1)}, u32[]{:S(2)}, u32[]{:S(2)}) collective-permute-start(bf16[192,256]{1,0:T(8,128)(2,1)S(1)} %collective-permute-done.1.rest_2_), channel_id=1, source_target_pairs={{0,4},{4,0},{8,12},{12,8},{16,20},{20,16},{24,28},{28,24},{1,5},{5... | collective-permute-start | bytes 294920 | tf_op jit(solution)/shard_map/ppermute | solution.py:174
  11.3 1.5 %copy-start.3 = (bf16[192,256]{1,0:T(8,128)(2,1)}, bf16[192,256]{1,0:T(8,128)(2,1)S(1)}, u32[]{:S(2)}) copy-start(bf16[192,256]{1,0:T(8,128)(2,1)S(1)} %collective-permute-done.rest_1_) | copy-start | bytes 294916
  11.3 1.4 %collective-permute-start.4 = (bf16[192,256]{1,0:T(8,128)(2,1)S(1)}, bf16[192,256]{1,0:T(8,128)(2,1)S(1)}, u32[]{:S(2)}, u32[]{:S(2)}) collective-permute-start(bf16[192,256]{1,0:T(8,128)(2,1)S(1)} %collective-permute-done.rest_1_), channel_id=1, source_target_pairs={{0,4},{4,0},{8,12},{12,8},{16,20},{20,16},{24,28},{28,24},{1,5},{5... | collective-permute-start | bytes 294920 | tf_op jit(solution)/shard_map/ppermute | solution.py:174
  12.4 0.6 %copy-start.4 = (bf16[192,256]{1,0:T(8,128)(2,1)}, bf16[192,256]{1,0:T(8,128)(2,1)S(1)}, u32[]{:S(2)}) copy-start(bf16[192,256]{1,0:T(8,128)(2,1)S(1)} %collective-permute-done.3.rest_4_) | copy-start | bytes 294916
  12.5 0.7 %copy-start.5 = (bf16[192,256]{1,0:T(8,128)(2,1)}, bf16[192,256]{1,0:T(8,128)(2,1)S(1)}, u32[]{:S(2)}) copy-start(bf16[192,256]{1,0:T(8,128)(2,1)S(1)} %collective-permute-done.6.rest_7_) | copy-start | bytes 294916
  12.6 0.6 %copy-start.6 = (bf16[192,256]{1,0:T(8,128)(2,1)}, bf16[192,256]{1,0:T(8,128)(2,1)S(1)}, u32[]{:S(2)}) copy-start(bf16[192,256]{1,0:T(8,128)(2,1)S(1)} %collective-permute-done.5.rest_6_) | copy-start | bytes 294916
  12.7 0.7 %copy-start.8 = (bf16[192,256]{1,0:T(8,128)(2,1)}, bf16[192,256]{1,0:T(8,128)(2,1)S(1)}, u32[]{:S(2)}) copy-start(bf16[192,256]{1,0:T(8,128)(2,1)S(1)} %collective-permute-done.4.rest_5_) | copy-start | bytes 294916
  13.4 16.8 %copy-start.12 = (bf16[192,256]{1,0:T(8,128)(2,1)S(1)}, bf16[192,256]{1,0:T(8,128)(2,1)}, u32[]{:S(2)}) copy-start(bf16[192,256]{1,0:T(8,128)(2,1)} %param.13) | copy-start | bytes 294916
  16.5 7.8 %collective-permute-start.7 = (bf16[192,256]{1,0:T(8,128)(2,1)}, bf16[192,256]{1,0:T(8,128)(2,1)S(1)}, u32[]{:S(2)}, u32[]{:S(2)}) collective-permute-start(bf16[192,256]{1,0:T(8,128)(2,1)} %get-tuple-element.9), channel_id=1, source_target_pairs={{0,1},{1,2},{2,3},{3,0},{4,5},{5,6},{6,7},{7,4},{8,9},{9,10},{10,1... | collective-permute-start | bytes 294920 | tf_op jit(solution)/shard_map/ppermute | solution.py:179
  18.3 10.1 %collective-permute-start.8 = (bf16[192,256]{1,0:T(8,128)(2,1)}, bf16[192,256]{1,0:T(8,128)(2,1)S(1)}, u32[]{:S(2)}, u32[]{:S(2)}) collective-permute-start(bf16[192,256]{1,0:T(8,128)(2,1)} %get-tuple-element.10), channel_id=1, source_target_pairs={{0,2},{1,3},{2,0},{3,1},{4,6},{5,7},{6,4},{7,5},{8,10},{9,11},{10,... | collective-permute-start | bytes 294920 | tf_op jit(solution)/shard_map/ppermute | solution.py:179
  20.5 7.9 %collective-permute-start.9 = (bf16[192,256]{1,0:T(8,128)(2,1)}, bf16[192,256]{1,0:T(8,128)(2,1)S(1)}, u32[]{:S(2)}, u32[]{:S(2)}) collective-permute-start(bf16[192,256]{1,0:T(8,128)(2,1)} %get-tuple-element.11), channel_id=1, source_target_pairs={{0,3},{1,0},{2,1},{3,2},{4,7},{5,4},{6,5},{7,6},{8,11},{9,8},{10,9... | collective-permute-start | bytes 294920 | tf_op jit(solution)/shard_map/ppermute | solution.py:179
  30.4 13.0 %copy-start.7 = (bf16[192,256]{1,0:T(8,128)(2,1)}, bf16[192,256]{1,0:T(8,128)(2,1)S(1)}, u32[]{:S(2)}) copy-start(bf16[192,256]{1,0:T(8,128)(2,1)S(1)} %convolution_convert_fusion.mine_ref) | copy-start | bytes 294916
  30.4 6.5 %collective-permute-start.12 = (bf16[192,256]{1,0:T(8,128)(2,1)S(1)}, bf16[192,256]{1,0:T(8,128)(2,1)S(1)}, u32[]{:S(2)}, u32[]{:S(2)}) collective-permute-start(bf16[192,256]{1,0:T(8,128)(2,1)S(1)} %convolution_convert_fusion.mine_ref), channel_id=1, source_target_pairs={{0,3},{1,0},{2,1},{3,2},{4,7},{5,4},{6,5},{7,6},{8,11},{9,8},{10,9... | collective-permute-start | bytes 294920 | tf_op jit(solution)/shard_map/ppermute | solution.py:181
  33.7 9.7 %collective-permute-start.11 = (bf16[192,256]{1,0:T(8,128)(2,1)S(1)}, bf16[192,256]{1,0:T(8,128)(2,1)S(1)}, u32[]{:S(2)}, u32[]{:S(2)}) collective-permute-start(bf16[192,256]{1,0:T(8,128)(2,1)S(1)} %convolution_convert_fusion.mine_ref), channel_id=1, source_target_pairs={{0,2},{1,3},{2,0},{3,1},{4,6},{5,7},{6,4},{7,5},{8,10},{9,11},{10,... | collective-permute-start | bytes 294920 | tf_op jit(solution)/shard_map/ppermute | solution.py:181
  34.4 8.9 %collective-permute-start.10 = (bf16[192,256]{1,0:T(8,128)(2,1)S(1)}, bf16[192,256]{1,0:T(8,128)(2,1)S(1)}, u32[]{:S(2)}, u32[]{:S(2)}) collective-permute-start(bf16[192,256]{1,0:T(8,128)(2,1)S(1)} %convolution_convert_fusion.mine_ref), channel_id=1, source_target_pairs={{0,1},{1,2},{2,3},{3,0},{4,5},{5,6},{6,7},{7,4},{8,9},{9,10},{10,1... | collective-permute-start | bytes 294920 | tf_op jit(solution)/shard_map/ppermute | solution.py:181
  36.9 6.5 %copy-start.9 = (bf16[192,256]{1,0:T(8,128)(2,1)}, bf16[192,256]{1,0:T(8,128)(2,1)S(1)}, u32[]{:S(2)}) copy-start(bf16[192,256]{1,0:T(8,128)(2,1)S(1)} %collective-permute-done.12.rest_2_) | copy-start | bytes 294916
  43.4 0.6 %copy-start.10 = (bf16[192,256]{1,0:T(8,128)(2,1)}, bf16[192,256]{1,0:T(8,128)(2,1)S(1)}, u32[]{:S(2)}) copy-start(bf16[192,256]{1,0:T(8,128)(2,1)S(1)} %collective-permute-done.11.rest_1_) | copy-start | bytes 294916
  43.4 0.7 %copy-start.11 = (bf16[192,256]{1,0:T(8,128)(2,1)}, bf16[192,256]{1,0:T(8,128)(2,1)S(1)}, u32[]{:S(2)}) copy-start(bf16[192,256]{1,0:T(8,128)(2,1)S(1)} %collective-permute-done.10.rest_0_) | copy-start | bytes 294916
  47.6 2.5 %collective-permute-start.13 = (f32[4,192,256]{2,1,0:T(8,128)}, f32[4,192,256]{2,1,0:T(8,128)S(1)}, u32[]{:S(2)}, u32[]{:S(2)}) collective-permute-start(f32[4,192,256]{2,1,0:T(8,128)} %get-tuple-element.13), channel_id=1, source_target_pairs={{0,4},{4,0},{8,12},{12,8},{16,20},{20,16},{24,28},{28,24},{1,5},{5... | collective-permute-start | bytes 2359304 | tf_op jit(solution)/shard_map/ppermute | solution.py:185
  51.4 6.6 %collective-permute-start.14 = (bf16[192,256]{1,0:T(8,128)(2,1)S(1)}, bf16[192,256]{1,0:T(8,128)(2,1)S(1)}, u32[]{:S(2)}, u32[]{:S(2)}) collective-permute-start(bf16[192,256]{1,0:T(8,128)(2,1)S(1)} %get-tuple-element.16), channel_id=1, source_target_pairs={{0,8},{4,12},{8,16},{12,20},{16,24},{20,28},{24,0},{28,4},{1,9},{5... | collective-permute-start | bytes 294920 | tf_op jit(solution)/shard_map/ppermute | solution.py:189
  51.5 7.2 %collective-permute-start.16 = (bf16[192,256]{1,0:T(8,128)(2,1)S(1)}, bf16[192,256]{1,0:T(8,128)(2,1)S(1)}, u32[]{:S(2)}, u32[]{:S(2)}) collective-permute-start(bf16[192,256]{1,0:T(8,128)(2,1)S(1)} %get-tuple-element.17), channel_id=1, source_target_pairs={{0,24},{4,28},{8,0},{12,4},{16,8},{20,12},{24,16},{28,20},{1,25},{... | collective-permute-start | bytes 294920 | tf_op jit(solution)/shard_map/ppermute | solution.py:189
  54.4 5.0 %collective-permute-start.15 = (bf16[192,256]{1,0:T(8,128)(2,1)S(1)}, bf16[192,256]{1,0:T(8,128)(2,1)S(1)}, u32[]{:S(2)}, u32[]{:S(2)}) collective-permute-start(bf16[192,256]{1,0:T(8,128)(2,1)S(1)} %get-tuple-element.18), channel_id=1, source_target_pairs={{0,16},{4,20},{8,24},{12,28},{16,0},{20,4},{24,8},{28,12},{1,17},{... | collective-permute-start | bytes 294920 | tf_op jit(solution)/shard_map/ppermute | solution.py:189

commit v9 on v7

--- a/solution.py
+++ b/solution.py
@@ -7,19 +7,8 @@
 from jax.experimental.pallas import tpu as pltpu
 from jax.sharding import PartitionSpec as P
 
-
-def silu_slope(mixed):
-    sigma = jax.nn.sigmoid(mixed)
-    return sigma * (1.0 + mixed * (1.0 - sigma))
-
-
-def dense_layer(summed, grad_rows, weight):
-    aggregated = summed.astype(jnp.bfloat16)
-    mixed = jnp.dot(aggregated, weight, preferred_element_type=jnp.float32)
-    activated = jax.nn.silu(mixed).astype(jnp.bfloat16)
-    scaled = (grad_rows.astype(jnp.float32) * silu_slope(mixed)).astype(jnp.bfloat16)
-    pulled = jnp.dot(scaled, weight.T, preferred_element_type=jnp.float32).astype(jnp.bfloat16)
-    return (activated, pulled)
+SMEM = pl.BlockSpec(memory_space=pltpu.SMEM)
+VMEM = pl.BlockSpec(memory_space=pltpu.VMEM)
 
 
 UNROLL = 4
@@ -76,16 +65,26 @@
     split_out(acc_ref, own_ref, send_refs, lax.axis_index("col"))
 
 
-def backward_kernel(n, rows_ref, cols_ref, info_ref, a_ref, mine_ref, *rest):
-    got_refs = rest[: n - 1]
-    near_ref, far_ref, block_ref, acc_ref = rest[n - 1:]
+def backward_kernel(n, rows_ref, cols_ref, info_ref, a_ref, weight_ref, *rest):
+    agg_refs, cot_refs = rest[:n], rest[n : 2 * n]
+    act_ref, near_ref, far_ref, agg_block, cot_block, act_block, block_ref, acc_ref = rest[2 * n :]
     tile = a_ref.shape[1]
-    chunk = mine_ref.shape[0]
+    chunk = agg_refs[0].shape[0]
     me = lax.axis_index("col")
-    block_ref[pl.ds(pl.multiple_of(me * chunk, 16), chunk), :] = mine_ref[...]
-    for shift in range(1, n):
+    for shift in range(n):
         start = pl.multiple_of(((me - shift + n) % n) * chunk, 16)
-        block_ref[pl.ds(start, chunk), :] = got_refs[shift - 1][...]
+        agg_block[pl.ds(start, chunk), :] = agg_refs[shift][...]
+        cot_block[pl.ds(start, chunk), :] = cot_refs[shift][...]
+    weight = weight_ref[...]
+    mixed = jnp.dot(agg_block[...], weight, preferred_element_type=jnp.float32)
+    sigma = jax.nn.sigmoid(mixed)
+    act_block[...] = mixed * sigma
+    act_ref[...] = act_block[pl.ds(pl.multiple_of(me * chunk, 8), chunk), :].astype(act_ref.dtype)
+    slope = sigma * (1.0 + mixed * (1.0 - sigma))
+    scaled = (cot_block[...].astype(jnp.float32) * slope).astype(jnp.bfloat16)
+    block_ref[...] = lax.dot_general(
+        scaled, weight, (((1,), (1,)), ((), ())), preferred_element_type=jnp.float32
+    ).astype(block_ref.dtype)
     acc_ref[...] = jnp.zeros_like(acc_ref)
 
     def product(k):
@@ -107,10 +106,6 @@
         owner = (chip + shift) % chips
         near_ref[shift] = acc_ref[pl.ds(pl.multiple_of((owner * 2 + core) * piece, 8), piece), :]
         far_ref[shift] = acc_ref[pl.ds(pl.multiple_of((owner * 2 + 1 - core) * piece, 8), piece), :]
-
-
-SMEM = pl.BlockSpec(memory_space=pltpu.SMEM)
-VMEM = pl.BlockSpec(memory_space=pltpu.VMEM)
 
 
 def tile_products(rows, cols, info, blocks, near, far, parts):
@@ -130,20 +125,24 @@
     )(rows, cols, info, blocks, near, far)
 
 
-def tile_products_t(rows, cols, info, blocks, mine, got, n_out, out_rows):
+def tile_products_t(rows, cols, info, blocks, weight, aggs, cots, n_out, out_rows):
     chunk = out_rows // n_out
-    width = mine.shape[1]
+    width = aggs[0].shape[1]
+    block_rows = len(aggs) * aggs[0].shape[0]
     stack = jax.ShapeDtypeStruct((n_out // 2, chunk, width), jnp.float32)
     return pl.pallas_call(
-        functools.partial(backward_kernel, len(got) + 1),
-        out_shape=(stack, stack),
-        in_specs=[SMEM, SMEM, SMEM, VMEM, VMEM] + [VMEM] * len(got),
-        out_specs=(VMEM, VMEM),
+        functools.partial(backward_kernel, len(aggs)),
+        out_shape=(jax.ShapeDtypeStruct(aggs[0].shape, jnp.bfloat16), stack, stack),
+        in_specs=[SMEM, SMEM, SMEM, VMEM, VMEM] + [VMEM] * (2 * len(aggs)),
+        out_specs=(VMEM, VMEM, VMEM),
         scratch_shapes=[
-            pltpu.VMEM(((len(got) + 1) * mine.shape[0], width), jnp.bfloat16),
+            pltpu.VMEM((block_rows, width), jnp.bfloat16),
+            pltpu.VMEM((block_rows, width), jnp.bfloat16),
+            pltpu.VMEM((block_rows, width), jnp.float32),
+            pltpu.VMEM((block_rows, width), jnp.bfloat16),
             pltpu.VMEM((out_rows, width), jnp.float32),
         ],
-    )(rows, cols, info, blocks, mine, *got)
+    )(rows, cols, info, blocks, weight, *aggs, *cots)
 
 
 def shifts(axis):
@@ -168,17 +167,20 @@
     n_col = lax.axis_size("col")
     own_rows = features.shape[0]
 
-    near = jnp.stack([features] + [lax.ppermute(features, "row", perm) for perm in chip_shifts(n_row)])
+    cots = [cotangent] + [lax.ppermute(cotangent, "col", perm) for perm in shifts("col")]
+    pieces = [features] + [lax.ppermute(features, "row", perm) for perm in chip_shifts(n_row)]
+    pieces, cots = lax.optimization_barrier((pieces, cots))
+    near = jnp.stack(pieces)
     far = lax.ppermute(near, "row", partner(n_row))
     info = tile_count.reshape(1)
     own, *send = tile_products(row_slots, col_slots, info, blocks, near, far, (n_col, own_rows))
     total = own
     for shift, perm in enumerate(shifts("col")):
         total = total + lax.ppermute(send[shift], "col", perm).astype(jnp.float32)
-    activated, pulled_own = dense_layer(total, cotangent, weight)
-    got = [lax.ppermute(pulled_own, "col", perm) for perm in shifts("col")]
-    near_g, far_g = tile_products_t(
-        row_slots, col_slots, info, blocks, pulled_own, got, n_row, n_row * own_rows
+    aggregated = total.astype(jnp.bfloat16)
+    aggs = [aggregated] + [lax.ppermute(aggregated, "col", perm) for perm in shifts("col")]
+    activated, near_g, far_g = tile_products_t(
+        row_slots, col_slots, info, blocks, weight, aggs, cots, n_row, n_row * own_rows
     )
     chip_sums = near_g + lax.ppermute(far_g, "row", partner(n_row))
     total_g = chip_sums[0]

time: 60.8 us -> 66.5 us (1.094)
  starting transfers between devices: 20.3 us -> 27.6 us
  matrix products: 2.01 us -> 0 us
  waiting for transfers between devices: 25.8 us -> 24.6 us
  other arithmetic: 2.89 us -> 3.91 us
    ppermute x3 -> x6, starting transfers between devices: 4.09 us -> 11.6 us  [the longest x3 6.41 us: on_device(): lax.ppermute(cotangent, 'col', perm)]
    ppermute x3, waiting for transfers between devices: 3.36 us -> 0.01 us  [on_device(): lax.ppermute(features, 'row', perm)]
    ppermute x3 -> x6, waiting for transfers between devices: 9.01 us -> 12 us  [the longest x3 7.96 us: on_device(): lax.ppermute(aggregated, 'col', perm)]
    dot_general x2 -> x0, matrix products: 2.01 us -> none  [the longest x1 1.79 us: dense_layer(): mixed = jnp.dot(aggregated, weight, preferred_element_type=jnp.float32)]
    ppermute x3, waiting for transfers between devices: 5.98 us -> 4.43 us  [on_device(): total = total + lax.ppermute(send[shift], 'col', perm).astype(jnp.float32)]
    ppermute x3, starting transfers between devices: 4.56 us -> 3.29 us  [on_device(): total_g = total_g + lax.ppermute(piece, 'row', perm).astype(jnp.float32)]
    ppermute x3, starting transfers between devices: 5.57 us -> 6.72 us  [on_device(): total = total + lax.ppermute(send[shift], 'col', perm).astype(jnp.float32)]
    convert_element_type x0 -> x1, other arithmetic: none -> 0.98 us  [on_device(): aggregated = total.astype(jnp.bfloat16)]
  transfers between devices with their start and end apart: 14 -> 17, of which waited for: 11 -> 12; matrix products, arithmetic and copies ran while one was open for 0% -> 0% of each run, Pallas kernels for 0% -> 0%
where the time goes in v9:
time: 66.5 us; the launch traced here: 66.4 us
  starting transfers between devices  27.6 us (42%)
  waiting for transfers between devices  24.6 us (37%)
  Pallas kernels  7.4 us (11%)
  other arithmetic  3.91 us (6%)
  local copies, waits for them, and re-layouts  1.44 us (2%)
  between operations  1.4 us (2%)
    ppermute x3, waiting for transfers between devices, on_device(): lax.ppermute(aggregated, 'col', perm)  7.96 us
    ppermute x3, starting transfers between devices, on_device(): total = total + lax.ppermute(send[shift], 'col', perm).astype(jnp.float32)  6.72 us
    ppermute x3, starting transfers between devices, on_device(): lax.ppermute(cotangent, 'col', perm)  6.41 us
    ppermute x3, starting transfers between devices, on_device(): lax.ppermute(features, 'row', perm)  5.99 us
    ppermute x3, starting transfers between devices, on_device(): lax.ppermute(aggregated, 'col', perm)  5.14 us
    ppermute x3, waiting for transfers between devices, on_device(): total_g = total_g + lax.ppermute(piece, 'row', perm).astype(jnp.float32)  4.69 us
    ppermute x3, waiting for transfers between devices, on_device(): total = total + lax.ppermute(send[shift], 'col', perm).astype(jnp.float32)  4.43 us
    pallas_call x1, Pallas kernels, tile_products_t(): pl.pallas_call(functools.partial(backward_kernel, len(aggs)), out_shape=(...  4.32 us
  transfers between devices with their start and end apart: 17, of which 12 were waited for; matrix products, arithmetic and copies ran while one was open for 0% of the time, Pallas kernels for 0%

profile of v9, /device:TPU:0, one launch (start us, length us, event | category | flops | bytes accessed | tf_op | source)
XLA Modules:
  0.0 66.4 jit_solution(2864848104138829522)
XLA Ops:
  0.6 3.1 %collective-permute-start.1 = (bf16[192,256]{1,0:T(8,128)(2,1)}, bf16[192,256]{1,0:T(8,128)(2,1)S(1)}, u32[]{:S(2)}, u32[]{:S(2)}) collective-permute-start(bf16[192,256]{1,0:T(8,128)(2,1)} %param.7), channel_id=1, source_target_pairs={{0,16},{4,20},{8,24},{12,28},{16,0},{20,4},{24,8},{28,12},{1,17},{... | collective-permute-start | bytes 294920 | tf_op jit(solution)/shard_map/ppermute | solution.py:171
  3.7 1.5 %collective-permute-start = (bf16[192,256]{1,0:T(8,128)(2,1)}, bf16[192,256]{1,0:T(8,128)(2,1)S(1)}, u32[]{:S(2)}, u32[]{:S(2)}) collective-permute-start(bf16[192,256]{1,0:T(8,128)(2,1)} %param.7), channel_id=1, source_target_pairs={{0,8},{4,12},{8,16},{12,20},{16,24},{20,28},{24,0},{28,4},{1,9},{5... | collective-permute-start | bytes 294920 | tf_op jit(solution)/shard_map/ppermute | solution.py:171
  5.2 1.4 %collective-permute-start.2 = (bf16[192,256]{1,0:T(8,128)(2,1)}, bf16[192,256]{1,0:T(8,128)(2,1)S(1)}, u32[]{:S(2)}, u32[]{:S(2)}) collective-permute-start(bf16[192,256]{1,0:T(8,128)(2,1)} %param.7), channel_id=1, source_target_pairs={{0,24},{4,28},{8,0},{12,4},{16,8},{20,12},{24,16},{28,20},{1,25},{... | collective-permute-start | bytes 294920 | tf_op jit(solution)/shard_map/ppermute | solution.py:171
  6.6 2.6 %collective-permute-start.4 = (bf16[192,256]{1,0:T(8,128)(2,1)}, bf16[192,256]{1,0:T(8,128)(2,1)S(1)}, u32[]{:S(2)}, u32[]{:S(2)}) collective-permute-start(bf16[192,256]{1,0:T(8,128)(2,1)} %rest_4_), channel_id=1, source_target_pairs={{0,2},{1,3},{2,0},{3,1},{4,6},{5,7},{6,4},{7,5},{8,10},{9,11},{10,... | collective-permute-start | bytes 294920 | tf_op jit(solution)/shard_map/ppermute | solution.py:170
  9.2 1.6 %collective-permute-start.3 = (bf16[192,256]{1,0:T(8,128)(2,1)}, bf16[192,256]{1,0:T(8,128)(2,1)S(1)}, u32[]{:S(2)}, u32[]{:S(2)}) collective-permute-start(bf16[192,256]{1,0:T(8,128)(2,1)} %rest_4_), channel_id=1, source_target_pairs={{0,1},{1,2},{2,3},{3,0},{4,5},{5,6},{6,7},{7,4},{8,9},{9,10},{10,1... | collective-permute-start | bytes 294920 | tf_op jit(solution)/shard_map/ppermute | solution.py:170
  10.8 2.2 %collective-permute-start.5 = (bf16[192,256]{1,0:T(8,128)(2,1)}, bf16[192,256]{1,0:T(8,128)(2,1)S(1)}, u32[]{:S(2)}, u32[]{:S(2)}) collective-permute-start(bf16[192,256]{1,0:T(8,128)(2,1)} %rest_4_), channel_id=1, source_target_pairs={{0,3},{1,0},{2,1},{3,2},{4,7},{5,4},{6,5},{7,6},{8,11},{9,8},{10,9... | collective-permute-start | bytes 294920 | tf_op jit(solution)/shard_map/ppermute | solution.py:170
  13.0 2.8 %collective-permute-done.4.rest_6_ = bf16[192,256]{1,0:T(8,128)(2,1)S(1)} collective-permute-done((bf16[192,256]{1,0:T(8,128)(2,1)}, bf16[192,256]{1,0:T(8,128)(2,1)S(1)}, u32[]{:S(2)}, u32[]{:S(2)}) %collective-permute-start.4) | collective-permute-done | bytes 98336 | tf_op jit(solution)/shard_map/ppermute | solution.py:170
  15.8 0.7 %collective-permute-done.3.rest_5_ = bf16[192,256]{1,0:T(8,128)(2,1)S(1)} collective-permute-done((bf16[192,256]{1,0:T(8,128)(2,1)}, bf16[192,256]{1,0:T(8,128)(2,1)S(1)}, u32[]{:S(2)}, u32[]{:S(2)}) %collective-permute-start.3) | collective-permute-done | bytes 98336 | tf_op jit(solution)/shard_map/ppermute | solution.py:170
  16.6 0.5 collective-permute-done.5.rest_7_
  17.0 1.0 %pad_maximum_fusion.near_ref = bf16[4,192,256]{2,1,0:T(8,128)(2,1)S(1)} fusion(bf16[1,192,256]{2,1,0:T(8,128)(2,1)S(1)} %bitcast.31, bf16[1,192,256]{2,1,0:T(8,128)(2,1)S(1)} %bitcast.29, bf16[1,192,256]{2,1,0:T(8,128)(2,1)S(1)} %bitcast.30, bf16[1,192,256]{2,1,0:T(8,128)(2,1)} %bitcast.28), kind=kLoop, calls=%fused_computation | loop fusion | flops 589824 | bytes 786432 | tf_op jit(solution)/shard_map/stack | solution.py:173
  18.8 1.0 %collective-permute-done.6.far_ref = bf16[4,192,256]{2,1,0:T(8,128)(2,1)S(1)} collective-permute-done((bf16[4,192,256]{2,1,0:T(8,128)(2,1)S(1)}, bf16[4,192,256]{2,1,0:T(8,128)(2,1)S(1)}, u32[]{:S(2)}, u32[]{:S(2)}) %collective-permute-start.6) | collective-permute-done | bytes 393248 | tf_op jit(solution)/shard_map/ppermute | solution.py:174
  19.8 0.7 %copy-done.2 = bf16[4,192,256]{2,1,0:T(8,128)(2,1)} copy-done((bf16[4,192,256]{2,1,0:T(8,128)(2,1)}, bf16[4,192,256]{2,1,0:T(8,128)(2,1)S(1)}, u32[]{:S(2)}) %copy-start.2) | copy-done | bytes 393240
  20.6 3.1 %shard_map.86 = (f32[192,256]{1,0:T(8,128)}, bf16[192,256]{1,0:T(8,128)(2,1)}, bf16[192,256]{1,0:T(8,128)(2,1)}, bf16[192,256]{1,0:T(8,128)(2,1)}) custom-call(s32[12]{0:T(128)} %bitcast.32, s32[12]{0:T(128)} %bitcast.34, s32[1]{0:T(128)} %bitcast.24.info_ref, bf16[12,256,256]{2,1,0:T(8,128)(2,1)} %bitcast.26, bf16[4,192,256]{2,1,0:T(8,128)(2,1)} %copy-done, ...), custom_call_target="tpu_custom_call" | custom-call | tf_op jit(solution)/shard_map/pallas_call | solution.py:115
  23.7 1.5 %collective-permute-start.7 = (bf16[192,256]{1,0:T(8,128)(2,1)}, bf16[192,256]{1,0:T(8,128)(2,1)S(1)}, u32[]{:S(2)}, u32[]{:S(2)}) collective-permute-start(bf16[192,256]{1,0:T(8,128)(2,1)} %get-tuple-element.22), channel_id=1, source_target_pairs={{0,1},{1,2},{2,3},{3,0},{4,5},{5,6},{6,7},{7,4},{8,9},{9,10},{10,1... | collective-permute-start | bytes 294920 | tf_op jit(solution)/shard_map/ppermute | solution.py:179
  25.2 2.4 %collective-permute-start.8 = (bf16[192,256]{1,0:T(8,128)(2,1)}, bf16[192,256]{1,0:T(8,128)(2,1)S(1)}, u32[]{:S(2)}, u32[]{:S(2)}) collective-permute-start(bf16[192,256]{1,0:T(8,128)(2,1)} %get-tuple-element.23), channel_id=1, source_target_pairs={{0,2},{1,3},{2,0},{3,1},{4,6},{5,7},{6,4},{7,5},{8,10},{9,11},{10,... | collective-permute-start | bytes 294920 | tf_op jit(solution)/shard_map/ppermute | solution.py:179
  27.6 2.8 %collective-permute-start.9 = (bf16[192,256]{1,0:T(8,128)(2,1)}, bf16[192,256]{1,0:T(8,128)(2,1)S(1)}, u32[]{:S(2)}, u32[]{:S(2)}) collective-permute-start(bf16[192,256]{1,0:T(8,128)(2,1)} %get-tuple-element.24), channel_id=1, source_target_pairs={{0,3},{1,0},{2,1},{3,2},{4,7},{5,4},{6,5},{7,6},{8,11},{9,8},{10,9... | collective-permute-start | bytes 294920 | tf_op jit(solution)/shard_map/ppermute | solution.py:179
  30.7 4.1 %collective-permute-done.8 = bf16[192,256]{1,0:T(8,128)(2,1)S(1)} collective-permute-done((bf16[192,256]{1,0:T(8,128)(2,1)}, bf16[192,256]{1,0:T(8,128)(2,1)S(1)}, u32[]{:S(2)}, u32[]{:S(2)}) %collective-permute-start.8) | collective-permute-done | bytes 98336 | tf_op jit(solution)/shard_map/ppermute | solution.py:179
  34.8 1.0 %add_convert_fusion.rest_0_ = bf16[192,256]{1,0:T(8,128)(2,1)S(1)} fusion(bf16[192,256]{1,0:T(8,128)(2,1)S(1)} %collective-permute-done.9, bf16[192,256]{1,0:T(8,128)(2,1)S(1)} %collective-permute-done.8, f32[192,256]{1,0:T(8,128)} %get-tuple-element.21, bf16[192,256]{1,0:T(8,128)(2,1)S(1)} %collective-permute-done.7), kind=kLoop, calls=%fused_computation.6 | loop fusion | flops 344064 | bytes 589824 | tf_op jit(solution)/shard_map/convert_element_type | solution.py:180
  35.8 4.5 %collective-permute-start.12 = (bf16[192,256]{1,0:T(8,128)(2,1)S(1)}, bf16[192,256]{1,0:T(8,128)(2,1)S(1)}, u32[]{:S(2)}, u32[]{:S(2)}) collective-permute-start(bf16[192,256]{1,0:T(8,128)(2,1)S(1)} %add_convert_fusion.rest_0_), channel_id=1, source_target_pairs={{0,3},{1,0},{2,1},{3,2},{4,7},{5,4},{6,5},{7,6},{8,11},{9,8},{10,9... | collective-permute-start | bytes 294920 | tf_op jit(solution)/shard_map/ppermute | solution.py:181
  40.3 0.6 collective-permute-start.10
  41.0 2.4 %collective-permute-done.12.rest_3_ = bf16[192,256]{1,0:T(8,128)(2,1)S(1)} collective-permute-done((bf16[192,256]{1,0:T(8,128)(2,1)S(1)}, bf16[192,256]{1,0:T(8,128)(2,1)S(1)}, u32[]{:S(2)}, u32[]{:S(2)}) %collective-permute-start.12) | collective-permute-done | bytes 98336 | tf_op jit(solution)/shard_map/ppermute | solution.py:181
  43.3 5.6 %collective-permute-done.11.rest_2_ = bf16[192,256]{1,0:T(8,128)(2,1)S(1)} collective-permute-done((bf16[192,256]{1,0:T(8,128)(2,1)S(1)}, bf16[192,256]{1,0:T(8,128)(2,1)S(1)}, u32[]{:S(2)}, u32[]{:S(2)}) %collective-permute-start.11) | collective-permute-done | bytes 98336 | tf_op jit(solution)/shard_map/ppermute | solution.py:181
  48.9 0.6 copy-done.7
  49.6 4.3 %shard_map.87 = (bf16[192,256]{1,0:T(8,128)(2,1)}, f32[4,192,256]{2,1,0:T(8,128)}, f32[4,192,256]{2,1,0:T(8,128)}) custom-call(s32[12]{0:T(128)} %bitcast.33, s32[12]{0:T(128)} %bitcast.35, s32[1]{0:T(128)} %bitcast.25.info_ref, bf16[12,256,256]{2,1,0:T(8,128)(2,1)} %bitcast.27, bf16[256,256]{1,0:T(8,128)(2,1)} %weight_ref.1, bf16[192,256]{1,0:T(8,128)(2,1)} %copy-done.1, ...), custom_call_target="tpu_custom_call" | custom-call | tf_op jit(solution)/shard_map/pallas_call | solution.py:133
  53.9 2.5 %collective-permute-done.13 = f32[4,192,256]{2,1,0:T(8,128)S(1)} collective-permute-done((f32[4,192,256]{2,1,0:T(8,128)}, f32[4,192,256]{2,1,0:T(8,128)S(1)}, u32[]{:S(2)}, u32[]{:S(2)}) %collective-permute-start.13) | collective-permute-done | bytes 786464 | tf_op jit(solution)/shard_map/ppermute | solution.py:185
  56.4 1.3 %fusion.4 = (bf16[4,192,256]{2,1,0:T(8,128)(2,1)S(1)}, f32[4,192,256]{2,1,0:T(8,128)S(1)}) fusion(f32[4,192,256]{2,1,0:T(8,128)} %get-tuple-element.30, f32[4,192,256]{2,1,0:T(8,128)S(1)} %collective-permute-done.13), kind=kLoop, calls=%fused_computation.10 | loop fusion | flops 393216 | bytes 2752512 | tf_op jit(solution)/shard_map/convert.2
  57.7 1.3 %collective-permute-start.14 = (bf16[192,256]{1,0:T(8,128)(2,1)S(1)}, bf16[192,256]{1,0:T(8,128)(2,1)S(1)}, u32[]{:S(2)}, u32[]{:S(2)}) collective-permute-start(bf16[192,256]{1,0:T(8,128)(2,1)S(1)} %get-tuple-element.34), channel_id=1, source_target_pairs={{0,8},{4,12},{8,16},{12,20},{16,24},{20,28},{24,0},{28,4},{1,9},{5... | collective-permute-start | bytes 294920 | tf_op jit(solution)/shard_map/ppermute | solution.py:189
  59.0 1.7 %collective-permute-start.16 = (bf16[192,256]{1,0:T(8,128)(2,1)S(1)}, bf16[192,256]{1,0:T(8,128)(2,1)S(1)}, u32[]{:S(2)}, u32[]{:S(2)}) collective-permute-start(bf16[192,256]{1,0:T(8,128)(2,1)S(1)} %get-tuple-element.35), channel_id=1, source_target_pairs={{0,24},{4,28},{8,0},{12,4},{16,8},{20,12},{24,16},{28,20},{1,25},{... | collective-permute-start | bytes 294920 | tf_op jit(solution)/shard_map/ppermute | solution.py:189
  60.7 0.3 collective-permute-start.15
  61.0 3.3 %collective-permute-done.14 = bf16[192,256]{1,0:T(8,128)(2,1)S(1)} collective-permute-done((bf16[192,256]{1,0:T(8,128)(2,1)S(1)}, bf16[192,256]{1,0:T(8,128)(2,1)S(1)}, u32[]{:S(2)}, u32[]{:S(2)}) %collective-permute-start.14) | collective-permute-done | bytes 98336 | tf_op jit(solution)/shard_map/ppermute | solution.py:189
  64.5 1.2 %collective-permute-done.15 = bf16[192,256]{1,0:T(8,128)(2,1)S(1)} collective-permute-done((bf16[192,256]{1,0:T(8,128)(2,1)S(1)}, bf16[192,256]{1,0:T(8,128)(2,1)S(1)}, u32[]{:S(2)}, u32[]{:S(2)}) %collective-permute-start.15) | collective-permute-done | bytes 98336 | tf_op jit(solution)/shard_map/ppermute | solution.py:189
  65.7 0.7 %fusion.3 = bf16[192,256]{1,0:T(8,128)(2,1)} fusion(f32[4,192,256]{2,1,0:T(8,128)S(1)} %get-tuple-element.33, bf16[192,256]{1,0:T(8,128)(2,1)S(1)} %collective-permute-done.16, bf16[192,256]{1,0:T(8,128)(2,1)S(1)} %collective-permute-done.15, bf16[192,256]{1,0:T(8,128)(2,1)S(1)} %collective-permute-done.14), kind=kLoop, calls=%fused_computation.5 | loop fusion | flops 344064 | bytes 589824 | tf_op jit(solution)/shard_map/convert_element_type | solution.py:190
  (27 shorter events, 0.7 us)
Async XLA Ops:
  0.6 10.2 %collective-permute-start.1 = (bf16[192,256]{1,0:T(8,128)(2,1)}, bf16[192,256]{1,0:T(8,128)(2,1)S(1)}, u32[]{:S(2)}, u32[]{:S(2)}) collective-permute-start(bf16[192,256]{1,0:T(8,128)(2,1)} %param.7), channel_id=1, source_target_pairs={{0,16},{4,20},{8,24},{12,28},{16,0},{20,4},{24,8},{28,12},{1,17},{... | collective-permute-start | bytes 294920 | tf_op jit(solution)/shard_map/ppermute | solution.py:171
  3.7 9.3 %collective-permute-start = (bf16[192,256]{1,0:T(8,128)(2,1)}, bf16[192,256]{1,0:T(8,128)(2,1)S(1)}, u32[]{:S(2)}, u32[]{:S(2)}) collective-permute-start(bf16[192,256]{1,0:T(8,128)(2,1)} %param.7), channel_id=1, source_target_pairs={{0,8},{4,12},{8,16},{12,20},{16,24},{20,28},{24,0},{28,4},{1,9},{5... | collective-permute-start | bytes 294920 | tf_op jit(solution)/shard_map/ppermute | solution.py:171
  5.2 7.9 %collective-permute-start.2 = (bf16[192,256]{1,0:T(8,128)(2,1)}, bf16[192,256]{1,0:T(8,128)(2,1)S(1)}, u32[]{:S(2)}, u32[]{:S(2)}) collective-permute-start(bf16[192,256]{1,0:T(8,128)(2,1)} %param.7), channel_id=1, source_target_pairs={{0,24},{4,28},{8,0},{12,4},{16,8},{20,12},{24,16},{28,20},{1,25},{... | collective-permute-start | bytes 294920 | tf_op jit(solution)/shard_map/ppermute | solution.py:171
  6.6 9.2 %collective-permute-start.4 = (bf16[192,256]{1,0:T(8,128)(2,1)}, bf16[192,256]{1,0:T(8,128)(2,1)S(1)}, u32[]{:S(2)}, u32[]{:S(2)}) collective-permute-start(bf16[192,256]{1,0:T(8,128)(2,1)} %rest_4_), channel_id=1, source_target_pairs={{0,2},{1,3},{2,0},{3,1},{4,6},{5,7},{6,4},{7,5},{8,10},{9,11},{10,... | collective-permute-start | bytes 294920 | tf_op jit(solution)/shard_map/ppermute | solution.py:170
  9.2 7.4 %collective-permute-start.3 = (bf16[192,256]{1,0:T(8,128)(2,1)}, bf16[192,256]{1,0:T(8,128)(2,1)S(1)}, u32[]{:S(2)}, u32[]{:S(2)}) collective-permute-start(bf16[192,256]{1,0:T(8,128)(2,1)} %rest_4_), channel_id=1, source_target_pairs={{0,1},{1,2},{2,3},{3,0},{4,5},{5,6},{6,7},{7,4},{8,9},{9,10},{10,1... | collective-permute-start | bytes 294920 | tf_op jit(solution)/shard_map/ppermute | solution.py:170
  10.8 6.3 %collective-permute-start.5 = (bf16[192,256]{1,0:T(8,128)(2,1)}, bf16[192,256]{1,0:T(8,128)(2,1)S(1)}, u32[]{:S(2)}, u32[]{:S(2)}) collective-permute-start(bf16[192,256]{1,0:T(8,128)(2,1)} %rest_4_), channel_id=1, source_target_pairs={{0,3},{1,0},{2,1},{3,2},{4,7},{5,4},{6,5},{7,6},{8,11},{9,8},{10,9... | collective-permute-start | bytes 294920 | tf_op jit(solution)/shard_map/ppermute | solution.py:170
  15.8 7.8 %copy-start.3 = (bf16[192,256]{1,0:T(8,128)(2,1)}, bf16[192,256]{1,0:T(8,128)(2,1)S(1)}, u32[]{:S(2)}) copy-start(bf16[192,256]{1,0:T(8,128)(2,1)S(1)} %collective-permute-done.4.rest_6_) | copy-start | bytes 294916
  16.6 7.1 %copy-start.4 = (bf16[192,256]{1,0:T(8,128)(2,1)}, bf16[192,256]{1,0:T(8,128)(2,1)S(1)}, u32[]{:S(2)}) copy-start(bf16[192,256]{1,0:T(8,128)(2,1)S(1)} %collective-permute-done.3.rest_5_) | copy-start | bytes 294916
  17.0 6.6 %copy-start.5 = (bf16[192,256]{1,0:T(8,128)(2,1)}, bf16[192,256]{1,0:T(8,128)(2,1)S(1)}, u32[]{:S(2)}) copy-start(bf16[192,256]{1,0:T(8,128)(2,1)S(1)} %collective-permute-done.5.rest_7_) | copy-start | bytes 294916
  18.0 1.8 %copy-start = (bf16[4,192,256]{2,1,0:T(8,128)(2,1)}, bf16[4,192,256]{2,1,0:T(8,128)(2,1)S(1)}, u32[]{:S(2)}) copy-start(bf16[4,192,256]{2,1,0:T(8,128)(2,1)S(1)} %pad_maximum_fusion.near_ref) | copy-start | bytes 1179652
  18.0 1.8 %collective-permute-start.6 = (bf16[4,192,256]{2,1,0:T(8,128)(2,1)S(1)}, bf16[4,192,256]{2,1,0:T(8,128)(2,1)S(1)}, u32[]{:S(2)}, u32[]{:S(2)}) collective-permute-start(bf16[4,192,256]{2,1,0:T(8,128)(2,1)S(1)} %pad_maximum_fusion.near_ref), channel_id=1, source_target_pairs={{0,4},{4,0},{8,12},{12,8},{16,20},{20,16},{24,28},{28,24},{1,5},{5... | collective-permute-start | bytes 1179656 | tf_op jit(solution)/shard_map/ppermute | solution.py:174
  19.8 0.8 %copy-start.2 = (bf16[4,192,256]{2,1,0:T(8,128)(2,1)}, bf16[4,192,256]{2,1,0:T(8,128)(2,1)S(1)}, u32[]{:S(2)}) copy-start(bf16[4,192,256]{2,1,0:T(8,128)(2,1)S(1)} %collective-permute-done.6.far_ref) | copy-start | bytes 1179652
  23.7 7.0 %collective-permute-start.7 = (bf16[192,256]{1,0:T(8,128)(2,1)}, bf16[192,256]{1,0:T(8,128)(2,1)S(1)}, u32[]{:S(2)}, u32[]{:S(2)}) collective-permute-start(bf16[192,256]{1,0:T(8,128)(2,1)} %get-tuple-element.22), channel_id=1, source_target_pairs={{0,1},{1,2},{2,3},{3,0},{4,5},{5,6},{6,7},{7,4},{8,9},{9,10},{10,1... | collective-permute-start | bytes 294920 | tf_op jit(solution)/shard_map/ppermute | solution.py:179
  25.2 9.6 %collective-permute-start.8 = (bf16[192,256]{1,0:T(8,128)(2,1)}, bf16[192,256]{1,0:T(8,128)(2,1)S(1)}, u32[]{:S(2)}, u32[]{:S(2)}) collective-permute-start(bf16[192,256]{1,0:T(8,128)(2,1)} %get-tuple-element.23), channel_id=1, source_target_pairs={{0,2},{1,3},{2,0},{3,1},{4,6},{5,7},{6,4},{7,5},{8,10},{9,11},{10,... | collective-permute-start | bytes 294920 | tf_op jit(solution)/shard_map/ppermute | solution.py:179
  27.6 7.3 %collective-permute-start.9 = (bf16[192,256]{1,0:T(8,128)(2,1)}, bf16[192,256]{1,0:T(8,128)(2,1)S(1)}, u32[]{:S(2)}, u32[]{:S(2)}) collective-permute-start(bf16[192,256]{1,0:T(8,128)(2,1)} %get-tuple-element.24), channel_id=1, source_target_pairs={{0,3},{1,0},{2,1},{3,2},{4,7},{5,4},{6,5},{7,6},{8,11},{9,8},{10,9... | collective-permute-start | bytes 294920 | tf_op jit(solution)/shard_map/ppermute | solution.py:179
  35.8 13.1 %copy-start.1 = (bf16[192,256]{1,0:T(8,128)(2,1)}, bf16[192,256]{1,0:T(8,128)(2,1)S(1)}, u32[]{:S(2)}) copy-start(bf16[192,256]{1,0:T(8,128)(2,1)S(1)} %add_convert_fusion.rest_0_) | copy-start | bytes 294916
  35.8 7.5 %collective-permute-start.12 = (bf16[192,256]{1,0:T(8,128)(2,1)S(1)}, bf16[192,256]{1,0:T(8,128)(2,1)S(1)}, u32[]{:S(2)}, u32[]{:S(2)}) collective-permute-start(bf16[192,256]{1,0:T(8,128)(2,1)S(1)} %add_convert_fusion.rest_0_), channel_id=1, source_target_pairs={{0,3},{1,0},{2,1},{3,2},{4,7},{5,4},{6,5},{7,6},{8,11},{9,8},{10,9... | collective-permute-start | bytes 294920 | tf_op jit(solution)/shard_map/ppermute | solution.py:181
  40.3 8.6 %collective-permute-start.11 = (bf16[192,256]{1,0:T(8,128)(2,1)S(1)}, bf16[192,256]{1,0:T(8,128)(2,1)S(1)}, u32[]{:S(2)}, u32[]{:S(2)}) collective-permute-start(bf16[192,256]{1,0:T(8,128)(2,1)S(1)} %add_convert_fusion.rest_0_), channel_id=1, source_target_pairs={{0,2},{1,3},{2,0},{3,1},{4,6},{5,7},{6,4},{7,5},{8,10},{9,11},{10,... | collective-permute-start | bytes 294920 | tf_op jit(solution)/shard_map/ppermute | solution.py:181
  40.3 8.6 %collective-permute-start.10 = (bf16[192,256]{1,0:T(8,128)(2,1)S(1)}, bf16[192,256]{1,0:T(8,128)(2,1)S(1)}, u32[]{:S(2)}, u32[]{:S(2)}) collective-permute-start(bf16[192,256]{1,0:T(8,128)(2,1)S(1)} %add_convert_fusion.rest_0_), channel_id=1, source_target_pairs={{0,1},{1,2},{2,3},{3,0},{4,5},{5,6},{6,7},{7,4},{8,9},{9,10},{10,1... | collective-permute-start | bytes 294920 | tf_op jit(solution)/shard_map/ppermute | solution.py:181
  43.3 5.6 %copy-start.6 = (bf16[192,256]{1,0:T(8,128)(2,1)}, bf16[192,256]{1,0:T(8,128)(2,1)S(1)}, u32[]{:S(2)}) copy-start(bf16[192,256]{1,0:T(8,128)(2,1)S(1)} %collective-permute-done.12.rest_3_) | copy-start | bytes 294916
  48.9 0.6 copy-start.7
  48.9 0.7 copy-start.8
  53.9 2.5 %collective-permute-start.13 = (f32[4,192,256]{2,1,0:T(8,128)}, f32[4,192,256]{2,1,0:T(8,128)S(1)}, u32[]{:S(2)}, u32[]{:S(2)}) collective-permute-start(f32[4,192,256]{2,1,0:T(8,128)} %get-tuple-element.31), channel_id=1, source_target_pairs={{0,4},{4,0},{8,12},{12,8},{16,20},{20,16},{24,28},{28,24},{1,5},{5... | collective-permute-start | bytes 2359304 | tf_op jit(solution)/shard_map/ppermute | solution.py:185
  57.7 6.6 %collective-permute-start.14 = (bf16[192,256]{1,0:T(8,128)(2,1)S(1)}, bf16[192,256]{1,0:T(8,128)(2,1)S(1)}, u32[]{:S(2)}, u32[]{:S(2)}) collective-permute-start(bf16[192,256]{1,0:T(8,128)(2,1)S(1)} %get-tuple-element.34), channel_id=1, source_target_pairs={{0,8},{4,12},{8,16},{12,20},{16,24},{20,28},{24,0},{28,4},{1,9},{5... | collective-permute-start | bytes 294920 | tf_op jit(solution)/shard_map/ppermute | solution.py:189
  59.0 5.5 %collective-permute-start.16 = (bf16[192,256]{1,0:T(8,128)(2,1)S(1)}, bf16[192,256]{1,0:T(8,128)(2,1)S(1)}, u32[]{:S(2)}, u32[]{:S(2)}) collective-permute-start(bf16[192,256]{1,0:T(8,128)(2,1)S(1)} %get-tuple-element.35), channel_id=1, source_target_pairs={{0,24},{4,28},{8,0},{12,4},{16,8},{20,12},{24,16},{28,20},{1,25},{... | collective-permute-start | bytes 294920 | tf_op jit(solution)/shard_map/ppermute | solution.py:189
  60.7 5.0 %collective-permute-start.15 = (bf16[192,256]{1,0:T(8,128)(2,1)S(1)}, bf16[192,256]{1,0:T(8,128)(2,1)S(1)}, u32[]{:S(2)}, u32[]{:S(2)}) collective-permute-start(bf16[192,256]{1,0:T(8,128)(2,1)S(1)} %get-tuple-element.36), channel_id=1, source_target_pairs={{0,16},{4,20},{8,24},{12,28},{16,0},{20,4},{24,8},{28,12},{1,17},{... | collective-permute-start | bytes 294920 | tf_op jit(solution)/shard_map/ppermute | solution.py:189

commit v10 on v7

--- a/solution.py
+++ b/solution.py
@@ -8,18 +8,31 @@
 from jax.sharding import PartitionSpec as P
 
 
-def silu_slope(mixed):
+def dense_kernel(n, own_ref, *rest):
+    got_refs = rest[: n - 1]
+    grad_ref, weight_ref, act_ref, pulled_ref = rest[n - 1:]
+    total = own_ref[...]
+    for got in got_refs:
+        total = total + got[...].astype(jnp.float32)
+    weight = weight_ref[...]
+    mixed = jnp.dot(total.astype(jnp.bfloat16), weight, preferred_element_type=jnp.float32)
     sigma = jax.nn.sigmoid(mixed)
-    return sigma * (1.0 + mixed * (1.0 - sigma))
-
-
-def dense_layer(summed, grad_rows, weight):
-    aggregated = summed.astype(jnp.bfloat16)
-    mixed = jnp.dot(aggregated, weight, preferred_element_type=jnp.float32)
-    activated = jax.nn.silu(mixed).astype(jnp.bfloat16)
-    scaled = (grad_rows.astype(jnp.float32) * silu_slope(mixed)).astype(jnp.bfloat16)
-    pulled = jnp.dot(scaled, weight.T, preferred_element_type=jnp.float32).astype(jnp.bfloat16)
-    return (activated, pulled)
+    act_ref[...] = (mixed * sigma).astype(act_ref.dtype)
+    slope = sigma * (1.0 + mixed * (1.0 - sigma))
+    scaled = (grad_ref[...].astype(jnp.float32) * slope).astype(jnp.bfloat16)
+    pulled_ref[...] = lax.dot_general(
+        scaled, weight, (((1,), (1,)), ((), ())), preferred_element_type=jnp.float32
+    ).astype(pulled_ref.dtype)
+
+
+def dense_layer_kernel(own, got, grad_rows, weight):
+    shape = jax.ShapeDtypeStruct(own.shape, jnp.bfloat16)
+    return pl.pallas_call(
+        functools.partial(dense_kernel, len(got) + 1),
+        out_shape=(shape, shape),
+        in_specs=[VMEM] * (len(got) + 3),
+        out_specs=(VMEM, VMEM),
+    )(own, *got, grad_rows, weight)
 
 
 UNROLL = 4
@@ -172,10 +185,8 @@
     far = lax.ppermute(near, "row", partner(n_row))
     info = tile_count.reshape(1)
     own, *send = tile_products(row_slots, col_slots, info, blocks, near, far, (n_col, own_rows))
-    total = own
-    for shift, perm in enumerate(shifts("col")):
-        total = total + lax.ppermute(send[shift], "col", perm).astype(jnp.float32)
-    activated, pulled_own = dense_layer(total, cotangent, weight)
+    got_f = [lax.ppermute(send[shift], "col", perm) for shift, perm in enumerate(shifts("col"))]
+    activated, pulled_own = dense_layer_kernel(own, got_f, cotangent, weight)
     got = [lax.ppermute(pulled_own, "col", perm) for perm in shifts("col")]
     near_g, far_g = tile_products_t(
         row_slots, col_slots, info, blocks, pulled_own, got, n_row, n_row * own_rows

time: 60.8 us -> 61.4 us (level)
  Pallas kernels: 6.78 us -> 8.93 us
  matrix products: 2.01 us -> 0 us
  local copies, waits for them, and re-layouts: 1.45 us -> 2.1 us
    pallas_call x0 -> x1, Pallas kernels: none -> 2.17 us  [dense_layer_kernel(): pl.pallas_call(functools.partial(dense_kernel, len(got) + 1), out_shape=(...]
    dot_general x2 -> x0, matrix products: 2.01 us -> none  [the longest x1 1.79 us: dense_layer(): mixed = jnp.dot(aggregated, weight, preferred_element_type=jnp.float32)]
    ppermute x3, starting transfers between devices: 4.56 us -> 3.86 us  [on_device(): total_g = total_g + lax.ppermute(piece, 'row', perm).astype(jnp.float32)]
    unnamed x16, local copies, waits for them, and re-layouts: 1.43 us -> 2.08 us
where the time goes in v10:
time: 61.4 us; the launch traced here: 61.2 us
  waiting for transfers between devices  25.9 us (42%)
  starting transfers between devices  20 us (33%)
  Pallas kernels  8.93 us (15%)
  other arithmetic  2.89 us (5%)
  local copies, waits for them, and re-layouts  2.1 us (3%)
  between operations  1.37 us (2%)
    ppermute x3, waiting for transfers between devices, on_device(): got = [lax.ppermute(pulled_own, 'col', perm) for perm in shifts('col')]  9.24 us
    ppermute x3, starting transfers between devices, on_device(): lax.ppermute(send[shift], 'col', perm)  6.04 us
    ppermute x3, starting transfers between devices, on_device(): lax.ppermute(features, 'row', perm)  5.97 us
    ppermute x3, waiting for transfers between devices, on_device(): lax.ppermute(send[shift], 'col', perm)  5.66 us
    ppermute x3, waiting for transfers between devices, on_device(): total_g = total_g + lax.ppermute(piece, 'row', perm).astype(jnp.float32)  4.13 us
    ppermute x3, starting transfers between devices, on_device(): got = [lax.ppermute(pulled_own, 'col', perm) for perm in shifts('col')]  4.03 us
    ppermute x3, starting transfers between devices, on_device(): total_g = total_g + lax.ppermute(piece, 'row', perm).astype(jnp.float32)  3.86 us
    pallas_call x1, Pallas kernels, tile_products_t(): pl.pallas_call(functools.partial(backward_kernel, len(got) + 1), out_shap...  3.65 us
  transfers between devices with their start and end apart: 14, of which 11 were waited for; matrix products, arithmetic and copies ran while one was open for 0% of the time, Pallas kernels for 0%

profile of v10, /device:TPU:0, one launch (start us, length us, event | category | flops | bytes accessed | tf_op | source)
XLA Modules:
  0.0 61.2 jit_solution(311726459436727380)
XLA Ops:
  0.6 3.0 %collective-permute-start = (bf16[192,256]{1,0:T(8,128)(2,1)}, bf16[192,256]{1,0:T(8,128)(2,1)S(1)}, u32[]{:S(2)}, u32[]{:S(2)}) collective-permute-start(bf16[192,256]{1,0:T(8,128)(2,1)} %param.7), channel_id=1, source_target_pairs={{0,8},{4,12},{8,16},{12,20},{16,24},{20,28},{24,0},{28,4},{1,9},{5... | collective-permute-start | bytes 294920 | tf_op jit(solution)/shard_map/ppermute | solution.py:184
  3.6 1.0 %collective-permute-start.2 = (bf16[192,256]{1,0:T(8,128)(2,1)}, bf16[192,256]{1,0:T(8,128)(2,1)S(1)}, u32[]{:S(2)}, u32[]{:S(2)}) collective-permute-start(bf16[192,256]{1,0:T(8,128)(2,1)} %param.7), channel_id=1, source_target_pairs={{0,24},{4,28},{8,0},{12,4},{16,8},{20,12},{24,16},{28,20},{1,25},{... | collective-permute-start | bytes 294920 | tf_op jit(solution)/shard_map/ppermute | solution.py:184
  4.7 1.9 %collective-permute-start.1 = (bf16[192,256]{1,0:T(8,128)(2,1)}, bf16[192,256]{1,0:T(8,128)(2,1)S(1)}, u32[]{:S(2)}, u32[]{:S(2)}) collective-permute-start(bf16[192,256]{1,0:T(8,128)(2,1)} %param.7), channel_id=1, source_target_pairs={{0,16},{4,20},{8,24},{12,28},{16,0},{20,4},{24,8},{28,12},{1,17},{... | collective-permute-start | bytes 294920 | tf_op jit(solution)/shard_map/ppermute | solution.py:184
  6.6 1.6 %collective-permute-done = bf16[192,256]{1,0:T(8,128)(2,1)S(1)} collective-permute-done((bf16[192,256]{1,0:T(8,128)(2,1)}, bf16[192,256]{1,0:T(8,128)(2,1)S(1)}, u32[]{:S(2)}, u32[]{:S(2)}) %collective-permute-start) | collective-permute-done | bytes 98336 | tf_op jit(solution)/shard_map/ppermute | solution.py:184
  8.3 1.7 %collective-permute-done.2 = bf16[192,256]{1,0:T(8,128)(2,1)S(1)} collective-permute-done((bf16[192,256]{1,0:T(8,128)(2,1)}, bf16[192,256]{1,0:T(8,128)(2,1)S(1)}, u32[]{:S(2)}, u32[]{:S(2)}) %collective-permute-start.2) | collective-permute-done | bytes 98336 | tf_op jit(solution)/shard_map/ppermute | solution.py:184
  10.0 0.9 %pad_maximum_fusion.near_ref = bf16[4,192,256]{2,1,0:T(8,128)(2,1)S(1)} fusion(bf16[1,192,256]{2,1,0:T(8,128)(2,1)S(1)} %bitcast.30, bf16[1,192,256]{2,1,0:T(8,128)(2,1)S(1)} %bitcast.31, bf16[1,192,256]{2,1,0:T(8,128)(2,1)S(1)} %bitcast.29, bf16[1,192,256]{2,1,0:T(8,128)(2,1)} %bitcast.28), kind=kLoop, calls=%fused_computation | loop fusion | flops 589824 | bytes 786432 | tf_op jit(solution)/shard_map/stack | solution.py:184
  10.9 0.1 collective-permute-start.3
  11.7 1.0 %collective-permute-done.3.far_ref = bf16[4,192,256]{2,1,0:T(8,128)(2,1)S(1)} collective-permute-done((bf16[4,192,256]{2,1,0:T(8,128)(2,1)S(1)}, bf16[4,192,256]{2,1,0:T(8,128)(2,1)S(1)}, u32[]{:S(2)}, u32[]{:S(2)}) %collective-permute-start.3) | collective-permute-done | bytes 393248 | tf_op jit(solution)/shard_map/ppermute | solution.py:185
  12.7 0.7 %copy-done.1 = bf16[4,192,256]{2,1,0:T(8,128)(2,1)} copy-done((bf16[4,192,256]{2,1,0:T(8,128)(2,1)}, bf16[4,192,256]{2,1,0:T(8,128)(2,1)S(1)}, u32[]{:S(2)}) %copy-start.1) | copy-done | bytes 393240
  13.5 3.1 %shard_map.86 = (f32[192,256]{1,0:T(8,128)}, bf16[192,256]{1,0:T(8,128)(2,1)}, bf16[192,256]{1,0:T(8,128)(2,1)}, bf16[192,256]{1,0:T(8,128)(2,1)}) custom-call(s32[12]{0:T(128)} %bitcast.32, s32[12]{0:T(128)} %bitcast.34, s32[1]{0:T(128)} %bitcast.24.info_ref, bf16[12,256,256]{2,1,0:T(8,128)(2,1)} %bitcast.26, bf16[4,192,256]{2,1,0:T(8,128)(2,1)} %copy-done, ...), custom_call_target="tpu_custom_call" | custom-call | tf_op jit(solution)/shard_map/pallas_call | solution.py:133
  16.6 1.7 %collective-permute-start.4 = (bf16[192,256]{1,0:T(8,128)(2,1)}, bf16[192,256]{1,0:T(8,128)(2,1)S(1)}, u32[]{:S(2)}, u32[]{:S(2)}) collective-permute-start(bf16[192,256]{1,0:T(8,128)(2,1)} %get-tuple-element.11), channel_id=1, source_target_pairs={{0,1},{1,2},{2,3},{3,0},{4,5},{5,6},{6,7},{7,4},{8,9},{9,10},{10,1... | collective-permute-start | bytes 294920 | tf_op jit(solution)/shard_map/ppermute | solution.py:188
  18.3 2.3 %collective-permute-start.5 = (bf16[192,256]{1,0:T(8,128)(2,1)}, bf16[192,256]{1,0:T(8,128)(2,1)S(1)}, u32[]{:S(2)}, u32[]{:S(2)}) collective-permute-start(bf16[192,256]{1,0:T(8,128)(2,1)} %get-tuple-element.12), channel_id=1, source_target_pairs={{0,2},{1,3},{2,0},{3,1},{4,6},{5,7},{6,4},{7,5},{8,10},{9,11},{10,... | collective-permute-start | bytes 294920 | tf_op jit(solution)/shard_map/ppermute | solution.py:188
  20.6 2.0 %collective-permute-start.6 = (bf16[192,256]{1,0:T(8,128)(2,1)}, bf16[192,256]{1,0:T(8,128)(2,1)S(1)}, u32[]{:S(2)}, u32[]{:S(2)}) collective-permute-start(bf16[192,256]{1,0:T(8,128)(2,1)} %get-tuple-element.13), channel_id=1, source_target_pairs={{0,3},{1,0},{2,1},{3,2},{4,7},{5,4},{6,5},{7,6},{8,11},{9,8},{10,9... | collective-permute-start | bytes 294920 | tf_op jit(solution)/shard_map/ppermute | solution.py:188
  22.6 1.7 %collective-permute-done.4.rest_0_ = bf16[192,256]{1,0:T(8,128)(2,1)S(1)} collective-permute-done((bf16[192,256]{1,0:T(8,128)(2,1)}, bf16[192,256]{1,0:T(8,128)(2,1)S(1)}, u32[]{:S(2)}, u32[]{:S(2)}) %collective-permute-start.4) | collective-permute-done | bytes 98336 | tf_op jit(solution)/shard_map/ppermute | solution.py:188
  24.3 3.9 %collective-permute-done.5.rest_1_ = bf16[192,256]{1,0:T(8,128)(2,1)S(1)} collective-permute-done((bf16[192,256]{1,0:T(8,128)(2,1)}, bf16[192,256]{1,0:T(8,128)(2,1)S(1)}, u32[]{:S(2)}, u32[]{:S(2)}) %collective-permute-start.5) | collective-permute-done | bytes 98336 | tf_op jit(solution)/shard_map/ppermute | solution.py:188
  28.3 0.6 %copy-done.6 = bf16[192,256]{1,0:T(8,128)(2,1)} copy-done((bf16[192,256]{1,0:T(8,128)(2,1)}, bf16[192,256]{1,0:T(8,128)(2,1)S(1)}, u32[]{:S(2)}) %copy-start.6) | copy-done | bytes 98328
  28.9 2.2 %shard_map.87 = (bf16[192,256]{1,0:T(8,128)(2,1)}, bf16[192,256]{1,0:T(8,128)(2,1)}) custom-call(f32[192,256]{1,0:T(8,128)} %get-tuple-element.10.own_ref, bf16[192,256]{1,0:T(8,128)(2,1)} %copy-done.5, bf16[192,256]{1,0:T(8,128)(2,1)} %copy-done.6, bf16[192,256]{1,0:T(8,128)(2,1)} %copy-done.7, bf16[192,256]{1,0:T(8,128)(2,1)} %rest_3_.1, ...), custom_call_target="tpu_custom_call" | custom-call | tf_op jit(solution)/shard_map/pallas_call | solution.py:30
  31.1 3.5 %collective-permute-start.9 = (bf16[192,256]{1,0:T(8,128)(2,1)}, bf16[192,256]{1,0:T(8,128)(2,1)S(1)}, u32[]{:S(2)}, u32[]{:S(2)}) collective-permute-start(bf16[192,256]{1,0:T(8,128)(2,1)} %get-tuple-element.15.mine_ref), channel_id=1, source_target_pairs={{0,3},{1,0},{2,1},{3,2},{4,7},{5,4},{6,5},{7,6},{8,11},{9,8},{10,9... | collective-permute-start | bytes 294920 | tf_op jit(solution)/shard_map/ppermute | solution.py:190
  34.6 0.6 collective-permute-start.8
  35.1 2.9 %collective-permute-done.9.rest_2_ = bf16[192,256]{1,0:T(8,128)(2,1)S(1)} collective-permute-done((bf16[192,256]{1,0:T(8,128)(2,1)}, bf16[192,256]{1,0:T(8,128)(2,1)S(1)}, u32[]{:S(2)}, u32[]{:S(2)}) %collective-permute-start.9) | collective-permute-done | bytes 98336 | tf_op jit(solution)/shard_map/ppermute | solution.py:190
  38.1 6.3 %collective-permute-done.8.rest_1_ = bf16[192,256]{1,0:T(8,128)(2,1)S(1)} collective-permute-done((bf16[192,256]{1,0:T(8,128)(2,1)}, bf16[192,256]{1,0:T(8,128)(2,1)S(1)}, u32[]{:S(2)}, u32[]{:S(2)}) %collective-permute-start.8) | collective-permute-done | bytes 98336 | tf_op jit(solution)/shard_map/ppermute | solution.py:190
  44.4 0.6 %copy-done.3 = bf16[192,256]{1,0:T(8,128)(2,1)} copy-done((bf16[192,256]{1,0:T(8,128)(2,1)}, bf16[192,256]{1,0:T(8,128)(2,1)S(1)}, u32[]{:S(2)}) %copy-start.3) | copy-done | bytes 98328
  45.1 3.7 %shard_map.88 = (f32[4,192,256]{2,1,0:T(8,128)}, f32[4,192,256]{2,1,0:T(8,128)}) custom-call(s32[12]{0:T(128)} %bitcast.33, s32[12]{0:T(128)} %bitcast.35, s32[1]{0:T(128)} %bitcast.25.info_ref, bf16[12,256,256]{2,1,0:T(8,128)(2,1)} %bitcast.27, bf16[192,256]{1,0:T(8,128)(2,1)} %get-tuple-element.15.mine_ref, bf16[192,256]{1,0:T(8,128)(2,1)} %copy-done.4, ...), custom_call_target="tpu_custom_call" | custom-call | tf_op jit(solution)/shard_map/pallas_call | solution.py:150
  48.7 2.5 %collective-permute-done.10 = f32[4,192,256]{2,1,0:T(8,128)S(1)} collective-permute-done((f32[4,192,256]{2,1,0:T(8,128)}, f32[4,192,256]{2,1,0:T(8,128)S(1)}, u32[]{:S(2)}, u32[]{:S(2)}) %collective-permute-start.10) | collective-permute-done | bytes 786464 | tf_op jit(solution)/shard_map/ppermute | solution.py:194
  51.2 1.3 %fusion.4 = (bf16[4,192,256]{2,1,0:T(8,128)(2,1)S(1)}, f32[4,192,256]{2,1,0:T(8,128)S(1)}) fusion(f32[4,192,256]{2,1,0:T(8,128)} %get-tuple-element.16, f32[4,192,256]{2,1,0:T(8,128)S(1)} %collective-permute-done.10), kind=kLoop, calls=%fused_computation.9 | loop fusion | flops 393216 | bytes 2752512 | tf_op jit(solution)/shard_map/convert.2
  52.5 2.0 %collective-permute-start.11 = (bf16[192,256]{1,0:T(8,128)(2,1)S(1)}, bf16[192,256]{1,0:T(8,128)(2,1)S(1)}, u32[]{:S(2)}, u32[]{:S(2)}) collective-permute-start(bf16[192,256]{1,0:T(8,128)(2,1)S(1)} %get-tuple-element.20), channel_id=1, source_target_pairs={{0,8},{4,12},{8,16},{12,20},{16,24},{20,28},{24,0},{28,4},{1,9},{5... | collective-permute-start | bytes 294920 | tf_op jit(solution)/shard_map/ppermute | solution.py:198
  54.5 1.0 %collective-permute-start.13 = (bf16[192,256]{1,0:T(8,128)(2,1)S(1)}, bf16[192,256]{1,0:T(8,128)(2,1)S(1)}, u32[]{:S(2)}, u32[]{:S(2)}) collective-permute-start(bf16[192,256]{1,0:T(8,128)(2,1)S(1)} %get-tuple-element.21), channel_id=1, source_target_pairs={{0,24},{4,28},{8,0},{12,4},{16,8},{20,12},{24,16},{28,20},{1,25},{... | collective-permute-start | bytes 294920 | tf_op jit(solution)/shard_map/ppermute | solution.py:198
  55.5 0.9 %collective-permute-start.12 = (bf16[192,256]{1,0:T(8,128)(2,1)S(1)}, bf16[192,256]{1,0:T(8,128)(2,1)S(1)}, u32[]{:S(2)}, u32[]{:S(2)}) collective-permute-start(bf16[192,256]{1,0:T(8,128)(2,1)S(1)} %get-tuple-element.22), channel_id=1, source_target_pairs={{0,16},{4,20},{8,24},{12,28},{16,0},{20,4},{24,8},{28,12},{1,17},{... | collective-permute-start | bytes 294920 | tf_op jit(solution)/shard_map/ppermute | solution.py:198
  56.4 2.8 %collective-permute-done.11 = bf16[192,256]{1,0:T(8,128)(2,1)S(1)} collective-permute-done((bf16[192,256]{1,0:T(8,128)(2,1)S(1)}, bf16[192,256]{1,0:T(8,128)(2,1)S(1)}, u32[]{:S(2)}, u32[]{:S(2)}) %collective-permute-start.11) | collective-permute-done | bytes 98336 | tf_op jit(solution)/shard_map/ppermute | solution.py:198
  59.1 0.7 %collective-permute-done.13 = bf16[192,256]{1,0:T(8,128)(2,1)S(1)} collective-permute-done((bf16[192,256]{1,0:T(8,128)(2,1)S(1)}, bf16[192,256]{1,0:T(8,128)(2,1)S(1)}, u32[]{:S(2)}, u32[]{:S(2)}) %collective-permute-start.13) | collective-permute-done | bytes 98336 | tf_op jit(solution)/shard_map/ppermute | solution.py:198
  59.8 0.7 %collective-permute-done.12 = bf16[192,256]{1,0:T(8,128)(2,1)S(1)} collective-permute-done((bf16[192,256]{1,0:T(8,128)(2,1)S(1)}, bf16[192,256]{1,0:T(8,128)(2,1)S(1)}, u32[]{:S(2)}, u32[]{:S(2)}) %collective-permute-start.12) | collective-permute-done | bytes 98336 | tf_op jit(solution)/shard_map/ppermute | solution.py:198
  60.5 0.7 %fusion.3 = bf16[192,256]{1,0:T(8,128)(2,1)} fusion(f32[4,192,256]{2,1,0:T(8,128)S(1)} %get-tuple-element.19, bf16[192,256]{1,0:T(8,128)(2,1)S(1)} %collective-permute-done.13, bf16[192,256]{1,0:T(8,128)(2,1)S(1)} %collective-permute-done.12, bf16[192,256]{1,0:T(8,128)(2,1)S(1)} %collective-permute-done.11), kind=kLoop, calls=%fused_computation.5 | loop fusion | flops 344064 | bytes 589824 | tf_op jit(solution)/shard_map/convert_element_type | solution.py:199
  (19 shorter events, 0.1 us)
Async XLA Ops:
  0.6 7.6 %collective-permute-start = (bf16[192,256]{1,0:T(8,128)(2,1)}, bf16[192,256]{1,0:T(8,128)(2,1)S(1)}, u32[]{:S(2)}, u32[]{:S(2)}) collective-permute-start(bf16[192,256]{1,0:T(8,128)(2,1)} %param.7), channel_id=1, source_target_pairs={{0,8},{4,12},{8,16},{12,20},{16,24},{20,28},{24,0},{28,4},{1,9},{5... | collective-permute-start | bytes 294920 | tf_op jit(solution)/shard_map/ppermute | solution.py:184
  3.6 6.3 %collective-permute-start.2 = (bf16[192,256]{1,0:T(8,128)(2,1)}, bf16[192,256]{1,0:T(8,128)(2,1)S(1)}, u32[]{:S(2)}, u32[]{:S(2)}) collective-permute-start(bf16[192,256]{1,0:T(8,128)(2,1)} %param.7), channel_id=1, source_target_pairs={{0,24},{4,28},{8,0},{12,4},{16,8},{20,12},{24,16},{28,20},{1,25},{... | collective-permute-start | bytes 294920 | tf_op jit(solution)/shard_map/ppermute | solution.py:184
  4.7 5.3 %collective-permute-start.1 = (bf16[192,256]{1,0:T(8,128)(2,1)}, bf16[192,256]{1,0:T(8,128)(2,1)S(1)}, u32[]{:S(2)}, u32[]{:S(2)}) collective-permute-start(bf16[192,256]{1,0:T(8,128)(2,1)} %param.7), channel_id=1, source_target_pairs={{0,16},{4,20},{8,24},{12,28},{16,0},{20,4},{24,8},{28,12},{1,17},{... | collective-permute-start | bytes 294920 | tf_op jit(solution)/shard_map/ppermute | solution.py:184
  10.9 1.8 %copy-start = (bf16[4,192,256]{2,1,0:T(8,128)(2,1)}, bf16[4,192,256]{2,1,0:T(8,128)(2,1)S(1)}, u32[]{:S(2)}) copy-start(bf16[4,192,256]{2,1,0:T(8,128)(2,1)S(1)} %pad_maximum_fusion.near_ref) | copy-start | bytes 1179652
  10.9 1.8 %collective-permute-start.3 = (bf16[4,192,256]{2,1,0:T(8,128)(2,1)S(1)}, bf16[4,192,256]{2,1,0:T(8,128)(2,1)S(1)}, u32[]{:S(2)}, u32[]{:S(2)}) collective-permute-start(bf16[4,192,256]{2,1,0:T(8,128)(2,1)S(1)} %pad_maximum_fusion.near_ref), channel_id=1, source_target_pairs={{0,4},{4,0},{8,12},{12,8},{16,20},{20,16},{24,28},{28,24},{1,5},{5... | collective-permute-start | bytes 1179656 | tf_op jit(solution)/shard_map/ppermute | solution.py:185
  12.7 0.7 %copy-start.1 = (bf16[4,192,256]{2,1,0:T(8,128)(2,1)}, bf16[4,192,256]{2,1,0:T(8,128)(2,1)S(1)}, u32[]{:S(2)}) copy-start(bf16[4,192,256]{2,1,0:T(8,128)(2,1)S(1)} %collective-permute-done.3.far_ref) | copy-start | bytes 1179652
  16.6 7.8 %collective-permute-start.4 = (bf16[192,256]{1,0:T(8,128)(2,1)}, bf16[192,256]{1,0:T(8,128)(2,1)S(1)}, u32[]{:S(2)}, u32[]{:S(2)}) collective-permute-start(bf16[192,256]{1,0:T(8,128)(2,1)} %get-tuple-element.11), channel_id=1, source_target_pairs={{0,1},{1,2},{2,3},{3,0},{4,5},{5,6},{6,7},{7,4},{8,9},{9,10},{10,1... | collective-permute-start | bytes 294920 | tf_op jit(solution)/shard_map/ppermute | solution.py:188
  18.3 10.0 %collective-permute-start.5 = (bf16[192,256]{1,0:T(8,128)(2,1)}, bf16[192,256]{1,0:T(8,128)(2,1)S(1)}, u32[]{:S(2)}, u32[]{:S(2)}) collective-permute-start(bf16[192,256]{1,0:T(8,128)(2,1)} %get-tuple-element.12), channel_id=1, source_target_pairs={{0,2},{1,3},{2,0},{3,1},{4,6},{5,7},{6,4},{7,5},{8,10},{9,11},{10,... | collective-permute-start | bytes 294920 | tf_op jit(solution)/shard_map/ppermute | solution.py:188
  20.6 7.7 %collective-permute-start.6 = (bf16[192,256]{1,0:T(8,128)(2,1)}, bf16[192,256]{1,0:T(8,128)(2,1)S(1)}, u32[]{:S(2)}, u32[]{:S(2)}) collective-permute-start(bf16[192,256]{1,0:T(8,128)(2,1)} %get-tuple-element.13), channel_id=1, source_target_pairs={{0,3},{1,0},{2,1},{3,2},{4,7},{5,4},{6,5},{7,6},{8,11},{9,8},{10,9... | collective-permute-start | bytes 294920 | tf_op jit(solution)/shard_map/ppermute | solution.py:188
  24.3 3.9 %copy-start.5 = (bf16[192,256]{1,0:T(8,128)(2,1)}, bf16[192,256]{1,0:T(8,128)(2,1)S(1)}, u32[]{:S(2)}) copy-start(bf16[192,256]{1,0:T(8,128)(2,1)S(1)} %collective-permute-done.4.rest_0_) | copy-start | bytes 294916
  28.3 0.6 %copy-start.6 = (bf16[192,256]{1,0:T(8,128)(2,1)}, bf16[192,256]{1,0:T(8,128)(2,1)S(1)}, u32[]{:S(2)}) copy-start(bf16[192,256]{1,0:T(8,128)(2,1)S(1)} %collective-permute-done.5.rest_1_) | copy-start | bytes 294916
  28.3 0.7 %copy-start.7 = (bf16[192,256]{1,0:T(8,128)(2,1)}, bf16[192,256]{1,0:T(8,128)(2,1)S(1)}, u32[]{:S(2)}) copy-start(bf16[192,256]{1,0:T(8,128)(2,1)S(1)} %collective-permute-done.6.rest_2_) | copy-start | bytes 294916
  31.1 7.0 %collective-permute-start.9 = (bf16[192,256]{1,0:T(8,128)(2,1)}, bf16[192,256]{1,0:T(8,128)(2,1)S(1)}, u32[]{:S(2)}, u32[]{:S(2)}) collective-permute-start(bf16[192,256]{1,0:T(8,128)(2,1)} %get-tuple-element.15.mine_ref), channel_id=1, source_target_pairs={{0,3},{1,0},{2,1},{3,2},{4,7},{5,4},{6,5},{7,6},{8,11},{9,8},{10,9... | collective-permute-start | bytes 294920 | tf_op jit(solution)/shard_map/ppermute | solution.py:190
  34.6 9.8 %collective-permute-start.8 = (bf16[192,256]{1,0:T(8,128)(2,1)}, bf16[192,256]{1,0:T(8,128)(2,1)S(1)}, u32[]{:S(2)}, u32[]{:S(2)}) collective-permute-start(bf16[192,256]{1,0:T(8,128)(2,1)} %get-tuple-element.15.mine_ref), channel_id=1, source_target_pairs={{0,2},{1,3},{2,0},{3,1},{4,6},{5,7},{6,4},{7,5},{8,10},{9,11},{10,... | collective-permute-start | bytes 294920 | tf_op jit(solution)/shard_map/ppermute | solution.py:190
  35.1 9.3 %collective-permute-start.7 = (bf16[192,256]{1,0:T(8,128)(2,1)}, bf16[192,256]{1,0:T(8,128)(2,1)S(1)}, u32[]{:S(2)}, u32[]{:S(2)}) collective-permute-start(bf16[192,256]{1,0:T(8,128)(2,1)} %get-tuple-element.15.mine_ref), channel_id=1, source_target_pairs={{0,1},{1,2},{2,3},{3,0},{4,5},{5,6},{6,7},{7,4},{8,9},{9,10},{10,1... | collective-permute-start | bytes 294920 | tf_op jit(solution)/shard_map/ppermute | solution.py:190
  38.1 6.3 %copy-start.2 = (bf16[192,256]{1,0:T(8,128)(2,1)}, bf16[192,256]{1,0:T(8,128)(2,1)S(1)}, u32[]{:S(2)}) copy-start(bf16[192,256]{1,0:T(8,128)(2,1)S(1)} %collective-permute-done.9.rest_2_) | copy-start | bytes 294916
  44.4 0.6 %copy-start.3 = (bf16[192,256]{1,0:T(8,128)(2,1)}, bf16[192,256]{1,0:T(8,128)(2,1)S(1)}, u32[]{:S(2)}) copy-start(bf16[192,256]{1,0:T(8,128)(2,1)S(1)} %collective-permute-done.8.rest_1_) | copy-start | bytes 294916
  44.4 0.7 %copy-start.4 = (bf16[192,256]{1,0:T(8,128)(2,1)}, bf16[192,256]{1,0:T(8,128)(2,1)S(1)}, u32[]{:S(2)}) copy-start(bf16[192,256]{1,0:T(8,128)(2,1)S(1)} %collective-permute-done.7.rest_0_) | copy-start | bytes 294916
  48.7 2.5 %collective-permute-start.10 = (f32[4,192,256]{2,1,0:T(8,128)}, f32[4,192,256]{2,1,0:T(8,128)S(1)}, u32[]{:S(2)}, u32[]{:S(2)}) collective-permute-start(f32[4,192,256]{2,1,0:T(8,128)} %get-tuple-element.17), channel_id=1, source_target_pairs={{0,4},{4,0},{8,12},{12,8},{16,20},{20,16},{24,28},{28,24},{1,5},{5... | collective-permute-start | bytes 2359304 | tf_op jit(solution)/shard_map/ppermute | solution.py:194
  52.5 6.6 %collective-permute-start.11 = (bf16[192,256]{1,0:T(8,128)(2,1)S(1)}, bf16[192,256]{1,0:T(8,128)(2,1)S(1)}, u32[]{:S(2)}, u32[]{:S(2)}) collective-permute-start(bf16[192,256]{1,0:T(8,128)(2,1)S(1)} %get-tuple-element.20), channel_id=1, source_target_pairs={{0,8},{4,12},{8,16},{12,20},{16,24},{20,28},{24,0},{28,4},{1,9},{5... | collective-permute-start | bytes 294920 | tf_op jit(solution)/shard_map/ppermute | solution.py:198
  54.5 5.3 %collective-permute-start.13 = (bf16[192,256]{1,0:T(8,128)(2,1)S(1)}, bf16[192,256]{1,0:T(8,128)(2,1)S(1)}, u32[]{:S(2)}, u32[]{:S(2)}) collective-permute-start(bf16[192,256]{1,0:T(8,128)(2,1)S(1)} %get-tuple-element.21), channel_id=1, source_target_pairs={{0,24},{4,28},{8,0},{12,4},{16,8},{20,12},{24,16},{28,20},{1,25},{... | collective-permute-start | bytes 294920 | tf_op jit(solution)/shard_map/ppermute | solution.py:198
  55.5 5.0 %collective-permute-start.12 = (bf16[192,256]{1,0:T(8,128)(2,1)S(1)}, bf16[192,256]{1,0:T(8,128)(2,1)S(1)}, u32[]{:S(2)}, u32[]{:S(2)}) collective-permute-start(bf16[192,256]{1,0:T(8,128)(2,1)S(1)} %get-tuple-element.22), channel_id=1, source_target_pairs={{0,16},{4,20},{8,24},{12,28},{16,0},{20,4},{24,8},{28,12},{1,17},{... | collective-permute-start | bytes 294920 | tf_op jit(solution)/shard_map/ppermute | solution.py:198

commit v11 on v7

--- a/solution.py
+++ b/solution.py
@@ -106,7 +106,9 @@
     for shift in range(chips):
         owner = (chip + shift) % chips
         near_ref[shift] = acc_ref[pl.ds(pl.multiple_of((owner * 2 + core) * piece, 8), piece), :]
-        far_ref[shift] = acc_ref[pl.ds(pl.multiple_of((owner * 2 + 1 - core) * piece, 8), piece), :]
+        far_ref[shift] = acc_ref[pl.ds(pl.multiple_of((owner * 2 + 1 - core) * piece, 8), piece), :].astype(
+            far_ref.dtype
+        )
 
 
 SMEM = pl.BlockSpec(memory_space=pltpu.SMEM)
@@ -133,10 +135,11 @@
 def tile_products_t(rows, cols, info, blocks, mine, got, n_out, out_rows):
     chunk = out_rows // n_out
     width = mine.shape[1]
-    stack = jax.ShapeDtypeStruct((n_out // 2, chunk, width), jnp.float32)
+    near = jax.ShapeDtypeStruct((n_out // 2, chunk, width), jnp.float32)
+    far = jax.ShapeDtypeStruct((n_out // 2, chunk, width), jnp.bfloat16)
     return pl.pallas_call(
         functools.partial(backward_kernel, len(got) + 1),
-        out_shape=(stack, stack),
+        out_shape=(near, far),
         in_specs=[SMEM, SMEM, SMEM, VMEM, VMEM] + [VMEM] * len(got),
         out_specs=(VMEM, VMEM),
         scratch_shapes=[
@@ -180,7 +183,7 @@
     near_g, far_g = tile_products_t(
         row_slots, col_slots, info, blocks, pulled_own, got, n_row, n_row * own_rows
     )
-    chip_sums = near_g + lax.ppermute(far_g, "row", partner(n_row))
+    chip_sums = near_g + lax.ppermute(far_g, "row", partner(n_row)).astype(jnp.float32)
     total_g = chip_sums[0]
     for shift, perm in enumerate(chip_shifts(n_row)):
         piece = chip_sums[shift + 1].astype(jnp.bfloat16)

time: 60.8 us -> 59.8 us (0.984)
  waiting for transfers between devices: 25.8 us -> 24.6 us
  starting transfers between devices: 20.3 us -> 21.2 us
  Pallas kernels: 6.78 us -> 6.05 us
    ppermute x3, starting transfers between devices: 4.56 us -> 5.38 us  [on_device(): total_g = total_g + lax.ppermute(piece, 'row', perm).astype(jnp.float32)]
  transfers between devices with their start and end apart: 14 -> 14, of which waited for: 11 -> 10; matrix products, arithmetic and copies ran while one was open for 0% -> 0% of each run, Pallas kernels for 0% -> 0%
where the time goes in v11:
time: 59.8 us; the launch traced here: 59.6 us
  waiting for transfers between devices  24.6 us (41%)
  starting transfers between devices  21.2 us (35%)
  Pallas kernels  6.05 us (10%)
  other arithmetic  2.88 us (5%)
  matrix products  2.01 us (3%)
  local copies, waits for them, and re-layouts  1.46 us (2%)
  between operations  1.39 us (2%)
    ppermute x3, waiting for transfers between devices, on_device(): got = [lax.ppermute(pulled_own, 'col', perm) for perm in shifts('col')]  8.95 us
    ppermute x3, starting transfers between devices, on_device(): lax.ppermute(features, 'row', perm)  5.97 us
    ppermute x3, waiting for transfers between devices, on_device(): total = total + lax.ppermute(send[shift], 'col', perm).astype(jnp.float32)  5.89 us
    ppermute x3, starting transfers between devices, on_device(): total = total + lax.ppermute(send[shift], 'col', perm).astype(jnp.float32)  5.63 us
    ppermute x3, starting transfers between devices, on_device(): total_g = total_g + lax.ppermute(piece, 'row', perm).astype(jnp.float32)  5.38 us
    ppermute x3, starting transfers between devices, on_device(): got = [lax.ppermute(pulled_own, 'col', perm) for perm in shifts('col')]  4.15 us
    ppermute x3, waiting for transfers between devices, on_device(): total_g = total_g + lax.ppermute(piece, 'row', perm).astype(jnp.float32)  3.46 us
    ppermute x3, waiting for transfers between devices, on_device(): lax.ppermute(features, 'row', perm)  3.36 us
  transfers between devices with their start and end apart: 14, of which 10 were waited for; matrix products, arithmetic and copies ran while one was open for 0% of the time, Pallas kernels for 0%

profile of v11, /device:TPU:0, one launch (start us, length us, event | category | flops | bytes accessed | tf_op | source)
XLA Modules:
  0.0 59.6 jit_solution(16534925013682029859)
XLA Ops:
  0.6 3.0 %collective-permute-start = (bf16[192,256]{1,0:T(8,128)(2,1)}, bf16[192,256]{1,0:T(8,128)(2,1)S(1)}, u32[]{:S(2)}, u32[]{:S(2)}) collective-permute-start(bf16[192,256]{1,0:T(8,128)(2,1)} %param.7), channel_id=1, source_target_pairs={{0,8},{4,12},{8,16},{12,20},{16,24},{20,28},{24,0},{28,4},{1,9},{5... | collective-permute-start | bytes 294920 | tf_op jit(solution)/shard_map/ppermute | solution.py:174
  3.7 1.0 %collective-permute-start.2 = (bf16[192,256]{1,0:T(8,128)(2,1)}, bf16[192,256]{1,0:T(8,128)(2,1)S(1)}, u32[]{:S(2)}, u32[]{:S(2)}) collective-permute-start(bf16[192,256]{1,0:T(8,128)(2,1)} %param.7), channel_id=1, source_target_pairs={{0,24},{4,28},{8,0},{12,4},{16,8},{20,12},{24,16},{28,20},{1,25},{... | collective-permute-start | bytes 294920 | tf_op jit(solution)/shard_map/ppermute | solution.py:174
  4.7 1.9 %collective-permute-start.1 = (bf16[192,256]{1,0:T(8,128)(2,1)}, bf16[192,256]{1,0:T(8,128)(2,1)S(1)}, u32[]{:S(2)}, u32[]{:S(2)}) collective-permute-start(bf16[192,256]{1,0:T(8,128)(2,1)} %param.7), channel_id=1, source_target_pairs={{0,16},{4,20},{8,24},{12,28},{16,0},{20,4},{24,8},{28,12},{1,17},{... | collective-permute-start | bytes 294920 | tf_op jit(solution)/shard_map/ppermute | solution.py:174
  6.6 1.6 %collective-permute-done = bf16[192,256]{1,0:T(8,128)(2,1)S(1)} collective-permute-done((bf16[192,256]{1,0:T(8,128)(2,1)}, bf16[192,256]{1,0:T(8,128)(2,1)S(1)}, u32[]{:S(2)}, u32[]{:S(2)}) %collective-permute-start) | collective-permute-done | bytes 98336 | tf_op jit(solution)/shard_map/ppermute | solution.py:174
  8.3 1.7 %collective-permute-done.2 = bf16[192,256]{1,0:T(8,128)(2,1)S(1)} collective-permute-done((bf16[192,256]{1,0:T(8,128)(2,1)}, bf16[192,256]{1,0:T(8,128)(2,1)S(1)}, u32[]{:S(2)}, u32[]{:S(2)}) %collective-permute-start.2) | collective-permute-done | bytes 98336 | tf_op jit(solution)/shard_map/ppermute | solution.py:174
  10.0 0.9 %pad_maximum_fusion.near_ref = bf16[4,192,256]{2,1,0:T(8,128)(2,1)S(1)} fusion(bf16[1,192,256]{2,1,0:T(8,128)(2,1)S(1)} %bitcast.32, bf16[1,192,256]{2,1,0:T(8,128)(2,1)S(1)} %bitcast.33, bf16[1,192,256]{2,1,0:T(8,128)(2,1)S(1)} %bitcast.31, bf16[1,192,256]{2,1,0:T(8,128)(2,1)} %bitcast.30), kind=kLoop, calls=%fused_computation.2 | loop fusion | flops 589824 | bytes 786432 | tf_op jit(solution)/shard_map/stack | solution.py:174
  10.9 0.1 collective-permute-start.3
  11.7 1.0 %collective-permute-done.3.far_ref = bf16[4,192,256]{2,1,0:T(8,128)(2,1)S(1)} collective-permute-done((bf16[4,192,256]{2,1,0:T(8,128)(2,1)S(1)}, bf16[4,192,256]{2,1,0:T(8,128)(2,1)S(1)}, u32[]{:S(2)}, u32[]{:S(2)}) %collective-permute-start.3) | collective-permute-done | bytes 393248 | tf_op jit(solution)/shard_map/ppermute | solution.py:175
  12.7 0.7 %copy-done.2 = bf16[4,192,256]{2,1,0:T(8,128)(2,1)} copy-done((bf16[4,192,256]{2,1,0:T(8,128)(2,1)}, bf16[4,192,256]{2,1,0:T(8,128)(2,1)S(1)}, u32[]{:S(2)}) %copy-start.2) | copy-done | bytes 393240
  13.5 2.9 %shard_map.86 = (f32[192,256]{1,0:T(8,128)}, bf16[192,256]{1,0:T(8,128)(2,1)}, bf16[192,256]{1,0:T(8,128)(2,1)}, bf16[192,256]{1,0:T(8,128)(2,1)}) custom-call(s32[12]{0:T(128)} %bitcast.34, s32[12]{0:T(128)} %bitcast.36, s32[1]{0:T(128)} %bitcast.26.info_ref, bf16[12,256,256]{2,1,0:T(8,128)(2,1)} %bitcast.28, bf16[4,192,256]{2,1,0:T(8,128)(2,1)} %copy-done.1, ...), custom_call_target="tpu_custom_call" | custom-call | tf_op jit(solution)/shard_map/pallas_call | solution.py:122
  16.3 2.3 %collective-permute-start.4 = (bf16[192,256]{1,0:T(8,128)(2,1)}, bf16[192,256]{1,0:T(8,128)(2,1)S(1)}, u32[]{:S(2)}, u32[]{:S(2)}) collective-permute-start(bf16[192,256]{1,0:T(8,128)(2,1)} %get-tuple-element.9), channel_id=1, source_target_pairs={{0,1},{1,2},{2,3},{3,0},{4,5},{5,6},{6,7},{7,4},{8,9},{9,10},{10,1... | collective-permute-start | bytes 294920 | tf_op jit(solution)/shard_map/ppermute | solution.py:180
  18.7 2.2 %collective-permute-start.5 = (bf16[192,256]{1,0:T(8,128)(2,1)}, bf16[192,256]{1,0:T(8,128)(2,1)S(1)}, u32[]{:S(2)}, u32[]{:S(2)}) collective-permute-start(bf16[192,256]{1,0:T(8,128)(2,1)} %get-tuple-element.10), channel_id=1, source_target_pairs={{0,2},{1,3},{2,0},{3,1},{4,6},{5,7},{6,4},{7,5},{8,10},{9,11},{10,... | collective-permute-start | bytes 294920 | tf_op jit(solution)/shard_map/ppermute | solution.py:180
  20.9 1.1 %collective-permute-start.6 = (bf16[192,256]{1,0:T(8,128)(2,1)}, bf16[192,256]{1,0:T(8,128)(2,1)S(1)}, u32[]{:S(2)}, u32[]{:S(2)}) collective-permute-start(bf16[192,256]{1,0:T(8,128)(2,1)} %get-tuple-element.11), channel_id=1, source_target_pairs={{0,3},{1,0},{2,1},{3,2},{4,7},{5,4},{6,5},{7,6},{8,11},{9,8},{10,9... | collective-permute-start | bytes 294920 | tf_op jit(solution)/shard_map/ppermute | solution.py:180
  22.0 2.3 %collective-permute-done.4 = bf16[192,256]{1,0:T(8,128)(2,1)S(1)} collective-permute-done((bf16[192,256]{1,0:T(8,128)(2,1)}, bf16[192,256]{1,0:T(8,128)(2,1)S(1)}, u32[]{:S(2)}, u32[]{:S(2)}) %collective-permute-start.4) | collective-permute-done | bytes 98336 | tf_op jit(solution)/shard_map/ppermute | solution.py:180
  24.3 3.6 %collective-permute-done.5 = bf16[192,256]{1,0:T(8,128)(2,1)S(1)} collective-permute-done((bf16[192,256]{1,0:T(8,128)(2,1)}, bf16[192,256]{1,0:T(8,128)(2,1)S(1)}, u32[]{:S(2)}, u32[]{:S(2)}) %collective-permute-start.5) | collective-permute-done | bytes 98336 | tf_op jit(solution)/shard_map/ppermute | solution.py:180
  27.9 1.8 %multiply_convert_fusion.1 = (bf16[192,256]{1,0:T(8,128)(2,1)}, f32[192,256]{1,0:T(8,128)S(1)}) fusion(bf16[256,256]{1,0:T(8,128)(2,1)S(1)} %copy-done, bf16[192,256]{1,0:T(8,128)(2,1)S(1)} %collective-permute-done.6, bf16[192,256]{1,0:T(8,128)(2,1)S(1)} %collective-permute-done.5, f32[192,256]{1,0:T(8,128)} %get-tuple-element.8, ...), kind=kOutput, calls=%fused_computation.9 | convolution fusion | flops 25755648 | bytes 917504 | tf_op jit(solution)/shard_map/dot_general | solution.py:18
  29.7 0.2 convolution_convert_fusion.mine_ref
  29.9 3.5 %collective-permute-start.9 = (bf16[192,256]{1,0:T(8,128)(2,1)S(1)}, bf16[192,256]{1,0:T(8,128)(2,1)S(1)}, u32[]{:S(2)}, u32[]{:S(2)}) collective-permute-start(bf16[192,256]{1,0:T(8,128)(2,1)S(1)} %convolution_convert_fusion.mine_ref), channel_id=1, source_target_pairs={{0,3},{1,0},{2,1},{3,2},{4,7},{5,4},{6,5},{7,6},{8,11},{9,8},{10,9... | collective-permute-start | bytes 294920 | tf_op jit(solution)/shard_map/ppermute | solution.py:182
  33.4 0.6 collective-permute-start.8
  34.0 0.1 collective-permute-start.7
  34.1 2.5 %collective-permute-done.9.rest_2_ = bf16[192,256]{1,0:T(8,128)(2,1)S(1)} collective-permute-done((bf16[192,256]{1,0:T(8,128)(2,1)S(1)}, bf16[192,256]{1,0:T(8,128)(2,1)S(1)}, u32[]{:S(2)}, u32[]{:S(2)}) %collective-permute-start.9) | collective-permute-done | bytes 98336 | tf_op jit(solution)/shard_map/ppermute | solution.py:182
  36.6 6.4 %collective-permute-done.8.rest_1_ = bf16[192,256]{1,0:T(8,128)(2,1)S(1)} collective-permute-done((bf16[192,256]{1,0:T(8,128)(2,1)S(1)}, bf16[192,256]{1,0:T(8,128)(2,1)S(1)}, u32[]{:S(2)}, u32[]{:S(2)}) %collective-permute-start.8) | collective-permute-done | bytes 98336 | tf_op jit(solution)/shard_map/ppermute | solution.py:182
  43.0 0.6 %copy-done.5 = bf16[192,256]{1,0:T(8,128)(2,1)} copy-done((bf16[192,256]{1,0:T(8,128)(2,1)}, bf16[192,256]{1,0:T(8,128)(2,1)S(1)}, u32[]{:S(2)}) %copy-start.5) | copy-done | bytes 98328
  43.7 3.2 %shard_map.87 = (f32[4,192,256]{2,1,0:T(8,128)}, bf16[4,192,256]{2,1,0:T(8,128)(2,1)}) custom-call(s32[12]{0:T(128)} %bitcast.35, s32[12]{0:T(128)} %bitcast.37, s32[1]{0:T(128)} %bitcast.27.info_ref, bf16[12,256,256]{2,1,0:T(8,128)(2,1)} %bitcast.29, bf16[192,256]{1,0:T(8,128)(2,1)} %copy-done.3, bf16[192,256]{1,0:T(8,128)(2,1)} %copy-done.6, ...), custom_call_target="tpu_custom_call" | custom-call | tf_op jit(solution)/shard_map/pallas_call | solution.py:140
  46.9 1.9 %collective-permute-done.10 = bf16[4,192,256]{2,1,0:T(8,128)(2,1)S(1)} collective-permute-done((bf16[4,192,256]{2,1,0:T(8,128)(2,1)}, bf16[4,192,256]{2,1,0:T(8,128)(2,1)S(1)}, u32[]{:S(2)}, u32[]{:S(2)}) %collective-permute-start.10) | collective-permute-done | bytes 393248 | tf_op jit(solution)/shard_map/ppermute | solution.py:186
  48.8 1.2 %fusion.6 = (bf16[4,192,256]{2,1,0:T(8,128)(2,1)S(1)}, f32[4,192,256]{2,1,0:T(8,128)S(1)}) fusion(f32[4,192,256]{2,1,0:T(8,128)} %get-tuple-element.12, bf16[4,192,256]{2,1,0:T(8,128)(2,1)S(1)} %collective-permute-done.10), kind=kLoop, calls=%fused_computation.17 | loop fusion | flops 589824 | bytes 2359296 | tf_op jit(solution)/shard_map/convert.2
  50.1 2.7 %collective-permute-start.11 = (bf16[192,256]{1,0:T(8,128)(2,1)S(1)}, bf16[192,256]{1,0:T(8,128)(2,1)S(1)}, u32[]{:S(2)}, u32[]{:S(2)}) collective-permute-start(bf16[192,256]{1,0:T(8,128)(2,1)S(1)} %get-tuple-element.16), channel_id=1, source_target_pairs={{0,8},{4,12},{8,16},{12,20},{16,24},{20,28},{24,0},{28,4},{1,9},{5... | collective-permute-start | bytes 294920 | tf_op jit(solution)/shard_map/ppermute | solution.py:190
  52.7 0.5 collective-permute-start.13
  53.2 2.2 %collective-permute-start.12 = (bf16[192,256]{1,0:T(8,128)(2,1)S(1)}, bf16[192,256]{1,0:T(8,128)(2,1)S(1)}, u32[]{:S(2)}, u32[]{:S(2)}) collective-permute-start(bf16[192,256]{1,0:T(8,128)(2,1)S(1)} %get-tuple-element.18), channel_id=1, source_target_pairs={{0,16},{4,20},{8,24},{12,28},{16,0},{20,4},{24,8},{28,12},{1,17},{... | collective-permute-start | bytes 294920 | tf_op jit(solution)/shard_map/ppermute | solution.py:190
  55.5 1.3 %collective-permute-done.11 = bf16[192,256]{1,0:T(8,128)(2,1)S(1)} collective-permute-done((bf16[192,256]{1,0:T(8,128)(2,1)S(1)}, bf16[192,256]{1,0:T(8,128)(2,1)S(1)}, u32[]{:S(2)}, u32[]{:S(2)}) %collective-permute-start.11) | collective-permute-done | bytes 98336 | tf_op jit(solution)/shard_map/ppermute | solution.py:190
  56.8 2.1 %collective-permute-done.13 = bf16[192,256]{1,0:T(8,128)(2,1)S(1)} collective-permute-done((bf16[192,256]{1,0:T(8,128)(2,1)S(1)}, bf16[192,256]{1,0:T(8,128)(2,1)S(1)}, u32[]{:S(2)}, u32[]{:S(2)}) %collective-permute-start.13) | collective-permute-done | bytes 98336 | tf_op jit(solution)/shard_map/ppermute | solution.py:190
  58.9 0.7 %fusion.3 = bf16[192,256]{1,0:T(8,128)(2,1)} fusion(f32[4,192,256]{2,1,0:T(8,128)S(1)} %get-tuple-element.15, bf16[192,256]{1,0:T(8,128)(2,1)S(1)} %collective-permute-done.13, bf16[192,256]{1,0:T(8,128)(2,1)S(1)} %collective-permute-done.12, bf16[192,256]{1,0:T(8,128)(2,1)S(1)} %collective-permute-done.11), kind=kLoop, calls=%fused_computation.7 | loop fusion | flops 344064 | bytes 589824 | tf_op jit(solution)/shard_map/convert_element_type | solution.py:191
  (20 shorter events, 0.1 us)
Async XLA Ops:
  0.6 27.2 %copy-start = (bf16[256,256]{1,0:T(8,128)(2,1)S(1)}, bf16[256,256]{1,0:T(8,128)(2,1)}, u32[]{:S(2)}) copy-start(bf16[256,256]{1,0:T(8,128)(2,1)} %param.12) | copy-start | bytes 393220
  0.6 7.6 %collective-permute-start = (bf16[192,256]{1,0:T(8,128)(2,1)}, bf16[192,256]{1,0:T(8,128)(2,1)S(1)}, u32[]{:S(2)}, u32[]{:S(2)}) collective-permute-start(bf16[192,256]{1,0:T(8,128)(2,1)} %param.7), channel_id=1, source_target_pairs={{0,8},{4,12},{8,16},{12,20},{16,24},{20,28},{24,0},{28,4},{1,9},{5... | collective-permute-start | bytes 294920 | tf_op jit(solution)/shard_map/ppermute | solution.py:174
  3.7 6.3 %collective-permute-start.2 = (bf16[192,256]{1,0:T(8,128)(2,1)}, bf16[192,256]{1,0:T(8,128)(2,1)S(1)}, u32[]{:S(2)}, u32[]{:S(2)}) collective-permute-start(bf16[192,256]{1,0:T(8,128)(2,1)} %param.7), channel_id=1, source_target_pairs={{0,24},{4,28},{8,0},{12,4},{16,8},{20,12},{24,16},{28,20},{1,25},{... | collective-permute-start | bytes 294920 | tf_op jit(solution)/shard_map/ppermute | solution.py:174
  4.7 5.3 %collective-permute-start.1 = (bf16[192,256]{1,0:T(8,128)(2,1)}, bf16[192,256]{1,0:T(8,128)(2,1)S(1)}, u32[]{:S(2)}, u32[]{:S(2)}) collective-permute-start(bf16[192,256]{1,0:T(8,128)(2,1)} %param.7), channel_id=1, source_target_pairs={{0,16},{4,20},{8,24},{12,28},{16,0},{20,4},{24,8},{28,12},{1,17},{... | collective-permute-start | bytes 294920 | tf_op jit(solution)/shard_map/ppermute | solution.py:174
  10.9 1.8 %copy-start.1 = (bf16[4,192,256]{2,1,0:T(8,128)(2,1)}, bf16[4,192,256]{2,1,0:T(8,128)(2,1)S(1)}, u32[]{:S(2)}) copy-start(bf16[4,192,256]{2,1,0:T(8,128)(2,1)S(1)} %pad_maximum_fusion.near_ref) | copy-start | bytes 1179652
  10.9 1.8 %collective-permute-start.3 = (bf16[4,192,256]{2,1,0:T(8,128)(2,1)S(1)}, bf16[4,192,256]{2,1,0:T(8,128)(2,1)S(1)}, u32[]{:S(2)}, u32[]{:S(2)}) collective-permute-start(bf16[4,192,256]{2,1,0:T(8,128)(2,1)S(1)} %pad_maximum_fusion.near_ref), channel_id=1, source_target_pairs={{0,4},{4,0},{8,12},{12,8},{16,20},{20,16},{24,28},{28,24},{1,5},{5... | collective-permute-start | bytes 1179656 | tf_op jit(solution)/shard_map/ppermute | solution.py:175
  12.7 0.7 %copy-start.2 = (bf16[4,192,256]{2,1,0:T(8,128)(2,1)}, bf16[4,192,256]{2,1,0:T(8,128)(2,1)S(1)}, u32[]{:S(2)}) copy-start(bf16[4,192,256]{2,1,0:T(8,128)(2,1)S(1)} %collective-permute-done.3.far_ref) | copy-start | bytes 1179652
  13.5 16.2 %copy-start.7 = (bf16[192,256]{1,0:T(8,128)(2,1)S(1)}, bf16[192,256]{1,0:T(8,128)(2,1)}, u32[]{:S(2)}) copy-start(bf16[192,256]{1,0:T(8,128)(2,1)} %param.13) | copy-start | bytes 294916
  16.3 7.9 %collective-permute-start.4 = (bf16[192,256]{1,0:T(8,128)(2,1)}, bf16[192,256]{1,0:T(8,128)(2,1)S(1)}, u32[]{:S(2)}, u32[]{:S(2)}) collective-permute-start(bf16[192,256]{1,0:T(8,128)(2,1)} %get-tuple-element.9), channel_id=1, source_target_pairs={{0,1},{1,2},{2,3},{3,0},{4,5},{5,6},{6,7},{7,4},{8,9},{9,10},{10,1... | collective-permute-start | bytes 294920 | tf_op jit(solution)/shard_map/ppermute | solution.py:180
  18.7 9.2 %collective-permute-start.5 = (bf16[192,256]{1,0:T(8,128)(2,1)}, bf16[192,256]{1,0:T(8,128)(2,1)S(1)}, u32[]{:S(2)}, u32[]{:S(2)}) collective-permute-start(bf16[192,256]{1,0:T(8,128)(2,1)} %get-tuple-element.10), channel_id=1, source_target_pairs={{0,2},{1,3},{2,0},{3,1},{4,6},{5,7},{6,4},{7,5},{8,10},{9,11},{10,... | collective-permute-start | bytes 294920 | tf_op jit(solution)/shard_map/ppermute | solution.py:180
  20.9 7.0 %collective-permute-start.6 = (bf16[192,256]{1,0:T(8,128)(2,1)}, bf16[192,256]{1,0:T(8,128)(2,1)S(1)}, u32[]{:S(2)}, u32[]{:S(2)}) collective-permute-start(bf16[192,256]{1,0:T(8,128)(2,1)} %get-tuple-element.11), channel_id=1, source_target_pairs={{0,3},{1,0},{2,1},{3,2},{4,7},{5,4},{6,5},{7,6},{8,11},{9,8},{10,9... | collective-permute-start | bytes 294920 | tf_op jit(solution)/shard_map/ppermute | solution.py:180
  29.9 13.1 %copy-start.3 = (bf16[192,256]{1,0:T(8,128)(2,1)}, bf16[192,256]{1,0:T(8,128)(2,1)S(1)}, u32[]{:S(2)}) copy-start(bf16[192,256]{1,0:T(8,128)(2,1)S(1)} %convolution_convert_fusion.mine_ref) | copy-start | bytes 294916
  29.9 6.7 %collective-permute-start.9 = (bf16[192,256]{1,0:T(8,128)(2,1)S(1)}, bf16[192,256]{1,0:T(8,128)(2,1)S(1)}, u32[]{:S(2)}, u32[]{:S(2)}) collective-permute-start(bf16[192,256]{1,0:T(8,128)(2,1)S(1)} %convolution_convert_fusion.mine_ref), channel_id=1, source_target_pairs={{0,3},{1,0},{2,1},{3,2},{4,7},{5,4},{6,5},{7,6},{8,11},{9,8},{10,9... | collective-permute-start | bytes 294920 | tf_op jit(solution)/shard_map/ppermute | solution.py:182
  33.4 9.6 %collective-permute-start.8 = (bf16[192,256]{1,0:T(8,128)(2,1)S(1)}, bf16[192,256]{1,0:T(8,128)(2,1)S(1)}, u32[]{:S(2)}, u32[]{:S(2)}) collective-permute-start(bf16[192,256]{1,0:T(8,128)(2,1)S(1)} %convolution_convert_fusion.mine_ref), channel_id=1, source_target_pairs={{0,2},{1,3},{2,0},{3,1},{4,6},{5,7},{6,4},{7,5},{8,10},{9,11},{10,... | collective-permute-start | bytes 294920 | tf_op jit(solution)/shard_map/ppermute | solution.py:182
  34.0 9.0 %collective-permute-start.7 = (bf16[192,256]{1,0:T(8,128)(2,1)S(1)}, bf16[192,256]{1,0:T(8,128)(2,1)S(1)}, u32[]{:S(2)}, u32[]{:S(2)}) collective-permute-start(bf16[192,256]{1,0:T(8,128)(2,1)S(1)} %convolution_convert_fusion.mine_ref), channel_id=1, source_target_pairs={{0,1},{1,2},{2,3},{3,0},{4,5},{5,6},{6,7},{7,4},{8,9},{9,10},{10,1... | collective-permute-start | bytes 294920 | tf_op jit(solution)/shard_map/ppermute | solution.py:182
  36.6 6.4 %copy-start.4 = (bf16[192,256]{1,0:T(8,128)(2,1)}, bf16[192,256]{1,0:T(8,128)(2,1)S(1)}, u32[]{:S(2)}) copy-start(bf16[192,256]{1,0:T(8,128)(2,1)S(1)} %collective-permute-done.9.rest_2_) | copy-start | bytes 294916
  43.0 0.6 %copy-start.5 = (bf16[192,256]{1,0:T(8,128)(2,1)}, bf16[192,256]{1,0:T(8,128)(2,1)S(1)}, u32[]{:S(2)}) copy-start(bf16[192,256]{1,0:T(8,128)(2,1)S(1)} %collective-permute-done.8.rest_1_) | copy-start | bytes 294916
  43.0 0.7 %copy-start.6 = (bf16[192,256]{1,0:T(8,128)(2,1)}, bf16[192,256]{1,0:T(8,128)(2,1)S(1)}, u32[]{:S(2)}) copy-start(bf16[192,256]{1,0:T(8,128)(2,1)S(1)} %collective-permute-done.7.rest_0_) | copy-start | bytes 294916
  46.9 1.9 %collective-permute-start.10 = (bf16[4,192,256]{2,1,0:T(8,128)(2,1)}, bf16[4,192,256]{2,1,0:T(8,128)(2,1)S(1)}, u32[]{:S(2)}, u32[]{:S(2)}) collective-permute-start(bf16[4,192,256]{2,1,0:T(8,128)(2,1)} %get-tuple-element.13), channel_id=1, source_target_pairs={{0,4},{4,0},{8,12},{12,8},{16,20},{20,16},{24,28},{28,24},{1,5},{5... | collective-permute-start | bytes 1179656 | tf_op jit(solution)/shard_map/ppermute | solution.py:186
  50.1 6.7 %collective-permute-start.11 = (bf16[192,256]{1,0:T(8,128)(2,1)S(1)}, bf16[192,256]{1,0:T(8,128)(2,1)S(1)}, u32[]{:S(2)}, u32[]{:S(2)}) collective-permute-start(bf16[192,256]{1,0:T(8,128)(2,1)S(1)} %get-tuple-element.16), channel_id=1, source_target_pairs={{0,8},{4,12},{8,16},{12,20},{16,24},{20,28},{24,0},{28,4},{1,9},{5... | collective-permute-start | bytes 294920 | tf_op jit(solution)/shard_map/ppermute | solution.py:190
  52.7 6.2 %collective-permute-start.13 = (bf16[192,256]{1,0:T(8,128)(2,1)S(1)}, bf16[192,256]{1,0:T(8,128)(2,1)S(1)}, u32[]{:S(2)}, u32[]{:S(2)}) collective-permute-start(bf16[192,256]{1,0:T(8,128)(2,1)S(1)} %get-tuple-element.17), channel_id=1, source_target_pairs={{0,24},{4,28},{8,0},{12,4},{16,8},{20,12},{24,16},{28,20},{1,25},{... | collective-permute-start | bytes 294920 | tf_op jit(solution)/shard_map/ppermute | solution.py:190
  53.2 5.7 %collective-permute-start.12 = (bf16[192,256]{1,0:T(8,128)(2,1)S(1)}, bf16[192,256]{1,0:T(8,128)(2,1)S(1)}, u32[]{:S(2)}, u32[]{:S(2)}) collective-permute-start(bf16[192,256]{1,0:T(8,128)(2,1)S(1)} %get-tuple-element.18), channel_id=1, source_target_pairs={{0,16},{4,20},{8,24},{12,28},{16,0},{20,4},{24,8},{28,12},{1,17},{... | collective-permute-start | bytes 294920 | tf_op jit(solution)/shard_map/ppermute | solution.py:190

commit v12 on v11

--- a/solution.py
+++ b/solution.py
@@ -25,6 +25,14 @@
 UNROLL = 4
 
 
+def peer(i, step, n):
+    return i ^ step if n & (n - 1) == 0 else (i + step) % n
+
+
+def source(i, step, n):
+    return i ^ step if n & (n - 1) == 0 else (i - step + n) % n
+
+
 def run_slots(count, product, place):
     def group(g, carry):
         base = g * UNROLL
@@ -46,7 +54,7 @@
     n = len(send_refs) + 1
     own_ref[...] = acc_ref[pl.ds(pl.multiple_of(me * chunk, 8), chunk), :]
     for shift in range(1, n):
-        start = pl.multiple_of(((me + shift) % n) * chunk, 8)
+        start = pl.multiple_of(peer(me, shift, n) * chunk, 8)
         send_refs[shift - 1][...] = acc_ref[pl.ds(start, chunk), :].astype(send_refs[shift - 1].dtype)
 
 
@@ -57,7 +65,7 @@
     me = lax.axis_index("row")
     core, chip = me % 2, me // 2
     for shift in range(chips):
-        owner = (chip - shift + chips) % chips
+        owner = source(chip, shift, chips)
         near = pl.multiple_of((owner * 2 + core) * piece, 16)
         far = pl.multiple_of((owner * 2 + 1 - core) * piece, 16)
         f_ref[pl.ds(near, piece), :] = near_ref[shift]
@@ -84,7 +92,7 @@
     me = lax.axis_index("col")
     block_ref[pl.ds(pl.multiple_of(me * chunk, 16), chunk), :] = mine_ref[...]
     for shift in range(1, n):
-        start = pl.multiple_of(((me - shift + n) % n) * chunk, 16)
+        start = pl.multiple_of(source(me, shift, n) * chunk, 16)
         block_ref[pl.ds(start, chunk), :] = got_refs[shift - 1][...]
     acc_ref[...] = jnp.zeros_like(acc_ref)
 
@@ -104,7 +112,7 @@
     me_row = lax.axis_index("row")
     core, chip = me_row % 2, me_row // 2
     for shift in range(chips):
-        owner = (chip + shift) % chips
+        owner = peer(chip, shift, chips)
         near_ref[shift] = acc_ref[pl.ds(pl.multiple_of((owner * 2 + core) * piece, 8), piece), :]
         far_ref[shift] = acc_ref[pl.ds(pl.multiple_of((owner * 2 + 1 - core) * piece, 8), piece), :].astype(
             far_ref.dtype
@@ -151,12 +159,12 @@
 
 def shifts(axis):
     n = lax.axis_size(axis)
-    return [[(i, (i + shift) % n) for i in range(n)] for shift in range(1, n)]
+    return [[(i, peer(i, shift, n)) for i in range(n)] for shift in range(1, n)]
 
 
 def chip_shifts(n):
     chips = n // 2
-    return [[(i, ((i // 2 + shift) % chips) * 2 + i % 2) for i in range(n)] for shift in range(1, chips)]
+    return [[(i, peer(i // 2, shift, chips) * 2 + i % 2) for i in range(n)] for shift in range(1, chips)]
 
 
 def partner(n):

time: 59.8 us -> 61.1 us (1.022)
  starting transfers between devices: 21.2 us -> 17 us
  waiting for transfers between devices: 24.6 us -> 28.3 us
  Pallas kernels: 6.05 us -> 7.39 us
    ppermute x3, waiting for transfers between devices: 3.36 us -> 6.08 us  [on_device(): lax.ppermute(features, 'row', perm)]
    ppermute x3, starting transfers between devices: 5.38 us -> 3.55 us  [on_device(): total_g = total_g + lax.ppermute(piece, 'row', perm).astype(jnp.float32)]
    ppermute x3, waiting for transfers between devices: 8.95 us -> 7.23 us  [on_device(): got = [lax.ppermute(pulled_own, 'col', perm) for perm in shifts('col')]]
    ppermute x3, waiting for transfers between devices: 5.89 us -> 7.42 us  [on_device(): total = total + lax.ppermute(send[shift], 'col', perm).astype(jnp.float32)]
    ppermute x3, starting transfers between devices: 5.97 us -> 4.57 us  [on_device(): lax.ppermute(features, 'row', perm)]
    ppermute x3, starting transfers between devices: 5.63 us -> 4.39 us  [on_device(): total = total + lax.ppermute(send[shift], 'col', perm).astype(jnp.float32)]
    ppermute x3, waiting for transfers between devices: 3.46 us -> 4.64 us  [on_device(): total_g = total_g + lax.ppermute(piece, 'row', perm).astype(jnp.float32)]
    pallas_call x1, Pallas kernels: 3.17 us -> 3.86 us  [tile_products_t(): pl.pallas_call(functools.partial(backward_kernel, len(got) + 1), out_shap...]
  transfers between devices with their start and end apart: 14 -> 14, of which waited for: 10 -> 12; matrix products, arithmetic and copies ran while one was open for 0% -> 0% of each run, Pallas kernels for 0% -> 0%
where the time goes in v12:
time: 61.1 us; the launch traced here: 60.5 us
  waiting for transfers between devices  28.3 us (46%)
  starting transfers between devices  17 us (28%)
  Pallas kernels  7.39 us (12%)
  other arithmetic  2.87 us (5%)
  matrix products  2.01 us (3%)
  local copies, waits for them, and re-layouts  1.46 us (2%)
  between operations  1.39 us (2%)
    ppermute x3, waiting for transfers between devices, on_device(): total = total + lax.ppermute(send[shift], 'col', perm).astype(jnp.float32)  7.42 us
    ppermute x3, waiting for transfers between devices, on_device(): got = [lax.ppermute(pulled_own, 'col', perm) for perm in shifts('col')]  7.23 us
    ppermute x3, waiting for transfers between devices, on_device(): lax.ppermute(features, 'row', perm)  6.08 us
    ppermute x3, waiting for transfers between devices, on_device(): total_g = total_g + lax.ppermute(piece, 'row', perm).astype(jnp.float32)  4.64 us
    ppermute x3, starting transfers between devices, on_device(): lax.ppermute(features, 'row', perm)  4.57 us
    ppermute x3, starting transfers between devices, on_device(): got = [lax.ppermute(pulled_own, 'col', perm) for perm in shifts('col')]  4.45 us
    ppermute x3, starting transfers between devices, on_device(): total = total + lax.ppermute(send[shift], 'col', perm).astype(jnp.float32)  4.39 us
    pallas_call x1, Pallas kernels, tile_products_t(): pl.pallas_call(functools.partial(backward_kernel, len(got) + 1), out_shap...  3.86 us
  transfers between devices with their start and end apart: 14, of which 12 were waited for; matrix products, arithmetic and copies ran while one was open for 0% of the time, Pallas kernels for 0%

profile of v12, /device:TPU:0, one launch (start us, length us, event | category | flops | bytes accessed | tf_op | source)
XLA Modules:
  0.0 60.5 jit_solution(2515567097553822183)
XLA Ops:
  0.6 3.0 %collective-permute-start = (bf16[192,256]{1,0:T(8,128)(2,1)}, bf16[192,256]{1,0:T(8,128)(2,1)S(1)}, u32[]{:S(2)}, u32[]{:S(2)}) collective-permute-start(bf16[192,256]{1,0:T(8,128)(2,1)} %param.7), channel_id=1, source_target_pairs={{0,8},{4,12},{8,0},{12,4},{16,24},{20,28},{24,16},{28,20},{1,9},{5... | collective-permute-start | bytes 294920 | tf_op jit(solution)/shard_map/ppermute | solution.py:182
  3.7 1.5 %collective-permute-start.2 = (bf16[192,256]{1,0:T(8,128)(2,1)}, bf16[192,256]{1,0:T(8,128)(2,1)S(1)}, u32[]{:S(2)}, u32[]{:S(2)}) collective-permute-start(bf16[192,256]{1,0:T(8,128)(2,1)} %param.7), channel_id=1, source_target_pairs={{0,24},{4,28},{8,16},{12,20},{16,8},{20,12},{24,0},{28,4},{1,25},{... | collective-permute-start | bytes 294920 | tf_op jit(solution)/shard_map/ppermute | solution.py:182
  5.2 1.9 %collective-permute-done = bf16[192,256]{1,0:T(8,128)(2,1)S(1)} collective-permute-done((bf16[192,256]{1,0:T(8,128)(2,1)}, bf16[192,256]{1,0:T(8,128)(2,1)S(1)}, u32[]{:S(2)}, u32[]{:S(2)}) %collective-permute-start) | collective-permute-done | bytes 98336 | tf_op jit(solution)/shard_map/ppermute | solution.py:182
  7.1 3.1 %collective-permute-done.2 = bf16[192,256]{1,0:T(8,128)(2,1)S(1)} collective-permute-done((bf16[192,256]{1,0:T(8,128)(2,1)}, bf16[192,256]{1,0:T(8,128)(2,1)S(1)}, u32[]{:S(2)}, u32[]{:S(2)}) %collective-permute-start.2) | collective-permute-done | bytes 98336 | tf_op jit(solution)/shard_map/ppermute | solution.py:182
  10.2 1.1 %collective-permute-done.1 = bf16[192,256]{1,0:T(8,128)(2,1)S(1)} collective-permute-done((bf16[192,256]{1,0:T(8,128)(2,1)}, bf16[192,256]{1,0:T(8,128)(2,1)S(1)}, u32[]{:S(2)}, u32[]{:S(2)}) %collective-permute-start.1) | collective-permute-done | bytes 98336 | tf_op jit(solution)/shard_map/ppermute | solution.py:182
  11.3 0.9 %pad_maximum_fusion.near_ref = bf16[4,192,256]{2,1,0:T(8,128)(2,1)S(1)} fusion(bf16[1,192,256]{2,1,0:T(8,128)(2,1)S(1)} %bitcast.32, bf16[1,192,256]{2,1,0:T(8,128)(2,1)S(1)} %bitcast.33, bf16[1,192,256]{2,1,0:T(8,128)(2,1)S(1)} %bitcast.31, bf16[1,192,256]{2,1,0:T(8,128)(2,1)} %bitcast.30), kind=kLoop, calls=%fused_computation.2 | loop fusion | flops 589824 | bytes 786432 | tf_op jit(solution)/shard_map/stack | solution.py:182
  13.0 1.0 %collective-permute-done.3.far_ref = bf16[4,192,256]{2,1,0:T(8,128)(2,1)S(1)} collective-permute-done((bf16[4,192,256]{2,1,0:T(8,128)(2,1)S(1)}, bf16[4,192,256]{2,1,0:T(8,128)(2,1)S(1)}, u32[]{:S(2)}, u32[]{:S(2)}) %collective-permute-start.3) | collective-permute-done | bytes 393248 | tf_op jit(solution)/shard_map/ppermute | solution.py:183
  14.1 0.7 %copy-done.2 = bf16[4,192,256]{2,1,0:T(8,128)(2,1)} copy-done((bf16[4,192,256]{2,1,0:T(8,128)(2,1)}, bf16[4,192,256]{2,1,0:T(8,128)(2,1)S(1)}, u32[]{:S(2)}) %copy-start.2) | copy-done | bytes 393240
  14.8 3.5 %shard_map.86 = (f32[192,256]{1,0:T(8,128)}, bf16[192,256]{1,0:T(8,128)(2,1)}, bf16[192,256]{1,0:T(8,128)(2,1)}, bf16[192,256]{1,0:T(8,128)(2,1)}) custom-call(s32[12]{0:T(128)} %bitcast.34, s32[12]{0:T(128)} %bitcast.36, s32[1]{0:T(128)} %bitcast.26.info_ref, bf16[12,256,256]{2,1,0:T(8,128)(2,1)} %bitcast.28, bf16[4,192,256]{2,1,0:T(8,128)(2,1)} %copy-done.1, ...), custom_call_target="tpu_custom_call" | custom-call | tf_op jit(solution)/shard_map/pallas_call | solution.py:130
  18.3 0.9 %collective-permute-start.4 = (bf16[192,256]{1,0:T(8,128)(2,1)}, bf16[192,256]{1,0:T(8,128)(2,1)S(1)}, u32[]{:S(2)}, u32[]{:S(2)}) collective-permute-start(bf16[192,256]{1,0:T(8,128)(2,1)} %get-tuple-element.9), channel_id=1, source_target_pairs={{0,1},{1,0},{2,3},{3,2},{4,5},{5,4},{6,7},{7,6},{8,9},{9,8},{10,11... | collective-permute-start | bytes 294920 | tf_op jit(solution)/shard_map/ppermute | solution.py:188
  19.2 2.8 %collective-permute-start.5 = (bf16[192,256]{1,0:T(8,128)(2,1)}, bf16[192,256]{1,0:T(8,128)(2,1)S(1)}, u32[]{:S(2)}, u32[]{:S(2)}) collective-permute-start(bf16[192,256]{1,0:T(8,128)(2,1)} %get-tuple-element.10), channel_id=1, source_target_pairs={{0,2},{1,3},{2,0},{3,1},{4,6},{5,7},{6,4},{7,5},{8,10},{9,11},{10,... | collective-permute-start | bytes 294920 | tf_op jit(solution)/shard_map/ppermute | solution.py:188
  22.0 0.7 %collective-permute-start.6 = (bf16[192,256]{1,0:T(8,128)(2,1)}, bf16[192,256]{1,0:T(8,128)(2,1)S(1)}, u32[]{:S(2)}, u32[]{:S(2)}) collective-permute-start(bf16[192,256]{1,0:T(8,128)(2,1)} %get-tuple-element.11), channel_id=1, source_target_pairs={{0,3},{1,2},{2,1},{3,0},{4,7},{5,6},{6,5},{7,4},{8,11},{9,10},{10,... | collective-permute-start | bytes 294920 | tf_op jit(solution)/shard_map/ppermute | solution.py:188
  22.7 0.4 collective-permute-done.4
  23.1 7.0 %collective-permute-done.5 = bf16[192,256]{1,0:T(8,128)(2,1)S(1)} collective-permute-done((bf16[192,256]{1,0:T(8,128)(2,1)}, bf16[192,256]{1,0:T(8,128)(2,1)S(1)}, u32[]{:S(2)}, u32[]{:S(2)}) %collective-permute-start.5) | collective-permute-done | bytes 98336 | tf_op jit(solution)/shard_map/ppermute | solution.py:188
  30.1 1.8 %multiply_convert_fusion.1 = (bf16[192,256]{1,0:T(8,128)(2,1)}, f32[192,256]{1,0:T(8,128)S(1)}) fusion(bf16[256,256]{1,0:T(8,128)(2,1)S(1)} %copy-done, bf16[192,256]{1,0:T(8,128)(2,1)S(1)} %collective-permute-done.6, bf16[192,256]{1,0:T(8,128)(2,1)S(1)} %collective-permute-done.5, f32[192,256]{1,0:T(8,128)} %get-tuple-element.8, ...), kind=kOutput, calls=%fused_computation.9 | convolution fusion | flops 25755648 | bytes 917504 | tf_op jit(solution)/shard_map/dot_general | solution.py:18
  31.9 0.2 convolution_convert_fusion.mine_ref
  32.2 2.9 %collective-permute-start.9 = (bf16[192,256]{1,0:T(8,128)(2,1)S(1)}, bf16[192,256]{1,0:T(8,128)(2,1)S(1)}, u32[]{:S(2)}, u32[]{:S(2)}) collective-permute-start(bf16[192,256]{1,0:T(8,128)(2,1)S(1)} %convolution_convert_fusion.mine_ref), channel_id=1, source_target_pairs={{0,3},{1,2},{2,1},{3,0},{4,7},{5,6},{6,5},{7,4},{8,11},{9,10},{10,... | collective-permute-start | bytes 294920 | tf_op jit(solution)/shard_map/ppermute | solution.py:190
  35.1 0.7 %collective-permute-start.8 = (bf16[192,256]{1,0:T(8,128)(2,1)S(1)}, bf16[192,256]{1,0:T(8,128)(2,1)S(1)}, u32[]{:S(2)}, u32[]{:S(2)}) collective-permute-start(bf16[192,256]{1,0:T(8,128)(2,1)S(1)} %convolution_convert_fusion.mine_ref), channel_id=1, source_target_pairs={{0,2},{1,3},{2,0},{3,1},{4,6},{5,7},{6,4},{7,5},{8,10},{9,11},{10,... | collective-permute-start | bytes 294920 | tf_op jit(solution)/shard_map/ppermute | solution.py:190
  35.7 0.9 %collective-permute-start.7 = (bf16[192,256]{1,0:T(8,128)(2,1)S(1)}, bf16[192,256]{1,0:T(8,128)(2,1)S(1)}, u32[]{:S(2)}, u32[]{:S(2)}) collective-permute-start(bf16[192,256]{1,0:T(8,128)(2,1)S(1)} %convolution_convert_fusion.mine_ref), channel_id=1, source_target_pairs={{0,1},{1,0},{2,3},{3,2},{4,5},{5,4},{6,7},{7,6},{8,9},{9,8},{10,11... | collective-permute-start | bytes 294920 | tf_op jit(solution)/shard_map/ppermute | solution.py:190
  36.6 2.6 %collective-permute-done.9.rest_2_ = bf16[192,256]{1,0:T(8,128)(2,1)S(1)} collective-permute-done((bf16[192,256]{1,0:T(8,128)(2,1)S(1)}, bf16[192,256]{1,0:T(8,128)(2,1)S(1)}, u32[]{:S(2)}, u32[]{:S(2)}) %collective-permute-start.9) | collective-permute-done | bytes 98336 | tf_op jit(solution)/shard_map/ppermute | solution.py:190
  39.2 4.6 %collective-permute-done.8.rest_1_ = bf16[192,256]{1,0:T(8,128)(2,1)S(1)} collective-permute-done((bf16[192,256]{1,0:T(8,128)(2,1)S(1)}, bf16[192,256]{1,0:T(8,128)(2,1)S(1)}, u32[]{:S(2)}, u32[]{:S(2)}) %collective-permute-start.8) | collective-permute-done | bytes 98336 | tf_op jit(solution)/shard_map/ppermute | solution.py:190
  43.9 0.6 %copy-done.5 = bf16[192,256]{1,0:T(8,128)(2,1)} copy-done((bf16[192,256]{1,0:T(8,128)(2,1)}, bf16[192,256]{1,0:T(8,128)(2,1)S(1)}, u32[]{:S(2)}) %copy-start.5) | copy-done | bytes 98328
  44.5 3.9 %shard_map.87 = (f32[4,192,256]{2,1,0:T(8,128)}, bf16[4,192,256]{2,1,0:T(8,128)(2,1)}) custom-call(s32[12]{0:T(128)} %bitcast.35, s32[12]{0:T(128)} %bitcast.37, s32[1]{0:T(128)} %bitcast.27.info_ref, bf16[12,256,256]{2,1,0:T(8,128)(2,1)} %bitcast.29, bf16[192,256]{1,0:T(8,128)(2,1)} %copy-done.3, bf16[192,256]{1,0:T(8,128)(2,1)} %copy-done.6, ...), custom_call_target="tpu_custom_call" | custom-call | tf_op jit(solution)/shard_map/pallas_call | solution.py:148
  48.4 1.9 %collective-permute-done.10 = bf16[4,192,256]{2,1,0:T(8,128)(2,1)S(1)} collective-permute-done((bf16[4,192,256]{2,1,0:T(8,128)(2,1)}, bf16[4,192,256]{2,1,0:T(8,128)(2,1)S(1)}, u32[]{:S(2)}, u32[]{:S(2)}) %collective-permute-start.10) | collective-permute-done | bytes 393248 | tf_op jit(solution)/shard_map/ppermute | solution.py:194
  50.3 1.2 %fusion.6 = (bf16[4,192,256]{2,1,0:T(8,128)(2,1)S(1)}, f32[4,192,256]{2,1,0:T(8,128)S(1)}) fusion(f32[4,192,256]{2,1,0:T(8,128)} %get-tuple-element.12, bf16[4,192,256]{2,1,0:T(8,128)(2,1)S(1)} %collective-permute-done.10), kind=kLoop, calls=%fused_computation.17 | loop fusion | flops 589824 | bytes 2359296 | tf_op jit(solution)/shard_map/convert.2
  51.6 1.0 %collective-permute-start.11 = (bf16[192,256]{1,0:T(8,128)(2,1)S(1)}, bf16[192,256]{1,0:T(8,128)(2,1)S(1)}, u32[]{:S(2)}, u32[]{:S(2)}) collective-permute-start(bf16[192,256]{1,0:T(8,128)(2,1)S(1)} %get-tuple-element.16), channel_id=1, source_target_pairs={{0,8},{4,12},{8,0},{12,4},{16,24},{20,28},{24,16},{28,20},{1,9},{5... | collective-permute-start | bytes 294920 | tf_op jit(solution)/shard_map/ppermute | solution.py:198
  52.6 0.4 collective-permute-start.13
  53.0 2.2 %collective-permute-start.12 = (bf16[192,256]{1,0:T(8,128)(2,1)S(1)}, bf16[192,256]{1,0:T(8,128)(2,1)S(1)}, u32[]{:S(2)}, u32[]{:S(2)}) collective-permute-start(bf16[192,256]{1,0:T(8,128)(2,1)S(1)} %get-tuple-element.18), channel_id=1, source_target_pairs={{0,16},{4,20},{8,24},{12,28},{16,0},{20,4},{24,8},{28,12},{1,17},{... | collective-permute-start | bytes 294920 | tf_op jit(solution)/shard_map/ppermute | solution.py:198
  55.2 2.2 %collective-permute-done.11 = bf16[192,256]{1,0:T(8,128)(2,1)S(1)} collective-permute-done((bf16[192,256]{1,0:T(8,128)(2,1)S(1)}, bf16[192,256]{1,0:T(8,128)(2,1)S(1)}, u32[]{:S(2)}, u32[]{:S(2)}) %collective-permute-start.11) | collective-permute-done | bytes 98336 | tf_op jit(solution)/shard_map/ppermute | solution.py:198
  57.3 0.8 %collective-permute-done.13 = bf16[192,256]{1,0:T(8,128)(2,1)S(1)} collective-permute-done((bf16[192,256]{1,0:T(8,128)(2,1)S(1)}, bf16[192,256]{1,0:T(8,128)(2,1)S(1)}, u32[]{:S(2)}, u32[]{:S(2)}) %collective-permute-start.13) | collective-permute-done | bytes 98336 | tf_op jit(solution)/shard_map/ppermute | solution.py:198
  58.1 1.7 %collective-permute-done.12 = bf16[192,256]{1,0:T(8,128)(2,1)S(1)} collective-permute-done((bf16[192,256]{1,0:T(8,128)(2,1)S(1)}, bf16[192,256]{1,0:T(8,128)(2,1)S(1)}, u32[]{:S(2)}, u32[]{:S(2)}) %collective-permute-start.12) | collective-permute-done | bytes 98336 | tf_op jit(solution)/shard_map/ppermute | solution.py:198
  59.8 0.7 %fusion.3 = bf16[192,256]{1,0:T(8,128)(2,1)} fusion(f32[4,192,256]{2,1,0:T(8,128)S(1)} %get-tuple-element.15, bf16[192,256]{1,0:T(8,128)(2,1)S(1)} %collective-permute-done.13, bf16[192,256]{1,0:T(8,128)(2,1)S(1)} %collective-permute-done.12, bf16[192,256]{1,0:T(8,128)(2,1)S(1)} %collective-permute-done.11), kind=kLoop, calls=%fused_computation.7 | loop fusion | flops 344064 | bytes 589824 | tf_op jit(solution)/shard_map/convert_element_type | solution.py:199
  (20 shorter events, 0.2 us)
Async XLA Ops:
  0.6 29.5 %copy-start = (bf16[256,256]{1,0:T(8,128)(2,1)S(1)}, bf16[256,256]{1,0:T(8,128)(2,1)}, u32[]{:S(2)}) copy-start(bf16[256,256]{1,0:T(8,128)(2,1)} %param.12) | copy-start | bytes 393220
  0.6 6.5 %collective-permute-start = (bf16[192,256]{1,0:T(8,128)(2,1)}, bf16[192,256]{1,0:T(8,128)(2,1)S(1)}, u32[]{:S(2)}, u32[]{:S(2)}) collective-permute-start(bf16[192,256]{1,0:T(8,128)(2,1)} %param.7), channel_id=1, source_target_pairs={{0,8},{4,12},{8,0},{12,4},{16,24},{20,28},{24,16},{28,20},{1,9},{5... | collective-permute-start | bytes 294920 | tf_op jit(solution)/shard_map/ppermute | solution.py:182
  3.7 6.5 %collective-permute-start.2 = (bf16[192,256]{1,0:T(8,128)(2,1)}, bf16[192,256]{1,0:T(8,128)(2,1)S(1)}, u32[]{:S(2)}, u32[]{:S(2)}) collective-permute-start(bf16[192,256]{1,0:T(8,128)(2,1)} %param.7), channel_id=1, source_target_pairs={{0,24},{4,28},{8,16},{12,20},{16,8},{20,12},{24,0},{28,4},{1,25},{... | collective-permute-start | bytes 294920 | tf_op jit(solution)/shard_map/ppermute | solution.py:182
  5.2 6.1 %collective-permute-start.1 = (bf16[192,256]{1,0:T(8,128)(2,1)}, bf16[192,256]{1,0:T(8,128)(2,1)S(1)}, u32[]{:S(2)}, u32[]{:S(2)}) collective-permute-start(bf16[192,256]{1,0:T(8,128)(2,1)} %param.7), channel_id=1, source_target_pairs={{0,16},{4,20},{8,24},{12,28},{16,0},{20,4},{24,8},{28,12},{1,17},{... | collective-permute-start | bytes 294920 | tf_op jit(solution)/shard_map/ppermute | solution.py:182
  12.3 1.8 %copy-start.1 = (bf16[4,192,256]{2,1,0:T(8,128)(2,1)}, bf16[4,192,256]{2,1,0:T(8,128)(2,1)S(1)}, u32[]{:S(2)}) copy-start(bf16[4,192,256]{2,1,0:T(8,128)(2,1)S(1)} %pad_maximum_fusion.near_ref) | copy-start | bytes 1179652
  12.3 1.8 %collective-permute-start.3 = (bf16[4,192,256]{2,1,0:T(8,128)(2,1)S(1)}, bf16[4,192,256]{2,1,0:T(8,128)(2,1)S(1)}, u32[]{:S(2)}, u32[]{:S(2)}) collective-permute-start(bf16[4,192,256]{2,1,0:T(8,128)(2,1)S(1)} %pad_maximum_fusion.near_ref), channel_id=1, source_target_pairs={{0,4},{4,0},{8,12},{12,8},{16,20},{20,16},{24,28},{28,24},{1,5},{5... | collective-permute-start | bytes 1179656 | tf_op jit(solution)/shard_map/ppermute | solution.py:183
  14.0 0.7 %copy-start.2 = (bf16[4,192,256]{2,1,0:T(8,128)(2,1)}, bf16[4,192,256]{2,1,0:T(8,128)(2,1)S(1)}, u32[]{:S(2)}) copy-start(bf16[4,192,256]{2,1,0:T(8,128)(2,1)S(1)} %collective-permute-done.3.far_ref) | copy-start | bytes 1179652
  14.8 17.1 %copy-start.7 = (bf16[192,256]{1,0:T(8,128)(2,1)S(1)}, bf16[192,256]{1,0:T(8,128)(2,1)}, u32[]{:S(2)}) copy-start(bf16[192,256]{1,0:T(8,128)(2,1)} %param.13) | copy-start | bytes 294916
  18.3 4.8 %collective-permute-start.4 = (bf16[192,256]{1,0:T(8,128)(2,1)}, bf16[192,256]{1,0:T(8,128)(2,1)S(1)}, u32[]{:S(2)}, u32[]{:S(2)}) collective-permute-start(bf16[192,256]{1,0:T(8,128)(2,1)} %get-tuple-element.9), channel_id=1, source_target_pairs={{0,1},{1,0},{2,3},{3,2},{4,5},{5,4},{6,7},{7,6},{8,9},{9,8},{10,11... | collective-permute-start | bytes 294920 | tf_op jit(solution)/shard_map/ppermute | solution.py:188
  19.2 10.9 %collective-permute-start.5 = (bf16[192,256]{1,0:T(8,128)(2,1)}, bf16[192,256]{1,0:T(8,128)(2,1)S(1)}, u32[]{:S(2)}, u32[]{:S(2)}) collective-permute-start(bf16[192,256]{1,0:T(8,128)(2,1)} %get-tuple-element.10), channel_id=1, source_target_pairs={{0,2},{1,3},{2,0},{3,1},{4,6},{5,7},{6,4},{7,5},{8,10},{9,11},{10,... | collective-permute-start | bytes 294920 | tf_op jit(solution)/shard_map/ppermute | solution.py:188
  22.0 8.1 %collective-permute-start.6 = (bf16[192,256]{1,0:T(8,128)(2,1)}, bf16[192,256]{1,0:T(8,128)(2,1)S(1)}, u32[]{:S(2)}, u32[]{:S(2)}) collective-permute-start(bf16[192,256]{1,0:T(8,128)(2,1)} %get-tuple-element.11), channel_id=1, source_target_pairs={{0,3},{1,2},{2,1},{3,0},{4,7},{5,6},{6,5},{7,4},{8,11},{9,10},{10,... | collective-permute-start | bytes 294920 | tf_op jit(solution)/shard_map/ppermute | solution.py:188
  32.2 11.7 %copy-start.3 = (bf16[192,256]{1,0:T(8,128)(2,1)}, bf16[192,256]{1,0:T(8,128)(2,1)S(1)}, u32[]{:S(2)}) copy-start(bf16[192,256]{1,0:T(8,128)(2,1)S(1)} %convolution_convert_fusion.mine_ref) | copy-start | bytes 294916
  32.2 7.0 %collective-permute-start.9 = (bf16[192,256]{1,0:T(8,128)(2,1)S(1)}, bf16[192,256]{1,0:T(8,128)(2,1)S(1)}, u32[]{:S(2)}, u32[]{:S(2)}) collective-permute-start(bf16[192,256]{1,0:T(8,128)(2,1)S(1)} %convolution_convert_fusion.mine_ref), channel_id=1, source_target_pairs={{0,3},{1,2},{2,1},{3,0},{4,7},{5,6},{6,5},{7,4},{8,11},{9,10},{10,... | collective-permute-start | bytes 294920 | tf_op jit(solution)/shard_map/ppermute | solution.py:190
  35.1 8.8 %collective-permute-start.8 = (bf16[192,256]{1,0:T(8,128)(2,1)S(1)}, bf16[192,256]{1,0:T(8,128)(2,1)S(1)}, u32[]{:S(2)}, u32[]{:S(2)}) collective-permute-start(bf16[192,256]{1,0:T(8,128)(2,1)S(1)} %convolution_convert_fusion.mine_ref), channel_id=1, source_target_pairs={{0,2},{1,3},{2,0},{3,1},{4,6},{5,7},{6,4},{7,5},{8,10},{9,11},{10,... | collective-permute-start | bytes 294920 | tf_op jit(solution)/shard_map/ppermute | solution.py:190
  35.7 8.1 %collective-permute-start.7 = (bf16[192,256]{1,0:T(8,128)(2,1)S(1)}, bf16[192,256]{1,0:T(8,128)(2,1)S(1)}, u32[]{:S(2)}, u32[]{:S(2)}) collective-permute-start(bf16[192,256]{1,0:T(8,128)(2,1)S(1)} %convolution_convert_fusion.mine_ref), channel_id=1, source_target_pairs={{0,1},{1,0},{2,3},{3,2},{4,5},{5,4},{6,7},{7,6},{8,9},{9,8},{10,11... | collective-permute-start | bytes 294920 | tf_op jit(solution)/shard_map/ppermute | solution.py:190
  39.2 4.7 %copy-start.4 = (bf16[192,256]{1,0:T(8,128)(2,1)}, bf16[192,256]{1,0:T(8,128)(2,1)S(1)}, u32[]{:S(2)}) copy-start(bf16[192,256]{1,0:T(8,128)(2,1)S(1)} %collective-permute-done.9.rest_2_) | copy-start | bytes 294916
  43.9 0.6 %copy-start.5 = (bf16[192,256]{1,0:T(8,128)(2,1)}, bf16[192,256]{1,0:T(8,128)(2,1)S(1)}, u32[]{:S(2)}) copy-start(bf16[192,256]{1,0:T(8,128)(2,1)S(1)} %collective-permute-done.8.rest_1_) | copy-start | bytes 294916
  43.9 0.7 %copy-start.6 = (bf16[192,256]{1,0:T(8,128)(2,1)}, bf16[192,256]{1,0:T(8,128)(2,1)S(1)}, u32[]{:S(2)}) copy-start(bf16[192,256]{1,0:T(8,128)(2,1)S(1)} %collective-permute-done.7.rest_0_) | copy-start | bytes 294916
  48.4 1.9 %collective-permute-start.10 = (bf16[4,192,256]{2,1,0:T(8,128)(2,1)}, bf16[4,192,256]{2,1,0:T(8,128)(2,1)S(1)}, u32[]{:S(2)}, u32[]{:S(2)}) collective-permute-start(bf16[4,192,256]{2,1,0:T(8,128)(2,1)} %get-tuple-element.13), channel_id=1, source_target_pairs={{0,4},{4,0},{8,12},{12,8},{16,20},{20,16},{24,28},{28,24},{1,5},{5... | collective-permute-start | bytes 1179656 | tf_op jit(solution)/shard_map/ppermute | solution.py:194
  51.6 5.7 %collective-permute-start.11 = (bf16[192,256]{1,0:T(8,128)(2,1)S(1)}, bf16[192,256]{1,0:T(8,128)(2,1)S(1)}, u32[]{:S(2)}, u32[]{:S(2)}) collective-permute-start(bf16[192,256]{1,0:T(8,128)(2,1)S(1)} %get-tuple-element.16), channel_id=1, source_target_pairs={{0,8},{4,12},{8,0},{12,4},{16,24},{20,28},{24,16},{28,20},{1,9},{5... | collective-permute-start | bytes 294920 | tf_op jit(solution)/shard_map/ppermute | solution.py:198
  52.6 5.6 %collective-permute-start.13 = (bf16[192,256]{1,0:T(8,128)(2,1)S(1)}, bf16[192,256]{1,0:T(8,128)(2,1)S(1)}, u32[]{:S(2)}, u32[]{:S(2)}) collective-permute-start(bf16[192,256]{1,0:T(8,128)(2,1)S(1)} %get-tuple-element.17), channel_id=1, source_target_pairs={{0,24},{4,28},{8,16},{12,20},{16,8},{20,12},{24,0},{28,4},{1,25},{... | collective-permute-start | bytes 294920 | tf_op jit(solution)/shard_map/ppermute | solution.py:198
  53.0 6.8 %collective-permute-start.12 = (bf16[192,256]{1,0:T(8,128)(2,1)S(1)}, bf16[192,256]{1,0:T(8,128)(2,1)S(1)}, u32[]{:S(2)}, u32[]{:S(2)}) collective-permute-start(bf16[192,256]{1,0:T(8,128)(2,1)S(1)} %get-tuple-element.18), channel_id=1, source_target_pairs={{0,16},{4,20},{8,24},{12,28},{16,0},{20,4},{24,8},{28,12},{1,17},{... | collective-permute-start | bytes 294920 | tf_op jit(solution)/shard_map/ppermute | solution.py:198

commit v13 on v11

--- a/solution.py
+++ b/solution.py
@@ -73,7 +73,13 @@
         acc_ref[rows, :] += value
 
     run_slots(jnp.minimum(info_ref[0], a_ref.shape[0]), product, place)
-    split_out(acc_ref, own_ref, send_refs, lax.axis_index("col"))
+    me = lax.axis_index("col")
+    chunk = own_ref.shape[0]
+    n = send_refs[0].shape[0]
+    own_ref[...] = acc_ref[pl.ds(pl.multiple_of(me * chunk, 8), chunk), :]
+    for dest in range(n):
+        send_refs[0][dest] = acc_ref[pl.ds(dest * chunk, chunk), :].astype(send_refs[0].dtype)
+    send_refs[0][me] = jnp.zeros(send_refs[0].shape[1:], send_refs[0].dtype)
 
 
 def backward_kernel(n, rows_ref, cols_ref, info_ref, a_ref, mine_ref, *rest):
@@ -121,10 +127,12 @@
     width = near.shape[2]
     return pl.pallas_call(
         forward_kernel,
-        out_shape=(jax.ShapeDtypeStruct((chunk, width), jnp.float32),)
-        + (jax.ShapeDtypeStruct((chunk, width), jnp.bfloat16),) * (parts[0] - 1),
+        out_shape=(
+            jax.ShapeDtypeStruct((chunk, width), jnp.float32),
+            jax.ShapeDtypeStruct((parts[0], chunk, width), jnp.bfloat16),
+        ),
         in_specs=[SMEM, SMEM, SMEM, VMEM, VMEM, VMEM],
-        out_specs=(VMEM,) * parts[0],
+        out_specs=(VMEM, VMEM),
         scratch_shapes=[
             pltpu.VMEM((2 * near.shape[0] * near.shape[1], width), jnp.bfloat16),
             pltpu.VMEM((out_rows, width), jnp.float32),
@@ -175,9 +183,8 @@
     far = lax.ppermute(near, "row", partner(n_row))
     info = tile_count.reshape(1)
     own, *send = tile_products(row_slots, col_slots, info, blocks, near, far, (n_col, own_rows))
-    total = own
-    for shift, perm in enumerate(shifts("col")):
-        total = total + lax.ppermute(send[shift], "col", perm).astype(jnp.float32)
+    got = lax.all_to_all(send[0], "col", 0, 0, tiled=False)
+    total = own + got.astype(jnp.float32).sum(0)
     activated, pulled_own = dense_layer(total, cotangent, weight)
     got = [lax.ppermute(pulled_own, "col", perm) for perm in shifts("col")]
     near_g, far_g = tile_products_t(

time: 59.8 us -> 63.4 us (1.060)
  blocking collectives: 0 us -> 17.2 us
  starting transfers between devices: 21.2 us -> 13.5 us
  waiting for transfers between devices: 24.6 us -> 18 us
    all_to_all x0 -> x1, blocking collectives: none -> 17.2 us  [on_device(): got = lax.all_to_all(send[0], 'col', 0, 0, tiled=False)]
    ppermute x3 -> x0, waiting for transfers between devices: 5.89 us -> none  [on_device(): total = total + lax.ppermute(send[shift], 'col', perm).astype(jnp.float32)]
    ppermute x3 -> x0, starting transfers between devices: 5.63 us -> none  [on_device(): total = total + lax.ppermute(send[shift], 'col', perm).astype(jnp.float32)]
    ppermute x3, starting transfers between devices: 4.15 us -> 2.28 us  [on_device(): got = [lax.ppermute(pulled_own, 'col', perm) for perm in shifts('col')]]
  transfers between devices with their start and end apart: 14 -> 11, of which waited for: 10 -> 8; matrix products, arithmetic and copies ran while one was open for 0% -> 0% of each run, Pallas kernels for 0% -> 0%
where the time goes in v13:
time: 63.4 us; the launch traced here: 63 us
  waiting for transfers between devices  18 us (28%)
  blocking collectives  17.2 us (27%)
  starting transfers between devices  13.5 us (21%)
  Pallas kernels  6.53 us (10%)
  other arithmetic  2.93 us (5%)
  matrix products  2.01 us (3%)
  local copies, waits for them, and re-layouts  1.44 us (2%)
  between operations  1.4 us (2%)
    all_to_all x1, blocking collectives, on_device(): got = lax.all_to_all(send[0], 'col', 0, 0, tiled=False)  17.2 us
    ppermute x3, waiting for transfers between devices, on_device(): got = [lax.ppermute(pulled_own, 'col', perm) for perm in shifts('col')]  8.35 us
    ppermute x3, starting transfers between devices, on_device(): lax.ppermute(features, 'row', perm)  5.97 us
    ppermute x3, starting transfers between devices, on_device(): total_g = total_g + lax.ppermute(piece, 'row', perm).astype(jnp.float32)  5.03 us
    ppermute x3, waiting for transfers between devices, on_device(): total_g = total_g + lax.ppermute(piece, 'row', perm).astype(jnp.float32)  3.46 us
    pallas_call x1, Pallas kernels, tile_products_t(): pl.pallas_call(functools.partial(backward_kernel, len(got) + 1), out_shap...  3.38 us
    ppermute x3, waiting for transfers between devices, on_device(): lax.ppermute(features, 'row', perm)  3.36 us
    pallas_call x1, Pallas kernels, tile_products(): pl.pallas_call(forward_kernel, out_shape=(jax.ShapeDtypeStruct((chunk, wi...  3.15 us
  transfers between devices with their start and end apart: 11, of which 8 were waited for; matrix products, arithmetic and copies ran while one was open for 0% of the time, Pallas kernels for 0%

profile of v13, /device:TPU:0, one launch (start us, length us, event | category | flops | bytes accessed | tf_op | source)
XLA Modules:
  0.0 63.0 jit_solution(10127697578202223498)
XLA Ops:
  0.6 0.0 copy-start
  0.6 3.0 %collective-permute-start = (bf16[192,256]{1,0:T(8,128)(2,1)}, bf16[192,256]{1,0:T(8,128)(2,1)S(1)}, u32[]{:S(2)}, u32[]{:S(2)}) collective-permute-start(bf16[192,256]{1,0:T(8,128)(2,1)} %param.7), channel_id=1, source_target_pairs={{0,8},{4,12},{8,16},{12,20},{16,24},{20,28},{24,0},{28,4},{1,9},{5... | collective-permute-start | bytes 294920 | tf_op jit(solution)/shard_map/ppermute | solution.py:182
  3.7 1.0 %collective-permute-start.2 = (bf16[192,256]{1,0:T(8,128)(2,1)}, bf16[192,256]{1,0:T(8,128)(2,1)S(1)}, u32[]{:S(2)}, u32[]{:S(2)}) collective-permute-start(bf16[192,256]{1,0:T(8,128)(2,1)} %param.7), channel_id=1, source_target_pairs={{0,24},{4,28},{8,0},{12,4},{16,8},{20,12},{24,16},{28,20},{1,25},{... | collective-permute-start | bytes 294920 | tf_op jit(solution)/shard_map/ppermute | solution.py:182
  4.7 1.9 %collective-permute-start.1 = (bf16[192,256]{1,0:T(8,128)(2,1)}, bf16[192,256]{1,0:T(8,128)(2,1)S(1)}, u32[]{:S(2)}, u32[]{:S(2)}) collective-permute-start(bf16[192,256]{1,0:T(8,128)(2,1)} %param.7), channel_id=1, source_target_pairs={{0,16},{4,20},{8,24},{12,28},{16,0},{20,4},{24,8},{28,12},{1,17},{... | collective-permute-start | bytes 294920 | tf_op jit(solution)/shard_map/ppermute | solution.py:182
  6.6 1.6 %collective-permute-done = bf16[192,256]{1,0:T(8,128)(2,1)S(1)} collective-permute-done((bf16[192,256]{1,0:T(8,128)(2,1)}, bf16[192,256]{1,0:T(8,128)(2,1)S(1)}, u32[]{:S(2)}, u32[]{:S(2)}) %collective-permute-start) | collective-permute-done | bytes 98336 | tf_op jit(solution)/shard_map/ppermute | solution.py:182
  8.3 1.7 %collective-permute-done.2 = bf16[192,256]{1,0:T(8,128)(2,1)S(1)} collective-permute-done((bf16[192,256]{1,0:T(8,128)(2,1)}, bf16[192,256]{1,0:T(8,128)(2,1)S(1)}, u32[]{:S(2)}, u32[]{:S(2)}) %collective-permute-start.2) | collective-permute-done | bytes 98336 | tf_op jit(solution)/shard_map/ppermute | solution.py:182
  10.0 0.9 %pad_maximum_fusion.near_ref = bf16[4,192,256]{2,1,0:T(8,128)(2,1)S(1)} fusion(bf16[1,192,256]{2,1,0:T(8,128)(2,1)S(1)} %bitcast.32, bf16[1,192,256]{2,1,0:T(8,128)(2,1)S(1)} %bitcast.33, bf16[1,192,256]{2,1,0:T(8,128)(2,1)S(1)} %bitcast.31, bf16[1,192,256]{2,1,0:T(8,128)(2,1)} %bitcast.30), kind=kLoop, calls=%fused_computation.3 | loop fusion | flops 589824 | bytes 786432 | tf_op jit(solution)/shard_map/stack | solution.py:182
  10.9 0.1 collective-permute-start.3
  11.7 1.0 %collective-permute-done.3.far_ref = bf16[4,192,256]{2,1,0:T(8,128)(2,1)S(1)} collective-permute-done((bf16[4,192,256]{2,1,0:T(8,128)(2,1)S(1)}, bf16[4,192,256]{2,1,0:T(8,128)(2,1)S(1)}, u32[]{:S(2)}, u32[]{:S(2)}) %collective-permute-start.3) | collective-permute-done | bytes 393248 | tf_op jit(solution)/shard_map/ppermute | solution.py:183
  12.7 0.7 %copy-done.2 = bf16[4,192,256]{2,1,0:T(8,128)(2,1)} copy-done((bf16[4,192,256]{2,1,0:T(8,128)(2,1)}, bf16[4,192,256]{2,1,0:T(8,128)(2,1)S(1)}, u32[]{:S(2)}) %copy-start.2) | copy-done | bytes 393240
  13.5 3.2 %shard_map.86 = (f32[192,256]{1,0:T(8,128)}, bf16[4,192,256]{2,1,0:T(8,128)(2,1)}) custom-call(s32[12]{0:T(128)} %bitcast.34, s32[12]{0:T(128)} %bitcast.36, s32[1]{0:T(128)} %bitcast.26.info_ref, bf16[12,256,256]{2,1,0:T(8,128)(2,1)} %bitcast.28, bf16[4,192,256]{2,1,0:T(8,128)(2,1)} %copy-done.1, bf16[4,192,256]{2,1,0:T(8,128)(2,1)} %copy-done.2), custom_call_target="tpu_custom_call" | custom-call | tf_op jit(solution)/shard_map/pallas_call | solution.py:128
  16.6 17.2 %all_to_all.5 = bf16[4,192,256]{2,1,0:T(8,128)(2,1)S(1)} all-to-all(bf16[4,192,256]{2,1,0:T(8,128)(2,1)} %get-tuple-element.7), channel_id=1, replica_groups=mesh['row'=8,'col'=4] {'col'}, dimensions={0} | all-to-all | bytes 786432 | tf_op jit(solution)/shard_map/all_to_all | solution.py:186
  33.9 1.8 %multiply_convert_fusion.1 = (bf16[192,256]{1,0:T(8,128)(2,1)}, f32[192,256]{1,0:T(8,128)S(1)}) fusion(bf16[256,256]{1,0:T(8,128)(2,1)S(1)} %copy-done, f32[192,256]{1,0:T(8,128)} %get-tuple-element.6, f32[192,256]{1,0:T(8,128)S(1)} %convert_reduce_fusion), kind=kOutput, calls=%fused_computation.10 | convolution fusion | flops 25509888 | bytes 819200 | tf_op jit(solution)/shard_map/dot_general | solution.py:18
  35.6 0.2 convolution_convert_fusion.mine_ref
  35.9 0.0 copy-start.3
  35.9 1.5 %collective-permute-start.6 = (bf16[192,256]{1,0:T(8,128)(2,1)S(1)}, bf16[192,256]{1,0:T(8,128)(2,1)S(1)}, u32[]{:S(2)}, u32[]{:S(2)}) collective-permute-start(bf16[192,256]{1,0:T(8,128)(2,1)S(1)} %convolution_convert_fusion.mine_ref), channel_id=1, source_target_pairs={{0,3},{1,0},{2,1},{3,2},{4,7},{5,4},{6,5},{7,6},{8,11},{9,8},{10,9... | collective-permute-start | bytes 294920 | tf_op jit(solution)/shard_map/ppermute | solution.py:189
  37.4 0.2 collective-permute-start.5
  37.6 0.6 collective-permute-start.4
  38.2 2.5 %collective-permute-done.6.rest_2_ = bf16[192,256]{1,0:T(8,128)(2,1)S(1)} collective-permute-done((bf16[192,256]{1,0:T(8,128)(2,1)S(1)}, bf16[192,256]{1,0:T(8,128)(2,1)S(1)}, u32[]{:S(2)}, u32[]{:S(2)}) %collective-permute-start.6) | collective-permute-done | bytes 98336 | tf_op jit(solution)/shard_map/ppermute | solution.py:189
  40.7 5.8 %collective-permute-done.5.rest_1_ = bf16[192,256]{1,0:T(8,128)(2,1)S(1)} collective-permute-done((bf16[192,256]{1,0:T(8,128)(2,1)S(1)}, bf16[192,256]{1,0:T(8,128)(2,1)S(1)}, u32[]{:S(2)}, u32[]{:S(2)}) %collective-permute-start.5) | collective-permute-done | bytes 98336 | tf_op jit(solution)/shard_map/ppermute | solution.py:189
  46.5 0.6 copy-done.5
  47.2 0.0 copy-done.6
  47.2 3.4 %shard_map.87 = (f32[4,192,256]{2,1,0:T(8,128)}, bf16[4,192,256]{2,1,0:T(8,128)(2,1)}) custom-call(s32[12]{0:T(128)} %bitcast.35, s32[12]{0:T(128)} %bitcast.37, s32[1]{0:T(128)} %bitcast.27.info_ref, bf16[12,256,256]{2,1,0:T(8,128)(2,1)} %bitcast.29, bf16[192,256]{1,0:T(8,128)(2,1)} %copy-done.3, bf16[192,256]{1,0:T(8,128)(2,1)} %copy-done.6, ...), custom_call_target="tpu_custom_call" | custom-call | tf_op jit(solution)/shard_map/pallas_call | solution.py:148
  50.6 0.1 collective-permute-start.7
  50.7 1.8 %collective-permute-done.7 = bf16[4,192,256]{2,1,0:T(8,128)(2,1)S(1)} collective-permute-done((bf16[4,192,256]{2,1,0:T(8,128)(2,1)}, bf16[4,192,256]{2,1,0:T(8,128)(2,1)S(1)}, u32[]{:S(2)}, u32[]{:S(2)}) %collective-permute-start.7) | collective-permute-done | bytes 393248 | tf_op jit(solution)/shard_map/ppermute | solution.py:193
  52.5 1.2 %fusion.6 = (bf16[4,192,256]{2,1,0:T(8,128)(2,1)S(1)}, f32[4,192,256]{2,1,0:T(8,128)S(1)}) fusion(f32[4,192,256]{2,1,0:T(8,128)} %get-tuple-element.8, bf16[4,192,256]{2,1,0:T(8,128)(2,1)S(1)} %collective-permute-done.7), kind=kLoop, calls=%fused_computation.18 | loop fusion | flops 589824 | bytes 2359296 | tf_op jit(solution)/shard_map/convert.2
  53.8 2.9 %collective-permute-start.8 = (bf16[192,256]{1,0:T(8,128)(2,1)S(1)}, bf16[192,256]{1,0:T(8,128)(2,1)S(1)}, u32[]{:S(2)}, u32[]{:S(2)}) collective-permute-start(bf16[192,256]{1,0:T(8,128)(2,1)S(1)} %get-tuple-element.12), channel_id=1, source_target_pairs={{0,8},{4,12},{8,16},{12,20},{16,24},{20,28},{24,0},{28,4},{1,9},{5... | collective-permute-start | bytes 294920 | tf_op jit(solution)/shard_map/ppermute | solution.py:197
  56.7 0.1 collective-permute-start.10
  56.8 2.1 %collective-permute-start.9 = (bf16[192,256]{1,0:T(8,128)(2,1)S(1)}, bf16[192,256]{1,0:T(8,128)(2,1)S(1)}, u32[]{:S(2)}, u32[]{:S(2)}) collective-permute-start(bf16[192,256]{1,0:T(8,128)(2,1)S(1)} %get-tuple-element.14), channel_id=1, source_target_pairs={{0,16},{4,20},{8,24},{12,28},{16,0},{20,4},{24,8},{28,12},{1,17},{... | collective-permute-start | bytes 294920 | tf_op jit(solution)/shard_map/ppermute | solution.py:197
  58.8 1.5 %collective-permute-done.8 = bf16[192,256]{1,0:T(8,128)(2,1)S(1)} collective-permute-done((bf16[192,256]{1,0:T(8,128)(2,1)S(1)}, bf16[192,256]{1,0:T(8,128)(2,1)S(1)}, u32[]{:S(2)}, u32[]{:S(2)}) %collective-permute-start.8) | collective-permute-done | bytes 98336 | tf_op jit(solution)/shard_map/ppermute | solution.py:197
  60.3 2.0 %collective-permute-done.10 = bf16[192,256]{1,0:T(8,128)(2,1)S(1)} collective-permute-done((bf16[192,256]{1,0:T(8,128)(2,1)S(1)}, bf16[192,256]{1,0:T(8,128)(2,1)S(1)}, u32[]{:S(2)}, u32[]{:S(2)}) %collective-permute-start.10) | collective-permute-done | bytes 98336 | tf_op jit(solution)/shard_map/ppermute | solution.py:197
  62.3 0.7 %fusion.3 = bf16[192,256]{1,0:T(8,128)(2,1)} fusion(f32[4,192,256]{2,1,0:T(8,128)S(1)} %get-tuple-element.11, bf16[192,256]{1,0:T(8,128)(2,1)S(1)} %collective-permute-done.10, bf16[192,256]{1,0:T(8,128)(2,1)S(1)} %collective-permute-done.9, bf16[192,256]{1,0:T(8,128)(2,1)S(1)} %collective-permute-done.8), kind=kLoop, calls=%fused_computation.8 | loop fusion | flops 344064 | bytes 589824 | tf_op jit(solution)/shard_map/convert_element_type | solution.py:198
  (16 shorter events, 0.1 us)
Async XLA Ops:
  0.6 33.2 %copy-start = (bf16[256,256]{1,0:T(8,128)(2,1)S(1)}, bf16[256,256]{1,0:T(8,128)(2,1)}, u32[]{:S(2)}) copy-start(bf16[256,256]{1,0:T(8,128)(2,1)} %param.12) | copy-start | bytes 393220
  0.6 7.6 %collective-permute-start = (bf16[192,256]{1,0:T(8,128)(2,1)}, bf16[192,256]{1,0:T(8,128)(2,1)S(1)}, u32[]{:S(2)}, u32[]{:S(2)}) collective-permute-start(bf16[192,256]{1,0:T(8,128)(2,1)} %param.7), channel_id=1, source_target_pairs={{0,8},{4,12},{8,16},{12,20},{16,24},{20,28},{24,0},{28,4},{1,9},{5... | collective-permute-start | bytes 294920 | tf_op jit(solution)/shard_map/ppermute | solution.py:182
  3.7 6.3 %collective-permute-start.2 = (bf16[192,256]{1,0:T(8,128)(2,1)}, bf16[192,256]{1,0:T(8,128)(2,1)S(1)}, u32[]{:S(2)}, u32[]{:S(2)}) collective-permute-start(bf16[192,256]{1,0:T(8,128)(2,1)} %param.7), channel_id=1, source_target_pairs={{0,24},{4,28},{8,0},{12,4},{16,8},{20,12},{24,16},{28,20},{1,25},{... | collective-permute-start | bytes 294920 | tf_op jit(solution)/shard_map/ppermute | solution.py:182
  4.7 5.3 %collective-permute-start.1 = (bf16[192,256]{1,0:T(8,128)(2,1)}, bf16[192,256]{1,0:T(8,128)(2,1)S(1)}, u32[]{:S(2)}, u32[]{:S(2)}) collective-permute-start(bf16[192,256]{1,0:T(8,128)(2,1)} %param.7), channel_id=1, source_target_pairs={{0,16},{4,20},{8,24},{12,28},{16,0},{20,4},{24,8},{28,12},{1,17},{... | collective-permute-start | bytes 294920 | tf_op jit(solution)/shard_map/ppermute | solution.py:182
  10.9 1.8 %copy-start.1 = (bf16[4,192,256]{2,1,0:T(8,128)(2,1)}, bf16[4,192,256]{2,1,0:T(8,128)(2,1)S(1)}, u32[]{:S(2)}) copy-start(bf16[4,192,256]{2,1,0:T(8,128)(2,1)S(1)} %pad_maximum_fusion.near_ref) | copy-start | bytes 1179652
  10.9 1.8 %collective-permute-start.3 = (bf16[4,192,256]{2,1,0:T(8,128)(2,1)S(1)}, bf16[4,192,256]{2,1,0:T(8,128)(2,1)S(1)}, u32[]{:S(2)}, u32[]{:S(2)}) collective-permute-start(bf16[4,192,256]{2,1,0:T(8,128)(2,1)S(1)} %pad_maximum_fusion.near_ref), channel_id=1, source_target_pairs={{0,4},{4,0},{8,12},{12,8},{16,20},{20,16},{24,28},{28,24},{1,5},{5... | collective-permute-start | bytes 1179656 | tf_op jit(solution)/shard_map/ppermute | solution.py:183
  12.7 0.7 %copy-start.2 = (bf16[4,192,256]{2,1,0:T(8,128)(2,1)}, bf16[4,192,256]{2,1,0:T(8,128)(2,1)S(1)}, u32[]{:S(2)}) copy-start(bf16[4,192,256]{2,1,0:T(8,128)(2,1)S(1)} %collective-permute-done.3.far_ref) | copy-start | bytes 1179652
  16.6 19.0 %copy-start.7 = (bf16[192,256]{1,0:T(8,128)(2,1)S(1)}, bf16[192,256]{1,0:T(8,128)(2,1)}, u32[]{:S(2)}) copy-start(bf16[192,256]{1,0:T(8,128)(2,1)} %param.13) | copy-start | bytes 294916
  35.9 10.7 %copy-start.3 = (bf16[192,256]{1,0:T(8,128)(2,1)}, bf16[192,256]{1,0:T(8,128)(2,1)S(1)}, u32[]{:S(2)}) copy-start(bf16[192,256]{1,0:T(8,128)(2,1)S(1)} %convolution_convert_fusion.mine_ref) | copy-start | bytes 294916
  35.9 4.8 %collective-permute-start.6 = (bf16[192,256]{1,0:T(8,128)(2,1)S(1)}, bf16[192,256]{1,0:T(8,128)(2,1)S(1)}, u32[]{:S(2)}, u32[]{:S(2)}) collective-permute-start(bf16[192,256]{1,0:T(8,128)(2,1)S(1)} %convolution_convert_fusion.mine_ref), channel_id=1, source_target_pairs={{0,3},{1,0},{2,1},{3,2},{4,7},{5,4},{6,5},{7,6},{8,11},{9,8},{10,9... | collective-permute-start | bytes 294920 | tf_op jit(solution)/shard_map/ppermute | solution.py:189
  37.4 9.1 %collective-permute-start.5 = (bf16[192,256]{1,0:T(8,128)(2,1)S(1)}, bf16[192,256]{1,0:T(8,128)(2,1)S(1)}, u32[]{:S(2)}, u32[]{:S(2)}) collective-permute-start(bf16[192,256]{1,0:T(8,128)(2,1)S(1)} %convolution_convert_fusion.mine_ref), channel_id=1, source_target_pairs={{0,2},{1,3},{2,0},{3,1},{4,6},{5,7},{6,4},{7,5},{8,10},{9,11},{10,... | collective-permute-start | bytes 294920 | tf_op jit(solution)/shard_map/ppermute | solution.py:189
  37.6 8.9 %collective-permute-start.4 = (bf16[192,256]{1,0:T(8,128)(2,1)S(1)}, bf16[192,256]{1,0:T(8,128)(2,1)S(1)}, u32[]{:S(2)}, u32[]{:S(2)}) collective-permute-start(bf16[192,256]{1,0:T(8,128)(2,1)S(1)} %convolution_convert_fusion.mine_ref), channel_id=1, source_target_pairs={{0,1},{1,2},{2,3},{3,0},{4,5},{5,6},{6,7},{7,4},{8,9},{9,10},{10,1... | collective-permute-start | bytes 294920 | tf_op jit(solution)/shard_map/ppermute | solution.py:189
  40.7 5.8 %copy-start.4 = (bf16[192,256]{1,0:T(8,128)(2,1)}, bf16[192,256]{1,0:T(8,128)(2,1)S(1)}, u32[]{:S(2)}) copy-start(bf16[192,256]{1,0:T(8,128)(2,1)S(1)} %collective-permute-done.6.rest_2_) | copy-start | bytes 294916
  46.5 0.6 %copy-start.5 = (bf16[192,256]{1,0:T(8,128)(2,1)}, bf16[192,256]{1,0:T(8,128)(2,1)S(1)}, u32[]{:S(2)}) copy-start(bf16[192,256]{1,0:T(8,128)(2,1)S(1)} %collective-permute-done.5.rest_1_) | copy-start | bytes 294916
  46.5 0.7 %copy-start.6 = (bf16[192,256]{1,0:T(8,128)(2,1)}, bf16[192,256]{1,0:T(8,128)(2,1)S(1)}, u32[]{:S(2)}) copy-start(bf16[192,256]{1,0:T(8,128)(2,1)S(1)} %collective-permute-done.4.rest_0_) | copy-start | bytes 294916
  50.6 1.9 %collective-permute-start.7 = (bf16[4,192,256]{2,1,0:T(8,128)(2,1)}, bf16[4,192,256]{2,1,0:T(8,128)(2,1)S(1)}, u32[]{:S(2)}, u32[]{:S(2)}) collective-permute-start(bf16[4,192,256]{2,1,0:T(8,128)(2,1)} %get-tuple-element.9), channel_id=1, source_target_pairs={{0,4},{4,0},{8,12},{12,8},{16,20},{20,16},{24,28},{28,24},{1,5},{5... | collective-permute-start | bytes 1179656 | tf_op jit(solution)/shard_map/ppermute | solution.py:193
  53.8 6.5 %collective-permute-start.8 = (bf16[192,256]{1,0:T(8,128)(2,1)S(1)}, bf16[192,256]{1,0:T(8,128)(2,1)S(1)}, u32[]{:S(2)}, u32[]{:S(2)}) collective-permute-start(bf16[192,256]{1,0:T(8,128)(2,1)S(1)} %get-tuple-element.12), channel_id=1, source_target_pairs={{0,8},{4,12},{8,16},{12,20},{16,24},{20,28},{24,0},{28,4},{1,9},{5... | collective-permute-start | bytes 294920 | tf_op jit(solution)/shard_map/ppermute | solution.py:197
  56.7 5.6 %collective-permute-start.10 = (bf16[192,256]{1,0:T(8,128)(2,1)S(1)}, bf16[192,256]{1,0:T(8,128)(2,1)S(1)}, u32[]{:S(2)}, u32[]{:S(2)}) collective-permute-start(bf16[192,256]{1,0:T(8,128)(2,1)S(1)} %get-tuple-element.13), channel_id=1, source_target_pairs={{0,24},{4,28},{8,0},{12,4},{16,8},{20,12},{24,16},{28,20},{1,25},{... | collective-permute-start | bytes 294920 | tf_op jit(solution)/shard_map/ppermute | solution.py:197
  56.8 5.5 %collective-permute-start.9 = (bf16[192,256]{1,0:T(8,128)(2,1)S(1)}, bf16[192,256]{1,0:T(8,128)(2,1)S(1)}, u32[]{:S(2)}, u32[]{:S(2)}) collective-permute-start(bf16[192,256]{1,0:T(8,128)(2,1)S(1)} %get-tuple-element.14), channel_id=1, source_target_pairs={{0,16},{4,20},{8,24},{12,28},{16,0},{20,4},{24,8},{28,12},{1,17},{... | collective-permute-start | bytes 294920 | tf_op jit(solution)/shard_map/ppermute | solution.py:197

commit v14 on v11

--- a/solution.py
+++ b/solution.py
@@ -23,6 +23,14 @@
 
 
 UNROLL = 4
+
+
+def gather_peer(i, step, n):
+    return i ^ step if n & (n - 1) == 0 else (i + step) % n
+
+
+def gather_source(i, step, n):
+    return i ^ step if n & (n - 1) == 0 else (i - step + n) % n
 
 
 def run_slots(count, product, place):
@@ -84,7 +92,7 @@
     me = lax.axis_index("col")
     block_ref[pl.ds(pl.multiple_of(me * chunk, 16), chunk), :] = mine_ref[...]
     for shift in range(1, n):
-        start = pl.multiple_of(((me - shift + n) % n) * chunk, 16)
+        start = pl.multiple_of(gather_source(me, shift, n) * chunk, 16)
         block_ref[pl.ds(start, chunk), :] = got_refs[shift - 1][...]
     acc_ref[...] = jnp.zeros_like(acc_ref)
 
@@ -179,7 +187,10 @@
     for shift, perm in enumerate(shifts("col")):
         total = total + lax.ppermute(send[shift], "col", perm).astype(jnp.float32)
     activated, pulled_own = dense_layer(total, cotangent, weight)
-    got = [lax.ppermute(pulled_own, "col", perm) for perm in shifts("col")]
+    got = [
+        lax.ppermute(pulled_own, "col", [(i, gather_peer(i, shift, n_col)) for i in range(n_col)])
+        for shift in range(1, n_col)
+    ]
     near_g, far_g = tile_products_t(
         row_slots, col_slots, info, blocks, pulled_own, got, n_row, n_row * own_rows
     )

time: 59.8 us -> 59.5 us (level)
  waiting for transfers between devices: 24.6 us -> 23.7 us
  starting transfers between devices: 21.2 us -> 21.9 us
where the time goes in v14:
time: 59.5 us; the launch traced here: 59.4 us
  waiting for transfers between devices  23.7 us (40%)
  starting transfers between devices  21.9 us (37%)
  Pallas kernels  6.05 us (10%)
  other arithmetic  2.88 us (5%)
  matrix products  2.01 us (3%)
  local copies, waits for them, and re-layouts  1.46 us (2%)
  between operations  1.39 us (2%)
    ppermute x3, waiting for transfers between devices, on_device(): lax.ppermute(pulled_own, 'col', [(i, gather_peer(i, shift, n_col)) for i...  8.35 us
    ppermute x3, starting transfers between devices, on_device(): lax.ppermute(features, 'row', perm)  5.97 us
    ppermute x3, starting transfers between devices, on_device(): total = total + lax.ppermute(send[shift], 'col', perm).astype(jnp.float32)  5.88 us
    ppermute x3, waiting for transfers between devices, on_device(): total = total + lax.ppermute(send[shift], 'col', perm).astype(jnp.float32)  5.64 us
    ppermute x3, starting transfers between devices, on_device(): total_g = total_g + lax.ppermute(piece, 'row', perm).astype(jnp.float32)  5.19 us
    ppermute x3, starting transfers between devices, on_device(): lax.ppermute(pulled_own, 'col', [(i, gather_peer(i, shift, n_col)) for i...  4.45 us
    ppermute x3, waiting for transfers between devices, on_device(): total_g = total_g + lax.ppermute(piece, 'row', perm).astype(jnp.float32)  3.69 us
    ppermute x3, waiting for transfers between devices, on_device(): lax.ppermute(features, 'row', perm)  3.36 us
  transfers between devices with their start and end apart: 14, of which 10 were waited for; matrix products, arithmetic and copies ran while one was open for 0% of the time, Pallas kernels for 0%

profile of v14, /device:TPU:0, one launch (start us, length us, event | category | flops | bytes accessed | tf_op | source)
XLA Modules:
  0.0 59.4 jit_solution(10369095269284242685)
XLA Ops:
  0.6 3.0 %collective-permute-start = (bf16[192,256]{1,0:T(8,128)(2,1)}, bf16[192,256]{1,0:T(8,128)(2,1)S(1)}, u32[]{:S(2)}, u32[]{:S(2)}) collective-permute-start(bf16[192,256]{1,0:T(8,128)(2,1)} %param.7), channel_id=1, source_target_pairs={{0,8},{4,12},{8,16},{12,20},{16,24},{20,28},{24,0},{28,4},{1,9},{5... | collective-permute-start | bytes 294920 | tf_op jit(solution)/shard_map/ppermute | solution.py:182
  3.7 1.0 %collective-permute-start.2 = (bf16[192,256]{1,0:T(8,128)(2,1)}, bf16[192,256]{1,0:T(8,128)(2,1)S(1)}, u32[]{:S(2)}, u32[]{:S(2)}) collective-permute-start(bf16[192,256]{1,0:T(8,128)(2,1)} %param.7), channel_id=1, source_target_pairs={{0,24},{4,28},{8,0},{12,4},{16,8},{20,12},{24,16},{28,20},{1,25},{... | collective-permute-start | bytes 294920 | tf_op jit(solution)/shard_map/ppermute | solution.py:182
  4.7 1.9 %collective-permute-start.1 = (bf16[192,256]{1,0:T(8,128)(2,1)}, bf16[192,256]{1,0:T(8,128)(2,1)S(1)}, u32[]{:S(2)}, u32[]{:S(2)}) collective-permute-start(bf16[192,256]{1,0:T(8,128)(2,1)} %param.7), channel_id=1, source_target_pairs={{0,16},{4,20},{8,24},{12,28},{16,0},{20,4},{24,8},{28,12},{1,17},{... | collective-permute-start | bytes 294920 | tf_op jit(solution)/shard_map/ppermute | solution.py:182
  6.6 1.6 %collective-permute-done = bf16[192,256]{1,0:T(8,128)(2,1)S(1)} collective-permute-done((bf16[192,256]{1,0:T(8,128)(2,1)}, bf16[192,256]{1,0:T(8,128)(2,1)S(1)}, u32[]{:S(2)}, u32[]{:S(2)}) %collective-permute-start) | collective-permute-done | bytes 98336 | tf_op jit(solution)/shard_map/ppermute | solution.py:182
  8.3 1.7 %collective-permute-done.2 = bf16[192,256]{1,0:T(8,128)(2,1)S(1)} collective-permute-done((bf16[192,256]{1,0:T(8,128)(2,1)}, bf16[192,256]{1,0:T(8,128)(2,1)S(1)}, u32[]{:S(2)}, u32[]{:S(2)}) %collective-permute-start.2) | collective-permute-done | bytes 98336 | tf_op jit(solution)/shard_map/ppermute | solution.py:182
  10.0 0.9 %pad_maximum_fusion.near_ref = bf16[4,192,256]{2,1,0:T(8,128)(2,1)S(1)} fusion(bf16[1,192,256]{2,1,0:T(8,128)(2,1)S(1)} %bitcast.32, bf16[1,192,256]{2,1,0:T(8,128)(2,1)S(1)} %bitcast.33, bf16[1,192,256]{2,1,0:T(8,128)(2,1)S(1)} %bitcast.31, bf16[1,192,256]{2,1,0:T(8,128)(2,1)} %bitcast.30), kind=kLoop, calls=%fused_computation.2 | loop fusion | flops 589824 | bytes 786432 | tf_op jit(solution)/shard_map/stack | solution.py:182
  11.7 1.0 %collective-permute-done.3.far_ref = bf16[4,192,256]{2,1,0:T(8,128)(2,1)S(1)} collective-permute-done((bf16[4,192,256]{2,1,0:T(8,128)(2,1)S(1)}, bf16[4,192,256]{2,1,0:T(8,128)(2,1)S(1)}, u32[]{:S(2)}, u32[]{:S(2)}) %collective-permute-start.3) | collective-permute-done | bytes 393248 | tf_op jit(solution)/shard_map/ppermute | solution.py:183
  12.7 0.7 %copy-done.2 = bf16[4,192,256]{2,1,0:T(8,128)(2,1)} copy-done((bf16[4,192,256]{2,1,0:T(8,128)(2,1)}, bf16[4,192,256]{2,1,0:T(8,128)(2,1)S(1)}, u32[]{:S(2)}) %copy-start.2) | copy-done | bytes 393240
  13.5 2.9 %shard_map.86 = (f32[192,256]{1,0:T(8,128)}, bf16[192,256]{1,0:T(8,128)(2,1)}, bf16[192,256]{1,0:T(8,128)(2,1)}, bf16[192,256]{1,0:T(8,128)(2,1)}) custom-call(s32[12]{0:T(128)} %bitcast.34, s32[12]{0:T(128)} %bitcast.36, s32[1]{0:T(128)} %bitcast.26.info_ref, bf16[12,256,256]{2,1,0:T(8,128)(2,1)} %bitcast.28, bf16[4,192,256]{2,1,0:T(8,128)(2,1)} %copy-done.1, ...), custom_call_target="tpu_custom_call" | custom-call | tf_op jit(solution)/shard_map/pallas_call | solution.py:130
  16.3 2.1 %collective-permute-start.4 = (bf16[192,256]{1,0:T(8,128)(2,1)}, bf16[192,256]{1,0:T(8,128)(2,1)S(1)}, u32[]{:S(2)}, u32[]{:S(2)}) collective-permute-start(bf16[192,256]{1,0:T(8,128)(2,1)} %get-tuple-element.9), channel_id=1, source_target_pairs={{0,1},{1,2},{2,3},{3,0},{4,5},{5,6},{6,7},{7,4},{8,9},{9,10},{10,1... | collective-permute-start | bytes 294920 | tf_op jit(solution)/shard_map/ppermute | solution.py:188
  18.4 2.4 %collective-permute-start.5 = (bf16[192,256]{1,0:T(8,128)(2,1)}, bf16[192,256]{1,0:T(8,128)(2,1)S(1)}, u32[]{:S(2)}, u32[]{:S(2)}) collective-permute-start(bf16[192,256]{1,0:T(8,128)(2,1)} %get-tuple-element.10), channel_id=1, source_target_pairs={{0,2},{1,3},{2,0},{3,1},{4,6},{5,7},{6,4},{7,5},{8,10},{9,11},{10,... | collective-permute-start | bytes 294920 | tf_op jit(solution)/shard_map/ppermute | solution.py:188
  20.8 1.4 %collective-permute-start.6 = (bf16[192,256]{1,0:T(8,128)(2,1)}, bf16[192,256]{1,0:T(8,128)(2,1)S(1)}, u32[]{:S(2)}, u32[]{:S(2)}) collective-permute-start(bf16[192,256]{1,0:T(8,128)(2,1)} %get-tuple-element.11), channel_id=1, source_target_pairs={{0,3},{1,0},{2,1},{3,2},{4,7},{5,4},{6,5},{7,6},{8,11},{9,8},{10,9... | collective-permute-start | bytes 294920 | tf_op jit(solution)/shard_map/ppermute | solution.py:188
  22.2 2.0 %collective-permute-done.4 = bf16[192,256]{1,0:T(8,128)(2,1)S(1)} collective-permute-done((bf16[192,256]{1,0:T(8,128)(2,1)}, bf16[192,256]{1,0:T(8,128)(2,1)S(1)}, u32[]{:S(2)}, u32[]{:S(2)}) %collective-permute-start.4) | collective-permute-done | bytes 98336 | tf_op jit(solution)/shard_map/ppermute | solution.py:188
  24.2 3.7 %collective-permute-done.5 = bf16[192,256]{1,0:T(8,128)(2,1)S(1)} collective-permute-done((bf16[192,256]{1,0:T(8,128)(2,1)}, bf16[192,256]{1,0:T(8,128)(2,1)S(1)}, u32[]{:S(2)}, u32[]{:S(2)}) %collective-permute-start.5) | collective-permute-done | bytes 98336 | tf_op jit(solution)/shard_map/ppermute | solution.py:188
  27.9 1.8 %multiply_convert_fusion.1 = (bf16[192,256]{1,0:T(8,128)(2,1)}, f32[192,256]{1,0:T(8,128)S(1)}) fusion(bf16[256,256]{1,0:T(8,128)(2,1)S(1)} %copy-done, bf16[192,256]{1,0:T(8,128)(2,1)S(1)} %collective-permute-done.6, bf16[192,256]{1,0:T(8,128)(2,1)S(1)} %collective-permute-done.5, f32[192,256]{1,0:T(8,128)} %get-tuple-element.8, ...), kind=kOutput, calls=%fused_computation.9 | convolution fusion | flops 25755648 | bytes 917504 | tf_op jit(solution)/shard_map/dot_general | solution.py:18
  29.7 0.2 convolution_convert_fusion.mine_ref
  29.9 3.8 %collective-permute-start.9 = (bf16[192,256]{1,0:T(8,128)(2,1)S(1)}, bf16[192,256]{1,0:T(8,128)(2,1)S(1)}, u32[]{:S(2)}, u32[]{:S(2)}) collective-permute-start(bf16[192,256]{1,0:T(8,128)(2,1)S(1)} %convolution_convert_fusion.mine_ref), channel_id=1, source_target_pairs={{0,3},{1,2},{2,1},{3,0},{4,7},{5,6},{6,5},{7,4},{8,11},{9,10},{10,... | collective-permute-start | bytes 294920 | tf_op jit(solution)/shard_map/ppermute | solution.py:191
  33.7 0.3 collective-permute-start.8
  34.0 0.4 collective-permute-start.7
  34.4 3.0 %collective-permute-done.9.rest_2_ = bf16[192,256]{1,0:T(8,128)(2,1)S(1)} collective-permute-done((bf16[192,256]{1,0:T(8,128)(2,1)S(1)}, bf16[192,256]{1,0:T(8,128)(2,1)S(1)}, u32[]{:S(2)}, u32[]{:S(2)}) %collective-permute-start.9) | collective-permute-done | bytes 98336 | tf_op jit(solution)/shard_map/ppermute | solution.py:191
  37.3 5.4 %collective-permute-done.8.rest_1_ = bf16[192,256]{1,0:T(8,128)(2,1)S(1)} collective-permute-done((bf16[192,256]{1,0:T(8,128)(2,1)S(1)}, bf16[192,256]{1,0:T(8,128)(2,1)S(1)}, u32[]{:S(2)}, u32[]{:S(2)}) %collective-permute-start.8) | collective-permute-done | bytes 98336 | tf_op jit(solution)/shard_map/ppermute | solution.py:191
  42.7 0.6 %copy-done.5 = bf16[192,256]{1,0:T(8,128)(2,1)} copy-done((bf16[192,256]{1,0:T(8,128)(2,1)}, bf16[192,256]{1,0:T(8,128)(2,1)S(1)}, u32[]{:S(2)}) %copy-start.5) | copy-done | bytes 98328
  43.4 3.2 %shard_map.87 = (f32[4,192,256]{2,1,0:T(8,128)}, bf16[4,192,256]{2,1,0:T(8,128)(2,1)}) custom-call(s32[12]{0:T(128)} %bitcast.35, s32[12]{0:T(128)} %bitcast.37, s32[1]{0:T(128)} %bitcast.27.info_ref, bf16[12,256,256]{2,1,0:T(8,128)(2,1)} %bitcast.29, bf16[192,256]{1,0:T(8,128)(2,1)} %copy-done.3, bf16[192,256]{1,0:T(8,128)(2,1)} %copy-done.6, ...), custom_call_target="tpu_custom_call" | custom-call | tf_op jit(solution)/shard_map/pallas_call | solution.py:148
  46.6 0.4 collective-permute-start.10
  46.9 1.6 %collective-permute-done.10 = bf16[4,192,256]{2,1,0:T(8,128)(2,1)S(1)} collective-permute-done((bf16[4,192,256]{2,1,0:T(8,128)(2,1)}, bf16[4,192,256]{2,1,0:T(8,128)(2,1)S(1)}, u32[]{:S(2)}, u32[]{:S(2)}) %collective-permute-start.10) | collective-permute-done | bytes 393248 | tf_op jit(solution)/shard_map/ppermute | solution.py:197
  48.5 1.2 %fusion.6 = (bf16[4,192,256]{2,1,0:T(8,128)(2,1)S(1)}, f32[4,192,256]{2,1,0:T(8,128)S(1)}) fusion(f32[4,192,256]{2,1,0:T(8,128)} %get-tuple-element.12, bf16[4,192,256]{2,1,0:T(8,128)(2,1)S(1)} %collective-permute-done.10), kind=kLoop, calls=%fused_computation.17 | loop fusion | flops 589824 | bytes 2359296 | tf_op jit(solution)/shard_map/convert.2
  49.8 2.8 %collective-permute-start.11 = (bf16[192,256]{1,0:T(8,128)(2,1)S(1)}, bf16[192,256]{1,0:T(8,128)(2,1)S(1)}, u32[]{:S(2)}, u32[]{:S(2)}) collective-permute-start(bf16[192,256]{1,0:T(8,128)(2,1)S(1)} %get-tuple-element.16), channel_id=1, source_target_pairs={{0,8},{4,12},{8,16},{12,20},{16,24},{20,28},{24,0},{28,4},{1,9},{5... | collective-permute-start | bytes 294920 | tf_op jit(solution)/shard_map/ppermute | solution.py:201
  52.6 0.6 collective-permute-start.13
  53.1 1.8 %collective-permute-start.12 = (bf16[192,256]{1,0:T(8,128)(2,1)S(1)}, bf16[192,256]{1,0:T(8,128)(2,1)S(1)}, u32[]{:S(2)}, u32[]{:S(2)}) collective-permute-start(bf16[192,256]{1,0:T(8,128)(2,1)S(1)} %get-tuple-element.18), channel_id=1, source_target_pairs={{0,16},{4,20},{8,24},{12,28},{16,0},{20,4},{24,8},{28,12},{1,17},{... | collective-permute-start | bytes 294920 | tf_op jit(solution)/shard_map/ppermute | solution.py:201
  55.0 1.7 %collective-permute-done.11 = bf16[192,256]{1,0:T(8,128)(2,1)S(1)} collective-permute-done((bf16[192,256]{1,0:T(8,128)(2,1)S(1)}, bf16[192,256]{1,0:T(8,128)(2,1)S(1)}, u32[]{:S(2)}, u32[]{:S(2)}) %collective-permute-start.11) | collective-permute-done | bytes 98336 | tf_op jit(solution)/shard_map/ppermute | solution.py:201
  56.7 2.0 %collective-permute-done.13 = bf16[192,256]{1,0:T(8,128)(2,1)S(1)} collective-permute-done((bf16[192,256]{1,0:T(8,128)(2,1)S(1)}, bf16[192,256]{1,0:T(8,128)(2,1)S(1)}, u32[]{:S(2)}, u32[]{:S(2)}) %collective-permute-start.13) | collective-permute-done | bytes 98336 | tf_op jit(solution)/shard_map/ppermute | solution.py:201
  58.7 0.7 %fusion.3 = bf16[192,256]{1,0:T(8,128)(2,1)} fusion(f32[4,192,256]{2,1,0:T(8,128)S(1)} %get-tuple-element.15, bf16[192,256]{1,0:T(8,128)(2,1)S(1)} %collective-permute-done.13, bf16[192,256]{1,0:T(8,128)(2,1)S(1)} %collective-permute-done.12, bf16[192,256]{1,0:T(8,128)(2,1)S(1)} %collective-permute-done.11), kind=kLoop, calls=%fused_computation.7 | loop fusion | flops 344064 | bytes 589824 | tf_op jit(solution)/shard_map/convert_element_type | solution.py:202
  (20 shorter events, 0.2 us)
Async XLA Ops:
  0.6 27.2 %copy-start = (bf16[256,256]{1,0:T(8,128)(2,1)S(1)}, bf16[256,256]{1,0:T(8,128)(2,1)}, u32[]{:S(2)}) copy-start(bf16[256,256]{1,0:T(8,128)(2,1)} %param.12) | copy-start | bytes 393220
  0.6 7.6 %collective-permute-start = (bf16[192,256]{1,0:T(8,128)(2,1)}, bf16[192,256]{1,0:T(8,128)(2,1)S(1)}, u32[]{:S(2)}, u32[]{:S(2)}) collective-permute-start(bf16[192,256]{1,0:T(8,128)(2,1)} %param.7), channel_id=1, source_target_pairs={{0,8},{4,12},{8,16},{12,20},{16,24},{20,28},{24,0},{28,4},{1,9},{5... | collective-permute-start | bytes 294920 | tf_op jit(solution)/shard_map/ppermute | solution.py:182
  3.7 6.3 %collective-permute-start.2 = (bf16[192,256]{1,0:T(8,128)(2,1)}, bf16[192,256]{1,0:T(8,128)(2,1)S(1)}, u32[]{:S(2)}, u32[]{:S(2)}) collective-permute-start(bf16[192,256]{1,0:T(8,128)(2,1)} %param.7), channel_id=1, source_target_pairs={{0,24},{4,28},{8,0},{12,4},{16,8},{20,12},{24,16},{28,20},{1,25},{... | collective-permute-start | bytes 294920 | tf_op jit(solution)/shard_map/ppermute | solution.py:182
  4.7 5.3 %collective-permute-start.1 = (bf16[192,256]{1,0:T(8,128)(2,1)}, bf16[192,256]{1,0:T(8,128)(2,1)S(1)}, u32[]{:S(2)}, u32[]{:S(2)}) collective-permute-start(bf16[192,256]{1,0:T(8,128)(2,1)} %param.7), channel_id=1, source_target_pairs={{0,16},{4,20},{8,24},{12,28},{16,0},{20,4},{24,8},{28,12},{1,17},{... | collective-permute-start | bytes 294920 | tf_op jit(solution)/shard_map/ppermute | solution.py:182
  10.9 1.8 %copy-start.1 = (bf16[4,192,256]{2,1,0:T(8,128)(2,1)}, bf16[4,192,256]{2,1,0:T(8,128)(2,1)S(1)}, u32[]{:S(2)}) copy-start(bf16[4,192,256]{2,1,0:T(8,128)(2,1)S(1)} %pad_maximum_fusion.near_ref) | copy-start | bytes 1179652
  10.9 1.8 %collective-permute-start.3 = (bf16[4,192,256]{2,1,0:T(8,128)(2,1)S(1)}, bf16[4,192,256]{2,1,0:T(8,128)(2,1)S(1)}, u32[]{:S(2)}, u32[]{:S(2)}) collective-permute-start(bf16[4,192,256]{2,1,0:T(8,128)(2,1)S(1)} %pad_maximum_fusion.near_ref), channel_id=1, source_target_pairs={{0,4},{4,0},{8,12},{12,8},{16,20},{20,16},{24,28},{28,24},{1,5},{5... | collective-permute-start | bytes 1179656 | tf_op jit(solution)/shard_map/ppermute | solution.py:183
  12.7 0.7 %copy-start.2 = (bf16[4,192,256]{2,1,0:T(8,128)(2,1)}, bf16[4,192,256]{2,1,0:T(8,128)(2,1)S(1)}, u32[]{:S(2)}) copy-start(bf16[4,192,256]{2,1,0:T(8,128)(2,1)S(1)} %collective-permute-done.3.far_ref) | copy-start | bytes 1179652
  13.5 16.2 %copy-start.7 = (bf16[192,256]{1,0:T(8,128)(2,1)S(1)}, bf16[192,256]{1,0:T(8,128)(2,1)}, u32[]{:S(2)}) copy-start(bf16[192,256]{1,0:T(8,128)(2,1)} %param.13) | copy-start | bytes 294916
  16.3 7.9 %collective-permute-start.4 = (bf16[192,256]{1,0:T(8,128)(2,1)}, bf16[192,256]{1,0:T(8,128)(2,1)S(1)}, u32[]{:S(2)}, u32[]{:S(2)}) collective-permute-start(bf16[192,256]{1,0:T(8,128)(2,1)} %get-tuple-element.9), channel_id=1, source_target_pairs={{0,1},{1,2},{2,3},{3,0},{4,5},{5,6},{6,7},{7,4},{8,9},{9,10},{10,1... | collective-permute-start | bytes 294920 | tf_op jit(solution)/shard_map/ppermute | solution.py:188
  18.4 9.4 %collective-permute-start.5 = (bf16[192,256]{1,0:T(8,128)(2,1)}, bf16[192,256]{1,0:T(8,128)(2,1)S(1)}, u32[]{:S(2)}, u32[]{:S(2)}) collective-permute-start(bf16[192,256]{1,0:T(8,128)(2,1)} %get-tuple-element.10), channel_id=1, source_target_pairs={{0,2},{1,3},{2,0},{3,1},{4,6},{5,7},{6,4},{7,5},{8,10},{9,11},{10,... | collective-permute-start | bytes 294920 | tf_op jit(solution)/shard_map/ppermute | solution.py:188
  20.8 7.1 %collective-permute-start.6 = (bf16[192,256]{1,0:T(8,128)(2,1)}, bf16[192,256]{1,0:T(8,128)(2,1)S(1)}, u32[]{:S(2)}, u32[]{:S(2)}) collective-permute-start(bf16[192,256]{1,0:T(8,128)(2,1)} %get-tuple-element.11), channel_id=1, source_target_pairs={{0,3},{1,0},{2,1},{3,2},{4,7},{5,4},{6,5},{7,6},{8,11},{9,8},{10,9... | collective-permute-start | bytes 294920 | tf_op jit(solution)/shard_map/ppermute | solution.py:188
  29.9 12.8 %copy-start.3 = (bf16[192,256]{1,0:T(8,128)(2,1)}, bf16[192,256]{1,0:T(8,128)(2,1)S(1)}, u32[]{:S(2)}) copy-start(bf16[192,256]{1,0:T(8,128)(2,1)S(1)} %convolution_convert_fusion.mine_ref) | copy-start | bytes 294916
  29.9 7.4 %collective-permute-start.9 = (bf16[192,256]{1,0:T(8,128)(2,1)S(1)}, bf16[192,256]{1,0:T(8,128)(2,1)S(1)}, u32[]{:S(2)}, u32[]{:S(2)}) collective-permute-start(bf16[192,256]{1,0:T(8,128)(2,1)S(1)} %convolution_convert_fusion.mine_ref), channel_id=1, source_target_pairs={{0,3},{1,2},{2,1},{3,0},{4,7},{5,6},{6,5},{7,4},{8,11},{9,10},{10,... | collective-permute-start | bytes 294920 | tf_op jit(solution)/shard_map/ppermute | solution.py:191
  33.7 9.0 %collective-permute-start.8 = (bf16[192,256]{1,0:T(8,128)(2,1)S(1)}, bf16[192,256]{1,0:T(8,128)(2,1)S(1)}, u32[]{:S(2)}, u32[]{:S(2)}) collective-permute-start(bf16[192,256]{1,0:T(8,128)(2,1)S(1)} %convolution_convert_fusion.mine_ref), channel_id=1, source_target_pairs={{0,2},{1,3},{2,0},{3,1},{4,6},{5,7},{6,4},{7,5},{8,10},{9,11},{10,... | collective-permute-start | bytes 294920 | tf_op jit(solution)/shard_map/ppermute | solution.py:191
  34.0 8.7 %collective-permute-start.7 = (bf16[192,256]{1,0:T(8,128)(2,1)S(1)}, bf16[192,256]{1,0:T(8,128)(2,1)S(1)}, u32[]{:S(2)}, u32[]{:S(2)}) collective-permute-start(bf16[192,256]{1,0:T(8,128)(2,1)S(1)} %convolution_convert_fusion.mine_ref), channel_id=1, source_target_pairs={{0,1},{1,0},{2,3},{3,2},{4,5},{5,4},{6,7},{7,6},{8,9},{9,8},{10,11... | collective-permute-start | bytes 294920 | tf_op jit(solution)/shard_map/ppermute | solution.py:191
  37.3 5.4 %copy-start.4 = (bf16[192,256]{1,0:T(8,128)(2,1)}, bf16[192,256]{1,0:T(8,128)(2,1)S(1)}, u32[]{:S(2)}) copy-start(bf16[192,256]{1,0:T(8,128)(2,1)S(1)} %collective-permute-done.9.rest_2_) | copy-start | bytes 294916
  42.7 0.6 %copy-start.5 = (bf16[192,256]{1,0:T(8,128)(2,1)}, bf16[192,256]{1,0:T(8,128)(2,1)S(1)}, u32[]{:S(2)}) copy-start(bf16[192,256]{1,0:T(8,128)(2,1)S(1)} %collective-permute-done.8.rest_1_) | copy-start | bytes 294916
  42.7 0.7 %copy-start.6 = (bf16[192,256]{1,0:T(8,128)(2,1)}, bf16[192,256]{1,0:T(8,128)(2,1)S(1)}, u32[]{:S(2)}) copy-start(bf16[192,256]{1,0:T(8,128)(2,1)S(1)} %collective-permute-done.7.rest_0_) | copy-start | bytes 294916
  46.6 1.9 %collective-permute-start.10 = (bf16[4,192,256]{2,1,0:T(8,128)(2,1)}, bf16[4,192,256]{2,1,0:T(8,128)(2,1)S(1)}, u32[]{:S(2)}, u32[]{:S(2)}) collective-permute-start(bf16[4,192,256]{2,1,0:T(8,128)(2,1)} %get-tuple-element.13), channel_id=1, source_target_pairs={{0,4},{4,0},{8,12},{12,8},{16,20},{20,16},{24,28},{28,24},{1,5},{5... | collective-permute-start | bytes 1179656 | tf_op jit(solution)/shard_map/ppermute | solution.py:197
  49.8 6.9 %collective-permute-start.11 = (bf16[192,256]{1,0:T(8,128)(2,1)S(1)}, bf16[192,256]{1,0:T(8,128)(2,1)S(1)}, u32[]{:S(2)}, u32[]{:S(2)}) collective-permute-start(bf16[192,256]{1,0:T(8,128)(2,1)S(1)} %get-tuple-element.16), channel_id=1, source_target_pairs={{0,8},{4,12},{8,16},{12,20},{16,24},{20,28},{24,0},{28,4},{1,9},{5... | collective-permute-start | bytes 294920 | tf_op jit(solution)/shard_map/ppermute | solution.py:201
  52.6 6.1 %collective-permute-start.13 = (bf16[192,256]{1,0:T(8,128)(2,1)S(1)}, bf16[192,256]{1,0:T(8,128)(2,1)S(1)}, u32[]{:S(2)}, u32[]{:S(2)}) collective-permute-start(bf16[192,256]{1,0:T(8,128)(2,1)S(1)} %get-tuple-element.17), channel_id=1, source_target_pairs={{0,24},{4,28},{8,0},{12,4},{16,8},{20,12},{24,16},{28,20},{1,25},{... | collective-permute-start | bytes 294920 | tf_op jit(solution)/shard_map/ppermute | solution.py:201
  53.1 5.5 %collective-permute-start.12 = (bf16[192,256]{1,0:T(8,128)(2,1)S(1)}, bf16[192,256]{1,0:T(8,128)(2,1)S(1)}, u32[]{:S(2)}, u32[]{:S(2)}) collective-permute-start(bf16[192,256]{1,0:T(8,128)(2,1)S(1)} %get-tuple-element.18), channel_id=1, source_target_pairs={{0,16},{4,20},{8,24},{12,28},{16,0},{20,4},{24,8},{28,12},{1,17},{... | collective-permute-start | bytes 294920 | tf_op jit(solution)/shard_map/ppermute | solution.py:201

commit v15 on v10

--- a/solution.py
+++ b/solution.py
@@ -10,7 +10,8 @@
 
 def dense_kernel(n, own_ref, *rest):
     got_refs = rest[: n - 1]
-    grad_ref, weight_ref, act_ref, pulled_ref = rest[n - 1:]
+    grad_ref, weight_ref, act_ref = rest[n - 1 : n + 2]
+    pulled_refs = rest[n + 2 :]
     total = own_ref[...]
     for got in got_refs:
         total = total + got[...].astype(jnp.float32)
@@ -20,18 +21,20 @@
     act_ref[...] = (mixed * sigma).astype(act_ref.dtype)
     slope = sigma * (1.0 + mixed * (1.0 - sigma))
     scaled = (grad_ref[...].astype(jnp.float32) * slope).astype(jnp.bfloat16)
-    pulled_ref[...] = lax.dot_general(
+    pulled = lax.dot_general(
         scaled, weight, (((1,), (1,)), ((), ())), preferred_element_type=jnp.float32
-    ).astype(pulled_ref.dtype)
+    ).astype(jnp.bfloat16)
+    for pulled_ref in pulled_refs:
+        pulled_ref[...] = pulled
 
 
 def dense_layer_kernel(own, got, grad_rows, weight):
     shape = jax.ShapeDtypeStruct(own.shape, jnp.bfloat16)
     return pl.pallas_call(
         functools.partial(dense_kernel, len(got) + 1),
-        out_shape=(shape, shape),
+        out_shape=(shape,) * (len(got) + 2),
         in_specs=[VMEM] * (len(got) + 3),
-        out_specs=(VMEM, VMEM),
+        out_specs=(VMEM,) * (len(got) + 2),
     )(own, *got, grad_rows, weight)
 
 
@@ -119,7 +122,9 @@
     for shift in range(chips):
         owner = (chip + shift) % chips
         near_ref[shift] = acc_ref[pl.ds(pl.multiple_of((owner * 2 + core) * piece, 8), piece), :]
-        far_ref[shift] = acc_ref[pl.ds(pl.multiple_of((owner * 2 + 1 - core) * piece, 8), piece), :]
+        far_ref[shift] = acc_ref[pl.ds(pl.multiple_of((owner * 2 + 1 - core) * piece, 8), piece), :].astype(
+            far_ref.dtype
+        )
 
 
 SMEM = pl.BlockSpec(memory_space=pltpu.SMEM)
@@ -146,10 +151,11 @@
 def tile_products_t(rows, cols, info, blocks, mine, got, n_out, out_rows):
     chunk = out_rows // n_out
     width = mine.shape[1]
-    stack = jax.ShapeDtypeStruct((n_out // 2, chunk, width), jnp.float32)
+    near = jax.ShapeDtypeStruct((n_out // 2, chunk, width), jnp.float32)
+    far = jax.ShapeDtypeStruct((n_out // 2, chunk, width), jnp.bfloat16)
     return pl.pallas_call(
         functools.partial(backward_kernel, len(got) + 1),
-        out_shape=(stack, stack),
+        out_shape=(near, far),
         in_specs=[SMEM, SMEM, SMEM, VMEM, VMEM] + [VMEM] * len(got),
         out_specs=(VMEM, VMEM),
         scratch_shapes=[
@@ -186,12 +192,12 @@
     info = tile_count.reshape(1)
     own, *send = tile_products(row_slots, col_slots, info, blocks, near, far, (n_col, own_rows))
     got_f = [lax.ppermute(send[shift], "col", perm) for shift, perm in enumerate(shifts("col"))]
-    activated, pulled_own = dense_layer_kernel(own, got_f, cotangent, weight)
-    got = [lax.ppermute(pulled_own, "col", perm) for perm in shifts("col")]
+    activated, pulled_own, *pulled_out = dense_layer_kernel(own, got_f, cotangent, weight)
+    got = [lax.ppermute(piece, "col", perm) for piece, perm in zip(pulled_out, shifts("col"))]
     near_g, far_g = tile_products_t(
         row_slots, col_slots, info, blocks, pulled_own, got, n_row, n_row * own_rows
     )
-    chip_sums = near_g + lax.ppermute(far_g, "row", partner(n_row))
+    chip_sums = near_g + lax.ppermute(far_g, "row", partner(n_row)).astype(jnp.float32)
     total_g = chip_sums[0]
     for shift, perm in enumerate(chip_shifts(n_row)):
         piece = chip_sums[shift + 1].astype(jnp.bfloat16)

time: 61.4 us -> 58.7 us (0.956)
  waiting for transfers between devices: 25.9 us -> 21 us
  starting transfers between devices: 20 us -> 21.2 us
  Pallas kernels: 8.93 us -> 9.63 us
    ppermute x4, waiting for transfers between devices: 11.7 us -> 7.94 us  [the longest x3 6.01 us: on_device(): lax.ppermute(piece, 'col', perm)]
    ppermute x3, starting transfers between devices: 3.86 us -> 4.71 us  [on_device(): total_g = total_g + lax.ppermute(piece, 'row', perm).astype(jnp.float32)]
    ppermute x4, starting transfers between devices: 4.03 us -> 4.76 us  [the longest x3 4.75 us: on_device(): lax.ppermute(piece, 'col', perm)]
    ppermute x3, waiting for transfers between devices: 4.13 us -> 3.46 us  [on_device(): total_g = total_g + lax.ppermute(piece, 'row', perm).astype(jnp.float32)]
  transfers between devices with their start and end apart: 14 -> 14, of which waited for: 11 -> 10; matrix products, arithmetic and copies ran while one was open for 0% -> 0% of each run, Pallas kernels for 0% -> 0%
where the time goes in v15:
time: 58.7 us; the launch traced here: 58.1 us
  starting transfers between devices  21.2 us (36%)
  waiting for transfers between devices  21 us (36%)
  Pallas kernels  9.63 us (16%)
  other arithmetic  2.88 us (5%)
  local copies, waits for them, and re-layouts  2.11 us (4%)
  between operations  1.37 us (2%)
    ppermute x3, waiting for transfers between devices, on_device(): lax.ppermute(piece, 'col', perm)  6.01 us
    ppermute x3, starting transfers between devices, on_device(): lax.ppermute(features, 'row', perm)  5.97 us
    ppermute x3, starting transfers between devices, on_device(): lax.ppermute(send[shift], 'col', perm)  5.64 us
    ppermute x3, waiting for transfers between devices, on_device(): lax.ppermute(send[shift], 'col', perm)  5.19 us
    ppermute x3, starting transfers between devices, on_device(): lax.ppermute(piece, 'col', perm)  4.75 us
    ppermute x3, starting transfers between devices, on_device(): total_g = total_g + lax.ppermute(piece, 'row', perm).astype(jnp.float32)  4.71 us
    pallas_call x1, Pallas kernels, tile_products_t(): pl.pallas_call(functools.partial(backward_kernel, len(got) + 1), out_shap...  3.86 us
    pallas_call x1, Pallas kernels, tile_products(): pl.pallas_call(forward_kernel, out_shape=(jax.ShapeDtypeStruct((chunk, wi...  3.5 us
  transfers between devices with their start and end apart: 14, of which 10 were waited for; matrix products, arithmetic and copies ran while one was open for 0% of the time, Pallas kernels for 0%

profile of v15, /device:TPU:0, one launch (start us, length us, event | category | flops | bytes accessed | tf_op | source)
XLA Modules:
  0.0 58.1 jit_solution(17588825068039607868)
XLA Ops:
  0.6 3.0 %collective-permute-start = (bf16[192,256]{1,0:T(8,128)(2,1)}, bf16[192,256]{1,0:T(8,128)(2,1)S(1)}, u32[]{:S(2)}, u32[]{:S(2)}) collective-permute-start(bf16[192,256]{1,0:T(8,128)(2,1)} %param.7), channel_id=1, source_target_pairs={{0,8},{4,12},{8,16},{12,20},{16,24},{20,28},{24,0},{28,4},{1,9},{5... | collective-permute-start | bytes 294920 | tf_op jit(solution)/shard_map/ppermute | solution.py:190
  3.6 1.0 %collective-permute-start.2 = (bf16[192,256]{1,0:T(8,128)(2,1)}, bf16[192,256]{1,0:T(8,128)(2,1)S(1)}, u32[]{:S(2)}, u32[]{:S(2)}) collective-permute-start(bf16[192,256]{1,0:T(8,128)(2,1)} %param.7), channel_id=1, source_target_pairs={{0,24},{4,28},{8,0},{12,4},{16,8},{20,12},{24,16},{28,20},{1,25},{... | collective-permute-start | bytes 294920 | tf_op jit(solution)/shard_map/ppermute | solution.py:190
  4.7 1.9 %collective-permute-start.1 = (bf16[192,256]{1,0:T(8,128)(2,1)}, bf16[192,256]{1,0:T(8,128)(2,1)S(1)}, u32[]{:S(2)}, u32[]{:S(2)}) collective-permute-start(bf16[192,256]{1,0:T(8,128)(2,1)} %param.7), channel_id=1, source_target_pairs={{0,16},{4,20},{8,24},{12,28},{16,0},{20,4},{24,8},{28,12},{1,17},{... | collective-permute-start | bytes 294920 | tf_op jit(solution)/shard_map/ppermute | solution.py:190
  6.6 1.6 %collective-permute-done = bf16[192,256]{1,0:T(8,128)(2,1)S(1)} collective-permute-done((bf16[192,256]{1,0:T(8,128)(2,1)}, bf16[192,256]{1,0:T(8,128)(2,1)S(1)}, u32[]{:S(2)}, u32[]{:S(2)}) %collective-permute-start) | collective-permute-done | bytes 98336 | tf_op jit(solution)/shard_map/ppermute | solution.py:190
  8.3 1.7 %collective-permute-done.2 = bf16[192,256]{1,0:T(8,128)(2,1)S(1)} collective-permute-done((bf16[192,256]{1,0:T(8,128)(2,1)}, bf16[192,256]{1,0:T(8,128)(2,1)S(1)}, u32[]{:S(2)}, u32[]{:S(2)}) %collective-permute-start.2) | collective-permute-done | bytes 98336 | tf_op jit(solution)/shard_map/ppermute | solution.py:190
  10.0 0.9 %pad_maximum_fusion.near_ref = bf16[4,192,256]{2,1,0:T(8,128)(2,1)S(1)} fusion(bf16[1,192,256]{2,1,0:T(8,128)(2,1)S(1)} %bitcast.30, bf16[1,192,256]{2,1,0:T(8,128)(2,1)S(1)} %bitcast.31, bf16[1,192,256]{2,1,0:T(8,128)(2,1)S(1)} %bitcast.29, bf16[1,192,256]{2,1,0:T(8,128)(2,1)} %bitcast.28), kind=kLoop, calls=%fused_computation.1 | loop fusion | flops 589824 | bytes 786432 | tf_op jit(solution)/shard_map/stack | solution.py:190
  10.9 0.1 collective-permute-start.3
  11.7 1.0 %collective-permute-done.3.far_ref = bf16[4,192,256]{2,1,0:T(8,128)(2,1)S(1)} collective-permute-done((bf16[4,192,256]{2,1,0:T(8,128)(2,1)S(1)}, bf16[4,192,256]{2,1,0:T(8,128)(2,1)S(1)}, u32[]{:S(2)}, u32[]{:S(2)}) %collective-permute-start.3) | collective-permute-done | bytes 393248 | tf_op jit(solution)/shard_map/ppermute | solution.py:191
  12.7 0.7 %copy-done.1 = bf16[4,192,256]{2,1,0:T(8,128)(2,1)} copy-done((bf16[4,192,256]{2,1,0:T(8,128)(2,1)}, bf16[4,192,256]{2,1,0:T(8,128)(2,1)S(1)}, u32[]{:S(2)}) %copy-start.1) | copy-done | bytes 393240
  13.5 3.5 %shard_map.86 = (f32[192,256]{1,0:T(8,128)}, bf16[192,256]{1,0:T(8,128)(2,1)}, bf16[192,256]{1,0:T(8,128)(2,1)}, bf16[192,256]{1,0:T(8,128)(2,1)}) custom-call(s32[12]{0:T(128)} %bitcast.32, s32[12]{0:T(128)} %bitcast.34, s32[1]{0:T(128)} %bitcast.24.info_ref, bf16[12,256,256]{2,1,0:T(8,128)(2,1)} %bitcast.26, bf16[4,192,256]{2,1,0:T(8,128)(2,1)} %copy-done, ...), custom_call_target="tpu_custom_call" | custom-call | tf_op jit(solution)/shard_map/pallas_call | solution.py:138
  17.0 1.3 %collective-permute-start.4 = (bf16[192,256]{1,0:T(8,128)(2,1)}, bf16[192,256]{1,0:T(8,128)(2,1)S(1)}, u32[]{:S(2)}, u32[]{:S(2)}) collective-permute-start(bf16[192,256]{1,0:T(8,128)(2,1)} %get-tuple-element.14), channel_id=1, source_target_pairs={{0,1},{1,2},{2,3},{3,0},{4,5},{5,6},{6,7},{7,4},{8,9},{9,10},{10,1... | collective-permute-start | bytes 294920 | tf_op jit(solution)/shard_map/ppermute | solution.py:194
  18.3 2.5 %collective-permute-start.5 = (bf16[192,256]{1,0:T(8,128)(2,1)}, bf16[192,256]{1,0:T(8,128)(2,1)S(1)}, u32[]{:S(2)}, u32[]{:S(2)}) collective-permute-start(bf16[192,256]{1,0:T(8,128)(2,1)} %get-tuple-element.15), channel_id=1, source_target_pairs={{0,2},{1,3},{2,0},{3,1},{4,6},{5,7},{6,4},{7,5},{8,10},{9,11},{10,... | collective-permute-start | bytes 294920 | tf_op jit(solution)/shard_map/ppermute | solution.py:194
  20.8 1.8 %collective-permute-start.6 = (bf16[192,256]{1,0:T(8,128)(2,1)}, bf16[192,256]{1,0:T(8,128)(2,1)S(1)}, u32[]{:S(2)}, u32[]{:S(2)}) collective-permute-start(bf16[192,256]{1,0:T(8,128)(2,1)} %get-tuple-element.16), channel_id=1, source_target_pairs={{0,3},{1,0},{2,1},{3,2},{4,7},{5,4},{6,5},{7,6},{8,11},{9,8},{10,9... | collective-permute-start | bytes 294920 | tf_op jit(solution)/shard_map/ppermute | solution.py:194
  22.6 2.0 %collective-permute-done.4.rest_0_ = bf16[192,256]{1,0:T(8,128)(2,1)S(1)} collective-permute-done((bf16[192,256]{1,0:T(8,128)(2,1)}, bf16[192,256]{1,0:T(8,128)(2,1)S(1)}, u32[]{:S(2)}, u32[]{:S(2)}) %collective-permute-start.4) | collective-permute-done | bytes 98336 | tf_op jit(solution)/shard_map/ppermute | solution.py:194
  24.6 3.2 %collective-permute-done.5.rest_1_ = bf16[192,256]{1,0:T(8,128)(2,1)S(1)} collective-permute-done((bf16[192,256]{1,0:T(8,128)(2,1)}, bf16[192,256]{1,0:T(8,128)(2,1)S(1)}, u32[]{:S(2)}, u32[]{:S(2)}) %collective-permute-start.5) | collective-permute-done | bytes 98336 | tf_op jit(solution)/shard_map/ppermute | solution.py:194
  27.8 0.6 %copy-done.6 = bf16[192,256]{1,0:T(8,128)(2,1)} copy-done((bf16[192,256]{1,0:T(8,128)(2,1)}, bf16[192,256]{1,0:T(8,128)(2,1)S(1)}, u32[]{:S(2)}) %copy-start.6) | copy-done | bytes 98328
  28.5 2.3 %shard_map.87 = (bf16[192,256]{1,0:T(8,128)(2,1)}, bf16[192,256]{1,0:T(8,128)(2,1)}, bf16[192,256]{1,0:T(8,128)(2,1)}, bf16[192,256]{1,0:T(8,128)(2,1)}, bf16[192,256]{1,0:T(8,128)(2,1)}) custom-call(f32[192,256]{1,0:T(8,128)} %get-tuple-element.13.own_ref, bf16[192,256]{1,0:T(8,128)(2,1)} %copy-done.5, bf16[192,256]{1,0:T(8,128)(2,1)} %copy-done.6, ...), custom_call_target="tpu_custom_call" | custom-call | tf_op jit(solution)/shard_map/pallas_call | solution.py:33
  30.7 2.4 %collective-permute-start.7 = (bf16[192,256]{1,0:T(8,128)(2,1)}, bf16[192,256]{1,0:T(8,128)(2,1)S(1)}, u32[]{:S(2)}, u32[]{:S(2)}) collective-permute-start(bf16[192,256]{1,0:T(8,128)(2,1)} %get-tuple-element.19), channel_id=1, source_target_pairs={{0,1},{1,2},{2,3},{3,0},{4,5},{5,6},{6,7},{7,4},{8,9},{9,10},{10,1... | collective-permute-start | bytes 294920 | tf_op jit(solution)/shard_map/ppermute | solution.py:196
  33.1 1.7 %collective-permute-start.8 = (bf16[192,256]{1,0:T(8,128)(2,1)}, bf16[192,256]{1,0:T(8,128)(2,1)S(1)}, u32[]{:S(2)}, u32[]{:S(2)}) collective-permute-start(bf16[192,256]{1,0:T(8,128)(2,1)} %get-tuple-element.20), channel_id=1, source_target_pairs={{0,2},{1,3},{2,0},{3,1},{4,6},{5,7},{6,4},{7,5},{8,10},{9,11},{10,... | collective-permute-start | bytes 294920 | tf_op jit(solution)/shard_map/ppermute | solution.py:196
  34.8 0.7 %collective-permute-start.9 = (bf16[192,256]{1,0:T(8,128)(2,1)}, bf16[192,256]{1,0:T(8,128)(2,1)S(1)}, u32[]{:S(2)}, u32[]{:S(2)}) collective-permute-start(bf16[192,256]{1,0:T(8,128)(2,1)} %get-tuple-element.21), channel_id=1, source_target_pairs={{0,3},{1,0},{2,1},{3,2},{4,7},{5,4},{6,5},{7,6},{8,11},{9,8},{10,9... | collective-permute-start | bytes 294920 | tf_op jit(solution)/shard_map/ppermute | solution.py:196
  35.5 2.9 %collective-permute-done.7.rest_0_ = bf16[192,256]{1,0:T(8,128)(2,1)S(1)} collective-permute-done((bf16[192,256]{1,0:T(8,128)(2,1)}, bf16[192,256]{1,0:T(8,128)(2,1)S(1)}, u32[]{:S(2)}, u32[]{:S(2)}) %collective-permute-start.7) | collective-permute-done | bytes 98336 | tf_op jit(solution)/shard_map/ppermute | solution.py:196
  38.4 3.1 %collective-permute-done.8.rest_1_ = bf16[192,256]{1,0:T(8,128)(2,1)S(1)} collective-permute-done((bf16[192,256]{1,0:T(8,128)(2,1)}, bf16[192,256]{1,0:T(8,128)(2,1)S(1)}, u32[]{:S(2)}, u32[]{:S(2)}) %collective-permute-start.8) | collective-permute-done | bytes 98336 | tf_op jit(solution)/shard_map/ppermute | solution.py:196
  41.5 0.6 %copy-done.3 = bf16[192,256]{1,0:T(8,128)(2,1)} copy-done((bf16[192,256]{1,0:T(8,128)(2,1)}, bf16[192,256]{1,0:T(8,128)(2,1)S(1)}, u32[]{:S(2)}) %copy-start.3) | copy-done | bytes 98328
  42.2 3.9 %shard_map.88 = (f32[4,192,256]{2,1,0:T(8,128)}, bf16[4,192,256]{2,1,0:T(8,128)(2,1)}) custom-call(s32[12]{0:T(128)} %bitcast.33, s32[12]{0:T(128)} %bitcast.35, s32[1]{0:T(128)} %bitcast.25.info_ref, bf16[12,256,256]{2,1,0:T(8,128)(2,1)} %bitcast.27, bf16[192,256]{1,0:T(8,128)(2,1)} %get-tuple-element.18.mine_ref, bf16[192,256]{1,0:T(8,128)(2,1)} %copy-done.2, ...), custom_call_target="tpu_custom_call" | custom-call | tf_op jit(solution)/shard_map/pallas_call | solution.py:156
  46.0 1.9 %collective-permute-done.10 = bf16[4,192,256]{2,1,0:T(8,128)(2,1)S(1)} collective-permute-done((bf16[4,192,256]{2,1,0:T(8,128)(2,1)}, bf16[4,192,256]{2,1,0:T(8,128)(2,1)S(1)}, u32[]{:S(2)}, u32[]{:S(2)}) %collective-permute-start.10) | collective-permute-done | bytes 393248 | tf_op jit(solution)/shard_map/ppermute | solution.py:200
  48.0 1.2 %fusion.4 = (bf16[4,192,256]{2,1,0:T(8,128)(2,1)S(1)}, f32[4,192,256]{2,1,0:T(8,128)S(1)}) fusion(f32[4,192,256]{2,1,0:T(8,128)} %get-tuple-element.22, bf16[4,192,256]{2,1,0:T(8,128)(2,1)S(1)} %collective-permute-done.10), kind=kLoop, calls=%fused_computation.10 | loop fusion | flops 589824 | bytes 2359296 | tf_op jit(solution)/shard_map/convert.2
  49.3 1.7 %collective-permute-start.11 = (bf16[192,256]{1,0:T(8,128)(2,1)S(1)}, bf16[192,256]{1,0:T(8,128)(2,1)S(1)}, u32[]{:S(2)}, u32[]{:S(2)}) collective-permute-start(bf16[192,256]{1,0:T(8,128)(2,1)S(1)} %get-tuple-element.26), channel_id=1, source_target_pairs={{0,8},{4,12},{8,16},{12,20},{16,24},{20,28},{24,0},{28,4},{1,9},{5... | collective-permute-start | bytes 294920 | tf_op jit(solution)/shard_map/ppermute | solution.py:204
  51.0 1.3 %collective-permute-start.13 = (bf16[192,256]{1,0:T(8,128)(2,1)S(1)}, bf16[192,256]{1,0:T(8,128)(2,1)S(1)}, u32[]{:S(2)}, u32[]{:S(2)}) collective-permute-start(bf16[192,256]{1,0:T(8,128)(2,1)S(1)} %get-tuple-element.27), channel_id=1, source_target_pairs={{0,24},{4,28},{8,0},{12,4},{16,8},{20,12},{24,16},{28,20},{1,25},{... | collective-permute-start | bytes 294920 | tf_op jit(solution)/shard_map/ppermute | solution.py:204
  52.2 1.7 %collective-permute-start.12 = (bf16[192,256]{1,0:T(8,128)(2,1)S(1)}, bf16[192,256]{1,0:T(8,128)(2,1)S(1)}, u32[]{:S(2)}, u32[]{:S(2)}) collective-permute-start(bf16[192,256]{1,0:T(8,128)(2,1)S(1)} %get-tuple-element.28), channel_id=1, source_target_pairs={{0,16},{4,20},{8,24},{12,28},{16,0},{20,4},{24,8},{28,12},{1,17},{... | collective-permute-start | bytes 294920 | tf_op jit(solution)/shard_map/ppermute | solution.py:204
  54.0 1.9 %collective-permute-done.11 = bf16[192,256]{1,0:T(8,128)(2,1)S(1)} collective-permute-done((bf16[192,256]{1,0:T(8,128)(2,1)S(1)}, bf16[192,256]{1,0:T(8,128)(2,1)S(1)}, u32[]{:S(2)}, u32[]{:S(2)}) %collective-permute-start.11) | collective-permute-done | bytes 98336 | tf_op jit(solution)/shard_map/ppermute | solution.py:204
  55.9 1.5 %collective-permute-done.13 = bf16[192,256]{1,0:T(8,128)(2,1)S(1)} collective-permute-done((bf16[192,256]{1,0:T(8,128)(2,1)S(1)}, bf16[192,256]{1,0:T(8,128)(2,1)S(1)}, u32[]{:S(2)}, u32[]{:S(2)}) %collective-permute-start.13) | collective-permute-done | bytes 98336 | tf_op jit(solution)/shard_map/ppermute | solution.py:204
  57.4 0.7 %fusion.3 = bf16[192,256]{1,0:T(8,128)(2,1)} fusion(f32[4,192,256]{2,1,0:T(8,128)S(1)} %get-tuple-element.25, bf16[192,256]{1,0:T(8,128)(2,1)S(1)} %collective-permute-done.13, bf16[192,256]{1,0:T(8,128)(2,1)S(1)} %collective-permute-done.12, bf16[192,256]{1,0:T(8,128)(2,1)S(1)} %collective-permute-done.11), kind=kLoop, calls=%fused_computation.6 | loop fusion | flops 344064 | bytes 589824 | tf_op jit(solution)/shard_map/convert_element_type | solution.py:205
  (19 shorter events, 0.1 us)
Async XLA Ops:
  0.6 7.6 %collective-permute-start = (bf16[192,256]{1,0:T(8,128)(2,1)}, bf16[192,256]{1,0:T(8,128)(2,1)S(1)}, u32[]{:S(2)}, u32[]{:S(2)}) collective-permute-start(bf16[192,256]{1,0:T(8,128)(2,1)} %param.7), channel_id=1, source_target_pairs={{0,8},{4,12},{8,16},{12,20},{16,24},{20,28},{24,0},{28,4},{1,9},{5... | collective-permute-start | bytes 294920 | tf_op jit(solution)/shard_map/ppermute | solution.py:190
  3.6 6.3 %collective-permute-start.2 = (bf16[192,256]{1,0:T(8,128)(2,1)}, bf16[192,256]{1,0:T(8,128)(2,1)S(1)}, u32[]{:S(2)}, u32[]{:S(2)}) collective-permute-start(bf16[192,256]{1,0:T(8,128)(2,1)} %param.7), channel_id=1, source_target_pairs={{0,24},{4,28},{8,0},{12,4},{16,8},{20,12},{24,16},{28,20},{1,25},{... | collective-permute-start | bytes 294920 | tf_op jit(solution)/shard_map/ppermute | solution.py:190
  4.7 5.3 %collective-permute-start.1 = (bf16[192,256]{1,0:T(8,128)(2,1)}, bf16[192,256]{1,0:T(8,128)(2,1)S(1)}, u32[]{:S(2)}, u32[]{:S(2)}) collective-permute-start(bf16[192,256]{1,0:T(8,128)(2,1)} %param.7), channel_id=1, source_target_pairs={{0,16},{4,20},{8,24},{12,28},{16,0},{20,4},{24,8},{28,12},{1,17},{... | collective-permute-start | bytes 294920 | tf_op jit(solution)/shard_map/ppermute | solution.py:190
  10.9 1.8 %copy-start = (bf16[4,192,256]{2,1,0:T(8,128)(2,1)}, bf16[4,192,256]{2,1,0:T(8,128)(2,1)S(1)}, u32[]{:S(2)}) copy-start(bf16[4,192,256]{2,1,0:T(8,128)(2,1)S(1)} %pad_maximum_fusion.near_ref) | copy-start | bytes 1179652
  10.9 1.8 %collective-permute-start.3 = (bf16[4,192,256]{2,1,0:T(8,128)(2,1)S(1)}, bf16[4,192,256]{2,1,0:T(8,128)(2,1)S(1)}, u32[]{:S(2)}, u32[]{:S(2)}) collective-permute-start(bf16[4,192,256]{2,1,0:T(8,128)(2,1)S(1)} %pad_maximum_fusion.near_ref), channel_id=1, source_target_pairs={{0,4},{4,0},{8,12},{12,8},{16,20},{20,16},{24,28},{28,24},{1,5},{5... | collective-permute-start | bytes 1179656 | tf_op jit(solution)/shard_map/ppermute | solution.py:191
  12.7 0.7 %copy-start.1 = (bf16[4,192,256]{2,1,0:T(8,128)(2,1)}, bf16[4,192,256]{2,1,0:T(8,128)(2,1)S(1)}, u32[]{:S(2)}) copy-start(bf16[4,192,256]{2,1,0:T(8,128)(2,1)S(1)} %collective-permute-done.3.far_ref) | copy-start | bytes 1179652
  17.0 7.6 %collective-permute-start.4 = (bf16[192,256]{1,0:T(8,128)(2,1)}, bf16[192,256]{1,0:T(8,128)(2,1)S(1)}, u32[]{:S(2)}, u32[]{:S(2)}) collective-permute-start(bf16[192,256]{1,0:T(8,128)(2,1)} %get-tuple-element.14), channel_id=1, source_target_pairs={{0,1},{1,2},{2,3},{3,0},{4,5},{5,6},{6,7},{7,4},{8,9},{9,10},{10,1... | collective-permute-start | bytes 294920 | tf_op jit(solution)/shard_map/ppermute | solution.py:194
  18.3 9.5 %collective-permute-start.5 = (bf16[192,256]{1,0:T(8,128)(2,1)}, bf16[192,256]{1,0:T(8,128)(2,1)S(1)}, u32[]{:S(2)}, u32[]{:S(2)}) collective-permute-start(bf16[192,256]{1,0:T(8,128)(2,1)} %get-tuple-element.15), channel_id=1, source_target_pairs={{0,2},{1,3},{2,0},{3,1},{4,6},{5,7},{6,4},{7,5},{8,10},{9,11},{10,... | collective-permute-start | bytes 294920 | tf_op jit(solution)/shard_map/ppermute | solution.py:194
  20.8 7.0 %collective-permute-start.6 = (bf16[192,256]{1,0:T(8,128)(2,1)}, bf16[192,256]{1,0:T(8,128)(2,1)S(1)}, u32[]{:S(2)}, u32[]{:S(2)}) collective-permute-start(bf16[192,256]{1,0:T(8,128)(2,1)} %get-tuple-element.16), channel_id=1, source_target_pairs={{0,3},{1,0},{2,1},{3,2},{4,7},{5,4},{6,5},{7,6},{8,11},{9,8},{10,9... | collective-permute-start | bytes 294920 | tf_op jit(solution)/shard_map/ppermute | solution.py:194
  24.6 3.2 %copy-start.5 = (bf16[192,256]{1,0:T(8,128)(2,1)}, bf16[192,256]{1,0:T(8,128)(2,1)S(1)}, u32[]{:S(2)}) copy-start(bf16[192,256]{1,0:T(8,128)(2,1)S(1)} %collective-permute-done.4.rest_0_) | copy-start | bytes 294916
  27.8 0.6 %copy-start.6 = (bf16[192,256]{1,0:T(8,128)(2,1)}, bf16[192,256]{1,0:T(8,128)(2,1)S(1)}, u32[]{:S(2)}) copy-start(bf16[192,256]{1,0:T(8,128)(2,1)S(1)} %collective-permute-done.5.rest_1_) | copy-start | bytes 294916
  27.8 0.7 %copy-start.7 = (bf16[192,256]{1,0:T(8,128)(2,1)}, bf16[192,256]{1,0:T(8,128)(2,1)S(1)}, u32[]{:S(2)}) copy-start(bf16[192,256]{1,0:T(8,128)(2,1)S(1)} %collective-permute-done.6.rest_2_) | copy-start | bytes 294916
  30.7 7.7 %collective-permute-start.7 = (bf16[192,256]{1,0:T(8,128)(2,1)}, bf16[192,256]{1,0:T(8,128)(2,1)S(1)}, u32[]{:S(2)}, u32[]{:S(2)}) collective-permute-start(bf16[192,256]{1,0:T(8,128)(2,1)} %get-tuple-element.19), channel_id=1, source_target_pairs={{0,1},{1,2},{2,3},{3,0},{4,5},{5,6},{6,7},{7,4},{8,9},{9,10},{10,1... | collective-permute-start | bytes 294920 | tf_op jit(solution)/shard_map/ppermute | solution.py:196
  33.1 8.4 %collective-permute-start.8 = (bf16[192,256]{1,0:T(8,128)(2,1)}, bf16[192,256]{1,0:T(8,128)(2,1)S(1)}, u32[]{:S(2)}, u32[]{:S(2)}) collective-permute-start(bf16[192,256]{1,0:T(8,128)(2,1)} %get-tuple-element.20), channel_id=1, source_target_pairs={{0,2},{1,3},{2,0},{3,1},{4,6},{5,7},{6,4},{7,5},{8,10},{9,11},{10,... | collective-permute-start | bytes 294920 | tf_op jit(solution)/shard_map/ppermute | solution.py:196
  34.8 6.7 %collective-permute-start.9 = (bf16[192,256]{1,0:T(8,128)(2,1)}, bf16[192,256]{1,0:T(8,128)(2,1)S(1)}, u32[]{:S(2)}, u32[]{:S(2)}) collective-permute-start(bf16[192,256]{1,0:T(8,128)(2,1)} %get-tuple-element.21), channel_id=1, source_target_pairs={{0,3},{1,0},{2,1},{3,2},{4,7},{5,4},{6,5},{7,6},{8,11},{9,8},{10,9... | collective-permute-start | bytes 294920 | tf_op jit(solution)/shard_map/ppermute | solution.py:196
  38.4 3.1 %copy-start.2 = (bf16[192,256]{1,0:T(8,128)(2,1)}, bf16[192,256]{1,0:T(8,128)(2,1)S(1)}, u32[]{:S(2)}) copy-start(bf16[192,256]{1,0:T(8,128)(2,1)S(1)} %collective-permute-done.7.rest_0_) | copy-start | bytes 294916
  41.5 0.6 %copy-start.3 = (bf16[192,256]{1,0:T(8,128)(2,1)}, bf16[192,256]{1,0:T(8,128)(2,1)S(1)}, u32[]{:S(2)}) copy-start(bf16[192,256]{1,0:T(8,128)(2,1)S(1)} %collective-permute-done.8.rest_1_) | copy-start | bytes 294916
  41.5 0.7 %copy-start.4 = (bf16[192,256]{1,0:T(8,128)(2,1)}, bf16[192,256]{1,0:T(8,128)(2,1)S(1)}, u32[]{:S(2)}) copy-start(bf16[192,256]{1,0:T(8,128)(2,1)S(1)} %collective-permute-done.9.rest_2_) | copy-start | bytes 294916
  46.0 1.9 %collective-permute-start.10 = (bf16[4,192,256]{2,1,0:T(8,128)(2,1)}, bf16[4,192,256]{2,1,0:T(8,128)(2,1)S(1)}, u32[]{:S(2)}, u32[]{:S(2)}) collective-permute-start(bf16[4,192,256]{2,1,0:T(8,128)(2,1)} %get-tuple-element.23), channel_id=1, source_target_pairs={{0,4},{4,0},{8,12},{12,8},{16,20},{20,16},{24,28},{28,24},{1,5},{5... | collective-permute-start | bytes 1179656 | tf_op jit(solution)/shard_map/ppermute | solution.py:200
  49.3 6.6 %collective-permute-start.11 = (bf16[192,256]{1,0:T(8,128)(2,1)S(1)}, bf16[192,256]{1,0:T(8,128)(2,1)S(1)}, u32[]{:S(2)}, u32[]{:S(2)}) collective-permute-start(bf16[192,256]{1,0:T(8,128)(2,1)S(1)} %get-tuple-element.26), channel_id=1, source_target_pairs={{0,8},{4,12},{8,16},{12,20},{16,24},{20,28},{24,0},{28,4},{1,9},{5... | collective-permute-start | bytes 294920 | tf_op jit(solution)/shard_map/ppermute | solution.py:204
  51.0 6.5 %collective-permute-start.13 = (bf16[192,256]{1,0:T(8,128)(2,1)S(1)}, bf16[192,256]{1,0:T(8,128)(2,1)S(1)}, u32[]{:S(2)}, u32[]{:S(2)}) collective-permute-start(bf16[192,256]{1,0:T(8,128)(2,1)S(1)} %get-tuple-element.27), channel_id=1, source_target_pairs={{0,24},{4,28},{8,0},{12,4},{16,8},{20,12},{24,16},{28,20},{1,25},{... | collective-permute-start | bytes 294920 | tf_op jit(solution)/shard_map/ppermute | solution.py:204
  52.2 5.2 %collective-permute-start.12 = (bf16[192,256]{1,0:T(8,128)(2,1)S(1)}, bf16[192,256]{1,0:T(8,128)(2,1)S(1)}, u32[]{:S(2)}, u32[]{:S(2)}) collective-permute-start(bf16[192,256]{1,0:T(8,128)(2,1)S(1)} %get-tuple-element.28), channel_id=1, source_target_pairs={{0,16},{4,20},{8,24},{12,28},{16,0},{20,4},{24,8},{28,12},{1,17},{... | collective-permute-start | bytes 294920 | tf_op jit(solution)/shard_map/ppermute | solution.py:204

commit v16 on v15

--- a/solution.py
+++ b/solution.py
@@ -187,7 +187,14 @@
     n_col = lax.axis_size("col")
     own_rows = features.shape[0]
 
-    near = jnp.stack([features] + [lax.ppermute(features, "row", perm) for perm in chip_shifts(n_row)])
+    where = lax.axis_index("row").astype(jnp.float32)
+    copies = [
+        features * (1.0 + 0.0 * (where + shift)).astype(features.dtype)
+        for shift in range(1, len(chip_shifts(n_row)) + 1)
+    ]
+    near = jnp.stack(
+        [features] + [lax.ppermute(c, "row", perm) for c, perm in zip(copies, chip_shifts(n_row))]
+    )
     far = lax.ppermute(near, "row", partner(n_row))
     info = tile_count.reshape(1)
     own, *send = tile_products(row_slots, col_slots, info, blocks, near, far, (n_col, own_rows))

time: 58.7 us -> 59.7 us (1.017)
  other arithmetic: 2.88 us -> 3.79 us
  waiting for transfers between devices: 21 us -> 21.8 us
  Pallas kernels: 9.63 us -> 8.88 us
    mul x0 -> x1, other arithmetic: none -> 0.92 us  [on_device(): features * (1.0 + 0.0 * (where + shift)).astype(features.dtype)]
    ppermute x3, waiting for transfers between devices: 5.19 us -> 5.79 us  [on_device(): lax.ppermute(send[shift], 'col', perm)]
  transfers between devices with their start and end apart: 14 -> 14, of which waited for: 10 -> 12; matrix products, arithmetic and copies ran while one was open for 0% -> 0% of each run, Pallas kernels for 0% -> 0%
where the time goes in v16:
time: 59.7 us; the launch traced here: 59 us
  waiting for transfers between devices  21.8 us (37%)
  starting transfers between devices  21.1 us (35%)
  Pallas kernels  8.88 us (15%)
  other arithmetic  3.79 us (6%)
  local copies, waits for them, and re-layouts  2.06 us (3%)
  between operations  1.4 us (2%)
    ppermute x3, waiting for transfers between devices, on_device(): lax.ppermute(piece, 'col', perm)  6.11 us
    ppermute x3, starting transfers between devices, on_device(): lax.ppermute(c, 'row', perm)  5.97 us
    ppermute x3, waiting for transfers between devices, on_device(): lax.ppermute(send[shift], 'col', perm)  5.79 us
    ppermute x3, starting transfers between devices, on_device(): lax.ppermute(send[shift], 'col', perm)  5.63 us
    ppermute x3, starting transfers between devices, on_device(): lax.ppermute(piece, 'col', perm)  4.82 us
    ppermute x3, starting transfers between devices, on_device(): total_g = total_g + lax.ppermute(piece, 'row', perm).astype(jnp.float32)  4.6 us
    ppermute x3, waiting for transfers between devices, on_device(): total_g = total_g + lax.ppermute(piece, 'row', perm).astype(jnp.float32)  3.75 us
    pallas_call x1, Pallas kernels, tile_products_t(): pl.pallas_call(functools.partial(backward_kernel, len(got) + 1), out_shap...  3.5 us
  transfers between devices with their start and end apart: 14, of which 12 were waited for; matrix products, arithmetic and copies ran while one was open for 0% of the time, Pallas kernels for 0%

profile of v16, /device:TPU:0, one launch (start us, length us, event | category | flops | bytes accessed | tf_op | source)
XLA Modules:
  0.0 59.0 jit_solution(18159396468790570303)
XLA Ops:
  0.7 0.9 %broadcast_multiply_fusion.2 = (bf16[192,256]{1,0:T(8,128)(2,1)S(1)}, bf16[192,256]{1,0:T(8,128)(2,1)S(1)}, bf16[192,256]{1,0:T(8,128)(2,1)S(1)}) fusion(bf16[192,256]{1,0:T(8,128)(2,1)} %param.7, bf16[]{:T(256)S(6)} %add.31, bf16[]{:T(256)S(6)} %add.35, bf16[]{:T(256)S(6)} %add.33), kind=kLoop, calls=%fused_computation.12 | loop fusion | flops 147456 | bytes 393222 | tf_op jit(solution)/shard_map/mul | solution.py:192
  1.6 3.0 %collective-permute-start = (bf16[192,256]{1,0:T(8,128)(2,1)S(1)}, bf16[192,256]{1,0:T(8,128)(2,1)S(1)}, u32[]{:S(2)}, u32[]{:S(2)}) collective-permute-start(bf16[192,256]{1,0:T(8,128)(2,1)S(1)} %get-tuple-element.29), channel_id=1, source_target_pairs={{0,8},{4,12},{8,16},{12,20},{16,24},{20,28},{24,0},{28,4},{1,9},{5... | collective-permute-start | bytes 294920 | tf_op jit(solution)/shard_map/ppermute | solution.py:196
  4.6 1.0 %collective-permute-start.2 = (bf16[192,256]{1,0:T(8,128)(2,1)S(1)}, bf16[192,256]{1,0:T(8,128)(2,1)S(1)}, u32[]{:S(2)}, u32[]{:S(2)}) collective-permute-start(bf16[192,256]{1,0:T(8,128)(2,1)S(1)} %get-tuple-element.30), channel_id=1, source_target_pairs={{0,24},{4,28},{8,0},{12,4},{16,8},{20,12},{24,16},{28,20},{1,25},{... | collective-permute-start | bytes 294920 | tf_op jit(solution)/shard_map/ppermute | solution.py:196
  5.6 1.9 %collective-permute-start.1 = (bf16[192,256]{1,0:T(8,128)(2,1)S(1)}, bf16[192,256]{1,0:T(8,128)(2,1)S(1)}, u32[]{:S(2)}, u32[]{:S(2)}) collective-permute-start(bf16[192,256]{1,0:T(8,128)(2,1)S(1)} %get-tuple-element.31), channel_id=1, source_target_pairs={{0,16},{4,20},{8,24},{12,28},{16,0},{20,4},{24,8},{28,12},{1,17},{... | collective-permute-start | bytes 294920 | tf_op jit(solution)/shard_map/ppermute | solution.py:196
  7.5 1.4 %collective-permute-done = bf16[192,256]{1,0:T(8,128)(2,1)S(1)} collective-permute-done((bf16[192,256]{1,0:T(8,128)(2,1)S(1)}, bf16[192,256]{1,0:T(8,128)(2,1)S(1)}, u32[]{:S(2)}, u32[]{:S(2)}) %collective-permute-start) | collective-permute-done | bytes 98336 | tf_op jit(solution)/shard_map/ppermute | solution.py:196
  9.0 1.7 %collective-permute-done.2 = bf16[192,256]{1,0:T(8,128)(2,1)S(1)} collective-permute-done((bf16[192,256]{1,0:T(8,128)(2,1)S(1)}, bf16[192,256]{1,0:T(8,128)(2,1)S(1)}, u32[]{:S(2)}, u32[]{:S(2)}) %collective-permute-start.2) | collective-permute-done | bytes 98336 | tf_op jit(solution)/shard_map/ppermute | solution.py:196
  10.7 0.9 %pad_maximum_fusion.near_ref = bf16[4,192,256]{2,1,0:T(8,128)(2,1)S(1)} fusion(bf16[1,192,256]{2,1,0:T(8,128)(2,1)S(1)} %bitcast.30, bf16[1,192,256]{2,1,0:T(8,128)(2,1)S(1)} %bitcast.31, bf16[1,192,256]{2,1,0:T(8,128)(2,1)S(1)} %bitcast.29, bf16[1,192,256]{2,1,0:T(8,128)(2,1)} %bitcast.28), kind=kLoop, calls=%fused_computation.1 | loop fusion | flops 589824 | bytes 786432 | tf_op jit(solution)/shard_map/stack | solution.py:195
  12.4 1.0 %collective-permute-done.3.far_ref = bf16[4,192,256]{2,1,0:T(8,128)(2,1)S(1)} collective-permute-done((bf16[4,192,256]{2,1,0:T(8,128)(2,1)S(1)}, bf16[4,192,256]{2,1,0:T(8,128)(2,1)S(1)}, u32[]{:S(2)}, u32[]{:S(2)}) %collective-permute-start.3) | collective-permute-done | bytes 393248 | tf_op jit(solution)/shard_map/ppermute | solution.py:198
  13.5 0.7 %copy-done.1 = bf16[4,192,256]{2,1,0:T(8,128)(2,1)} copy-done((bf16[4,192,256]{2,1,0:T(8,128)(2,1)}, bf16[4,192,256]{2,1,0:T(8,128)(2,1)S(1)}, u32[]{:S(2)}) %copy-start.1) | copy-done | bytes 393240
  14.2 3.1 %shard_map.86 = (f32[192,256]{1,0:T(8,128)}, bf16[192,256]{1,0:T(8,128)(2,1)}, bf16[192,256]{1,0:T(8,128)(2,1)}, bf16[192,256]{1,0:T(8,128)(2,1)}) custom-call(s32[12]{0:T(128)} %bitcast.32, s32[12]{0:T(128)} %bitcast.34, s32[1]{0:T(128)} %bitcast.24.info_ref, bf16[12,256,256]{2,1,0:T(8,128)(2,1)} %bitcast.26, bf16[4,192,256]{2,1,0:T(8,128)(2,1)} %copy-done, ...), custom_call_target="tpu_custom_call" | custom-call | tf_op jit(solution)/shard_map/pallas_call | solution.py:138
  17.3 2.1 %collective-permute-start.4 = (bf16[192,256]{1,0:T(8,128)(2,1)}, bf16[192,256]{1,0:T(8,128)(2,1)S(1)}, u32[]{:S(2)}, u32[]{:S(2)}) collective-permute-start(bf16[192,256]{1,0:T(8,128)(2,1)} %get-tuple-element.14), channel_id=1, source_target_pairs={{0,1},{1,2},{2,3},{3,0},{4,5},{5,6},{6,7},{7,4},{8,9},{9,10},{10,1... | collective-permute-start | bytes 294920 | tf_op jit(solution)/shard_map/ppermute | solution.py:201
  19.4 2.6 %collective-permute-start.5 = (bf16[192,256]{1,0:T(8,128)(2,1)}, bf16[192,256]{1,0:T(8,128)(2,1)S(1)}, u32[]{:S(2)}, u32[]{:S(2)}) collective-permute-start(bf16[192,256]{1,0:T(8,128)(2,1)} %get-tuple-element.15), channel_id=1, source_target_pairs={{0,2},{1,3},{2,0},{3,1},{4,6},{5,7},{6,4},{7,5},{8,10},{9,11},{10,... | collective-permute-start | bytes 294920 | tf_op jit(solution)/shard_map/ppermute | solution.py:201
  22.0 0.9 %collective-permute-start.6 = (bf16[192,256]{1,0:T(8,128)(2,1)}, bf16[192,256]{1,0:T(8,128)(2,1)S(1)}, u32[]{:S(2)}, u32[]{:S(2)}) collective-permute-start(bf16[192,256]{1,0:T(8,128)(2,1)} %get-tuple-element.16), channel_id=1, source_target_pairs={{0,3},{1,0},{2,1},{3,2},{4,7},{5,4},{6,5},{7,6},{8,11},{9,8},{10,9... | collective-permute-start | bytes 294920 | tf_op jit(solution)/shard_map/ppermute | solution.py:201
  22.9 2.4 %collective-permute-done.4.rest_0_ = bf16[192,256]{1,0:T(8,128)(2,1)S(1)} collective-permute-done((bf16[192,256]{1,0:T(8,128)(2,1)}, bf16[192,256]{1,0:T(8,128)(2,1)S(1)}, u32[]{:S(2)}, u32[]{:S(2)}) %collective-permute-start.4) | collective-permute-done | bytes 98336 | tf_op jit(solution)/shard_map/ppermute | solution.py:201
  25.3 3.3 %collective-permute-done.5.rest_1_ = bf16[192,256]{1,0:T(8,128)(2,1)S(1)} collective-permute-done((bf16[192,256]{1,0:T(8,128)(2,1)}, bf16[192,256]{1,0:T(8,128)(2,1)S(1)}, u32[]{:S(2)}, u32[]{:S(2)}) %collective-permute-start.5) | collective-permute-done | bytes 98336 | tf_op jit(solution)/shard_map/ppermute | solution.py:201
  28.7 0.5 copy-done.6
  29.4 2.3 %shard_map.87 = (bf16[192,256]{1,0:T(8,128)(2,1)}, bf16[192,256]{1,0:T(8,128)(2,1)}, bf16[192,256]{1,0:T(8,128)(2,1)}, bf16[192,256]{1,0:T(8,128)(2,1)}, bf16[192,256]{1,0:T(8,128)(2,1)}) custom-call(f32[192,256]{1,0:T(8,128)} %get-tuple-element.13.own_ref, bf16[192,256]{1,0:T(8,128)(2,1)} %copy-done.5, bf16[192,256]{1,0:T(8,128)(2,1)} %copy-done.6, ...), custom_call_target="tpu_custom_call" | custom-call | tf_op jit(solution)/shard_map/pallas_call | solution.py:33
  31.6 2.5 %collective-permute-start.7 = (bf16[192,256]{1,0:T(8,128)(2,1)}, bf16[192,256]{1,0:T(8,128)(2,1)S(1)}, u32[]{:S(2)}, u32[]{:S(2)}) collective-permute-start(bf16[192,256]{1,0:T(8,128)(2,1)} %get-tuple-element.19), channel_id=1, source_target_pairs={{0,1},{1,2},{2,3},{3,0},{4,5},{5,6},{6,7},{7,4},{8,9},{9,10},{10,1... | collective-permute-start | bytes 294920 | tf_op jit(solution)/shard_map/ppermute | solution.py:203
  34.1 1.5 %collective-permute-start.8 = (bf16[192,256]{1,0:T(8,128)(2,1)}, bf16[192,256]{1,0:T(8,128)(2,1)S(1)}, u32[]{:S(2)}, u32[]{:S(2)}) collective-permute-start(bf16[192,256]{1,0:T(8,128)(2,1)} %get-tuple-element.20), channel_id=1, source_target_pairs={{0,2},{1,3},{2,0},{3,1},{4,6},{5,7},{6,4},{7,5},{8,10},{9,11},{10,... | collective-permute-start | bytes 294920 | tf_op jit(solution)/shard_map/ppermute | solution.py:203
  35.6 0.9 %collective-permute-start.9 = (bf16[192,256]{1,0:T(8,128)(2,1)}, bf16[192,256]{1,0:T(8,128)(2,1)S(1)}, u32[]{:S(2)}, u32[]{:S(2)}) collective-permute-start(bf16[192,256]{1,0:T(8,128)(2,1)} %get-tuple-element.21), channel_id=1, source_target_pairs={{0,3},{1,0},{2,1},{3,2},{4,7},{5,4},{6,5},{7,6},{8,11},{9,8},{10,9... | collective-permute-start | bytes 294920 | tf_op jit(solution)/shard_map/ppermute | solution.py:203
  36.5 2.9 %collective-permute-done.7.rest_0_ = bf16[192,256]{1,0:T(8,128)(2,1)S(1)} collective-permute-done((bf16[192,256]{1,0:T(8,128)(2,1)}, bf16[192,256]{1,0:T(8,128)(2,1)S(1)}, u32[]{:S(2)}, u32[]{:S(2)}) %collective-permute-start.7) | collective-permute-done | bytes 98336 | tf_op jit(solution)/shard_map/ppermute | solution.py:203
  39.4 3.2 %collective-permute-done.8.rest_1_ = bf16[192,256]{1,0:T(8,128)(2,1)S(1)} collective-permute-done((bf16[192,256]{1,0:T(8,128)(2,1)}, bf16[192,256]{1,0:T(8,128)(2,1)S(1)}, u32[]{:S(2)}, u32[]{:S(2)}) %collective-permute-start.8) | collective-permute-done | bytes 98336 | tf_op jit(solution)/shard_map/ppermute | solution.py:203
  42.6 0.6 %copy-done.3 = bf16[192,256]{1,0:T(8,128)(2,1)} copy-done((bf16[192,256]{1,0:T(8,128)(2,1)}, bf16[192,256]{1,0:T(8,128)(2,1)S(1)}, u32[]{:S(2)}) %copy-start.3) | copy-done | bytes 98328
  43.2 3.5 %shard_map.88 = (f32[4,192,256]{2,1,0:T(8,128)}, bf16[4,192,256]{2,1,0:T(8,128)(2,1)}) custom-call(s32[12]{0:T(128)} %bitcast.33, s32[12]{0:T(128)} %bitcast.35, s32[1]{0:T(128)} %bitcast.25.info_ref, bf16[12,256,256]{2,1,0:T(8,128)(2,1)} %bitcast.27, bf16[192,256]{1,0:T(8,128)(2,1)} %get-tuple-element.18.mine_ref, bf16[192,256]{1,0:T(8,128)(2,1)} %copy-done.2, ...), custom_call_target="tpu_custom_call" | custom-call | tf_op jit(solution)/shard_map/pallas_call | solution.py:156
  46.8 1.9 %collective-permute-done.10 = bf16[4,192,256]{2,1,0:T(8,128)(2,1)S(1)} collective-permute-done((bf16[4,192,256]{2,1,0:T(8,128)(2,1)}, bf16[4,192,256]{2,1,0:T(8,128)(2,1)S(1)}, u32[]{:S(2)}, u32[]{:S(2)}) %collective-permute-start.10) | collective-permute-done | bytes 393248 | tf_op jit(solution)/shard_map/ppermute | solution.py:207
  48.7 1.2 %fusion.4 = (bf16[4,192,256]{2,1,0:T(8,128)(2,1)S(1)}, f32[4,192,256]{2,1,0:T(8,128)S(1)}) fusion(f32[4,192,256]{2,1,0:T(8,128)} %get-tuple-element.22, bf16[4,192,256]{2,1,0:T(8,128)(2,1)S(1)} %collective-permute-done.10), kind=kLoop, calls=%fused_computation.13 | loop fusion | flops 589824 | bytes 2359296 | tf_op jit(solution)/shard_map/convert.2
  50.0 2.1 %collective-permute-start.11 = (bf16[192,256]{1,0:T(8,128)(2,1)S(1)}, bf16[192,256]{1,0:T(8,128)(2,1)S(1)}, u32[]{:S(2)}, u32[]{:S(2)}) collective-permute-start(bf16[192,256]{1,0:T(8,128)(2,1)S(1)} %get-tuple-element.26), channel_id=1, source_target_pairs={{0,8},{4,12},{8,16},{12,20},{16,24},{20,28},{24,0},{28,4},{1,9},{5... | collective-permute-start | bytes 294920 | tf_op jit(solution)/shard_map/ppermute | solution.py:211
  52.1 1.1 %collective-permute-start.13 = (bf16[192,256]{1,0:T(8,128)(2,1)S(1)}, bf16[192,256]{1,0:T(8,128)(2,1)S(1)}, u32[]{:S(2)}, u32[]{:S(2)}) collective-permute-start(bf16[192,256]{1,0:T(8,128)(2,1)S(1)} %get-tuple-element.27), channel_id=1, source_target_pairs={{0,24},{4,28},{8,0},{12,4},{16,8},{20,12},{24,16},{28,20},{1,25},{... | collective-permute-start | bytes 294920 | tf_op jit(solution)/shard_map/ppermute | solution.py:211
  53.2 1.4 %collective-permute-start.12 = (bf16[192,256]{1,0:T(8,128)(2,1)S(1)}, bf16[192,256]{1,0:T(8,128)(2,1)S(1)}, u32[]{:S(2)}, u32[]{:S(2)}) collective-permute-start(bf16[192,256]{1,0:T(8,128)(2,1)S(1)} %get-tuple-element.28), channel_id=1, source_target_pairs={{0,16},{4,20},{8,24},{12,28},{16,0},{20,4},{24,8},{28,12},{1,17},{... | collective-permute-start | bytes 294920 | tf_op jit(solution)/shard_map/ppermute | solution.py:211
  54.6 2.2 %collective-permute-done.11 = bf16[192,256]{1,0:T(8,128)(2,1)S(1)} collective-permute-done((bf16[192,256]{1,0:T(8,128)(2,1)S(1)}, bf16[192,256]{1,0:T(8,128)(2,1)S(1)}, u32[]{:S(2)}, u32[]{:S(2)}) %collective-permute-start.11) | collective-permute-done | bytes 98336 | tf_op jit(solution)/shard_map/ppermute | solution.py:211
  56.8 1.4 %collective-permute-done.13 = bf16[192,256]{1,0:T(8,128)(2,1)S(1)} collective-permute-done((bf16[192,256]{1,0:T(8,128)(2,1)S(1)}, bf16[192,256]{1,0:T(8,128)(2,1)S(1)}, u32[]{:S(2)}, u32[]{:S(2)}) %collective-permute-start.13) | collective-permute-done | bytes 98336 | tf_op jit(solution)/shard_map/ppermute | solution.py:211
  58.3 0.7 %fusion.3 = bf16[192,256]{1,0:T(8,128)(2,1)} fusion(f32[4,192,256]{2,1,0:T(8,128)S(1)} %get-tuple-element.25, bf16[192,256]{1,0:T(8,128)(2,1)S(1)} %collective-permute-done.13, bf16[192,256]{1,0:T(8,128)(2,1)S(1)} %collective-permute-done.12, bf16[192,256]{1,0:T(8,128)(2,1)S(1)} %collective-permute-done.11), kind=kLoop, calls=%fused_computation.6 | loop fusion | flops 344064 | bytes 589824 | tf_op jit(solution)/shard_map/convert_element_type | solution.py:212
  (20 shorter events, 0.6 us)
Async XLA Ops:
  1.6 7.4 %collective-permute-start = (bf16[192,256]{1,0:T(8,128)(2,1)S(1)}, bf16[192,256]{1,0:T(8,128)(2,1)S(1)}, u32[]{:S(2)}, u32[]{:S(2)}) collective-permute-start(bf16[192,256]{1,0:T(8,128)(2,1)S(1)} %get-tuple-element.29), channel_id=1, source_target_pairs={{0,8},{4,12},{8,16},{12,20},{16,24},{20,28},{24,0},{28,4},{1,9},{5... | collective-permute-start | bytes 294920 | tf_op jit(solution)/shard_map/ppermute | solution.py:196
  4.6 6.1 %collective-permute-start.2 = (bf16[192,256]{1,0:T(8,128)(2,1)S(1)}, bf16[192,256]{1,0:T(8,128)(2,1)S(1)}, u32[]{:S(2)}, u32[]{:S(2)}) collective-permute-start(bf16[192,256]{1,0:T(8,128)(2,1)S(1)} %get-tuple-element.30), channel_id=1, source_target_pairs={{0,24},{4,28},{8,0},{12,4},{16,8},{20,12},{24,16},{28,20},{1,25},{... | collective-permute-start | bytes 294920 | tf_op jit(solution)/shard_map/ppermute | solution.py:196
  5.6 5.1 %collective-permute-start.1 = (bf16[192,256]{1,0:T(8,128)(2,1)S(1)}, bf16[192,256]{1,0:T(8,128)(2,1)S(1)}, u32[]{:S(2)}, u32[]{:S(2)}) collective-permute-start(bf16[192,256]{1,0:T(8,128)(2,1)S(1)} %get-tuple-element.31), channel_id=1, source_target_pairs={{0,16},{4,20},{8,24},{12,28},{16,0},{20,4},{24,8},{28,12},{1,17},{... | collective-permute-start | bytes 294920 | tf_op jit(solution)/shard_map/ppermute | solution.py:196
  11.7 1.8 %copy-start = (bf16[4,192,256]{2,1,0:T(8,128)(2,1)}, bf16[4,192,256]{2,1,0:T(8,128)(2,1)S(1)}, u32[]{:S(2)}) copy-start(bf16[4,192,256]{2,1,0:T(8,128)(2,1)S(1)} %pad_maximum_fusion.near_ref) | copy-start | bytes 1179652
  11.7 1.8 %collective-permute-start.3 = (bf16[4,192,256]{2,1,0:T(8,128)(2,1)S(1)}, bf16[4,192,256]{2,1,0:T(8,128)(2,1)S(1)}, u32[]{:S(2)}, u32[]{:S(2)}) collective-permute-start(bf16[4,192,256]{2,1,0:T(8,128)(2,1)S(1)} %pad_maximum_fusion.near_ref), channel_id=1, source_target_pairs={{0,4},{4,0},{8,12},{12,8},{16,20},{20,16},{24,28},{28,24},{1,5},{5... | collective-permute-start | bytes 1179656 | tf_op jit(solution)/shard_map/ppermute | solution.py:198
  13.5 0.7 %copy-start.1 = (bf16[4,192,256]{2,1,0:T(8,128)(2,1)}, bf16[4,192,256]{2,1,0:T(8,128)(2,1)S(1)}, u32[]{:S(2)}) copy-start(bf16[4,192,256]{2,1,0:T(8,128)(2,1)S(1)} %collective-permute-done.3.far_ref) | copy-start | bytes 1179652
  17.3 8.0 %collective-permute-start.4 = (bf16[192,256]{1,0:T(8,128)(2,1)}, bf16[192,256]{1,0:T(8,128)(2,1)S(1)}, u32[]{:S(2)}, u32[]{:S(2)}) collective-permute-start(bf16[192,256]{1,0:T(8,128)(2,1)} %get-tuple-element.14), channel_id=1, source_target_pairs={{0,1},{1,2},{2,3},{3,0},{4,5},{5,6},{6,7},{7,4},{8,9},{9,10},{10,1... | collective-permute-start | bytes 294920 | tf_op jit(solution)/shard_map/ppermute | solution.py:201
  19.4 9.2 %collective-permute-start.5 = (bf16[192,256]{1,0:T(8,128)(2,1)}, bf16[192,256]{1,0:T(8,128)(2,1)S(1)}, u32[]{:S(2)}, u32[]{:S(2)}) collective-permute-start(bf16[192,256]{1,0:T(8,128)(2,1)} %get-tuple-element.15), channel_id=1, source_target_pairs={{0,2},{1,3},{2,0},{3,1},{4,6},{5,7},{6,4},{7,5},{8,10},{9,11},{10,... | collective-permute-start | bytes 294920 | tf_op jit(solution)/shard_map/ppermute | solution.py:201
  22.0 6.7 %collective-permute-start.6 = (bf16[192,256]{1,0:T(8,128)(2,1)}, bf16[192,256]{1,0:T(8,128)(2,1)S(1)}, u32[]{:S(2)}, u32[]{:S(2)}) collective-permute-start(bf16[192,256]{1,0:T(8,128)(2,1)} %get-tuple-element.16), channel_id=1, source_target_pairs={{0,3},{1,0},{2,1},{3,2},{4,7},{5,4},{6,5},{7,6},{8,11},{9,8},{10,9... | collective-permute-start | bytes 294920 | tf_op jit(solution)/shard_map/ppermute | solution.py:201
  25.3 3.4 %copy-start.5 = (bf16[192,256]{1,0:T(8,128)(2,1)}, bf16[192,256]{1,0:T(8,128)(2,1)S(1)}, u32[]{:S(2)}) copy-start(bf16[192,256]{1,0:T(8,128)(2,1)S(1)} %collective-permute-done.4.rest_0_) | copy-start | bytes 294916
  28.6 0.6 %copy-start.6 = (bf16[192,256]{1,0:T(8,128)(2,1)}, bf16[192,256]{1,0:T(8,128)(2,1)S(1)}, u32[]{:S(2)}) copy-start(bf16[192,256]{1,0:T(8,128)(2,1)S(1)} %collective-permute-done.5.rest_1_) | copy-start | bytes 294916
  28.7 0.6 %copy-start.7 = (bf16[192,256]{1,0:T(8,128)(2,1)}, bf16[192,256]{1,0:T(8,128)(2,1)S(1)}, u32[]{:S(2)}) copy-start(bf16[192,256]{1,0:T(8,128)(2,1)S(1)} %collective-permute-done.6.rest_2_) | copy-start | bytes 294916
  31.6 7.7 %collective-permute-start.7 = (bf16[192,256]{1,0:T(8,128)(2,1)}, bf16[192,256]{1,0:T(8,128)(2,1)S(1)}, u32[]{:S(2)}, u32[]{:S(2)}) collective-permute-start(bf16[192,256]{1,0:T(8,128)(2,1)} %get-tuple-element.19), channel_id=1, source_target_pairs={{0,1},{1,2},{2,3},{3,0},{4,5},{5,6},{6,7},{7,4},{8,9},{9,10},{10,1... | collective-permute-start | bytes 294920 | tf_op jit(solution)/shard_map/ppermute | solution.py:203
  34.1 8.5 %collective-permute-start.8 = (bf16[192,256]{1,0:T(8,128)(2,1)}, bf16[192,256]{1,0:T(8,128)(2,1)S(1)}, u32[]{:S(2)}, u32[]{:S(2)}) collective-permute-start(bf16[192,256]{1,0:T(8,128)(2,1)} %get-tuple-element.20), channel_id=1, source_target_pairs={{0,2},{1,3},{2,0},{3,1},{4,6},{5,7},{6,4},{7,5},{8,10},{9,11},{10,... | collective-permute-start | bytes 294920 | tf_op jit(solution)/shard_map/ppermute | solution.py:203
  35.6 7.0 %collective-permute-start.9 = (bf16[192,256]{1,0:T(8,128)(2,1)}, bf16[192,256]{1,0:T(8,128)(2,1)S(1)}, u32[]{:S(2)}, u32[]{:S(2)}) collective-permute-start(bf16[192,256]{1,0:T(8,128)(2,1)} %get-tuple-element.21), channel_id=1, source_target_pairs={{0,3},{1,0},{2,1},{3,2},{4,7},{5,4},{6,5},{7,6},{8,11},{9,8},{10,9... | collective-permute-start | bytes 294920 | tf_op jit(solution)/shard_map/ppermute | solution.py:203
  39.4 3.2 %copy-start.2 = (bf16[192,256]{1,0:T(8,128)(2,1)}, bf16[192,256]{1,0:T(8,128)(2,1)S(1)}, u32[]{:S(2)}) copy-start(bf16[192,256]{1,0:T(8,128)(2,1)S(1)} %collective-permute-done.7.rest_0_) | copy-start | bytes 294916
  42.6 0.6 %copy-start.3 = (bf16[192,256]{1,0:T(8,128)(2,1)}, bf16[192,256]{1,0:T(8,128)(2,1)S(1)}, u32[]{:S(2)}) copy-start(bf16[192,256]{1,0:T(8,128)(2,1)S(1)} %collective-permute-done.8.rest_1_) | copy-start | bytes 294916
  42.6 0.7 %copy-start.4 = (bf16[192,256]{1,0:T(8,128)(2,1)}, bf16[192,256]{1,0:T(8,128)(2,1)S(1)}, u32[]{:S(2)}) copy-start(bf16[192,256]{1,0:T(8,128)(2,1)S(1)} %collective-permute-done.9.rest_2_) | copy-start | bytes 294916
  46.8 1.9 %collective-permute-start.10 = (bf16[4,192,256]{2,1,0:T(8,128)(2,1)}, bf16[4,192,256]{2,1,0:T(8,128)(2,1)S(1)}, u32[]{:S(2)}, u32[]{:S(2)}) collective-permute-start(bf16[4,192,256]{2,1,0:T(8,128)(2,1)} %get-tuple-element.23), channel_id=1, source_target_pairs={{0,4},{4,0},{8,12},{12,8},{16,20},{20,16},{24,28},{28,24},{1,5},{5... | collective-permute-start | bytes 1179656 | tf_op jit(solution)/shard_map/ppermute | solution.py:207
  50.0 6.8 %collective-permute-start.11 = (bf16[192,256]{1,0:T(8,128)(2,1)S(1)}, bf16[192,256]{1,0:T(8,128)(2,1)S(1)}, u32[]{:S(2)}, u32[]{:S(2)}) collective-permute-start(bf16[192,256]{1,0:T(8,128)(2,1)S(1)} %get-tuple-element.26), channel_id=1, source_target_pairs={{0,8},{4,12},{8,16},{12,20},{16,24},{20,28},{24,0},{28,4},{1,9},{5... | collective-permute-start | bytes 294920 | tf_op jit(solution)/shard_map/ppermute | solution.py:211
  52.1 6.1 %collective-permute-start.13 = (bf16[192,256]{1,0:T(8,128)(2,1)S(1)}, bf16[192,256]{1,0:T(8,128)(2,1)S(1)}, u32[]{:S(2)}, u32[]{:S(2)}) collective-permute-start(bf16[192,256]{1,0:T(8,128)(2,1)S(1)} %get-tuple-element.27), channel_id=1, source_target_pairs={{0,24},{4,28},{8,0},{12,4},{16,8},{20,12},{24,16},{28,20},{1,25},{... | collective-permute-start | bytes 294920 | tf_op jit(solution)/shard_map/ppermute | solution.py:211
  53.2 5.1 %collective-permute-start.12 = (bf16[192,256]{1,0:T(8,128)(2,1)S(1)}, bf16[192,256]{1,0:T(8,128)(2,1)S(1)}, u32[]{:S(2)}, u32[]{:S(2)}) collective-permute-start(bf16[192,256]{1,0:T(8,128)(2,1)S(1)} %get-tuple-element.28), channel_id=1, source_target_pairs={{0,16},{4,20},{8,24},{12,28},{16,0},{20,4},{24,8},{28,12},{1,17},{... | collective-permute-start | bytes 294920 | tf_op jit(solution)/shard_map/ppermute | solution.py:211

commit v17 on v15

--- a/solution.py
+++ b/solution.py
@@ -192,7 +192,18 @@
     info = tile_count.reshape(1)
     own, *send = tile_products(row_slots, col_slots, info, blocks, near, far, (n_col, own_rows))
     got_f = [lax.ppermute(send[shift], "col", perm) for shift, perm in enumerate(shifts("col"))]
-    activated, pulled_own, *pulled_out = dense_layer_kernel(own, got_f, cotangent, weight)
+    total = own
+    for piece in got_f:
+        total = total + piece.astype(jnp.float32)
+    mixed = jnp.dot(total.astype(jnp.bfloat16), weight, preferred_element_type=jnp.float32)
+    activated = jax.nn.silu(mixed).astype(jnp.bfloat16)
+    sigma = jax.nn.sigmoid(mixed)
+    scaled = (cotangent.astype(jnp.float32) * (sigma * (1.0 + mixed * (1.0 - sigma)))).astype(jnp.bfloat16)
+    pulled_own = jnp.dot(scaled, weight.T, preferred_element_type=jnp.float32).astype(jnp.bfloat16)
+    where = lax.axis_index("col").astype(jnp.float32)
+    pulled_out = [
+        pulled_own * (1.0 + 0.0 * (where + shift)).astype(jnp.bfloat16) for shift in range(1, n_col)
+    ]
     got = [lax.ppermute(piece, "col", perm) for piece, perm in zip(pulled_out, shifts("col"))]
     near_g, far_g = tile_products_t(
         row_slots, col_slots, info, blocks, pulled_own, got, n_row, n_row * own_rows

time: 58.7 us -> 60.2 us (1.026)
  waiting for transfers between devices: 21 us -> 24.4 us
  Pallas kernels: 9.63 us -> 6.46 us
  matrix products: 0 us -> 2.66 us
  local copies, waits for them, and re-layouts: 2.11 us -> 1.46 us
    ppermute x3, waiting for transfers between devices: 6.01 us -> 8.84 us  [on_device(): lax.ppermute(piece, 'col', perm)]
    dot_general x0 -> x2, matrix products: none -> 2.66 us  [the longest x1 1.79 us: on_device(): jnp.dot(total.astype(jnp.bfloat16), weight, preferred_element_type=jnp.fl...]
    pallas_call x1 -> x0, Pallas kernels: 2.26 us -> none  [dense_layer_kernel(): pl.pallas_call(functools.partial(dense_kernel, len(got) + 1), out_shape=(...]
    unnamed x16 -> x14, local copies, waits for them, and re-layouts: 2.08 us -> 1.44 us
  transfers between devices with their start and end apart: 14 -> 14, of which waited for: 10 -> 11; matrix products, arithmetic and copies ran while one was open for 0% -> 0% of each run, Pallas kernels for 0% -> 0%
where the time goes in v17:
time: 60.2 us; the launch traced here: 59.8 us
  waiting for transfers between devices  24.4 us (41%)
  starting transfers between devices  20.6 us (34%)
  Pallas kernels  6.46 us (11%)
  other arithmetic  2.88 us (5%)
  matrix products  2.66 us (4%)
  local copies, waits for them, and re-layouts  1.46 us (2%)
  between operations  1.37 us (2%)
    ppermute x3, waiting for transfers between devices, on_device(): lax.ppermute(piece, 'col', perm)  8.84 us
    ppermute x3, starting transfers between devices, on_device(): lax.ppermute(send[shift], 'col', perm)  6.09 us
    ppermute x3, starting transfers between devices, on_device(): lax.ppermute(features, 'row', perm)  5.97 us
    ppermute x3, waiting for transfers between devices, on_device(): lax.ppermute(send[shift], 'col', perm)  5.43 us
    ppermute x3, starting transfers between devices, on_device(): total_g = total_g + lax.ppermute(piece, 'row', perm).astype(jnp.float32)  4.28 us
    ppermute x3, starting transfers between devices, on_device(): lax.ppermute(piece, 'col', perm)  4.21 us
    ppermute x3, waiting for transfers between devices, on_device(): total_g = total_g + lax.ppermute(piece, 'row', perm).astype(jnp.float32)  3.77 us
    pallas_call x1, Pallas kernels, tile_products_t(): pl.pallas_call(functools.partial(backward_kernel, len(got) + 1), out_shap...  3.4 us
  transfers between devices with their start and end apart: 14, of which 11 were waited for; matrix products, arithmetic and copies ran while one was open for 0% of the time, Pallas kernels for 0%

profile of v17, /device:TPU:0, one launch (start us, length us, event | category | flops | bytes accessed | tf_op | source)
XLA Modules:
  0.0 59.8 jit_solution(7598232474596010331)
XLA Ops:
  0.6 3.0 %collective-permute-start = (bf16[192,256]{1,0:T(8,128)(2,1)}, bf16[192,256]{1,0:T(8,128)(2,1)S(1)}, u32[]{:S(2)}, u32[]{:S(2)}) collective-permute-start(bf16[192,256]{1,0:T(8,128)(2,1)} %param.7), channel_id=1, source_target_pairs={{0,8},{4,12},{8,16},{12,20},{16,24},{20,28},{24,0},{28,4},{1,9},{5... | collective-permute-start | bytes 294920 | tf_op jit(solution)/shard_map/ppermute | solution.py:190
  3.7 1.0 %collective-permute-start.2 = (bf16[192,256]{1,0:T(8,128)(2,1)}, bf16[192,256]{1,0:T(8,128)(2,1)S(1)}, u32[]{:S(2)}, u32[]{:S(2)}) collective-permute-start(bf16[192,256]{1,0:T(8,128)(2,1)} %param.7), channel_id=1, source_target_pairs={{0,24},{4,28},{8,0},{12,4},{16,8},{20,12},{24,16},{28,20},{1,25},{... | collective-permute-start | bytes 294920 | tf_op jit(solution)/shard_map/ppermute | solution.py:190
  4.7 1.9 %collective-permute-start.1 = (bf16[192,256]{1,0:T(8,128)(2,1)}, bf16[192,256]{1,0:T(8,128)(2,1)S(1)}, u32[]{:S(2)}, u32[]{:S(2)}) collective-permute-start(bf16[192,256]{1,0:T(8,128)(2,1)} %param.7), channel_id=1, source_target_pairs={{0,16},{4,20},{8,24},{12,28},{16,0},{20,4},{24,8},{28,12},{1,17},{... | collective-permute-start | bytes 294920 | tf_op jit(solution)/shard_map/ppermute | solution.py:190
  6.6 1.6 %collective-permute-done = bf16[192,256]{1,0:T(8,128)(2,1)S(1)} collective-permute-done((bf16[192,256]{1,0:T(8,128)(2,1)}, bf16[192,256]{1,0:T(8,128)(2,1)S(1)}, u32[]{:S(2)}, u32[]{:S(2)}) %collective-permute-start) | collective-permute-done | bytes 98336 | tf_op jit(solution)/shard_map/ppermute | solution.py:190
  8.3 1.7 %collective-permute-done.2 = bf16[192,256]{1,0:T(8,128)(2,1)S(1)} collective-permute-done((bf16[192,256]{1,0:T(8,128)(2,1)}, bf16[192,256]{1,0:T(8,128)(2,1)S(1)}, u32[]{:S(2)}, u32[]{:S(2)}) %collective-permute-start.2) | collective-permute-done | bytes 98336 | tf_op jit(solution)/shard_map/ppermute | solution.py:190
  10.0 0.9 %pad_maximum_fusion.near_ref = bf16[4,192,256]{2,1,0:T(8,128)(2,1)S(1)} fusion(bf16[1,192,256]{2,1,0:T(8,128)(2,1)S(1)} %bitcast.32, bf16[1,192,256]{2,1,0:T(8,128)(2,1)S(1)} %bitcast.33, bf16[1,192,256]{2,1,0:T(8,128)(2,1)S(1)} %bitcast.31, bf16[1,192,256]{2,1,0:T(8,128)(2,1)} %bitcast.30), kind=kLoop, calls=%fused_computation.2 | loop fusion | flops 589824 | bytes 786432 | tf_op jit(solution)/shard_map/stack | solution.py:190
  11.7 1.0 %collective-permute-done.3.far_ref = bf16[4,192,256]{2,1,0:T(8,128)(2,1)S(1)} collective-permute-done((bf16[4,192,256]{2,1,0:T(8,128)(2,1)S(1)}, bf16[4,192,256]{2,1,0:T(8,128)(2,1)S(1)}, u32[]{:S(2)}, u32[]{:S(2)}) %collective-permute-start.3) | collective-permute-done | bytes 393248 | tf_op jit(solution)/shard_map/ppermute | solution.py:191
  12.7 0.7 %copy-done.2 = bf16[4,192,256]{2,1,0:T(8,128)(2,1)} copy-done((bf16[4,192,256]{2,1,0:T(8,128)(2,1)}, bf16[4,192,256]{2,1,0:T(8,128)(2,1)S(1)}, u32[]{:S(2)}) %copy-start.2) | copy-done | bytes 393240
  13.5 3.1 %shard_map.86 = (f32[192,256]{1,0:T(8,128)}, bf16[192,256]{1,0:T(8,128)(2,1)}, bf16[192,256]{1,0:T(8,128)(2,1)}, bf16[192,256]{1,0:T(8,128)(2,1)}) custom-call(s32[12]{0:T(128)} %bitcast.34, s32[12]{0:T(128)} %bitcast.36, s32[1]{0:T(128)} %bitcast.26.info_ref, bf16[12,256,256]{2,1,0:T(8,128)(2,1)} %bitcast.28, bf16[4,192,256]{2,1,0:T(8,128)(2,1)} %copy-done.1, ...), custom_call_target="tpu_custom_call" | custom-call | tf_op jit(solution)/shard_map/pallas_call | solution.py:138
  16.5 1.8 %collective-permute-start.4 = (bf16[192,256]{1,0:T(8,128)(2,1)}, bf16[192,256]{1,0:T(8,128)(2,1)S(1)}, u32[]{:S(2)}, u32[]{:S(2)}) collective-permute-start(bf16[192,256]{1,0:T(8,128)(2,1)} %get-tuple-element.9), channel_id=1, source_target_pairs={{0,1},{1,2},{2,3},{3,0},{4,5},{5,6},{6,7},{7,4},{8,9},{9,10},{10,1... | collective-permute-start | bytes 294920 | tf_op jit(solution)/shard_map/ppermute | solution.py:194
  18.3 2.3 %collective-permute-start.5 = (bf16[192,256]{1,0:T(8,128)(2,1)}, bf16[192,256]{1,0:T(8,128)(2,1)S(1)}, u32[]{:S(2)}, u32[]{:S(2)}) collective-permute-start(bf16[192,256]{1,0:T(8,128)(2,1)} %get-tuple-element.10), channel_id=1, source_target_pairs={{0,2},{1,3},{2,0},{3,1},{4,6},{5,7},{6,4},{7,5},{8,10},{9,11},{10,... | collective-permute-start | bytes 294920 | tf_op jit(solution)/shard_map/ppermute | solution.py:194
  20.6 2.0 %collective-permute-start.6 = (bf16[192,256]{1,0:T(8,128)(2,1)}, bf16[192,256]{1,0:T(8,128)(2,1)S(1)}, u32[]{:S(2)}, u32[]{:S(2)}) collective-permute-start(bf16[192,256]{1,0:T(8,128)(2,1)} %get-tuple-element.11), channel_id=1, source_target_pairs={{0,3},{1,0},{2,1},{3,2},{4,7},{5,4},{6,5},{7,6},{8,11},{9,8},{10,9... | collective-permute-start | bytes 294920 | tf_op jit(solution)/shard_map/ppermute | solution.py:194
  22.6 1.7 %collective-permute-done.4 = bf16[192,256]{1,0:T(8,128)(2,1)S(1)} collective-permute-done((bf16[192,256]{1,0:T(8,128)(2,1)}, bf16[192,256]{1,0:T(8,128)(2,1)S(1)}, u32[]{:S(2)}, u32[]{:S(2)}) %collective-permute-start.4) | collective-permute-done | bytes 98336 | tf_op jit(solution)/shard_map/ppermute | solution.py:194
  24.3 3.7 %collective-permute-done.5 = bf16[192,256]{1,0:T(8,128)(2,1)S(1)} collective-permute-done((bf16[192,256]{1,0:T(8,128)(2,1)}, bf16[192,256]{1,0:T(8,128)(2,1)S(1)}, u32[]{:S(2)}, u32[]{:S(2)}) %collective-permute-start.5) | collective-permute-done | bytes 98336 | tf_op jit(solution)/shard_map/ppermute | solution.py:194
  28.1 1.8 %multiply_convert_fusion.1 = (bf16[192,256]{1,0:T(8,128)(2,1)}, f32[192,256]{1,0:T(8,128)S(1)}) fusion(bf16[256,256]{1,0:T(8,128)(2,1)S(1)} %copy-done, bf16[192,256]{1,0:T(8,128)(2,1)S(1)} %collective-permute-done.6, bf16[192,256]{1,0:T(8,128)(2,1)S(1)} %collective-permute-done.5, f32[192,256]{1,0:T(8,128)} %get-tuple-element.8, ...), kind=kOutput, calls=%fused_computation.9 | convolution fusion | flops 25755648 | bytes 917504 | tf_op jit(solution)/shard_map/dot_general | solution.py:198
  29.9 0.9 %broadcast_multiply_fusion = (bf16[192,256]{1,0:T(8,128)(2,1)S(1)}, bf16[192,256]{1,0:T(8,128)(2,1)S(1)}, bf16[192,256]{1,0:T(8,128)(2,1)S(1)}, bf16[192,256]{1,0:T(8,128)(2,1)}) fusion(bf16[]{:T(256)S(6)} %add.57, bf16[]{:T(256)S(6)} %add.55, bf16[]{:T(256)S(6)} %add.53, bf16[256,256]{1,0:T(8,128)(2,1)S(1)} %copy-done, ...), kind=kOutput, calls=%fused_computation.16 | convolution fusion | flops 25853952 | bytes 819206 | tf_op jit(solution)/shard_map/dot_general | solution.py:202
  30.7 3.6 %collective-permute-start.9 = (bf16[192,256]{1,0:T(8,128)(2,1)S(1)}, bf16[192,256]{1,0:T(8,128)(2,1)S(1)}, u32[]{:S(2)}, u32[]{:S(2)}) collective-permute-start(bf16[192,256]{1,0:T(8,128)(2,1)S(1)} %get-tuple-element.19), channel_id=1, source_target_pairs={{0,3},{1,0},{2,1},{3,2},{4,7},{5,4},{6,5},{7,6},{8,11},{9,8},{10,9... | collective-permute-start | bytes 294920 | tf_op jit(solution)/shard_map/ppermute | solution.py:207
  34.4 0.4 collective-permute-start.8
  34.8 0.2 collective-permute-start.7
  34.9 2.6 %collective-permute-done.9.rest_2_ = bf16[192,256]{1,0:T(8,128)(2,1)S(1)} collective-permute-done((bf16[192,256]{1,0:T(8,128)(2,1)S(1)}, bf16[192,256]{1,0:T(8,128)(2,1)S(1)}, u32[]{:S(2)}, u32[]{:S(2)}) %collective-permute-start.9) | collective-permute-done | bytes 98336 | tf_op jit(solution)/shard_map/ppermute | solution.py:207
  37.6 6.2 %collective-permute-done.8.rest_1_ = bf16[192,256]{1,0:T(8,128)(2,1)S(1)} collective-permute-done((bf16[192,256]{1,0:T(8,128)(2,1)S(1)}, bf16[192,256]{1,0:T(8,128)(2,1)S(1)}, u32[]{:S(2)}, u32[]{:S(2)}) %collective-permute-start.8) | collective-permute-done | bytes 98336 | tf_op jit(solution)/shard_map/ppermute | solution.py:207
  43.8 0.6 %copy-done.4 = bf16[192,256]{1,0:T(8,128)(2,1)} copy-done((bf16[192,256]{1,0:T(8,128)(2,1)}, bf16[192,256]{1,0:T(8,128)(2,1)S(1)}, u32[]{:S(2)}) %copy-start.4) | copy-done | bytes 98328
  44.5 3.4 %shard_map.87 = (f32[4,192,256]{2,1,0:T(8,128)}, bf16[4,192,256]{2,1,0:T(8,128)(2,1)}) custom-call(s32[12]{0:T(128)} %bitcast.35, s32[12]{0:T(128)} %bitcast.37, s32[1]{0:T(128)} %bitcast.27.info_ref, bf16[12,256,256]{2,1,0:T(8,128)(2,1)} %bitcast.29, bf16[192,256]{1,0:T(8,128)(2,1)} %get-tuple-element.24.mine_ref, bf16[192,256]{1,0:T(8,128)(2,1)} %copy-done.5, ...), custom_call_target="tpu_custom_call" | custom-call | tf_op jit(solution)/shard_map/pallas_call | solution.py:156
  47.9 1.9 %collective-permute-done.10 = bf16[4,192,256]{2,1,0:T(8,128)(2,1)S(1)} collective-permute-done((bf16[4,192,256]{2,1,0:T(8,128)(2,1)}, bf16[4,192,256]{2,1,0:T(8,128)(2,1)S(1)}, u32[]{:S(2)}, u32[]{:S(2)}) %collective-permute-start.10) | collective-permute-done | bytes 393248 | tf_op jit(solution)/shard_map/ppermute | solution.py:211
  49.8 1.2 %fusion.6 = (bf16[4,192,256]{2,1,0:T(8,128)(2,1)S(1)}, f32[4,192,256]{2,1,0:T(8,128)S(1)}) fusion(f32[4,192,256]{2,1,0:T(8,128)} %get-tuple-element.12, bf16[4,192,256]{2,1,0:T(8,128)(2,1)S(1)} %collective-permute-done.10), kind=kLoop, calls=%fused_computation.20 | loop fusion | flops 589824 | bytes 2359296 | tf_op jit(solution)/shard_map/convert.2
  51.1 1.7 %collective-permute-start.11 = (bf16[192,256]{1,0:T(8,128)(2,1)S(1)}, bf16[192,256]{1,0:T(8,128)(2,1)S(1)}, u32[]{:S(2)}, u32[]{:S(2)}) collective-permute-start(bf16[192,256]{1,0:T(8,128)(2,1)S(1)} %get-tuple-element.16), channel_id=1, source_target_pairs={{0,8},{4,12},{8,16},{12,20},{16,24},{20,28},{24,0},{28,4},{1,9},{5... | collective-permute-start | bytes 294920 | tf_op jit(solution)/shard_map/ppermute | solution.py:215
  52.8 1.3 %collective-permute-start.13 = (bf16[192,256]{1,0:T(8,128)(2,1)S(1)}, bf16[192,256]{1,0:T(8,128)(2,1)S(1)}, u32[]{:S(2)}, u32[]{:S(2)}) collective-permute-start(bf16[192,256]{1,0:T(8,128)(2,1)S(1)} %get-tuple-element.17), channel_id=1, source_target_pairs={{0,24},{4,28},{8,0},{12,4},{16,8},{20,12},{24,16},{28,20},{1,25},{... | collective-permute-start | bytes 294920 | tf_op jit(solution)/shard_map/ppermute | solution.py:215
  54.1 1.3 %collective-permute-start.12 = (bf16[192,256]{1,0:T(8,128)(2,1)S(1)}, bf16[192,256]{1,0:T(8,128)(2,1)S(1)}, u32[]{:S(2)}, u32[]{:S(2)}) collective-permute-start(bf16[192,256]{1,0:T(8,128)(2,1)S(1)} %get-tuple-element.18), channel_id=1, source_target_pairs={{0,16},{4,20},{8,24},{12,28},{16,0},{20,4},{24,8},{28,12},{1,17},{... | collective-permute-start | bytes 294920 | tf_op jit(solution)/shard_map/ppermute | solution.py:215
  55.4 2.3 %collective-permute-done.11 = bf16[192,256]{1,0:T(8,128)(2,1)S(1)} collective-permute-done((bf16[192,256]{1,0:T(8,128)(2,1)S(1)}, bf16[192,256]{1,0:T(8,128)(2,1)S(1)}, u32[]{:S(2)}, u32[]{:S(2)}) %collective-permute-start.11) | collective-permute-done | bytes 98336 | tf_op jit(solution)/shard_map/ppermute | solution.py:215
  57.6 1.2 %collective-permute-done.13 = bf16[192,256]{1,0:T(8,128)(2,1)S(1)} collective-permute-done((bf16[192,256]{1,0:T(8,128)(2,1)S(1)}, bf16[192,256]{1,0:T(8,128)(2,1)S(1)}, u32[]{:S(2)}, u32[]{:S(2)}) %collective-permute-start.13) | collective-permute-done | bytes 98336 | tf_op jit(solution)/shard_map/ppermute | solution.py:215
  58.8 0.3 collective-permute-done.12
  59.1 0.7 %fusion.3 = bf16[192,256]{1,0:T(8,128)(2,1)} fusion(f32[4,192,256]{2,1,0:T(8,128)S(1)} %get-tuple-element.15, bf16[192,256]{1,0:T(8,128)(2,1)S(1)} %collective-permute-done.13, bf16[192,256]{1,0:T(8,128)(2,1)S(1)} %collective-permute-done.12, bf16[192,256]{1,0:T(8,128)(2,1)S(1)} %collective-permute-done.11), kind=kLoop, calls=%fused_computation.7 | loop fusion | flops 344064 | bytes 589824 | tf_op jit(solution)/shard_map/convert_element_type | solution.py:216
  (18 shorter events, 0.2 us)
Async XLA Ops:
  0.6 27.4 %copy-start = (bf16[256,256]{1,0:T(8,128)(2,1)S(1)}, bf16[256,256]{1,0:T(8,128)(2,1)}, u32[]{:S(2)}) copy-start(bf16[256,256]{1,0:T(8,128)(2,1)} %param.12) | copy-start | bytes 393220
  0.6 7.6 %collective-permute-start = (bf16[192,256]{1,0:T(8,128)(2,1)}, bf16[192,256]{1,0:T(8,128)(2,1)S(1)}, u32[]{:S(2)}, u32[]{:S(2)}) collective-permute-start(bf16[192,256]{1,0:T(8,128)(2,1)} %param.7), channel_id=1, source_target_pairs={{0,8},{4,12},{8,16},{12,20},{16,24},{20,28},{24,0},{28,4},{1,9},{5... | collective-permute-start | bytes 294920 | tf_op jit(solution)/shard_map/ppermute | solution.py:190
  3.7 6.3 %collective-permute-start.2 = (bf16[192,256]{1,0:T(8,128)(2,1)}, bf16[192,256]{1,0:T(8,128)(2,1)S(1)}, u32[]{:S(2)}, u32[]{:S(2)}) collective-permute-start(bf16[192,256]{1,0:T(8,128)(2,1)} %param.7), channel_id=1, source_target_pairs={{0,24},{4,28},{8,0},{12,4},{16,8},{20,12},{24,16},{28,20},{1,25},{... | collective-permute-start | bytes 294920 | tf_op jit(solution)/shard_map/ppermute | solution.py:190
  4.7 5.3 %collective-permute-start.1 = (bf16[192,256]{1,0:T(8,128)(2,1)}, bf16[192,256]{1,0:T(8,128)(2,1)S(1)}, u32[]{:S(2)}, u32[]{:S(2)}) collective-permute-start(bf16[192,256]{1,0:T(8,128)(2,1)} %param.7), channel_id=1, source_target_pairs={{0,16},{4,20},{8,24},{12,28},{16,0},{20,4},{24,8},{28,12},{1,17},{... | collective-permute-start | bytes 294920 | tf_op jit(solution)/shard_map/ppermute | solution.py:190
  10.9 1.8 %copy-start.1 = (bf16[4,192,256]{2,1,0:T(8,128)(2,1)}, bf16[4,192,256]{2,1,0:T(8,128)(2,1)S(1)}, u32[]{:S(2)}) copy-start(bf16[4,192,256]{2,1,0:T(8,128)(2,1)S(1)} %pad_maximum_fusion.near_ref) | copy-start | bytes 1179652
  10.9 1.8 %collective-permute-start.3 = (bf16[4,192,256]{2,1,0:T(8,128)(2,1)S(1)}, bf16[4,192,256]{2,1,0:T(8,128)(2,1)S(1)}, u32[]{:S(2)}, u32[]{:S(2)}) collective-permute-start(bf16[4,192,256]{2,1,0:T(8,128)(2,1)S(1)} %pad_maximum_fusion.near_ref), channel_id=1, source_target_pairs={{0,4},{4,0},{8,12},{12,8},{16,20},{20,16},{24,28},{28,24},{1,5},{5... | collective-permute-start | bytes 1179656 | tf_op jit(solution)/shard_map/ppermute | solution.py:191
  12.7 0.7 %copy-start.2 = (bf16[4,192,256]{2,1,0:T(8,128)(2,1)}, bf16[4,192,256]{2,1,0:T(8,128)(2,1)S(1)}, u32[]{:S(2)}) copy-start(bf16[4,192,256]{2,1,0:T(8,128)(2,1)S(1)} %collective-permute-done.3.far_ref) | copy-start | bytes 1179652
  13.5 16.4 %copy-start.6 = (bf16[192,256]{1,0:T(8,128)(2,1)S(1)}, bf16[192,256]{1,0:T(8,128)(2,1)}, u32[]{:S(2)}) copy-start(bf16[192,256]{1,0:T(8,128)(2,1)} %param.13) | copy-start | bytes 294916
  16.5 7.8 %collective-permute-start.4 = (bf16[192,256]{1,0:T(8,128)(2,1)}, bf16[192,256]{1,0:T(8,128)(2,1)S(1)}, u32[]{:S(2)}, u32[]{:S(2)}) collective-permute-start(bf16[192,256]{1,0:T(8,128)(2,1)} %get-tuple-element.9), channel_id=1, source_target_pairs={{0,1},{1,2},{2,3},{3,0},{4,5},{5,6},{6,7},{7,4},{8,9},{9,10},{10,1... | collective-permute-start | bytes 294920 | tf_op jit(solution)/shard_map/ppermute | solution.py:194
  18.3 9.8 %collective-permute-start.5 = (bf16[192,256]{1,0:T(8,128)(2,1)}, bf16[192,256]{1,0:T(8,128)(2,1)S(1)}, u32[]{:S(2)}, u32[]{:S(2)}) collective-permute-start(bf16[192,256]{1,0:T(8,128)(2,1)} %get-tuple-element.10), channel_id=1, source_target_pairs={{0,2},{1,3},{2,0},{3,1},{4,6},{5,7},{6,4},{7,5},{8,10},{9,11},{10,... | collective-permute-start | bytes 294920 | tf_op jit(solution)/shard_map/ppermute | solution.py:194
  20.6 7.4 %collective-permute-start.6 = (bf16[192,256]{1,0:T(8,128)(2,1)}, bf16[192,256]{1,0:T(8,128)(2,1)S(1)}, u32[]{:S(2)}, u32[]{:S(2)}) collective-permute-start(bf16[192,256]{1,0:T(8,128)(2,1)} %get-tuple-element.11), channel_id=1, source_target_pairs={{0,3},{1,0},{2,1},{3,2},{4,7},{5,4},{6,5},{7,6},{8,11},{9,8},{10,9... | collective-permute-start | bytes 294920 | tf_op jit(solution)/shard_map/ppermute | solution.py:194
  30.7 6.8 %collective-permute-start.9 = (bf16[192,256]{1,0:T(8,128)(2,1)S(1)}, bf16[192,256]{1,0:T(8,128)(2,1)S(1)}, u32[]{:S(2)}, u32[]{:S(2)}) collective-permute-start(bf16[192,256]{1,0:T(8,128)(2,1)S(1)} %get-tuple-element.19), channel_id=1, source_target_pairs={{0,3},{1,0},{2,1},{3,2},{4,7},{5,4},{6,5},{7,6},{8,11},{9,8},{10,9... | collective-permute-start | bytes 294920 | tf_op jit(solution)/shard_map/ppermute | solution.py:207
  34.4 9.4 %collective-permute-start.8 = (bf16[192,256]{1,0:T(8,128)(2,1)S(1)}, bf16[192,256]{1,0:T(8,128)(2,1)S(1)}, u32[]{:S(2)}, u32[]{:S(2)}) collective-permute-start(bf16[192,256]{1,0:T(8,128)(2,1)S(1)} %get-tuple-element.20), channel_id=1, source_target_pairs={{0,2},{1,3},{2,0},{3,1},{4,6},{5,7},{6,4},{7,5},{8,10},{9,11},{10,... | collective-permute-start | bytes 294920 | tf_op jit(solution)/shard_map/ppermute | solution.py:207
  34.8 9.0 %collective-permute-start.7 = (bf16[192,256]{1,0:T(8,128)(2,1)S(1)}, bf16[192,256]{1,0:T(8,128)(2,1)S(1)}, u32[]{:S(2)}, u32[]{:S(2)}) collective-permute-start(bf16[192,256]{1,0:T(8,128)(2,1)S(1)} %get-tuple-element.21), channel_id=1, source_target_pairs={{0,1},{1,2},{2,3},{3,0},{4,5},{5,6},{6,7},{7,4},{8,9},{9,10},{10,1... | collective-permute-start | bytes 294920 | tf_op jit(solution)/shard_map/ppermute | solution.py:207
  37.6 6.2 %copy-start.3 = (bf16[192,256]{1,0:T(8,128)(2,1)}, bf16[192,256]{1,0:T(8,128)(2,1)S(1)}, u32[]{:S(2)}) copy-start(bf16[192,256]{1,0:T(8,128)(2,1)S(1)} %collective-permute-done.9.rest_2_) | copy-start | bytes 294916
  43.8 0.6 %copy-start.4 = (bf16[192,256]{1,0:T(8,128)(2,1)}, bf16[192,256]{1,0:T(8,128)(2,1)S(1)}, u32[]{:S(2)}) copy-start(bf16[192,256]{1,0:T(8,128)(2,1)S(1)} %collective-permute-done.8.rest_1_) | copy-start | bytes 294916
  43.8 0.7 %copy-start.5 = (bf16[192,256]{1,0:T(8,128)(2,1)}, bf16[192,256]{1,0:T(8,128)(2,1)S(1)}, u32[]{:S(2)}) copy-start(bf16[192,256]{1,0:T(8,128)(2,1)S(1)} %collective-permute-done.7.rest_0_) | copy-start | bytes 294916
  47.9 1.9 %collective-permute-start.10 = (bf16[4,192,256]{2,1,0:T(8,128)(2,1)}, bf16[4,192,256]{2,1,0:T(8,128)(2,1)S(1)}, u32[]{:S(2)}, u32[]{:S(2)}) collective-permute-start(bf16[4,192,256]{2,1,0:T(8,128)(2,1)} %get-tuple-element.13), channel_id=1, source_target_pairs={{0,4},{4,0},{8,12},{12,8},{16,20},{20,16},{24,28},{28,24},{1,5},{5... | collective-permute-start | bytes 1179656 | tf_op jit(solution)/shard_map/ppermute | solution.py:211
  51.1 6.6 %collective-permute-start.11 = (bf16[192,256]{1,0:T(8,128)(2,1)S(1)}, bf16[192,256]{1,0:T(8,128)(2,1)S(1)}, u32[]{:S(2)}, u32[]{:S(2)}) collective-permute-start(bf16[192,256]{1,0:T(8,128)(2,1)S(1)} %get-tuple-element.16), channel_id=1, source_target_pairs={{0,8},{4,12},{8,16},{12,20},{16,24},{20,28},{24,0},{28,4},{1,9},{5... | collective-permute-start | bytes 294920 | tf_op jit(solution)/shard_map/ppermute | solution.py:215
  52.8 6.1 %collective-permute-start.13 = (bf16[192,256]{1,0:T(8,128)(2,1)S(1)}, bf16[192,256]{1,0:T(8,128)(2,1)S(1)}, u32[]{:S(2)}, u32[]{:S(2)}) collective-permute-start(bf16[192,256]{1,0:T(8,128)(2,1)S(1)} %get-tuple-element.17), channel_id=1, source_target_pairs={{0,24},{4,28},{8,0},{12,4},{16,8},{20,12},{24,16},{28,20},{1,25},{... | collective-permute-start | bytes 294920 | tf_op jit(solution)/shard_map/ppermute | solution.py:215
  54.1 5.1 %collective-permute-start.12 = (bf16[192,256]{1,0:T(8,128)(2,1)S(1)}, bf16[192,256]{1,0:T(8,128)(2,1)S(1)}, u32[]{:S(2)}, u32[]{:S(2)}) collective-permute-start(bf16[192,256]{1,0:T(8,128)(2,1)S(1)} %get-tuple-element.18), channel_id=1, source_target_pairs={{0,16},{4,20},{8,24},{12,28},{16,0},{20,4},{24,8},{28,12},{1,17},{... | collective-permute-start | bytes 294920 | tf_op jit(solution)/shard_map/ppermute | solution.py:215

commit v18 on v15

--- a/solution.py
+++ b/solution.py
@@ -38,6 +38,22 @@
     )(own, *got, grad_rows, weight)
 
 
+def chip_sum_kernel(near_ref, far_ref, own_ref, *send_refs):
+    own_ref[...] = near_ref[0] + far_ref[0].astype(jnp.float32)
+    for shift, send_ref in enumerate(send_refs, start=1):
+        send_ref[...] = (near_ref[shift] + far_ref[shift].astype(jnp.float32)).astype(send_ref.dtype)
+
+
+def chip_sums(near, far):
+    piece = jax.ShapeDtypeStruct(near.shape[1:], jnp.bfloat16)
+    return pl.pallas_call(
+        chip_sum_kernel,
+        out_shape=(jax.ShapeDtypeStruct(near.shape[1:], jnp.float32),) + (piece,) * (near.shape[0] - 1),
+        in_specs=[VMEM, VMEM],
+        out_specs=(VMEM,) * near.shape[0],
+    )(near, far)
+
+
 UNROLL = 4
 
 
@@ -197,10 +213,8 @@
     near_g, far_g = tile_products_t(
         row_slots, col_slots, info, blocks, pulled_own, got, n_row, n_row * own_rows
     )
-    chip_sums = near_g + lax.ppermute(far_g, "row", partner(n_row)).astype(jnp.float32)
-    total_g = chip_sums[0]
-    for shift, perm in enumerate(chip_shifts(n_row)):
-        piece = chip_sums[shift + 1].astype(jnp.bfloat16)
+    total_g, *pieces = chip_sums(near_g, lax.ppermute(far_g, "row", partner(n_row)))
+    for piece, perm in zip(pieces, chip_shifts(n_row)):
         total_g = total_g + lax.ppermute(piece, "row", perm).astype(jnp.float32)
     return (activated, total_g.astype(jnp.bfloat16))
 

time: 58.7 us -> 61.2 us (1.043)
  starting transfers between devices: 21.2 us -> 22.4 us
  local copies, waits for them, and re-layouts: 2.11 us -> 2.85 us
  Pallas kernels: 9.63 us -> 10.3 us
    pallas_call x0 -> x1, Pallas kernels: none -> 2.02 us  [chip_sums(): pl.pallas_call(chip_sum_kernel, out_shape=(jax.ShapeDtypeStruct(near.shap...]
    another operation x1 -> x0, other arithmetic: 1.24 us -> none
    convert_element_type x1, other arithmetic: 0.69 us -> 1.62 us  [on_device(): return (activated, total_g.astype(jnp.bfloat16))]
    unnamed x16 -> x18, local copies, waits for them, and re-layouts: 2.08 us -> 2.85 us
    pallas_call x1, Pallas kernels: 3.86 us -> 3.17 us  [tile_products_t(): pl.pallas_call(functools.partial(backward_kernel, len(got) + 1), out_shap...]
    pallas_call x1, Pallas kernels: 3.5 us -> 2.85 us  [tile_products(): pl.pallas_call(forward_kernel, out_shape=(jax.ShapeDtypeStruct((chunk, wi...]
    ppermute x1, starting transfers between devices: 0.01 us -> 0.62 us  [on_device(): lax.ppermute(far_g, 'row', partner(n_row))]
where the time goes in v18:
time: 61.2 us; the launch traced here: 60.9 us
  starting transfers between devices  22.4 us (37%)
  waiting for transfers between devices  21.5 us (35%)
  Pallas kernels  10.3 us (17%)
  local copies, waits for them, and re-layouts  2.85 us (5%)
  other arithmetic  2.56 us (4%)
  between operations  1.35 us (2%)
    ppermute x3, waiting for transfers between devices, on_device(): lax.ppermute(piece, 'col', perm)  6.1 us
    ppermute x3, starting transfers between devices, on_device(): lax.ppermute(send[shift], 'col', perm)  6.01 us
    ppermute x3, starting transfers between devices, on_device(): lax.ppermute(features, 'row', perm)  5.97 us
    ppermute x3, waiting for transfers between devices, on_device(): lax.ppermute(send[shift], 'col', perm)  5.74 us
    ppermute x3, starting transfers between devices, on_device(): lax.ppermute(piece, 'col', perm)  4.95 us
    ppermute x3, starting transfers between devices, on_device(): total_g = total_g + lax.ppermute(piece, 'row', perm).astype(jnp.float32)  4.8 us
    ppermute x3, waiting for transfers between devices, on_device(): total_g = total_g + lax.ppermute(piece, 'row', perm).astype(jnp.float32)  3.66 us
    ppermute x3, waiting for transfers between devices, on_device(): lax.ppermute(features, 'row', perm)  3.36 us
  transfers between devices with their start and end apart: 14, of which 10 were waited for; matrix products, arithmetic and copies ran while one was open for 0% of the time, Pallas kernels for 0%

profile of v18, /device:TPU:0, one launch (start us, length us, event | category | flops | bytes accessed | tf_op | source)
XLA Modules:
  0.0 60.9 jit_solution(7754642474247868776)
XLA Ops:
  0.6 3.0 %collective-permute-start = (bf16[192,256]{1,0:T(8,128)(2,1)}, bf16[192,256]{1,0:T(8,128)(2,1)S(1)}, u32[]{:S(2)}, u32[]{:S(2)}) collective-permute-start(bf16[192,256]{1,0:T(8,128)(2,1)} %param.7), channel_id=1, source_target_pairs={{0,8},{4,12},{8,16},{12,20},{16,24},{20,28},{24,0},{28,4},{1,9},{5... | collective-permute-start | bytes 294920 | tf_op jit(solution)/shard_map/ppermute | solution.py:206
  3.6 1.0 %collective-permute-start.2 = (bf16[192,256]{1,0:T(8,128)(2,1)}, bf16[192,256]{1,0:T(8,128)(2,1)S(1)}, u32[]{:S(2)}, u32[]{:S(2)}) collective-permute-start(bf16[192,256]{1,0:T(8,128)(2,1)} %param.7), channel_id=1, source_target_pairs={{0,24},{4,28},{8,0},{12,4},{16,8},{20,12},{24,16},{28,20},{1,25},{... | collective-permute-start | bytes 294920 | tf_op jit(solution)/shard_map/ppermute | solution.py:206
  4.7 1.9 %collective-permute-start.1 = (bf16[192,256]{1,0:T(8,128)(2,1)}, bf16[192,256]{1,0:T(8,128)(2,1)S(1)}, u32[]{:S(2)}, u32[]{:S(2)}) collective-permute-start(bf16[192,256]{1,0:T(8,128)(2,1)} %param.7), channel_id=1, source_target_pairs={{0,16},{4,20},{8,24},{12,28},{16,0},{20,4},{24,8},{28,12},{1,17},{... | collective-permute-start | bytes 294920 | tf_op jit(solution)/shard_map/ppermute | solution.py:206
  6.6 1.6 %collective-permute-done = bf16[192,256]{1,0:T(8,128)(2,1)S(1)} collective-permute-done((bf16[192,256]{1,0:T(8,128)(2,1)}, bf16[192,256]{1,0:T(8,128)(2,1)S(1)}, u32[]{:S(2)}, u32[]{:S(2)}) %collective-permute-start) | collective-permute-done | bytes 98336 | tf_op jit(solution)/shard_map/ppermute | solution.py:206
  8.3 1.7 %collective-permute-done.2 = bf16[192,256]{1,0:T(8,128)(2,1)S(1)} collective-permute-done((bf16[192,256]{1,0:T(8,128)(2,1)}, bf16[192,256]{1,0:T(8,128)(2,1)S(1)}, u32[]{:S(2)}, u32[]{:S(2)}) %collective-permute-start.2) | collective-permute-done | bytes 98336 | tf_op jit(solution)/shard_map/ppermute | solution.py:206
  10.0 0.9 %pad_maximum_fusion.near_ref = bf16[4,192,256]{2,1,0:T(8,128)(2,1)S(1)} fusion(bf16[1,192,256]{2,1,0:T(8,128)(2,1)S(1)} %bitcast.14, bf16[1,192,256]{2,1,0:T(8,128)(2,1)S(1)} %bitcast.15, bf16[1,192,256]{2,1,0:T(8,128)(2,1)S(1)} %bitcast.13, bf16[1,192,256]{2,1,0:T(8,128)(2,1)} %bitcast.12), kind=kLoop, calls=%fused_computation | loop fusion | flops 589824 | bytes 786432 | tf_op jit(solution)/shard_map/stack | solution.py:206
  11.7 1.0 %collective-permute-done.3.far_ref = bf16[4,192,256]{2,1,0:T(8,128)(2,1)S(1)} collective-permute-done((bf16[4,192,256]{2,1,0:T(8,128)(2,1)S(1)}, bf16[4,192,256]{2,1,0:T(8,128)(2,1)S(1)}, u32[]{:S(2)}, u32[]{:S(2)}) %collective-permute-start.3) | collective-permute-done | bytes 393248 | tf_op jit(solution)/shard_map/ppermute | solution.py:207
  12.7 0.7 %copy-done.1 = bf16[4,192,256]{2,1,0:T(8,128)(2,1)} copy-done((bf16[4,192,256]{2,1,0:T(8,128)(2,1)}, bf16[4,192,256]{2,1,0:T(8,128)(2,1)S(1)}, u32[]{:S(2)}) %copy-start.1) | copy-done | bytes 393240
  13.5 2.9 %shard_map.86 = (f32[192,256]{1,0:T(8,128)}, bf16[192,256]{1,0:T(8,128)(2,1)}, bf16[192,256]{1,0:T(8,128)(2,1)}, bf16[192,256]{1,0:T(8,128)(2,1)}) custom-call(s32[12]{0:T(128)} %bitcast.16, s32[12]{0:T(128)} %bitcast.18, s32[1]{0:T(128)} %bitcast.8.info_ref, bf16[12,256,256]{2,1,0:T(8,128)(2,1)} %bitcast.10, bf16[4,192,256]{2,1,0:T(8,128)(2,1)} %copy-done, ...), custom_call_target="tpu_custom_call" | custom-call | tf_op jit(solution)/shard_map/pallas_call | solution.py:154
  16.3 1.7 %collective-permute-start.4 = (bf16[192,256]{1,0:T(8,128)(2,1)}, bf16[192,256]{1,0:T(8,128)(2,1)S(1)}, u32[]{:S(2)}, u32[]{:S(2)}) collective-permute-start(bf16[192,256]{1,0:T(8,128)(2,1)} %get-tuple-element.18), channel_id=1, source_target_pairs={{0,1},{1,2},{2,3},{3,0},{4,5},{5,6},{6,7},{7,4},{8,9},{9,10},{10,1... | collective-permute-start | bytes 294920 | tf_op jit(solution)/shard_map/ppermute | solution.py:210
  18.0 2.6 %collective-permute-start.5 = (bf16[192,256]{1,0:T(8,128)(2,1)}, bf16[192,256]{1,0:T(8,128)(2,1)S(1)}, u32[]{:S(2)}, u32[]{:S(2)}) collective-permute-start(bf16[192,256]{1,0:T(8,128)(2,1)} %get-tuple-element.19), channel_id=1, source_target_pairs={{0,2},{1,3},{2,0},{3,1},{4,6},{5,7},{6,4},{7,5},{8,10},{9,11},{10,... | collective-permute-start | bytes 294920 | tf_op jit(solution)/shard_map/ppermute | solution.py:210
  20.6 1.7 %collective-permute-start.6 = (bf16[192,256]{1,0:T(8,128)(2,1)}, bf16[192,256]{1,0:T(8,128)(2,1)S(1)}, u32[]{:S(2)}, u32[]{:S(2)}) collective-permute-start(bf16[192,256]{1,0:T(8,128)(2,1)} %get-tuple-element.20), channel_id=1, source_target_pairs={{0,3},{1,0},{2,1},{3,2},{4,7},{5,4},{6,5},{7,6},{8,11},{9,8},{10,9... | collective-permute-start | bytes 294920 | tf_op jit(solution)/shard_map/ppermute | solution.py:210
  22.3 1.8 %collective-permute-done.4.rest_0_ = bf16[192,256]{1,0:T(8,128)(2,1)S(1)} collective-permute-done((bf16[192,256]{1,0:T(8,128)(2,1)}, bf16[192,256]{1,0:T(8,128)(2,1)S(1)}, u32[]{:S(2)}, u32[]{:S(2)}) %collective-permute-start.4) | collective-permute-done | bytes 98336 | tf_op jit(solution)/shard_map/ppermute | solution.py:210
  24.1 4.0 %collective-permute-done.5.rest_1_ = bf16[192,256]{1,0:T(8,128)(2,1)S(1)} collective-permute-done((bf16[192,256]{1,0:T(8,128)(2,1)}, bf16[192,256]{1,0:T(8,128)(2,1)S(1)}, u32[]{:S(2)}, u32[]{:S(2)}) %collective-permute-start.5) | collective-permute-done | bytes 98336 | tf_op jit(solution)/shard_map/ppermute | solution.py:210
  28.1 0.6 %copy-done.7 = bf16[192,256]{1,0:T(8,128)(2,1)} copy-done((bf16[192,256]{1,0:T(8,128)(2,1)}, bf16[192,256]{1,0:T(8,128)(2,1)S(1)}, u32[]{:S(2)}) %copy-start.7) | copy-done | bytes 98328
  28.7 2.3 %shard_map.87 = (bf16[192,256]{1,0:T(8,128)(2,1)}, bf16[192,256]{1,0:T(8,128)(2,1)}, bf16[192,256]{1,0:T(8,128)(2,1)}, bf16[192,256]{1,0:T(8,128)(2,1)}, bf16[192,256]{1,0:T(8,128)(2,1)}) custom-call(f32[192,256]{1,0:T(8,128)} %get-tuple-element.17.own_ref, bf16[192,256]{1,0:T(8,128)(2,1)} %copy-done.6, bf16[192,256]{1,0:T(8,128)(2,1)} %copy-done.7, ...), custom_call_target="tpu_custom_call" | custom-call | tf_op jit(solution)/shard_map/pallas_call | solution.py:33
  31.0 2.6 %collective-permute-start.7 = (bf16[192,256]{1,0:T(8,128)(2,1)}, bf16[192,256]{1,0:T(8,128)(2,1)S(1)}, u32[]{:S(2)}, u32[]{:S(2)}) collective-permute-start(bf16[192,256]{1,0:T(8,128)(2,1)} %get-tuple-element.23), channel_id=1, source_target_pairs={{0,1},{1,2},{2,3},{3,0},{4,5},{5,6},{6,7},{7,4},{8,9},{9,10},{10,1... | collective-permute-start | bytes 294920 | tf_op jit(solution)/shard_map/ppermute | solution.py:212
  33.6 1.4 %collective-permute-start.8 = (bf16[192,256]{1,0:T(8,128)(2,1)}, bf16[192,256]{1,0:T(8,128)(2,1)S(1)}, u32[]{:S(2)}, u32[]{:S(2)}) collective-permute-start(bf16[192,256]{1,0:T(8,128)(2,1)} %get-tuple-element.24), channel_id=1, source_target_pairs={{0,2},{1,3},{2,0},{3,1},{4,6},{5,7},{6,4},{7,5},{8,10},{9,11},{10,... | collective-permute-start | bytes 294920 | tf_op jit(solution)/shard_map/ppermute | solution.py:212
  35.0 0.9 %collective-permute-start.9 = (bf16[192,256]{1,0:T(8,128)(2,1)}, bf16[192,256]{1,0:T(8,128)(2,1)S(1)}, u32[]{:S(2)}, u32[]{:S(2)}) collective-permute-start(bf16[192,256]{1,0:T(8,128)(2,1)} %get-tuple-element.25), channel_id=1, source_target_pairs={{0,3},{1,0},{2,1},{3,2},{4,7},{5,4},{6,5},{7,6},{8,11},{9,8},{10,9... | collective-permute-start | bytes 294920 | tf_op jit(solution)/shard_map/ppermute | solution.py:212
  35.9 2.8 %collective-permute-done.7.rest_0_ = bf16[192,256]{1,0:T(8,128)(2,1)S(1)} collective-permute-done((bf16[192,256]{1,0:T(8,128)(2,1)}, bf16[192,256]{1,0:T(8,128)(2,1)S(1)}, u32[]{:S(2)}, u32[]{:S(2)}) %collective-permute-start.7) | collective-permute-done | bytes 98336 | tf_op jit(solution)/shard_map/ppermute | solution.py:212
  38.8 3.3 %collective-permute-done.8.rest_1_ = bf16[192,256]{1,0:T(8,128)(2,1)S(1)} collective-permute-done((bf16[192,256]{1,0:T(8,128)(2,1)}, bf16[192,256]{1,0:T(8,128)(2,1)S(1)}, u32[]{:S(2)}, u32[]{:S(2)}) %collective-permute-start.8) | collective-permute-done | bytes 98336 | tf_op jit(solution)/shard_map/ppermute | solution.py:212
  42.1 0.6 %copy-done.4 = bf16[192,256]{1,0:T(8,128)(2,1)} copy-done((bf16[192,256]{1,0:T(8,128)(2,1)}, bf16[192,256]{1,0:T(8,128)(2,1)S(1)}, u32[]{:S(2)}) %copy-start.4) | copy-done | bytes 98328
  42.7 3.2 %shard_map.88 = (f32[4,192,256]{2,1,0:T(8,128)}, bf16[4,192,256]{2,1,0:T(8,128)(2,1)}) custom-call(s32[12]{0:T(128)} %bitcast.17, s32[12]{0:T(128)} %bitcast.19, s32[1]{0:T(128)} %bitcast.9.info_ref, bf16[12,256,256]{2,1,0:T(8,128)(2,1)} %bitcast.11, bf16[192,256]{1,0:T(8,128)(2,1)} %get-tuple-element.22.mine_ref, bf16[192,256]{1,0:T(8,128)(2,1)} %copy-done.3, ...), custom_call_target="tpu_custom_call" | custom-call | tf_op jit(solution)/shard_map/pallas_call | solution.py:172
  46.5 1.6 %collective-permute-done.10.far_ref = bf16[4,192,256]{2,1,0:T(8,128)(2,1)S(1)} collective-permute-done((bf16[4,192,256]{2,1,0:T(8,128)(2,1)}, bf16[4,192,256]{2,1,0:T(8,128)(2,1)S(1)}, u32[]{:S(2)}, u32[]{:S(2)}) %collective-permute-start.10) | collective-permute-done | bytes 393248 | tf_op jit(solution)/shard_map/ppermute | solution.py:216
  48.1 0.8 %copy-done.2 = bf16[4,192,256]{2,1,0:T(8,128)(2,1)} copy-done((bf16[4,192,256]{2,1,0:T(8,128)(2,1)}, bf16[4,192,256]{2,1,0:T(8,128)(2,1)S(1)}, u32[]{:S(2)}) %copy-start.2) | copy-done | bytes 393240
  48.8 2.0 %shard_map.89 = (f32[192,256]{1,0:T(8,128)}, bf16[192,256]{1,0:T(8,128)(2,1)}, bf16[192,256]{1,0:T(8,128)(2,1)}, bf16[192,256]{1,0:T(8,128)(2,1)}) custom-call(f32[4,192,256]{2,1,0:T(8,128)} %get-tuple-element.26.near_ref, bf16[4,192,256]{2,1,0:T(8,128)(2,1)} %copy-done.2), custom_call_target="tpu_custom_call" | custom-call | tf_op jit(solution)/shard_map/pallas_call | solution.py:49
  50.9 1.8 %collective-permute-start.11 = (bf16[192,256]{1,0:T(8,128)(2,1)}, bf16[192,256]{1,0:T(8,128)(2,1)S(1)}, u32[]{:S(2)}, u32[]{:S(2)}) collective-permute-start(bf16[192,256]{1,0:T(8,128)(2,1)} %get-tuple-element.29), channel_id=1, source_target_pairs={{0,8},{4,12},{8,16},{12,20},{16,24},{20,28},{24,0},{28,4},{1,9},{5... | collective-permute-start | bytes 294920 | tf_op jit(solution)/shard_map/ppermute | solution.py:218
  52.7 1.8 %collective-permute-start.12 = (bf16[192,256]{1,0:T(8,128)(2,1)}, bf16[192,256]{1,0:T(8,128)(2,1)S(1)}, u32[]{:S(2)}, u32[]{:S(2)}) collective-permute-start(bf16[192,256]{1,0:T(8,128)(2,1)} %get-tuple-element.30), channel_id=1, source_target_pairs={{0,16},{4,20},{8,24},{12,28},{16,0},{20,4},{24,8},{28,12},{1,17},{... | collective-permute-start | bytes 294920 | tf_op jit(solution)/shard_map/ppermute | solution.py:218
  54.4 1.2 %collective-permute-start.13 = (bf16[192,256]{1,0:T(8,128)(2,1)}, bf16[192,256]{1,0:T(8,128)(2,1)S(1)}, u32[]{:S(2)}, u32[]{:S(2)}) collective-permute-start(bf16[192,256]{1,0:T(8,128)(2,1)} %get-tuple-element.31), channel_id=1, source_target_pairs={{0,24},{4,28},{8,0},{12,4},{16,8},{20,12},{24,16},{28,20},{1,25},{... | collective-permute-start | bytes 294920 | tf_op jit(solution)/shard_map/ppermute | solution.py:218
  55.7 2.1 %collective-permute-done.11 = bf16[192,256]{1,0:T(8,128)(2,1)S(1)} collective-permute-done((bf16[192,256]{1,0:T(8,128)(2,1)}, bf16[192,256]{1,0:T(8,128)(2,1)S(1)}, u32[]{:S(2)}, u32[]{:S(2)}) %collective-permute-start.11) | collective-permute-done | bytes 98336 | tf_op jit(solution)/shard_map/ppermute | solution.py:218
  57.7 1.6 %collective-permute-done.12 = bf16[192,256]{1,0:T(8,128)(2,1)S(1)} collective-permute-done((bf16[192,256]{1,0:T(8,128)(2,1)}, bf16[192,256]{1,0:T(8,128)(2,1)S(1)}, u32[]{:S(2)}, u32[]{:S(2)}) %collective-permute-start.12) | collective-permute-done | bytes 98336 | tf_op jit(solution)/shard_map/ppermute | solution.py:218
  59.3 1.6 %add_convert_fusion = bf16[192,256]{1,0:T(8,128)(2,1)} fusion(bf16[192,256]{1,0:T(8,128)(2,1)S(1)} %collective-permute-done.13, bf16[192,256]{1,0:T(8,128)(2,1)S(1)} %collective-permute-done.12, f32[192,256]{1,0:T(8,128)} %get-tuple-element.28, bf16[192,256]{1,0:T(8,128)(2,1)S(1)} %collective-permute-done.11), kind=kLoop, calls=%fused_computation.1 | loop fusion | flops 344064 | bytes 589824 | tf_op jit(solution)/shard_map/convert_element_type | solution.py:219
  (20 shorter events, 0.8 us)
Async XLA Ops:
  0.6 7.6 %collective-permute-start = (bf16[192,256]{1,0:T(8,128)(2,1)}, bf16[192,256]{1,0:T(8,128)(2,1)S(1)}, u32[]{:S(2)}, u32[]{:S(2)}) collective-permute-start(bf16[192,256]{1,0:T(8,128)(2,1)} %param.7), channel_id=1, source_target_pairs={{0,8},{4,12},{8,16},{12,20},{16,24},{20,28},{24,0},{28,4},{1,9},{5... | collective-permute-start | bytes 294920 | tf_op jit(solution)/shard_map/ppermute | solution.py:206
  3.6 6.3 %collective-permute-start.2 = (bf16[192,256]{1,0:T(8,128)(2,1)}, bf16[192,256]{1,0:T(8,128)(2,1)S(1)}, u32[]{:S(2)}, u32[]{:S(2)}) collective-permute-start(bf16[192,256]{1,0:T(8,128)(2,1)} %param.7), channel_id=1, source_target_pairs={{0,24},{4,28},{8,0},{12,4},{16,8},{20,12},{24,16},{28,20},{1,25},{... | collective-permute-start | bytes 294920 | tf_op jit(solution)/shard_map/ppermute | solution.py:206
  4.7 5.3 %collective-permute-start.1 = (bf16[192,256]{1,0:T(8,128)(2,1)}, bf16[192,256]{1,0:T(8,128)(2,1)S(1)}, u32[]{:S(2)}, u32[]{:S(2)}) collective-permute-start(bf16[192,256]{1,0:T(8,128)(2,1)} %param.7), channel_id=1, source_target_pairs={{0,16},{4,20},{8,24},{12,28},{16,0},{20,4},{24,8},{28,12},{1,17},{... | collective-permute-start | bytes 294920 | tf_op jit(solution)/shard_map/ppermute | solution.py:206
  10.9 1.8 %copy-start = (bf16[4,192,256]{2,1,0:T(8,128)(2,1)}, bf16[4,192,256]{2,1,0:T(8,128)(2,1)S(1)}, u32[]{:S(2)}) copy-start(bf16[4,192,256]{2,1,0:T(8,128)(2,1)S(1)} %pad_maximum_fusion.near_ref) | copy-start | bytes 1179652
  10.9 1.8 %collective-permute-start.3 = (bf16[4,192,256]{2,1,0:T(8,128)(2,1)S(1)}, bf16[4,192,256]{2,1,0:T(8,128)(2,1)S(1)}, u32[]{:S(2)}, u32[]{:S(2)}) collective-permute-start(bf16[4,192,256]{2,1,0:T(8,128)(2,1)S(1)} %pad_maximum_fusion.near_ref), channel_id=1, source_target_pairs={{0,4},{4,0},{8,12},{12,8},{16,20},{20,16},{24,28},{28,24},{1,5},{5... | collective-permute-start | bytes 1179656 | tf_op jit(solution)/shard_map/ppermute | solution.py:207
  12.7 0.7 %copy-start.1 = (bf16[4,192,256]{2,1,0:T(8,128)(2,1)}, bf16[4,192,256]{2,1,0:T(8,128)(2,1)S(1)}, u32[]{:S(2)}) copy-start(bf16[4,192,256]{2,1,0:T(8,128)(2,1)S(1)} %collective-permute-done.3.far_ref) | copy-start | bytes 1179652
  16.3 7.8 %collective-permute-start.4 = (bf16[192,256]{1,0:T(8,128)(2,1)}, bf16[192,256]{1,0:T(8,128)(2,1)S(1)}, u32[]{:S(2)}, u32[]{:S(2)}) collective-permute-start(bf16[192,256]{1,0:T(8,128)(2,1)} %get-tuple-element.18), channel_id=1, source_target_pairs={{0,1},{1,2},{2,3},{3,0},{4,5},{5,6},{6,7},{7,4},{8,9},{9,10},{10,1... | collective-permute-start | bytes 294920 | tf_op jit(solution)/shard_map/ppermute | solution.py:210
  18.0 10.1 %collective-permute-start.5 = (bf16[192,256]{1,0:T(8,128)(2,1)}, bf16[192,256]{1,0:T(8,128)(2,1)S(1)}, u32[]{:S(2)}, u32[]{:S(2)}) collective-permute-start(bf16[192,256]{1,0:T(8,128)(2,1)} %get-tuple-element.19), channel_id=1, source_target_pairs={{0,2},{1,3},{2,0},{3,1},{4,6},{5,7},{6,4},{7,5},{8,10},{9,11},{10,... | collective-permute-start | bytes 294920 | tf_op jit(solution)/shard_map/ppermute | solution.py:210
  20.6 7.5 %collective-permute-start.6 = (bf16[192,256]{1,0:T(8,128)(2,1)}, bf16[192,256]{1,0:T(8,128)(2,1)S(1)}, u32[]{:S(2)}, u32[]{:S(2)}) collective-permute-start(bf16[192,256]{1,0:T(8,128)(2,1)} %get-tuple-element.20), channel_id=1, source_target_pairs={{0,3},{1,0},{2,1},{3,2},{4,7},{5,4},{6,5},{7,6},{8,11},{9,8},{10,9... | collective-permute-start | bytes 294920 | tf_op jit(solution)/shard_map/ppermute | solution.py:210
  24.1 4.0 %copy-start.6 = (bf16[192,256]{1,0:T(8,128)(2,1)}, bf16[192,256]{1,0:T(8,128)(2,1)S(1)}, u32[]{:S(2)}) copy-start(bf16[192,256]{1,0:T(8,128)(2,1)S(1)} %collective-permute-done.4.rest_0_) | copy-start | bytes 294916
  28.1 0.6 %copy-start.7 = (bf16[192,256]{1,0:T(8,128)(2,1)}, bf16[192,256]{1,0:T(8,128)(2,1)S(1)}, u32[]{:S(2)}) copy-start(bf16[192,256]{1,0:T(8,128)(2,1)S(1)} %collective-permute-done.5.rest_1_) | copy-start | bytes 294916
  28.1 0.7 %copy-start.8 = (bf16[192,256]{1,0:T(8,128)(2,1)}, bf16[192,256]{1,0:T(8,128)(2,1)S(1)}, u32[]{:S(2)}) copy-start(bf16[192,256]{1,0:T(8,128)(2,1)S(1)} %collective-permute-done.6.rest_2_) | copy-start | bytes 294916
  31.0 7.8 %collective-permute-start.7 = (bf16[192,256]{1,0:T(8,128)(2,1)}, bf16[192,256]{1,0:T(8,128)(2,1)S(1)}, u32[]{:S(2)}, u32[]{:S(2)}) collective-permute-start(bf16[192,256]{1,0:T(8,128)(2,1)} %get-tuple-element.23), channel_id=1, source_target_pairs={{0,1},{1,2},{2,3},{3,0},{4,5},{5,6},{6,7},{7,4},{8,9},{9,10},{10,1... | collective-permute-start | bytes 294920 | tf_op jit(solution)/shard_map/ppermute | solution.py:212
  33.6 8.5 %collective-permute-start.8 = (bf16[192,256]{1,0:T(8,128)(2,1)}, bf16[192,256]{1,0:T(8,128)(2,1)S(1)}, u32[]{:S(2)}, u32[]{:S(2)}) collective-permute-start(bf16[192,256]{1,0:T(8,128)(2,1)} %get-tuple-element.24), channel_id=1, source_target_pairs={{0,2},{1,3},{2,0},{3,1},{4,6},{5,7},{6,4},{7,5},{8,10},{9,11},{10,... | collective-permute-start | bytes 294920 | tf_op jit(solution)/shard_map/ppermute | solution.py:212
  35.0 7.0 %collective-permute-start.9 = (bf16[192,256]{1,0:T(8,128)(2,1)}, bf16[192,256]{1,0:T(8,128)(2,1)S(1)}, u32[]{:S(2)}, u32[]{:S(2)}) collective-permute-start(bf16[192,256]{1,0:T(8,128)(2,1)} %get-tuple-element.25), channel_id=1, source_target_pairs={{0,3},{1,0},{2,1},{3,2},{4,7},{5,4},{6,5},{7,6},{8,11},{9,8},{10,9... | collective-permute-start | bytes 294920 | tf_op jit(solution)/shard_map/ppermute | solution.py:212
  38.8 3.3 %copy-start.3 = (bf16[192,256]{1,0:T(8,128)(2,1)}, bf16[192,256]{1,0:T(8,128)(2,1)S(1)}, u32[]{:S(2)}) copy-start(bf16[192,256]{1,0:T(8,128)(2,1)S(1)} %collective-permute-done.7.rest_0_) | copy-start | bytes 294916
  42.0 0.6 %copy-start.4 = (bf16[192,256]{1,0:T(8,128)(2,1)}, bf16[192,256]{1,0:T(8,128)(2,1)S(1)}, u32[]{:S(2)}) copy-start(bf16[192,256]{1,0:T(8,128)(2,1)S(1)} %collective-permute-done.8.rest_1_) | copy-start | bytes 294916
  42.0 0.7 %copy-start.5 = (bf16[192,256]{1,0:T(8,128)(2,1)}, bf16[192,256]{1,0:T(8,128)(2,1)S(1)}, u32[]{:S(2)}) copy-start(bf16[192,256]{1,0:T(8,128)(2,1)S(1)} %collective-permute-done.9.rest_2_) | copy-start | bytes 294916
  45.9 2.2 %collective-permute-start.10 = (bf16[4,192,256]{2,1,0:T(8,128)(2,1)}, bf16[4,192,256]{2,1,0:T(8,128)(2,1)S(1)}, u32[]{:S(2)}, u32[]{:S(2)}) collective-permute-start(bf16[4,192,256]{2,1,0:T(8,128)(2,1)} %get-tuple-element.27), channel_id=1, source_target_pairs={{0,4},{4,0},{8,12},{12,8},{16,20},{20,16},{24,28},{28,24},{1,5},{5... | collective-permute-start | bytes 1179656 | tf_op jit(solution)/shard_map/ppermute | solution.py:216
  48.1 0.8 %copy-start.2 = (bf16[4,192,256]{2,1,0:T(8,128)(2,1)}, bf16[4,192,256]{2,1,0:T(8,128)(2,1)S(1)}, u32[]{:S(2)}) copy-start(bf16[4,192,256]{2,1,0:T(8,128)(2,1)S(1)} %collective-permute-done.10.far_ref) | copy-start | bytes 1179652
  50.9 6.9 %collective-permute-start.11 = (bf16[192,256]{1,0:T(8,128)(2,1)}, bf16[192,256]{1,0:T(8,128)(2,1)S(1)}, u32[]{:S(2)}, u32[]{:S(2)}) collective-permute-start(bf16[192,256]{1,0:T(8,128)(2,1)} %get-tuple-element.29), channel_id=1, source_target_pairs={{0,8},{4,12},{8,16},{12,20},{16,24},{20,28},{24,0},{28,4},{1,9},{5... | collective-permute-start | bytes 294920 | tf_op jit(solution)/shard_map/ppermute | solution.py:218
  52.7 6.6 %collective-permute-start.12 = (bf16[192,256]{1,0:T(8,128)(2,1)}, bf16[192,256]{1,0:T(8,128)(2,1)S(1)}, u32[]{:S(2)}, u32[]{:S(2)}) collective-permute-start(bf16[192,256]{1,0:T(8,128)(2,1)} %get-tuple-element.30), channel_id=1, source_target_pairs={{0,16},{4,20},{8,24},{12,28},{16,0},{20,4},{24,8},{28,12},{1,17},{... | collective-permute-start | bytes 294920 | tf_op jit(solution)/shard_map/ppermute | solution.py:218
  54.4 4.9 %collective-permute-start.13 = (bf16[192,256]{1,0:T(8,128)(2,1)}, bf16[192,256]{1,0:T(8,128)(2,1)S(1)}, u32[]{:S(2)}, u32[]{:S(2)}) collective-permute-start(bf16[192,256]{1,0:T(8,128)(2,1)} %get-tuple-element.31), channel_id=1, source_target_pairs={{0,24},{4,28},{8,0},{12,4},{16,8},{20,12},{24,16},{28,20},{1,25},{... | collective-permute-start | bytes 294920 | tf_op jit(solution)/shard_map/ppermute | solution.py:218

commit v19 on v15

--- a/solution.py
+++ b/solution.py
@@ -38,7 +38,7 @@
     )(own, *got, grad_rows, weight)
 
 
-UNROLL = 4
+UNROLL = 6
 
 
 def run_slots(count, product, place):

time: 58.7 us -> 58.9 us (level)
  waiting for transfers between devices: 21 us -> 22 us
  starting transfers between devices: 21.2 us -> 20.6 us
    ppermute x3, waiting for transfers between devices: 5.19 us -> 5.84 us  [on_device(): lax.ppermute(send[shift], 'col', perm)]
  transfers between devices with their start and end apart: 14 -> 14, of which waited for: 10 -> 12; matrix products, arithmetic and copies ran while one was open for 0% -> 0% of each run, Pallas kernels for 0% -> 0%
where the time goes in v19:
time: 58.9 us; the launch traced here: 58.6 us
  waiting for transfers between devices  22 us (37%)
  starting transfers between devices  20.6 us (35%)
  Pallas kernels  9.71 us (16%)
  other arithmetic  2.88 us (5%)
  local copies, waits for them, and re-layouts  2.06 us (3%)
  between operations  1.37 us (2%)
    ppermute x3, waiting for transfers between devices, on_device(): lax.ppermute(piece, 'col', perm)  6.24 us
    ppermute x3, starting transfers between devices, on_device(): lax.ppermute(features, 'row', perm)  5.97 us
    ppermute x3, waiting for transfers between devices, on_device(): lax.ppermute(send[shift], 'col', perm)  5.84 us
    ppermute x3, starting transfers between devices, on_device(): lax.ppermute(send[shift], 'col', perm)  5.07 us
    ppermute x3, starting transfers between devices, on_device(): lax.ppermute(piece, 'col', perm)  4.92 us
    ppermute x3, starting transfers between devices, on_device(): total_g = total_g + lax.ppermute(piece, 'row', perm).astype(jnp.float32)  4.55 us
    pallas_call x1, Pallas kernels, tile_products_t(): pl.pallas_call(functools.partial(backward_kernel, len(got) + 1), out_shap...  3.96 us
    ppermute x3, waiting for transfers between devices, on_device(): total_g = total_g + lax.ppermute(piece, 'row', perm).astype(jnp.float32)  3.59 us
  transfers between devices with their start and end apart: 14, of which 12 were waited for; matrix products, arithmetic and copies ran while one was open for 0% of the time, Pallas kernels for 0%

profile of v19, /device:TPU:0, one launch (start us, length us, event | category | flops | bytes accessed | tf_op | source)
XLA Modules:
  0.0 58.6 jit_solution(3615645841571720248)
XLA Ops:
  0.6 3.0 %collective-permute-start = (bf16[192,256]{1,0:T(8,128)(2,1)}, bf16[192,256]{1,0:T(8,128)(2,1)S(1)}, u32[]{:S(2)}, u32[]{:S(2)}) collective-permute-start(bf16[192,256]{1,0:T(8,128)(2,1)} %param.7), channel_id=1, source_target_pairs={{0,8},{4,12},{8,16},{12,20},{16,24},{20,28},{24,0},{28,4},{1,9},{5... | collective-permute-start | bytes 294920 | tf_op jit(solution)/shard_map/ppermute | solution.py:190
  3.6 1.0 %collective-permute-start.2 = (bf16[192,256]{1,0:T(8,128)(2,1)}, bf16[192,256]{1,0:T(8,128)(2,1)S(1)}, u32[]{:S(2)}, u32[]{:S(2)}) collective-permute-start(bf16[192,256]{1,0:T(8,128)(2,1)} %param.7), channel_id=1, source_target_pairs={{0,24},{4,28},{8,0},{12,4},{16,8},{20,12},{24,16},{28,20},{1,25},{... | collective-permute-start | bytes 294920 | tf_op jit(solution)/shard_map/ppermute | solution.py:190
  4.7 1.9 %collective-permute-start.1 = (bf16[192,256]{1,0:T(8,128)(2,1)}, bf16[192,256]{1,0:T(8,128)(2,1)S(1)}, u32[]{:S(2)}, u32[]{:S(2)}) collective-permute-start(bf16[192,256]{1,0:T(8,128)(2,1)} %param.7), channel_id=1, source_target_pairs={{0,16},{4,20},{8,24},{12,28},{16,0},{20,4},{24,8},{28,12},{1,17},{... | collective-permute-start | bytes 294920 | tf_op jit(solution)/shard_map/ppermute | solution.py:190
  6.6 1.6 %collective-permute-done = bf16[192,256]{1,0:T(8,128)(2,1)S(1)} collective-permute-done((bf16[192,256]{1,0:T(8,128)(2,1)}, bf16[192,256]{1,0:T(8,128)(2,1)S(1)}, u32[]{:S(2)}, u32[]{:S(2)}) %collective-permute-start) | collective-permute-done | bytes 98336 | tf_op jit(solution)/shard_map/ppermute | solution.py:190
  8.3 1.7 %collective-permute-done.2 = bf16[192,256]{1,0:T(8,128)(2,1)S(1)} collective-permute-done((bf16[192,256]{1,0:T(8,128)(2,1)}, bf16[192,256]{1,0:T(8,128)(2,1)S(1)}, u32[]{:S(2)}, u32[]{:S(2)}) %collective-permute-start.2) | collective-permute-done | bytes 98336 | tf_op jit(solution)/shard_map/ppermute | solution.py:190
  10.0 0.9 %pad_maximum_fusion.near_ref = bf16[4,192,256]{2,1,0:T(8,128)(2,1)S(1)} fusion(bf16[1,192,256]{2,1,0:T(8,128)(2,1)S(1)} %bitcast.30, bf16[1,192,256]{2,1,0:T(8,128)(2,1)S(1)} %bitcast.31, bf16[1,192,256]{2,1,0:T(8,128)(2,1)S(1)} %bitcast.29, bf16[1,192,256]{2,1,0:T(8,128)(2,1)} %bitcast.28), kind=kLoop, calls=%fused_computation.1 | loop fusion | flops 589824 | bytes 786432 | tf_op jit(solution)/shard_map/stack | solution.py:190
  11.7 1.0 %collective-permute-done.3.far_ref = bf16[4,192,256]{2,1,0:T(8,128)(2,1)S(1)} collective-permute-done((bf16[4,192,256]{2,1,0:T(8,128)(2,1)S(1)}, bf16[4,192,256]{2,1,0:T(8,128)(2,1)S(1)}, u32[]{:S(2)}, u32[]{:S(2)}) %collective-permute-start.3) | collective-permute-done | bytes 393248 | tf_op jit(solution)/shard_map/ppermute | solution.py:191
  12.7 0.7 %copy-done.1 = bf16[4,192,256]{2,1,0:T(8,128)(2,1)} copy-done((bf16[4,192,256]{2,1,0:T(8,128)(2,1)}, bf16[4,192,256]{2,1,0:T(8,128)(2,1)S(1)}, u32[]{:S(2)}) %copy-start.1) | copy-done | bytes 393240
  13.5 3.5 %shard_map.86 = (f32[192,256]{1,0:T(8,128)}, bf16[192,256]{1,0:T(8,128)(2,1)}, bf16[192,256]{1,0:T(8,128)(2,1)}, bf16[192,256]{1,0:T(8,128)(2,1)}) custom-call(s32[12]{0:T(128)} %bitcast.32, s32[12]{0:T(128)} %bitcast.34, s32[1]{0:T(128)} %bitcast.24.info_ref, bf16[12,256,256]{2,1,0:T(8,128)(2,1)} %bitcast.26, bf16[4,192,256]{2,1,0:T(8,128)(2,1)} %copy-done, ...), custom_call_target="tpu_custom_call" | custom-call | tf_op jit(solution)/shard_map/pallas_call | solution.py:138
  16.9 1.1 %collective-permute-start.4 = (bf16[192,256]{1,0:T(8,128)(2,1)}, bf16[192,256]{1,0:T(8,128)(2,1)S(1)}, u32[]{:S(2)}, u32[]{:S(2)}) collective-permute-start(bf16[192,256]{1,0:T(8,128)(2,1)} %get-tuple-element.14), channel_id=1, source_target_pairs={{0,1},{1,2},{2,3},{3,0},{4,5},{5,6},{6,7},{7,4},{8,9},{9,10},{10,1... | collective-permute-start | bytes 294920 | tf_op jit(solution)/shard_map/ppermute | solution.py:194
  18.1 2.6 %collective-permute-start.5 = (bf16[192,256]{1,0:T(8,128)(2,1)}, bf16[192,256]{1,0:T(8,128)(2,1)S(1)}, u32[]{:S(2)}, u32[]{:S(2)}) collective-permute-start(bf16[192,256]{1,0:T(8,128)(2,1)} %get-tuple-element.15), channel_id=1, source_target_pairs={{0,2},{1,3},{2,0},{3,1},{4,6},{5,7},{6,4},{7,5},{8,10},{9,11},{10,... | collective-permute-start | bytes 294920 | tf_op jit(solution)/shard_map/ppermute | solution.py:194
  20.7 1.3 %collective-permute-start.6 = (bf16[192,256]{1,0:T(8,128)(2,1)}, bf16[192,256]{1,0:T(8,128)(2,1)S(1)}, u32[]{:S(2)}, u32[]{:S(2)}) collective-permute-start(bf16[192,256]{1,0:T(8,128)(2,1)} %get-tuple-element.16), channel_id=1, source_target_pairs={{0,3},{1,0},{2,1},{3,2},{4,7},{5,4},{6,5},{7,6},{8,11},{9,8},{10,9... | collective-permute-start | bytes 294920 | tf_op jit(solution)/shard_map/ppermute | solution.py:194
  22.0 2.2 %collective-permute-done.4.rest_0_ = bf16[192,256]{1,0:T(8,128)(2,1)S(1)} collective-permute-done((bf16[192,256]{1,0:T(8,128)(2,1)}, bf16[192,256]{1,0:T(8,128)(2,1)S(1)}, u32[]{:S(2)}, u32[]{:S(2)}) %collective-permute-start.4) | collective-permute-done | bytes 98336 | tf_op jit(solution)/shard_map/ppermute | solution.py:194
  24.2 3.6 %collective-permute-done.5.rest_1_ = bf16[192,256]{1,0:T(8,128)(2,1)S(1)} collective-permute-done((bf16[192,256]{1,0:T(8,128)(2,1)}, bf16[192,256]{1,0:T(8,128)(2,1)S(1)}, u32[]{:S(2)}, u32[]{:S(2)}) %collective-permute-start.5) | collective-permute-done | bytes 98336 | tf_op jit(solution)/shard_map/ppermute | solution.py:194
  27.9 0.6 %copy-done.6 = bf16[192,256]{1,0:T(8,128)(2,1)} copy-done((bf16[192,256]{1,0:T(8,128)(2,1)}, bf16[192,256]{1,0:T(8,128)(2,1)S(1)}, u32[]{:S(2)}) %copy-start.6) | copy-done | bytes 98328
  28.5 2.3 %shard_map.87 = (bf16[192,256]{1,0:T(8,128)(2,1)}, bf16[192,256]{1,0:T(8,128)(2,1)}, bf16[192,256]{1,0:T(8,128)(2,1)}, bf16[192,256]{1,0:T(8,128)(2,1)}, bf16[192,256]{1,0:T(8,128)(2,1)}) custom-call(f32[192,256]{1,0:T(8,128)} %get-tuple-element.13.own_ref, bf16[192,256]{1,0:T(8,128)(2,1)} %copy-done.5, bf16[192,256]{1,0:T(8,128)(2,1)} %copy-done.6, ...), custom_call_target="tpu_custom_call" | custom-call | tf_op jit(solution)/shard_map/pallas_call | solution.py:33
  30.8 2.6 %collective-permute-start.7 = (bf16[192,256]{1,0:T(8,128)(2,1)}, bf16[192,256]{1,0:T(8,128)(2,1)S(1)}, u32[]{:S(2)}, u32[]{:S(2)}) collective-permute-start(bf16[192,256]{1,0:T(8,128)(2,1)} %get-tuple-element.19), channel_id=1, source_target_pairs={{0,1},{1,2},{2,3},{3,0},{4,5},{5,6},{6,7},{7,4},{8,9},{9,10},{10,1... | collective-permute-start | bytes 294920 | tf_op jit(solution)/shard_map/ppermute | solution.py:196
  33.4 1.9 %collective-permute-start.8 = (bf16[192,256]{1,0:T(8,128)(2,1)}, bf16[192,256]{1,0:T(8,128)(2,1)S(1)}, u32[]{:S(2)}, u32[]{:S(2)}) collective-permute-start(bf16[192,256]{1,0:T(8,128)(2,1)} %get-tuple-element.20), channel_id=1, source_target_pairs={{0,2},{1,3},{2,0},{3,1},{4,6},{5,7},{6,4},{7,5},{8,10},{9,11},{10,... | collective-permute-start | bytes 294920 | tf_op jit(solution)/shard_map/ppermute | solution.py:196
  35.2 0.5 collective-permute-start.9
  35.7 2.8 %collective-permute-done.7.rest_0_ = bf16[192,256]{1,0:T(8,128)(2,1)S(1)} collective-permute-done((bf16[192,256]{1,0:T(8,128)(2,1)}, bf16[192,256]{1,0:T(8,128)(2,1)S(1)}, u32[]{:S(2)}, u32[]{:S(2)}) %collective-permute-start.7) | collective-permute-done | bytes 98336 | tf_op jit(solution)/shard_map/ppermute | solution.py:196
  38.5 3.3 %collective-permute-done.8.rest_1_ = bf16[192,256]{1,0:T(8,128)(2,1)S(1)} collective-permute-done((bf16[192,256]{1,0:T(8,128)(2,1)}, bf16[192,256]{1,0:T(8,128)(2,1)S(1)}, u32[]{:S(2)}, u32[]{:S(2)}) %collective-permute-start.8) | collective-permute-done | bytes 98336 | tf_op jit(solution)/shard_map/ppermute | solution.py:196
  41.8 0.2 collective-permute-done.9.rest_2_
  42.0 0.5 copy-done.3
  42.6 4.0 %shard_map.88 = (f32[4,192,256]{2,1,0:T(8,128)}, bf16[4,192,256]{2,1,0:T(8,128)(2,1)}) custom-call(s32[12]{0:T(128)} %bitcast.33, s32[12]{0:T(128)} %bitcast.35, s32[1]{0:T(128)} %bitcast.25.info_ref, bf16[12,256,256]{2,1,0:T(8,128)(2,1)} %bitcast.27, bf16[192,256]{1,0:T(8,128)(2,1)} %get-tuple-element.18.mine_ref, bf16[192,256]{1,0:T(8,128)(2,1)} %copy-done.2, ...), custom_call_target="tpu_custom_call" | custom-call | tf_op jit(solution)/shard_map/pallas_call | solution.py:156
  46.6 1.9 %collective-permute-done.10 = bf16[4,192,256]{2,1,0:T(8,128)(2,1)S(1)} collective-permute-done((bf16[4,192,256]{2,1,0:T(8,128)(2,1)}, bf16[4,192,256]{2,1,0:T(8,128)(2,1)S(1)}, u32[]{:S(2)}, u32[]{:S(2)}) %collective-permute-start.10) | collective-permute-done | bytes 393248 | tf_op jit(solution)/shard_map/ppermute | solution.py:200
  48.5 1.2 %fusion.4 = (bf16[4,192,256]{2,1,0:T(8,128)(2,1)S(1)}, f32[4,192,256]{2,1,0:T(8,128)S(1)}) fusion(f32[4,192,256]{2,1,0:T(8,128)} %get-tuple-element.22, bf16[4,192,256]{2,1,0:T(8,128)(2,1)S(1)} %collective-permute-done.10), kind=kLoop, calls=%fused_computation.10 | loop fusion | flops 589824 | bytes 2359296 | tf_op jit(solution)/shard_map/convert.2
  49.8 1.3 %collective-permute-start.11 = (bf16[192,256]{1,0:T(8,128)(2,1)S(1)}, bf16[192,256]{1,0:T(8,128)(2,1)S(1)}, u32[]{:S(2)}, u32[]{:S(2)}) collective-permute-start(bf16[192,256]{1,0:T(8,128)(2,1)S(1)} %get-tuple-element.26), channel_id=1, source_target_pairs={{0,8},{4,12},{8,16},{12,20},{16,24},{20,28},{24,0},{28,4},{1,9},{5... | collective-permute-start | bytes 294920 | tf_op jit(solution)/shard_map/ppermute | solution.py:204
  51.0 1.7 %collective-permute-start.13 = (bf16[192,256]{1,0:T(8,128)(2,1)S(1)}, bf16[192,256]{1,0:T(8,128)(2,1)S(1)}, u32[]{:S(2)}, u32[]{:S(2)}) collective-permute-start(bf16[192,256]{1,0:T(8,128)(2,1)S(1)} %get-tuple-element.27), channel_id=1, source_target_pairs={{0,24},{4,28},{8,0},{12,4},{16,8},{20,12},{24,16},{28,20},{1,25},{... | collective-permute-start | bytes 294920 | tf_op jit(solution)/shard_map/ppermute | solution.py:204
  52.8 1.6 %collective-permute-start.12 = (bf16[192,256]{1,0:T(8,128)(2,1)S(1)}, bf16[192,256]{1,0:T(8,128)(2,1)S(1)}, u32[]{:S(2)}, u32[]{:S(2)}) collective-permute-start(bf16[192,256]{1,0:T(8,128)(2,1)S(1)} %get-tuple-element.28), channel_id=1, source_target_pairs={{0,16},{4,20},{8,24},{12,28},{16,0},{20,4},{24,8},{28,12},{1,17},{... | collective-permute-start | bytes 294920 | tf_op jit(solution)/shard_map/ppermute | solution.py:204
  54.3 2.1 %collective-permute-done.11 = bf16[192,256]{1,0:T(8,128)(2,1)S(1)} collective-permute-done((bf16[192,256]{1,0:T(8,128)(2,1)S(1)}, bf16[192,256]{1,0:T(8,128)(2,1)S(1)}, u32[]{:S(2)}, u32[]{:S(2)}) %collective-permute-start.11) | collective-permute-done | bytes 98336 | tf_op jit(solution)/shard_map/ppermute | solution.py:204
  56.4 1.4 %collective-permute-done.13 = bf16[192,256]{1,0:T(8,128)(2,1)S(1)} collective-permute-done((bf16[192,256]{1,0:T(8,128)(2,1)S(1)}, bf16[192,256]{1,0:T(8,128)(2,1)S(1)}, u32[]{:S(2)}, u32[]{:S(2)}) %collective-permute-start.13) | collective-permute-done | bytes 98336 | tf_op jit(solution)/shard_map/ppermute | solution.py:204
  57.9 0.7 %fusion.3 = bf16[192,256]{1,0:T(8,128)(2,1)} fusion(f32[4,192,256]{2,1,0:T(8,128)S(1)} %get-tuple-element.25, bf16[192,256]{1,0:T(8,128)(2,1)S(1)} %collective-permute-done.13, bf16[192,256]{1,0:T(8,128)(2,1)S(1)} %collective-permute-done.12, bf16[192,256]{1,0:T(8,128)(2,1)S(1)} %collective-permute-done.11), kind=kLoop, calls=%fused_computation.6 | loop fusion | flops 344064 | bytes 589824 | tf_op jit(solution)/shard_map/convert_element_type | solution.py:205
  (19 shorter events, 0.5 us)
Async XLA Ops:
  0.6 7.6 %collective-permute-start = (bf16[192,256]{1,0:T(8,128)(2,1)}, bf16[192,256]{1,0:T(8,128)(2,1)S(1)}, u32[]{:S(2)}, u32[]{:S(2)}) collective-permute-start(bf16[192,256]{1,0:T(8,128)(2,1)} %param.7), channel_id=1, source_target_pairs={{0,8},{4,12},{8,16},{12,20},{16,24},{20,28},{24,0},{28,4},{1,9},{5... | collective-permute-start | bytes 294920 | tf_op jit(solution)/shard_map/ppermute | solution.py:190
  3.6 6.3 %collective-permute-start.2 = (bf16[192,256]{1,0:T(8,128)(2,1)}, bf16[192,256]{1,0:T(8,128)(2,1)S(1)}, u32[]{:S(2)}, u32[]{:S(2)}) collective-permute-start(bf16[192,256]{1,0:T(8,128)(2,1)} %param.7), channel_id=1, source_target_pairs={{0,24},{4,28},{8,0},{12,4},{16,8},{20,12},{24,16},{28,20},{1,25},{... | collective-permute-start | bytes 294920 | tf_op jit(solution)/shard_map/ppermute | solution.py:190
  4.7 5.3 %collective-permute-start.1 = (bf16[192,256]{1,0:T(8,128)(2,1)}, bf16[192,256]{1,0:T(8,128)(2,1)S(1)}, u32[]{:S(2)}, u32[]{:S(2)}) collective-permute-start(bf16[192,256]{1,0:T(8,128)(2,1)} %param.7), channel_id=1, source_target_pairs={{0,16},{4,20},{8,24},{12,28},{16,0},{20,4},{24,8},{28,12},{1,17},{... | collective-permute-start | bytes 294920 | tf_op jit(solution)/shard_map/ppermute | solution.py:190
  10.9 1.8 %copy-start = (bf16[4,192,256]{2,1,0:T(8,128)(2,1)}, bf16[4,192,256]{2,1,0:T(8,128)(2,1)S(1)}, u32[]{:S(2)}) copy-start(bf16[4,192,256]{2,1,0:T(8,128)(2,1)S(1)} %pad_maximum_fusion.near_ref) | copy-start | bytes 1179652
  10.9 1.8 %collective-permute-start.3 = (bf16[4,192,256]{2,1,0:T(8,128)(2,1)S(1)}, bf16[4,192,256]{2,1,0:T(8,128)(2,1)S(1)}, u32[]{:S(2)}, u32[]{:S(2)}) collective-permute-start(bf16[4,192,256]{2,1,0:T(8,128)(2,1)S(1)} %pad_maximum_fusion.near_ref), channel_id=1, source_target_pairs={{0,4},{4,0},{8,12},{12,8},{16,20},{20,16},{24,28},{28,24},{1,5},{5... | collective-permute-start | bytes 1179656 | tf_op jit(solution)/shard_map/ppermute | solution.py:191
  12.7 0.7 %copy-start.1 = (bf16[4,192,256]{2,1,0:T(8,128)(2,1)}, bf16[4,192,256]{2,1,0:T(8,128)(2,1)S(1)}, u32[]{:S(2)}) copy-start(bf16[4,192,256]{2,1,0:T(8,128)(2,1)S(1)} %collective-permute-done.3.far_ref) | copy-start | bytes 1179652
  16.9 7.3 %collective-permute-start.4 = (bf16[192,256]{1,0:T(8,128)(2,1)}, bf16[192,256]{1,0:T(8,128)(2,1)S(1)}, u32[]{:S(2)}, u32[]{:S(2)}) collective-permute-start(bf16[192,256]{1,0:T(8,128)(2,1)} %get-tuple-element.14), channel_id=1, source_target_pairs={{0,1},{1,2},{2,3},{3,0},{4,5},{5,6},{6,7},{7,4},{8,9},{9,10},{10,1... | collective-permute-start | bytes 294920 | tf_op jit(solution)/shard_map/ppermute | solution.py:194
  18.1 9.8 %collective-permute-start.5 = (bf16[192,256]{1,0:T(8,128)(2,1)}, bf16[192,256]{1,0:T(8,128)(2,1)S(1)}, u32[]{:S(2)}, u32[]{:S(2)}) collective-permute-start(bf16[192,256]{1,0:T(8,128)(2,1)} %get-tuple-element.15), channel_id=1, source_target_pairs={{0,2},{1,3},{2,0},{3,1},{4,6},{5,7},{6,4},{7,5},{8,10},{9,11},{10,... | collective-permute-start | bytes 294920 | tf_op jit(solution)/shard_map/ppermute | solution.py:194
  20.7 7.2 %collective-permute-start.6 = (bf16[192,256]{1,0:T(8,128)(2,1)}, bf16[192,256]{1,0:T(8,128)(2,1)S(1)}, u32[]{:S(2)}, u32[]{:S(2)}) collective-permute-start(bf16[192,256]{1,0:T(8,128)(2,1)} %get-tuple-element.16), channel_id=1, source_target_pairs={{0,3},{1,0},{2,1},{3,2},{4,7},{5,4},{6,5},{7,6},{8,11},{9,8},{10,9... | collective-permute-start | bytes 294920 | tf_op jit(solution)/shard_map/ppermute | solution.py:194
  24.2 3.6 %copy-start.5 = (bf16[192,256]{1,0:T(8,128)(2,1)}, bf16[192,256]{1,0:T(8,128)(2,1)S(1)}, u32[]{:S(2)}) copy-start(bf16[192,256]{1,0:T(8,128)(2,1)S(1)} %collective-permute-done.4.rest_0_) | copy-start | bytes 294916
  27.9 0.6 %copy-start.6 = (bf16[192,256]{1,0:T(8,128)(2,1)}, bf16[192,256]{1,0:T(8,128)(2,1)S(1)}, u32[]{:S(2)}) copy-start(bf16[192,256]{1,0:T(8,128)(2,1)S(1)} %collective-permute-done.5.rest_1_) | copy-start | bytes 294916
  27.9 0.7 %copy-start.7 = (bf16[192,256]{1,0:T(8,128)(2,1)}, bf16[192,256]{1,0:T(8,128)(2,1)S(1)}, u32[]{:S(2)}) copy-start(bf16[192,256]{1,0:T(8,128)(2,1)S(1)} %collective-permute-done.6.rest_2_) | copy-start | bytes 294916
  30.8 7.7 %collective-permute-start.7 = (bf16[192,256]{1,0:T(8,128)(2,1)}, bf16[192,256]{1,0:T(8,128)(2,1)S(1)}, u32[]{:S(2)}, u32[]{:S(2)}) collective-permute-start(bf16[192,256]{1,0:T(8,128)(2,1)} %get-tuple-element.19), channel_id=1, source_target_pairs={{0,1},{1,2},{2,3},{3,0},{4,5},{5,6},{6,7},{7,4},{8,9},{9,10},{10,1... | collective-permute-start | bytes 294920 | tf_op jit(solution)/shard_map/ppermute | solution.py:196
  33.4 8.4 %collective-permute-start.8 = (bf16[192,256]{1,0:T(8,128)(2,1)}, bf16[192,256]{1,0:T(8,128)(2,1)S(1)}, u32[]{:S(2)}, u32[]{:S(2)}) collective-permute-start(bf16[192,256]{1,0:T(8,128)(2,1)} %get-tuple-element.20), channel_id=1, source_target_pairs={{0,2},{1,3},{2,0},{3,1},{4,6},{5,7},{6,4},{7,5},{8,10},{9,11},{10,... | collective-permute-start | bytes 294920 | tf_op jit(solution)/shard_map/ppermute | solution.py:196
  35.2 6.7 %collective-permute-start.9 = (bf16[192,256]{1,0:T(8,128)(2,1)}, bf16[192,256]{1,0:T(8,128)(2,1)S(1)}, u32[]{:S(2)}, u32[]{:S(2)}) collective-permute-start(bf16[192,256]{1,0:T(8,128)(2,1)} %get-tuple-element.21), channel_id=1, source_target_pairs={{0,3},{1,0},{2,1},{3,2},{4,7},{5,4},{6,5},{7,6},{8,11},{9,8},{10,9... | collective-permute-start | bytes 294920 | tf_op jit(solution)/shard_map/ppermute | solution.py:196
  38.5 3.4 %copy-start.2 = (bf16[192,256]{1,0:T(8,128)(2,1)}, bf16[192,256]{1,0:T(8,128)(2,1)S(1)}, u32[]{:S(2)}) copy-start(bf16[192,256]{1,0:T(8,128)(2,1)S(1)} %collective-permute-done.7.rest_0_) | copy-start | bytes 294916
  41.8 0.6 %copy-start.3 = (bf16[192,256]{1,0:T(8,128)(2,1)}, bf16[192,256]{1,0:T(8,128)(2,1)S(1)}, u32[]{:S(2)}) copy-start(bf16[192,256]{1,0:T(8,128)(2,1)S(1)} %collective-permute-done.8.rest_1_) | copy-start | bytes 294916
  42.0 0.6 %copy-start.4 = (bf16[192,256]{1,0:T(8,128)(2,1)}, bf16[192,256]{1,0:T(8,128)(2,1)S(1)}, u32[]{:S(2)}) copy-start(bf16[192,256]{1,0:T(8,128)(2,1)S(1)} %collective-permute-done.9.rest_2_) | copy-start | bytes 294916
  46.6 1.9 %collective-permute-start.10 = (bf16[4,192,256]{2,1,0:T(8,128)(2,1)}, bf16[4,192,256]{2,1,0:T(8,128)(2,1)S(1)}, u32[]{:S(2)}, u32[]{:S(2)}) collective-permute-start(bf16[4,192,256]{2,1,0:T(8,128)(2,1)} %get-tuple-element.23), channel_id=1, source_target_pairs={{0,4},{4,0},{8,12},{12,8},{16,20},{20,16},{24,28},{28,24},{1,5},{5... | collective-permute-start | bytes 1179656 | tf_op jit(solution)/shard_map/ppermute | solution.py:200
  49.8 6.6 %collective-permute-start.11 = (bf16[192,256]{1,0:T(8,128)(2,1)S(1)}, bf16[192,256]{1,0:T(8,128)(2,1)S(1)}, u32[]{:S(2)}, u32[]{:S(2)}) collective-permute-start(bf16[192,256]{1,0:T(8,128)(2,1)S(1)} %get-tuple-element.26), channel_id=1, source_target_pairs={{0,8},{4,12},{8,16},{12,20},{16,24},{20,28},{24,0},{28,4},{1,9},{5... | collective-permute-start | bytes 294920 | tf_op jit(solution)/shard_map/ppermute | solution.py:204
  51.0 6.7 %collective-permute-start.13 = (bf16[192,256]{1,0:T(8,128)(2,1)S(1)}, bf16[192,256]{1,0:T(8,128)(2,1)S(1)}, u32[]{:S(2)}, u32[]{:S(2)}) collective-permute-start(bf16[192,256]{1,0:T(8,128)(2,1)S(1)} %get-tuple-element.27), channel_id=1, source_target_pairs={{0,24},{4,28},{8,0},{12,4},{16,8},{20,12},{24,16},{28,20},{1,25},{... | collective-permute-start | bytes 294920 | tf_op jit(solution)/shard_map/ppermute | solution.py:204
  52.8 5.1 %collective-permute-start.12 = (bf16[192,256]{1,0:T(8,128)(2,1)S(1)}, bf16[192,256]{1,0:T(8,128)(2,1)S(1)}, u32[]{:S(2)}, u32[]{:S(2)}) collective-permute-start(bf16[192,256]{1,0:T(8,128)(2,1)S(1)} %get-tuple-element.28), channel_id=1, source_target_pairs={{0,16},{4,20},{8,24},{12,28},{16,0},{20,4},{24,8},{28,12},{1,17},{... | collective-permute-start | bytes 294920 | tf_op jit(solution)/shard_map/ppermute | solution.py:204

commit v20 on v15

--- a/solution.py
+++ b/solution.py
@@ -94,7 +94,7 @@
 
 def backward_kernel(n, rows_ref, cols_ref, info_ref, a_ref, mine_ref, *rest):
     got_refs = rest[: n - 1]
-    near_ref, far_ref, block_ref, acc_ref = rest[n - 1:]
+    own_ref, near_ref, far_ref, block_ref, acc_ref = rest[n - 1:]
     tile = a_ref.shape[1]
     chunk = mine_ref.shape[0]
     me = lax.axis_index("col")
@@ -115,13 +115,17 @@
         acc_ref[cols, :] += value
 
     run_slots(jnp.minimum(info_ref[0], a_ref.shape[0]), product, place)
-    chips = near_ref.shape[0]
-    piece = near_ref.shape[1]
+    chips = far_ref.shape[0]
+    piece = far_ref.shape[1]
     me_row = lax.axis_index("row")
     core, chip = me_row % 2, me_row // 2
+    own_ref[...] = acc_ref[pl.ds(pl.multiple_of(me_row * piece, 8), piece), :]
     for shift in range(chips):
         owner = (chip + shift) % chips
-        near_ref[shift] = acc_ref[pl.ds(pl.multiple_of((owner * 2 + core) * piece, 8), piece), :]
+        if shift:
+            near_ref[shift - 1] = acc_ref[
+                pl.ds(pl.multiple_of((owner * 2 + core) * piece, 8), piece), :
+            ].astype(near_ref.dtype)
         far_ref[shift] = acc_ref[pl.ds(pl.multiple_of((owner * 2 + 1 - core) * piece, 8), piece), :].astype(
             far_ref.dtype
         )
@@ -151,13 +155,14 @@
 def tile_products_t(rows, cols, info, blocks, mine, got, n_out, out_rows):
     chunk = out_rows // n_out
     width = mine.shape[1]
-    near = jax.ShapeDtypeStruct((n_out // 2, chunk, width), jnp.float32)
+    own = jax.ShapeDtypeStruct((chunk, width), jnp.float32)
+    near = jax.ShapeDtypeStruct((n_out // 2 - 1, chunk, width), jnp.bfloat16)
     far = jax.ShapeDtypeStruct((n_out // 2, chunk, width), jnp.bfloat16)
     return pl.pallas_call(
         functools.partial(backward_kernel, len(got) + 1),
-        out_shape=(near, far),
+        out_shape=(own, near, far),
         in_specs=[SMEM, SMEM, SMEM, VMEM, VMEM] + [VMEM] * len(got),
-        out_specs=(VMEM, VMEM),
+        out_specs=(VMEM, VMEM, VMEM),
         scratch_shapes=[
             pltpu.VMEM(((len(got) + 1) * mine.shape[0], width), jnp.bfloat16),
             pltpu.VMEM((out_rows, width), jnp.float32),
@@ -194,13 +199,13 @@
     got_f = [lax.ppermute(send[shift], "col", perm) for shift, perm in enumerate(shifts("col"))]
     activated, pulled_own, *pulled_out = dense_layer_kernel(own, got_f, cotangent, weight)
     got = [lax.ppermute(piece, "col", perm) for piece, perm in zip(pulled_out, shifts("col"))]
-    near_g, far_g = tile_products_t(
+    own_g, near_g, far_g = tile_products_t(
         row_slots, col_slots, info, blocks, pulled_own, got, n_row, n_row * own_rows
     )
-    chip_sums = near_g + lax.ppermute(far_g, "row", partner(n_row)).astype(jnp.float32)
-    total_g = chip_sums[0]
+    swapped = lax.ppermute(far_g, "row", partner(n_row)).astype(jnp.float32)
+    total_g = own_g + swapped[0]
     for shift, perm in enumerate(chip_shifts(n_row)):
-        piece = chip_sums[shift + 1].astype(jnp.bfloat16)
+        piece = (near_g[shift].astype(jnp.float32) + swapped[shift + 1]).astype(jnp.bfloat16)
         total_g = total_g + lax.ppermute(piece, "row", perm).astype(jnp.float32)
     return (activated, total_g.astype(jnp.bfloat16))
 

time: 58.7 us -> 58.3 us (level)
  Pallas kernels: 9.63 us -> 8.14 us
  waiting for transfers between devices: 21 us -> 22.2 us
    another operation x1 -> x0, other arithmetic: 1.24 us -> none
    convert_element_type x0 -> x2, other arithmetic: none -> 1.13 us  [the longest x1 1.07 us: on_device(): (near_g[shift].astype(jnp.float32) + swapped[shift + 1]).astype(jnp.bfloa...]
    ppermute x3, waiting for transfers between devices: 5.19 us -> 6.32 us  [on_device(): lax.ppermute(send[shift], 'col', perm)]
    pallas_call x1, Pallas kernels: 3.86 us -> 3.03 us  [tile_products_t(): pl.pallas_call(functools.partial(backward_kernel, len(got) + 1), out_shap...]
    pallas_call x1, Pallas kernels: 3.5 us -> 2.84 us  [tile_products(): pl.pallas_call(forward_kernel, out_shape=(jax.ShapeDtypeStruct((chunk, wi...]
    unnamed x16 -> x18, local copies, waits for them, and re-layouts: 2.08 us -> 2.08 us
  transfers between devices with their start and end apart: 14 -> 14, of which waited for: 10 -> 11; matrix products, arithmetic and copies ran while one was open for 0% -> 0% of each run, Pallas kernels for 0% -> 0%
where the time goes in v20:
time: 58.3 us; the launch traced here: 57.6 us
  waiting for transfers between devices  22.2 us (38%)
  starting transfers between devices  21.1 us (36%)
  Pallas kernels  8.14 us (14%)
  other arithmetic  2.77 us (5%)
  local copies, waits for them, and re-layouts  2.08 us (4%)
  between operations  1.36 us (2%)
    ppermute x3, waiting for transfers between devices, on_device(): lax.ppermute(send[shift], 'col', perm)  6.32 us
    ppermute x3, waiting for transfers between devices, on_device(): lax.ppermute(piece, 'col', perm)  6.07 us
    ppermute x3, starting transfers between devices, on_device(): lax.ppermute(features, 'row', perm)  5.97 us
    ppermute x3, starting transfers between devices, on_device(): lax.ppermute(send[shift], 'col', perm)  5.64 us
    ppermute x3, starting transfers between devices, on_device(): lax.ppermute(piece, 'col', perm)  4.93 us
    ppermute x3, starting transfers between devices, on_device(): total_g = total_g + lax.ppermute(piece, 'row', perm).astype(jnp.float32)  4.31 us
    ppermute x3, waiting for transfers between devices, on_device(): total_g = total_g + lax.ppermute(piece, 'row', perm).astype(jnp.float32)  3.62 us
    ppermute x3, waiting for transfers between devices, on_device(): lax.ppermute(features, 'row', perm)  3.36 us
  transfers between devices with their start and end apart: 14, of which 11 were waited for; matrix products, arithmetic and copies ran while one was open for 0% of the time, Pallas kernels for 0%

profile of v20, /device:TPU:0, one launch (start us, length us, event | category | flops | bytes accessed | tf_op | source)
XLA Modules:
  0.0 57.6 jit_solution(13129083645411709916)
XLA Ops:
  0.6 3.0 %collective-permute-start = (bf16[192,256]{1,0:T(8,128)(2,1)}, bf16[192,256]{1,0:T(8,128)(2,1)S(1)}, u32[]{:S(2)}, u32[]{:S(2)}) collective-permute-start(bf16[192,256]{1,0:T(8,128)(2,1)} %param.7), channel_id=1, source_target_pairs={{0,8},{4,12},{8,16},{12,20},{16,24},{20,28},{24,0},{28,4},{1,9},{5... | collective-permute-start | bytes 294920 | tf_op jit(solution)/shard_map/ppermute | solution.py:195
  3.6 1.0 %collective-permute-start.2 = (bf16[192,256]{1,0:T(8,128)(2,1)}, bf16[192,256]{1,0:T(8,128)(2,1)S(1)}, u32[]{:S(2)}, u32[]{:S(2)}) collective-permute-start(bf16[192,256]{1,0:T(8,128)(2,1)} %param.7), channel_id=1, source_target_pairs={{0,24},{4,28},{8,0},{12,4},{16,8},{20,12},{24,16},{28,20},{1,25},{... | collective-permute-start | bytes 294920 | tf_op jit(solution)/shard_map/ppermute | solution.py:195
  4.7 1.9 %collective-permute-start.1 = (bf16[192,256]{1,0:T(8,128)(2,1)}, bf16[192,256]{1,0:T(8,128)(2,1)S(1)}, u32[]{:S(2)}, u32[]{:S(2)}) collective-permute-start(bf16[192,256]{1,0:T(8,128)(2,1)} %param.7), channel_id=1, source_target_pairs={{0,16},{4,20},{8,24},{12,28},{16,0},{20,4},{24,8},{28,12},{1,17},{... | collective-permute-start | bytes 294920 | tf_op jit(solution)/shard_map/ppermute | solution.py:195
  6.6 1.6 %collective-permute-done = bf16[192,256]{1,0:T(8,128)(2,1)S(1)} collective-permute-done((bf16[192,256]{1,0:T(8,128)(2,1)}, bf16[192,256]{1,0:T(8,128)(2,1)S(1)}, u32[]{:S(2)}, u32[]{:S(2)}) %collective-permute-start) | collective-permute-done | bytes 98336 | tf_op jit(solution)/shard_map/ppermute | solution.py:195
  8.3 1.7 %collective-permute-done.2 = bf16[192,256]{1,0:T(8,128)(2,1)S(1)} collective-permute-done((bf16[192,256]{1,0:T(8,128)(2,1)}, bf16[192,256]{1,0:T(8,128)(2,1)S(1)}, u32[]{:S(2)}, u32[]{:S(2)}) %collective-permute-start.2) | collective-permute-done | bytes 98336 | tf_op jit(solution)/shard_map/ppermute | solution.py:195
  10.0 0.9 %pad_maximum_fusion.near_ref = bf16[4,192,256]{2,1,0:T(8,128)(2,1)S(1)} fusion(bf16[1,192,256]{2,1,0:T(8,128)(2,1)S(1)} %bitcast.32, bf16[1,192,256]{2,1,0:T(8,128)(2,1)S(1)} %bitcast.33, bf16[1,192,256]{2,1,0:T(8,128)(2,1)S(1)} %bitcast.31, bf16[1,192,256]{2,1,0:T(8,128)(2,1)} %bitcast.30), kind=kLoop, calls=%fused_computation | loop fusion | flops 589824 | bytes 786432 | tf_op jit(solution)/shard_map/stack | solution.py:195
  11.7 1.0 %collective-permute-done.3.far_ref = bf16[4,192,256]{2,1,0:T(8,128)(2,1)S(1)} collective-permute-done((bf16[4,192,256]{2,1,0:T(8,128)(2,1)S(1)}, bf16[4,192,256]{2,1,0:T(8,128)(2,1)S(1)}, u32[]{:S(2)}, u32[]{:S(2)}) %collective-permute-start.3) | collective-permute-done | bytes 393248 | tf_op jit(solution)/shard_map/ppermute | solution.py:196
  12.7 0.7 %copy-done.1 = bf16[4,192,256]{2,1,0:T(8,128)(2,1)} copy-done((bf16[4,192,256]{2,1,0:T(8,128)(2,1)}, bf16[4,192,256]{2,1,0:T(8,128)(2,1)S(1)}, u32[]{:S(2)}) %copy-start.1) | copy-done | bytes 393240
  13.5 2.8 %shard_map.86 = (f32[192,256]{1,0:T(8,128)}, bf16[192,256]{1,0:T(8,128)(2,1)}, bf16[192,256]{1,0:T(8,128)(2,1)}, bf16[192,256]{1,0:T(8,128)(2,1)}) custom-call(s32[12]{0:T(128)} %bitcast.34, s32[12]{0:T(128)} %bitcast.36, s32[1]{0:T(128)} %bitcast.26.info_ref, bf16[12,256,256]{2,1,0:T(8,128)(2,1)} %bitcast.28, bf16[4,192,256]{2,1,0:T(8,128)(2,1)} %copy-done, ...), custom_call_target="tpu_custom_call" | custom-call | tf_op jit(solution)/shard_map/pallas_call | solution.py:142
  16.3 1.9 %collective-permute-start.4 = (bf16[192,256]{1,0:T(8,128)(2,1)}, bf16[192,256]{1,0:T(8,128)(2,1)S(1)}, u32[]{:S(2)}, u32[]{:S(2)}) collective-permute-start(bf16[192,256]{1,0:T(8,128)(2,1)} %get-tuple-element.15), channel_id=1, source_target_pairs={{0,1},{1,2},{2,3},{3,0},{4,5},{5,6},{6,7},{7,4},{8,9},{9,10},{10,1... | collective-permute-start | bytes 294920 | tf_op jit(solution)/shard_map/ppermute | solution.py:199
  18.2 2.6 %collective-permute-start.5 = (bf16[192,256]{1,0:T(8,128)(2,1)}, bf16[192,256]{1,0:T(8,128)(2,1)S(1)}, u32[]{:S(2)}, u32[]{:S(2)}) collective-permute-start(bf16[192,256]{1,0:T(8,128)(2,1)} %get-tuple-element.16), channel_id=1, source_target_pairs={{0,2},{1,3},{2,0},{3,1},{4,6},{5,7},{6,4},{7,5},{8,10},{9,11},{10,... | collective-permute-start | bytes 294920 | tf_op jit(solution)/shard_map/ppermute | solution.py:199
  20.8 1.2 %collective-permute-start.6 = (bf16[192,256]{1,0:T(8,128)(2,1)}, bf16[192,256]{1,0:T(8,128)(2,1)S(1)}, u32[]{:S(2)}, u32[]{:S(2)}) collective-permute-start(bf16[192,256]{1,0:T(8,128)(2,1)} %get-tuple-element.17), channel_id=1, source_target_pairs={{0,3},{1,0},{2,1},{3,2},{4,7},{5,4},{6,5},{7,6},{8,11},{9,8},{10,9... | collective-permute-start | bytes 294920 | tf_op jit(solution)/shard_map/ppermute | solution.py:199
  21.9 2.2 %collective-permute-done.4.rest_0_ = bf16[192,256]{1,0:T(8,128)(2,1)S(1)} collective-permute-done((bf16[192,256]{1,0:T(8,128)(2,1)}, bf16[192,256]{1,0:T(8,128)(2,1)S(1)}, u32[]{:S(2)}, u32[]{:S(2)}) %collective-permute-start.4) | collective-permute-done | bytes 98336 | tf_op jit(solution)/shard_map/ppermute | solution.py:199
  24.2 4.1 %collective-permute-done.5.rest_1_ = bf16[192,256]{1,0:T(8,128)(2,1)S(1)} collective-permute-done((bf16[192,256]{1,0:T(8,128)(2,1)}, bf16[192,256]{1,0:T(8,128)(2,1)S(1)}, u32[]{:S(2)}, u32[]{:S(2)}) %collective-permute-start.5) | collective-permute-done | bytes 98336 | tf_op jit(solution)/shard_map/ppermute | solution.py:199
  28.3 0.6 %copy-done.7 = bf16[192,256]{1,0:T(8,128)(2,1)} copy-done((bf16[192,256]{1,0:T(8,128)(2,1)}, bf16[192,256]{1,0:T(8,128)(2,1)S(1)}, u32[]{:S(2)}) %copy-start.7) | copy-done | bytes 98328
  28.9 2.3 %shard_map.87 = (bf16[192,256]{1,0:T(8,128)(2,1)}, bf16[192,256]{1,0:T(8,128)(2,1)}, bf16[192,256]{1,0:T(8,128)(2,1)}, bf16[192,256]{1,0:T(8,128)(2,1)}, bf16[192,256]{1,0:T(8,128)(2,1)}) custom-call(f32[192,256]{1,0:T(8,128)} %get-tuple-element.14.own_ref, bf16[192,256]{1,0:T(8,128)(2,1)} %copy-done.6, bf16[192,256]{1,0:T(8,128)(2,1)} %copy-done.7, ...), custom_call_target="tpu_custom_call" | custom-call | tf_op jit(solution)/shard_map/pallas_call | solution.py:33
  31.2 2.6 %collective-permute-start.7 = (bf16[192,256]{1,0:T(8,128)(2,1)}, bf16[192,256]{1,0:T(8,128)(2,1)S(1)}, u32[]{:S(2)}, u32[]{:S(2)}) collective-permute-start(bf16[192,256]{1,0:T(8,128)(2,1)} %get-tuple-element.20), channel_id=1, source_target_pairs={{0,1},{1,2},{2,3},{3,0},{4,5},{5,6},{6,7},{7,4},{8,9},{9,10},{10,1... | collective-permute-start | bytes 294920 | tf_op jit(solution)/shard_map/ppermute | solution.py:201
  33.8 1.2 %collective-permute-start.8 = (bf16[192,256]{1,0:T(8,128)(2,1)}, bf16[192,256]{1,0:T(8,128)(2,1)S(1)}, u32[]{:S(2)}, u32[]{:S(2)}) collective-permute-start(bf16[192,256]{1,0:T(8,128)(2,1)} %get-tuple-element.21), channel_id=1, source_target_pairs={{0,2},{1,3},{2,0},{3,1},{4,6},{5,7},{6,4},{7,5},{8,10},{9,11},{10,... | collective-permute-start | bytes 294920 | tf_op jit(solution)/shard_map/ppermute | solution.py:201
  35.0 1.2 %collective-permute-start.9 = (bf16[192,256]{1,0:T(8,128)(2,1)}, bf16[192,256]{1,0:T(8,128)(2,1)S(1)}, u32[]{:S(2)}, u32[]{:S(2)}) collective-permute-start(bf16[192,256]{1,0:T(8,128)(2,1)} %get-tuple-element.22), channel_id=1, source_target_pairs={{0,3},{1,0},{2,1},{3,2},{4,7},{5,4},{6,5},{7,6},{8,11},{9,8},{10,9... | collective-permute-start | bytes 294920 | tf_op jit(solution)/shard_map/ppermute | solution.py:201
  36.1 2.8 %collective-permute-done.7.rest_0_ = bf16[192,256]{1,0:T(8,128)(2,1)S(1)} collective-permute-done((bf16[192,256]{1,0:T(8,128)(2,1)}, bf16[192,256]{1,0:T(8,128)(2,1)S(1)}, u32[]{:S(2)}, u32[]{:S(2)}) %collective-permute-start.7) | collective-permute-done | bytes 98336 | tf_op jit(solution)/shard_map/ppermute | solution.py:201
  38.9 3.3 %collective-permute-done.8.rest_1_ = bf16[192,256]{1,0:T(8,128)(2,1)S(1)} collective-permute-done((bf16[192,256]{1,0:T(8,128)(2,1)}, bf16[192,256]{1,0:T(8,128)(2,1)S(1)}, u32[]{:S(2)}, u32[]{:S(2)}) %collective-permute-start.8) | collective-permute-done | bytes 98336 | tf_op jit(solution)/shard_map/ppermute | solution.py:201
  42.2 0.6 %copy-done.4 = bf16[192,256]{1,0:T(8,128)(2,1)} copy-done((bf16[192,256]{1,0:T(8,128)(2,1)}, bf16[192,256]{1,0:T(8,128)(2,1)S(1)}, u32[]{:S(2)}) %copy-start.4) | copy-done | bytes 98328
  42.9 3.0 %shard_map.88 = (f32[192,256]{1,0:T(8,128)}, bf16[3,192,256]{2,1,0:T(8,128)(2,1)}, bf16[4,192,256]{2,1,0:T(8,128)(2,1)}) custom-call(s32[12]{0:T(128)} %bitcast.35, s32[12]{0:T(128)} %bitcast.37, s32[1]{0:T(128)} %bitcast.27.info_ref, bf16[12,256,256]{2,1,0:T(8,128)(2,1)} %bitcast.29, bf16[192,256]{1,0:T(8,128)(2,1)} %get-tuple-element.19.mine_ref, ...), custom_call_target="tpu_custom_call" | custom-call | tf_op jit(solution)/shard_map/pallas_call | solution.py:161
  46.1 1.8 %collective-permute-done.10 = bf16[4,192,256]{2,1,0:T(8,128)(2,1)S(1)} collective-permute-done((bf16[4,192,256]{2,1,0:T(8,128)(2,1)}, bf16[4,192,256]{2,1,0:T(8,128)(2,1)S(1)}, u32[]{:S(2)}, u32[]{:S(2)}) %collective-permute-start.10) | collective-permute-done | bytes 393248 | tf_op jit(solution)/shard_map/ppermute | solution.py:205
  47.9 1.1 %fusion.8 = (bf16[192,256]{1,0:T(8,128)(2,1)S(1)}, bf16[192,256]{1,0:T(8,128)(2,1)S(1)}, bf16[192,256]{1,0:T(8,128)(2,1)S(1)}) fusion(f32[4,192,256]{2,1,0:T(8,128)S(1)} %convert_element_type.45, bf16[3,192,256]{2,1,0:T(8,128)(2,1)} %get-tuple-element.25), kind=kLoop, calls=%fused_computation.13 | loop fusion | flops 442368 | bytes 1179648 | tf_op jit(solution)/shard_map/convert_element_type | solution.py:208
  49.0 2.0 %collective-permute-start.11 = (bf16[192,256]{1,0:T(8,128)(2,1)S(1)}, bf16[192,256]{1,0:T(8,128)(2,1)S(1)}, u32[]{:S(2)}, u32[]{:S(2)}) collective-permute-start(bf16[192,256]{1,0:T(8,128)(2,1)S(1)} %get-tuple-element.26), channel_id=1, source_target_pairs={{0,8},{4,12},{8,16},{12,20},{16,24},{20,28},{24,0},{28,4},{1,9},{5... | collective-permute-start | bytes 294920 | tf_op jit(solution)/shard_map/ppermute | solution.py:209
  51.0 1.0 %collective-permute-start.13 = (bf16[192,256]{1,0:T(8,128)(2,1)S(1)}, bf16[192,256]{1,0:T(8,128)(2,1)S(1)}, u32[]{:S(2)}, u32[]{:S(2)}) collective-permute-start(bf16[192,256]{1,0:T(8,128)(2,1)S(1)} %get-tuple-element.27), channel_id=1, source_target_pairs={{0,24},{4,28},{8,0},{12,4},{16,8},{20,12},{24,16},{28,20},{1,25},{... | collective-permute-start | bytes 294920 | tf_op jit(solution)/shard_map/ppermute | solution.py:209
  52.0 1.3 %collective-permute-start.12 = (bf16[192,256]{1,0:T(8,128)(2,1)S(1)}, bf16[192,256]{1,0:T(8,128)(2,1)S(1)}, u32[]{:S(2)}, u32[]{:S(2)}) collective-permute-start(bf16[192,256]{1,0:T(8,128)(2,1)S(1)} %get-tuple-element.28), channel_id=1, source_target_pairs={{0,16},{4,20},{8,24},{12,28},{16,0},{20,4},{24,8},{28,12},{1,17},{... | collective-permute-start | bytes 294920 | tf_op jit(solution)/shard_map/ppermute | solution.py:209
  53.3 2.2 %collective-permute-done.11 = bf16[192,256]{1,0:T(8,128)(2,1)S(1)} collective-permute-done((bf16[192,256]{1,0:T(8,128)(2,1)S(1)}, bf16[192,256]{1,0:T(8,128)(2,1)S(1)}, u32[]{:S(2)}, u32[]{:S(2)}) %collective-permute-start.11) | collective-permute-done | bytes 98336 | tf_op jit(solution)/shard_map/ppermute | solution.py:209
  55.5 1.3 %collective-permute-done.13 = bf16[192,256]{1,0:T(8,128)(2,1)S(1)} collective-permute-done((bf16[192,256]{1,0:T(8,128)(2,1)S(1)}, bf16[192,256]{1,0:T(8,128)(2,1)S(1)}, u32[]{:S(2)}, u32[]{:S(2)}) %collective-permute-start.13) | collective-permute-done | bytes 98336 | tf_op jit(solution)/shard_map/ppermute | solution.py:209
  56.8 0.2 collective-permute-done.12
  56.9 0.7 %fusion.7 = bf16[192,256]{1,0:T(8,128)(2,1)} fusion(f32[192,256]{1,0:T(8,128)S(1)} %copy-done.2, f32[4,192,256]{2,1,0:T(8,128)S(1)} %convert_element_type.45, bf16[192,256]{1,0:T(8,128)(2,1)S(1)} %collective-permute-done.13, bf16[192,256]{1,0:T(8,128)(2,1)S(1)} %collective-permute-done.12, bf16[192,256]{1,0:T(8,128)(2,1)S(1)} %collective-permute-done.11), kind=kLoop, calls=%fused_computation.12 | loop fusion | flops 393216 | bytes 786432 | tf_op jit(solution)/shard_map/convert_element_type | solution.py:210
  (21 shorter events, 0.4 us)
Async XLA Ops:
  0.6 7.6 %collective-permute-start = (bf16[192,256]{1,0:T(8,128)(2,1)}, bf16[192,256]{1,0:T(8,128)(2,1)S(1)}, u32[]{:S(2)}, u32[]{:S(2)}) collective-permute-start(bf16[192,256]{1,0:T(8,128)(2,1)} %param.7), channel_id=1, source_target_pairs={{0,8},{4,12},{8,16},{12,20},{16,24},{20,28},{24,0},{28,4},{1,9},{5... | collective-permute-start | bytes 294920 | tf_op jit(solution)/shard_map/ppermute | solution.py:195
  3.6 6.3 %collective-permute-start.2 = (bf16[192,256]{1,0:T(8,128)(2,1)}, bf16[192,256]{1,0:T(8,128)(2,1)S(1)}, u32[]{:S(2)}, u32[]{:S(2)}) collective-permute-start(bf16[192,256]{1,0:T(8,128)(2,1)} %param.7), channel_id=1, source_target_pairs={{0,24},{4,28},{8,0},{12,4},{16,8},{20,12},{24,16},{28,20},{1,25},{... | collective-permute-start | bytes 294920 | tf_op jit(solution)/shard_map/ppermute | solution.py:195
  4.7 5.3 %collective-permute-start.1 = (bf16[192,256]{1,0:T(8,128)(2,1)}, bf16[192,256]{1,0:T(8,128)(2,1)S(1)}, u32[]{:S(2)}, u32[]{:S(2)}) collective-permute-start(bf16[192,256]{1,0:T(8,128)(2,1)} %param.7), channel_id=1, source_target_pairs={{0,16},{4,20},{8,24},{12,28},{16,0},{20,4},{24,8},{28,12},{1,17},{... | collective-permute-start | bytes 294920 | tf_op jit(solution)/shard_map/ppermute | solution.py:195
  10.9 1.8 %copy-start = (bf16[4,192,256]{2,1,0:T(8,128)(2,1)}, bf16[4,192,256]{2,1,0:T(8,128)(2,1)S(1)}, u32[]{:S(2)}) copy-start(bf16[4,192,256]{2,1,0:T(8,128)(2,1)S(1)} %pad_maximum_fusion.near_ref) | copy-start | bytes 1179652
  10.9 1.8 %collective-permute-start.3 = (bf16[4,192,256]{2,1,0:T(8,128)(2,1)S(1)}, bf16[4,192,256]{2,1,0:T(8,128)(2,1)S(1)}, u32[]{:S(2)}, u32[]{:S(2)}) collective-permute-start(bf16[4,192,256]{2,1,0:T(8,128)(2,1)S(1)} %pad_maximum_fusion.near_ref), channel_id=1, source_target_pairs={{0,4},{4,0},{8,12},{12,8},{16,20},{20,16},{24,28},{28,24},{1,5},{5... | collective-permute-start | bytes 1179656 | tf_op jit(solution)/shard_map/ppermute | solution.py:196
  12.7 0.7 %copy-start.1 = (bf16[4,192,256]{2,1,0:T(8,128)(2,1)}, bf16[4,192,256]{2,1,0:T(8,128)(2,1)S(1)}, u32[]{:S(2)}) copy-start(bf16[4,192,256]{2,1,0:T(8,128)(2,1)S(1)} %collective-permute-done.3.far_ref) | copy-start | bytes 1179652
  16.3 7.9 %collective-permute-start.4 = (bf16[192,256]{1,0:T(8,128)(2,1)}, bf16[192,256]{1,0:T(8,128)(2,1)S(1)}, u32[]{:S(2)}, u32[]{:S(2)}) collective-permute-start(bf16[192,256]{1,0:T(8,128)(2,1)} %get-tuple-element.15), channel_id=1, source_target_pairs={{0,1},{1,2},{2,3},{3,0},{4,5},{5,6},{6,7},{7,4},{8,9},{9,10},{10,1... | collective-permute-start | bytes 294920 | tf_op jit(solution)/shard_map/ppermute | solution.py:199
  18.2 10.1 %collective-permute-start.5 = (bf16[192,256]{1,0:T(8,128)(2,1)}, bf16[192,256]{1,0:T(8,128)(2,1)S(1)}, u32[]{:S(2)}, u32[]{:S(2)}) collective-permute-start(bf16[192,256]{1,0:T(8,128)(2,1)} %get-tuple-element.16), channel_id=1, source_target_pairs={{0,2},{1,3},{2,0},{3,1},{4,6},{5,7},{6,4},{7,5},{8,10},{9,11},{10,... | collective-permute-start | bytes 294920 | tf_op jit(solution)/shard_map/ppermute | solution.py:199
  20.8 7.5 %collective-permute-start.6 = (bf16[192,256]{1,0:T(8,128)(2,1)}, bf16[192,256]{1,0:T(8,128)(2,1)S(1)}, u32[]{:S(2)}, u32[]{:S(2)}) collective-permute-start(bf16[192,256]{1,0:T(8,128)(2,1)} %get-tuple-element.17), channel_id=1, source_target_pairs={{0,3},{1,0},{2,1},{3,2},{4,7},{5,4},{6,5},{7,6},{8,11},{9,8},{10,9... | collective-permute-start | bytes 294920 | tf_op jit(solution)/shard_map/ppermute | solution.py:199
  24.2 4.1 %copy-start.6 = (bf16[192,256]{1,0:T(8,128)(2,1)}, bf16[192,256]{1,0:T(8,128)(2,1)S(1)}, u32[]{:S(2)}) copy-start(bf16[192,256]{1,0:T(8,128)(2,1)S(1)} %collective-permute-done.4.rest_0_) | copy-start | bytes 294916
  28.2 0.6 %copy-start.7 = (bf16[192,256]{1,0:T(8,128)(2,1)}, bf16[192,256]{1,0:T(8,128)(2,1)S(1)}, u32[]{:S(2)}) copy-start(bf16[192,256]{1,0:T(8,128)(2,1)S(1)} %collective-permute-done.5.rest_1_) | copy-start | bytes 294916
  28.3 0.7 %copy-start.8 = (bf16[192,256]{1,0:T(8,128)(2,1)}, bf16[192,256]{1,0:T(8,128)(2,1)S(1)}, u32[]{:S(2)}) copy-start(bf16[192,256]{1,0:T(8,128)(2,1)S(1)} %collective-permute-done.6.rest_2_) | copy-start | bytes 294916
  31.2 7.7 %collective-permute-start.7 = (bf16[192,256]{1,0:T(8,128)(2,1)}, bf16[192,256]{1,0:T(8,128)(2,1)S(1)}, u32[]{:S(2)}, u32[]{:S(2)}) collective-permute-start(bf16[192,256]{1,0:T(8,128)(2,1)} %get-tuple-element.20), channel_id=1, source_target_pairs={{0,1},{1,2},{2,3},{3,0},{4,5},{5,6},{6,7},{7,4},{8,9},{9,10},{10,1... | collective-permute-start | bytes 294920 | tf_op jit(solution)/shard_map/ppermute | solution.py:201
  33.8 8.4 %collective-permute-start.8 = (bf16[192,256]{1,0:T(8,128)(2,1)}, bf16[192,256]{1,0:T(8,128)(2,1)S(1)}, u32[]{:S(2)}, u32[]{:S(2)}) collective-permute-start(bf16[192,256]{1,0:T(8,128)(2,1)} %get-tuple-element.21), channel_id=1, source_target_pairs={{0,2},{1,3},{2,0},{3,1},{4,6},{5,7},{6,4},{7,5},{8,10},{9,11},{10,... | collective-permute-start | bytes 294920 | tf_op jit(solution)/shard_map/ppermute | solution.py:201
  35.0 7.2 %collective-permute-start.9 = (bf16[192,256]{1,0:T(8,128)(2,1)}, bf16[192,256]{1,0:T(8,128)(2,1)S(1)}, u32[]{:S(2)}, u32[]{:S(2)}) collective-permute-start(bf16[192,256]{1,0:T(8,128)(2,1)} %get-tuple-element.22), channel_id=1, source_target_pairs={{0,3},{1,0},{2,1},{3,2},{4,7},{5,4},{6,5},{7,6},{8,11},{9,8},{10,9... | collective-permute-start | bytes 294920 | tf_op jit(solution)/shard_map/ppermute | solution.py:201
  38.9 3.3 %copy-start.3 = (bf16[192,256]{1,0:T(8,128)(2,1)}, bf16[192,256]{1,0:T(8,128)(2,1)S(1)}, u32[]{:S(2)}) copy-start(bf16[192,256]{1,0:T(8,128)(2,1)S(1)} %collective-permute-done.7.rest_0_) | copy-start | bytes 294916
  42.2 0.6 %copy-start.4 = (bf16[192,256]{1,0:T(8,128)(2,1)}, bf16[192,256]{1,0:T(8,128)(2,1)S(1)}, u32[]{:S(2)}) copy-start(bf16[192,256]{1,0:T(8,128)(2,1)S(1)} %collective-permute-done.8.rest_1_) | copy-start | bytes 294916
  42.2 0.7 %copy-start.5 = (bf16[192,256]{1,0:T(8,128)(2,1)}, bf16[192,256]{1,0:T(8,128)(2,1)S(1)}, u32[]{:S(2)}) copy-start(bf16[192,256]{1,0:T(8,128)(2,1)S(1)} %collective-permute-done.9.rest_2_) | copy-start | bytes 294916
  45.9 11.0 %copy-start.2 = (f32[192,256]{1,0:T(8,128)S(1)}, f32[192,256]{1,0:T(8,128)}, u32[]{:S(2)}) copy-start(f32[192,256]{1,0:T(8,128)} %get-tuple-element.23) | copy-start | bytes 589828
  45.9 1.9 %collective-permute-start.10 = (bf16[4,192,256]{2,1,0:T(8,128)(2,1)}, bf16[4,192,256]{2,1,0:T(8,128)(2,1)S(1)}, u32[]{:S(2)}, u32[]{:S(2)}) collective-permute-start(bf16[4,192,256]{2,1,0:T(8,128)(2,1)} %get-tuple-element.24), channel_id=1, source_target_pairs={{0,4},{4,0},{8,12},{12,8},{16,20},{20,16},{24,28},{28,24},{1,5},{5... | collective-permute-start | bytes 1179656 | tf_op jit(solution)/shard_map/ppermute | solution.py:205
  49.0 6.5 %collective-permute-start.11 = (bf16[192,256]{1,0:T(8,128)(2,1)S(1)}, bf16[192,256]{1,0:T(8,128)(2,1)S(1)}, u32[]{:S(2)}, u32[]{:S(2)}) collective-permute-start(bf16[192,256]{1,0:T(8,128)(2,1)S(1)} %get-tuple-element.26), channel_id=1, source_target_pairs={{0,8},{4,12},{8,16},{12,20},{16,24},{20,28},{24,0},{28,4},{1,9},{5... | collective-permute-start | bytes 294920 | tf_op jit(solution)/shard_map/ppermute | solution.py:209
  51.0 5.8 %collective-permute-start.13 = (bf16[192,256]{1,0:T(8,128)(2,1)S(1)}, bf16[192,256]{1,0:T(8,128)(2,1)S(1)}, u32[]{:S(2)}, u32[]{:S(2)}) collective-permute-start(bf16[192,256]{1,0:T(8,128)(2,1)S(1)} %get-tuple-element.27), channel_id=1, source_target_pairs={{0,24},{4,28},{8,0},{12,4},{16,8},{20,12},{24,16},{28,20},{1,25},{... | collective-permute-start | bytes 294920 | tf_op jit(solution)/shard_map/ppermute | solution.py:209
  52.0 5.0 %collective-permute-start.12 = (bf16[192,256]{1,0:T(8,128)(2,1)S(1)}, bf16[192,256]{1,0:T(8,128)(2,1)S(1)}, u32[]{:S(2)}, u32[]{:S(2)}) collective-permute-start(bf16[192,256]{1,0:T(8,128)(2,1)S(1)} %get-tuple-element.28), channel_id=1, source_target_pairs={{0,16},{4,20},{8,24},{12,28},{16,0},{20,4},{24,8},{28,12},{1,17},{... | collective-permute-start | bytes 294920 | tf_op jit(solution)/shard_map/ppermute | solution.py:209
